TPU v7x, 128 devices: a whole 4x4x4 slice. The times are simulated.
128 devices in a mesh: req: 64 (over z, x, y), mlp: 2 (over core).
Axes of the slice: x: 4, y: 4, z: 4, core: 2. Of those that a mesh axis runs over, the one named last changes fastest.
Arguments:
- resid: bfloat16 [2048, 2048], P('req'), may hold values from -50 to 50
- q_in: bfloat16 [2048, 2048], P('req', 'mlp'), may hold values from -36 to 36
- kv_in: bfloat16 [2048, 2, 512], P('req', None, 'mlp'), may hold values from -36 to 36
- parents: int32 [128, 16], P('req'), may hold values from -1 to 14, as said below
- counts: int32 [128], P('req'), may hold values from 8 to 16, as said below
- accept_leaf: int32 [128], P('req'), may hold values from 0 to 15, as said below
- cache: bfloat16 [4096, 2, 128, 512], P('req', None, None, 'mlp'), may hold values from -6 to 6
- held_table: int32 [128, 48], P('req'), may hold values from 0 to 63, as said below
- held_len: int32 [128], P('req'), may hold values from 1 to 6144, as said below
- prev_owner: int32 [64], P('req'), may hold values from 0 to 63, as said below
- w_out: bfloat16 [2048, 2048], P('mlp'), may hold values from -0.125 to 0.125
- gain_mid: bfloat16 [2048], replicated, may hold values from 0.099609375 to 1.8984375
- w_in: bfloat16 [2, 8192, 2048], P(None, ('req', 'mlp')), may hold values from -0.125 to 0.125
- w_down: bfloat16 [8192, 2048], P(('req', 'mlp')), may hold values from -0.0625 to 0.0625
- gain_next: bfloat16 [2048], replicated, may hold values from 0.099609375 to 1.8984375
- w_next: bfloat16 [2048, 3072], P(None, 'mlp'), may hold values from -0.125 to 0.125
Outputs:
- hidden_out: bfloat16 [2048, 2048], P('req')
- next_qkv: bfloat16 [2048, 3072], P('req', 'mlp')
- accepted_kv: bfloat16 [2048, 2, 512], P('req', None, 'mlp')
Inputs may be any that keep to these rules, and one draw needn't show every extreme that they name: parents[r, 0] is -1; for i of 1 or more parents[r, i] lies in 0 to i - 1. Draft tokens 0 to counts[r] - 1 of request r are live; some request has 16. `accept_leaf`: a live draft token of the request. `held_len`: entry 2 d holds the length of request 2 d, entry 2 d + 1 that of request 2 e + 1 where prev_owner[e] = d; some entry is 6144; the pages used by the two caches of one index of req are distinct. `held_table`: rows 2 d and 2 d + 1 belong to index d of req, as in held_len. `prev_owner`: one cycle through all indices of req, so never d itself.
All inputs are finite; a program needn't handle non-finite values.
Results may differ from a plain program's by a relative error of at most 0.014.
Values may be sent and summed in bfloat16 or wider, within the bound.
No kernel may reach another device: no remote copies, remote signals or barrier semaphores. Data moves between devices by JAX's collectives and lax.ppermute only.
A program may use at most 128 MiB of HBM per device.

v0:
```python
import math

import jax
import jax.numpy as jnp
from jax import lax
from jax.sharding import PartitionSpec as P

HEAD_DIM = 64
GROUP = 4


norm_eps = 1e-05
masked_score = -1e30


def ancestors(parents):
    count_nodes = parents.shape[-1]
    nodes = jnp.arange(count_nodes, dtype=jnp.int32)
    reach = (parents[..., :, None] == nodes).astype(jnp.float32) + jnp.eye(
        count_nodes, dtype=jnp.float32
    )
    for step in range(count_nodes.bit_length()):
        reach = jnp.minimum(
            jnp.einsum("sij,sjk->sik", reach, reach, precision=lax.Precision.HIGHEST), 1.0
        )
    return reach


def rms_scale(rows, gain):
    values = rows.astype(jnp.float32)
    factor = lax.rsqrt(jnp.mean(values * values, axis=-1, keepdims=True) + norm_eps)
    return (values * factor * gain.astype(jnp.float32)).astype(jnp.bfloat16)


def swiglu_rows(rows, w_in, w_down):
    dims = (((1,), (1,)), ((), ()))
    gate = lax.dot_general(rows, w_in[0], dims, preferred_element_type=jnp.float32)
    up_part = lax.dot_general(rows, w_in[1], dims, preferred_element_type=jnp.float32)
    hidden = (jax.nn.silu(gate) * up_part).astype(jnp.bfloat16)
    return jnp.dot(hidden, w_down, preferred_element_type=jnp.float32)


def compact_path(reach, leaves, rows):
    count_nodes = reach.shape[-1]
    nodes = jnp.arange(count_nodes, dtype=jnp.int32)
    leaf_hot = (nodes[None, :] == leaves[:, None]).astype(jnp.float32)
    path = jnp.einsum("si,sij->sj", leaf_hot, reach, precision=lax.Precision.HIGHEST)
    ranks = jnp.cumsum(path, axis=1) - path
    places = nodes.astype(jnp.float32)
    select = path[:, None, :] * (ranks[:, None, :] == places[None, :, None]).astype(jnp.float32)
    return jnp.einsum(
        "spj,sjw->spw", select.astype(jnp.bfloat16), rows, preferred_element_type=jnp.float32
    ).astype(jnp.bfloat16)


def per_device(
    resid,
    q_in,
    kv_in,
    parents,
    counts,
    accept_leaf,
    cache,
    held_table,
    held_len,
    prev_owner,
    w_out,
    gain_mid,
    w_in,
    w_down,
    gain_next,
    w_next,
):
    tree_len = parents.shape[1]
    kv_width = kv_in.shape[2]
    kv_local = kv_width // HEAD_DIM
    scale = HEAD_DIM ** (-0.5)
    queries = q_in.reshape(2, tree_len, kv_local, GROUP, HEAD_DIM)
    every_query = lax.all_gather(q_in[tree_len:], "req", axis=0, tiled=True)
    owner_list = lax.all_gather(prev_owner, "req", axis=0, tiled=True)
    device_id = lax.axis_index("req")
    senders = jnp.arange(owner_list.shape[0], dtype=jnp.int32)
    sender = jnp.sum(jnp.where(owner_list == device_id, senders, 0))
    foreign = lax.dynamic_slice_in_dim(every_query, sender * tree_len, tree_len, 0)
    held_queries = jnp.stack([q_in[:tree_len], foreign]).reshape(
        2, tree_len, kv_local, GROUP, HEAD_DIM
    )
    page_len = cache.shape[2]
    block_pages = math.gcd(held_table.shape[1], max(1, 1024 // page_len))
    block_keys = block_pages * page_len
    num_blocks = held_table.shape[1] // block_pages
    positions = jnp.arange(block_keys, dtype=jnp.int32)

    def attend_block(block, state):
        running, total, accum = state
        page_ids = lax.dynamic_slice_in_dim(held_table, block * block_pages, block_pages, 1)
        gathered = cache[page_ids]
        key_rows = gathered[:, :, 0].reshape(2, block_keys, kv_local, HEAD_DIM)
        value_rows = gathered[:, :, 1].reshape(2, block_keys, kv_local, HEAD_DIM)
        scores = (
            jnp.einsum(
                "sqghe,skge->sghqk", held_queries, key_rows, preferred_element_type=jnp.float32
            )
            * scale
        )
        visible = (block * block_keys + positions)[None, :] < held_len[:, None]
        visible = visible[:, None, None, None, :]
        scores = jnp.where(visible, scores, masked_score)
        newest = jnp.maximum(running, jnp.max(scores, axis=-1))
        weights = jnp.where(visible, jnp.exp(scores - newest[..., None]), 0.0)
        factor = jnp.exp(running - newest)
        total = total * factor + jnp.sum(weights, axis=-1)
        update = jnp.einsum(
            "sghqk,skge->sghqe",
            weights,
            value_rows.astype(jnp.float32),
            precision=lax.Precision.HIGHEST,
        )
        accum = accum * factor[..., None] + update
        return (newest, total, accum)

    stat_shape = (2, kv_local, GROUP, tree_len)
    start_state = (
        jnp.full(stat_shape, masked_score, jnp.float32),
        jnp.zeros(stat_shape, jnp.float32),
        jnp.zeros(stat_shape + (HEAD_DIM,), jnp.float32),
    )
    running, total, accum = lax.fori_loop(0, num_blocks, attend_block, start_state)
    cache_out = accum / total[..., None]
    sent_out = jnp.transpose(cache_out[1], (2, 0, 1, 3)).reshape(
        tree_len, kv_local * GROUP * HEAD_DIM
    )
    sent_max = jnp.transpose(running[1], (2, 0, 1)).reshape(tree_len, kv_local * GROUP)
    sent_total = jnp.transpose(total[1], (2, 0, 1)).reshape(tree_len, kv_local * GROUP)
    back_out, back_max, back_total = (
        lax.all_gather(sent_out.astype(jnp.bfloat16), "req", axis=0, tiled=True).astype(
            sent_out.dtype
        ),
        lax.all_gather(sent_max.astype(jnp.bfloat16), "req", axis=0, tiled=True).astype(
            sent_max.dtype
        ),
        lax.all_gather(sent_total.astype(jnp.bfloat16), "req", axis=0, tiled=True).astype(
            sent_total.dtype
        ),
    )
    first_row = prev_owner[0] * tree_len
    recv_out = lax.dynamic_slice_in_dim(back_out, first_row, tree_len, 0).reshape(
        tree_len, kv_local, GROUP, HEAD_DIM
    )
    recv_max = lax.dynamic_slice_in_dim(back_max, first_row, tree_len, 0).reshape(
        tree_len, kv_local, GROUP
    )
    recv_total = lax.dynamic_slice_in_dim(back_total, first_row, tree_len, 0).reshape(
        tree_len, kv_local, GROUP
    )
    part_out = jnp.stack([cache_out[0], jnp.transpose(recv_out, (1, 2, 0, 3))])
    part_max = jnp.stack([running[0], jnp.transpose(recv_max, (1, 2, 0))])
    part_total = jnp.stack([total[0], jnp.transpose(recv_total, (1, 2, 0))])
    reach = ancestors(parents)
    live = jnp.arange(tree_len, dtype=jnp.int32)[None, :] < counts[:, None]
    allowed = ((reach > 0.5) & live[:, None, :])[:, None, None, :, :]
    draft_keys = kv_in[:, 0].reshape(2, tree_len, kv_local, HEAD_DIM)
    draft_values = kv_in[:, 1].reshape(2, tree_len, kv_local, HEAD_DIM)
    tree_scores = (
        jnp.einsum("sqghe,skge->sghqk", queries, draft_keys, preferred_element_type=jnp.float32)
        * scale
    )
    tree_scores = jnp.where(allowed, tree_scores, masked_score)
    tree_max = jnp.max(tree_scores, axis=-1)
    tree_weights = jnp.where(allowed, jnp.exp(tree_scores - tree_max[..., None]), 0.0)
    tree_total = jnp.sum(tree_weights, axis=-1)
    tree_accum = jnp.einsum(
        "sghqk,skge->sghqe",
        tree_weights,
        draft_values.astype(jnp.float32),
        precision=lax.Precision.HIGHEST,
    )
    overall = jnp.maximum(part_max, tree_max)
    cache_weight = part_total * jnp.exp(part_max - overall)
    tree_weight = jnp.exp(tree_max - overall)
    merged = (part_out * cache_weight[..., None] + tree_accum * tree_weight[..., None]) / (
        cache_weight + tree_total * tree_weight
    )[..., None]
    attended = (
        jnp.transpose(merged, (0, 3, 1, 2, 4))
        .reshape(2 * tree_len, kv_local * GROUP * HEAD_DIM)
        .astype(jnp.bfloat16)
    )
    partial_proj = jnp.dot(attended, w_out, preferred_element_type=jnp.float32)
    projected = lax.psum(partial_proj, "mlp")
    mixed = (resid.astype(jnp.float32) + projected).astype(jnp.bfloat16)
    normed = rms_scale(mixed, gain_mid)
    column = lax.axis_index("mlp")
    half_count = normed.shape[0] // lax.axis_size("mlp")
    every_row = lax.all_gather(normed, "req", axis=0, tiled=True)
    mlp_half = lax.psum_scatter(
        swiglu_rows(every_row, w_in, w_down), ("req", "mlp"), scatter_dimension=0, tiled=True
    )
    base_half = lax.dynamic_slice_in_dim(mixed, column * half_count, half_count, 0)
    out_half = (base_half.astype(jnp.float32) + mlp_half).astype(jnp.bfloat16)
    hidden_out = lax.all_gather(out_half, "mlp", axis=0, tiled=True)
    next_normed = rms_scale(hidden_out, gain_next)
    next_qkv = jnp.dot(next_normed, w_next, preferred_element_type=jnp.float32).astype(jnp.bfloat16)
    accepted = compact_path(reach, accept_leaf, kv_in.reshape(2, tree_len, 2 * kv_width))
    accepted_kv = accepted.reshape(2 * tree_len, 2, kv_width)
    return (hidden_out, next_qkv, accepted_kv)


def solution(mesh):
    placed = (
        P("req", None),
        P("req", "mlp"),
        P("req", None, "mlp"),
        P("req", None),
        P("req"),
        P("req"),
        P("req", None, None, "mlp"),
        P("req", None),
        P("req"),
        P("req"),
        P("mlp", None),
        P(),
        P(None, ("req", "mlp"), None),
        P(("req", "mlp"), None),
        P(),
        P(None, "mlp"),
    )
    return jax.shard_map(
        per_device,
        mesh=mesh,
        in_specs=placed,
        out_specs=(P("req", None), P("req", "mlp"), P("req", None, "mlp")),
        check_vma=False,
    )
```

profile of v0, /device:TPU:1, one launch (start us, length us, event | category | flops | bytes accessed | tf_op | source)
XLA Modules:
  0.0 1359.0 jit_solution(10207673933406862889)
XLA Ops:
  7.2 1.4 fusion.82
  9.4 1.2 dynamic-slice
  11.3 21.2 %all-reduce = s32[64]{0:T(128)S(1)} all-reduce(s32[64]{0:T(128)S(1)} %dynamic-update-slice), channel_id=1, replica_groups=mesh['req'=64,'mlp'=2] {'req'}, use_global_device_ids=true, to_apply=%add | all-reduce | flops 64 | bytes 512
  33.9 45.6 %all-gather.4.cloned.1.call-done = bf16[1024,1024]{1,0:T(8,128)(2,1)} async-done(((bf16[16,1024]{1,0:T(8,128)(2,1)}), bf16[1024,1024]{1,0:T(8,128)(2,1)}) %all-gather.4.cloned.1.call-update) | async-done | bytes 2097168 | tf_op jit(solution)/shard_map/all_gather | solution.py:79
  80.5 114.8 %while.18 = (s32[]{:T(128)}, f32[2,4,4,16]{3,2,1,0:T(4,128)}, f32[2,4,4,16]{3,2,1,0:T(4,128)}, f32[2,4,4,16,64]{4,3,2,1,0:T(8,128)}, s32[2]{0:T(128)}, /*index=5...) while((s32[]{:T(128)}, f32[2,4,4,16]{3,2,1,0:T(4,128)}, ...), condition=%wide.region_4.5_spmd.clone, body=%wide.region_1.4_spmd.clone.sunk | while | flops 476158528 | bytes 25580284 | solution.py:128
  81.3 4.1 gather_fusion
  85.4 1.2 fusion.112
  89.8 1.4 fusion.113
  92.5 1.7 copy.95
  94.2 1.3 reshape.267
  95.5 3.5 fusion.115
  100.4 4.1 gather_fusion
  104.5 1.2 fusion.112
  108.9 1.4 fusion.113
  111.6 1.7 copy.95
  113.3 1.3 reshape.267
  114.6 3.5 fusion.115
  119.6 4.1 gather_fusion
  123.6 1.2 fusion.112
  128.1 1.4 fusion.113
  130.7 1.7 copy.95
  132.4 1.3 reshape.267
  133.7 3.5 fusion.115
  138.7 4.1 gather_fusion
  147.2 1.4 fusion.113
  149.9 1.7 copy.95
  151.6 1.3 reshape.267
  152.9 3.5 fusion.115
  157.8 4.1 gather_fusion
  166.4 1.4 fusion.113
  169.0 1.7 copy.95
  170.7 1.3 reshape.267
  172.0 3.5 fusion.115
  177.0 4.1 gather_fusion
  185.5 1.4 fusion.113
  188.1 1.7 copy.95
  189.9 1.3 reshape.267
  191.1 3.5 fusion.115
  202.6 146.0 %all_gather.24 = bf16[1024,16]{1,0:T(8,128)(2,1)S(1)} all-gather(bf16[16,16]{1,0:T(8,128)(2,1)S(1)} %copy.53), channel_id=1, replica_groups=mesh['req'=64,'mlp'=2] {'req'}, dimensions={0}, use_global_device_ids=true | all-gather | bytes 33280 | tf_op jit(solution)/shard_map/all_gather | solution.py:142
  348.6 143.2 %all_gather.25 = bf16[1024,16]{1,0:T(8,128)(2,1)S(1)} all-gather(bf16[16,16]{1,0:T(8,128)(2,1)S(1)} %copy.55), channel_id=1, replica_groups=mesh['req'=64,'mlp'=2] {'req'}, dimensions={0}, use_global_device_ids=true | all-gather | bytes 33280 | tf_op jit(solution)/shard_map/all_gather | solution.py:139
  493.8 3.8 fusion.84
  497.6 75.8 %all-reduce.3.cloned.1.call-done = f32[32,2048]{1,0:T(8,128)} async-done(((f32[32,2048]{1,0:T(8,128)}), f32[32,2048]{1,0:T(8,128)}) %all-reduce.3.cloned.1.call-update) | async-done | bytes 262160 | tf_op jit(solution)/shard_map/psum | solution.py:190
  575.5 81.2 %all-gather.8.cloned.1.call-done = bf16[2048,2048]{1,0:T(8,128)(2,1)} async-done(((bf16[32,2048]{1,0:T(8,128)(2,1)}), bf16[2048,2048]{1,0:T(8,128)(2,1)}) %all-gather.8.cloned.1.call-update) | async-done | bytes 8388624 | tf_op jit(solution)/shard_map/all_gather | solution.py:195
  656.8 6.0 fusion.44
  662.8 14.1 %fusion.28 = f32[2048,2048]{1,0:T(8,128)} fusion(bf16[64,2048]{1,0:T(8,128)(2,1)S(1)} %copy-done, bf16[2048,2048]{1,0:T(8,128)(2,1)} %all-gather.8.cloned.1.call-done, f32[2048,64]{0,1:T(8,128)S(1)} %fusion.44, bf16[2,64,2048]{2,1,0:T(8,128)(2,1)S(1)} %copy-done.7), kind=kOutput, calls=%fused_computation.40 | convolution fusion | flops 1074528256 | bytes 26214400 | tf_op jit(solution)/shard_map/dot_general | solution.py:40
  679.0 657.7 %reduce-scatter.2.cloned.1.call-done = f32[16,2048]{1,0:T(8,128)} async-done(((f32[2048,2048]{1,0:T(8,128)}), f32[16,2048]{1,0:T(8,128)}) %reduce-scatter.2.cloned.1.call-update) | async-done | bytes 131088 | tf_op jit(solution)/shard_map/reduce_scatter | solution.py:196
  1337.6 9.4 all_gather.27
  1347.2 4.7 convolution_convert_fusion
  (223 shorter events, 56.6 us)
Async XLA Ops:
  7.2 655.7 %copy-start = (bf16[64,2048]{1,0:T(8,128)(2,1)S(1)}, bf16[64,2048]{1,0:T(8,128)(2,1)}, u32[]{:S(2)}) copy-start(bf16[64,2048]{1,0:T(8,128)(2,1)} %param.31) | copy-start | bytes 786436
  7.2 72.3 %all-gather.4.cloned.1.call-start = ((), (), s32[]{:S(2)}) async-start(), calls=%async_computation.1 | async-start | bytes 2129920 | tf_op jit(solution)/shard_map/all_gather | solution.py:79
  8.7 483.4 %all-gather.6.cloned.1.call-start = ((), (), s32[]{:S(2)}) async-start(), calls=%async_computation.2 | async-start | bytes 2129920 | tf_op jit(solution)/shard_map/all_gather | solution.py:136
  86.6 1.3 copy-start.10
  87.9 1.1 copy-start.3
  89.1 2.2 copy-start.1
  89.1 2.2 copy-start.4
  91.9 0.6 copy-start.5
  105.6 1.3 copy-start.10
  107.0 1.1 copy-start.3
  108.1 2.2 copy-start.1
  108.1 2.2 copy-start.4
  111.0 0.6 copy-start.5
  124.8 1.3 copy-start.10
  126.1 1.1 copy-start.3
  127.3 2.2 copy-start.1
  127.3 2.2 copy-start.4
  130.1 0.6 copy-start.5
  143.9 1.3 copy-start.10
  145.3 1.1 copy-start.3
  146.4 2.2 copy-start.1
  146.4 2.2 copy-start.4
  149.3 0.6 copy-start.5
  163.1 1.3 copy-start.10
  164.4 1.1 copy-start.3
  165.6 2.2 copy-start.1
  165.6 2.2 copy-start.4
  168.4 0.6 copy-start.5
  182.2 1.3 copy-start.10
  183.6 1.1 copy-start.3
  184.7 2.2 copy-start.1
  184.7 2.2 copy-start.4
  187.5 0.6 copy-start.5
  195.3 7.1 copy-start.6
  195.3 7.1 copy-start.2
  197.2 376.2 %all-reduce.3.cloned.1.call-start = ((), (), s32[]{:S(2)}) async-start(), calls=%async_computation.3 | async-start | bytes 524288 | tf_op jit(solution)/shard_map/psum | solution.py:190
  493.7 3.9 copy-start.11
  493.7 79.7 %copy-start.9 = (bf16[32,2048]{1,0:T(8,128)(2,1)S(1)}, bf16[32,2048]{1,0:T(8,128)(2,1)}, u32[]{:S(2)}) copy-start(bf16[32,2048]{1,0:T(8,128)(2,1)} %param.18) | copy-start | bytes 393220
  493.8 163.0 %copy-start.7 = (bf16[2,64,2048]{2,1,0:T(8,128)(2,1)S(1)}, bf16[2,64,2048]{2,1,0:T(8,128)(2,1)}, u32[]{:S(2)}) copy-start(bf16[2,64,2048]{2,1,0:T(8,128)(2,1)} %param.30) | copy-start | bytes 1572868
  497.6 159.2 %all-gather.8.cloned.1.call-start = ((), (), s32[]{:S(2)}) async-start(), calls=%async_computation.4 | async-start | bytes 8519680 | tf_op jit(solution)/shard_map/all_gather | solution.py:195
  575.3 761.4 %reduce-scatter.2.cloned.1.call-start = ((), (), s32[]{:S(2)}) async-start(), calls=%async_computation.5 | async-start | bytes 16908288 | tf_op jit(solution)/shard_map/reduce_scatter | solution.py:196
  676.9 0.8 copy-start.8
  676.9 0.8 copy-start.12
  676.9 0.8 copy-start.13
Sparse Core Ops, SparseCore 0:
  11.5 67.9 all-gather.3
  197.3 63.2 all-gather.5
  497.7 75.6 all-reduce.2
  577.1 79.6 all-gather.7
  677.1 659.5 reduce-scatter.1
where the time goes:
time: 1360 us
  waiting for transfers between devices  860 us (63%)
  blocking collectives  320 us (24%)
  local copies, waits for them, and re-layouts  74.7 us (5%)
  matrix products  59.4 us (4%)
  other arithmetic  28.5 us (2%)
  between operations  15.3 us (1%)
    reduce_scatter x1, waiting for transfers between devices, per_device(): lax.psum_scatter(swiglu_rows(every_row, w_in, w_down), ('req', 'mlp'), sc...  658 us
    all_gather x1, blocking collectives, per_device(): lax.all_gather(sent_total.astype(jnp.bfloat16), 'req', axis=0, tiled=True)  146 us
    all_gather x1, blocking collectives, per_device(): lax.all_gather(sent_max.astype(jnp.bfloat16), 'req', axis=0, tiled=True)  143 us
    all_gather x1, waiting for transfers between devices, per_device(): every_row = lax.all_gather(normed, 'req', axis=0, tiled=True)  81.2 us
    psum x1, waiting for transfers between devices, per_device(): projected = lax.psum(partial_proj, 'mlp')  75.8 us
    all_gather x1, waiting for transfers between devices, per_device(): every_query = lax.all_gather(q_in[tree_len:], 'req', axis=0, tiled=True)  45.6 us
  transfers between devices with their start and end apart: 5, of which 4 were waited for; matrix products, arithmetic and copies ran while one was open for 1% of the time, Pallas kernels for 0%

commit v1 on v0

--- a/solution.py
+++ b/solution.py
@@ -3,14 +3,24 @@
 import jax
 import jax.numpy as jnp
 from jax import lax
-from jax.sharding import PartitionSpec as P
+from jax.sharding import Mesh, PartitionSpec as P
 
 HEAD_DIM = 64
 GROUP = 4
 
 
+TAG = 128
+REQ = ("a", "b")
+GROUP_SPLIT = 4
+
 norm_eps = 1e-05
 masked_score = -1e30
+
+
+def split_hi_lo(values):
+    high = values.astype(jnp.bfloat16)
+    low = (values - high.astype(jnp.float32)).astype(jnp.bfloat16)
+    return jnp.concatenate([high, low], axis=1)
 
 
 def ancestors(parents):
@@ -76,12 +86,15 @@
     kv_local = kv_width // HEAD_DIM
     scale = HEAD_DIM ** (-0.5)
     queries = q_in.reshape(2, tree_len, kv_local, GROUP, HEAD_DIM)
-    every_query = lax.all_gather(q_in[tree_len:], "req", axis=0, tiled=True)
-    owner_list = lax.all_gather(prev_owner, "req", axis=0, tiled=True)
-    device_id = lax.axis_index("req")
-    senders = jnp.arange(owner_list.shape[0], dtype=jnp.int32)
-    sender = jnp.sum(jnp.where(owner_list == device_id, senders, 0))
-    foreign = lax.dynamic_slice_in_dim(every_query, sender * tree_len, tree_len, 0)
+    device_id = lax.axis_index(REQ)
+    q_width = q_in.shape[1]
+    dest_col = jnp.broadcast_to(prev_owner[0].astype(q_in.dtype), (tree_len, TAG))
+    q_packet = jnp.concatenate([q_in[tree_len:], dest_col], axis=1)
+    every_query = lax.all_gather(q_packet, REQ, axis=0, tiled=False)
+    dests = every_query[:, 0, q_width].astype(jnp.int32)
+    senders = jnp.arange(dests.shape[0], dtype=jnp.int32)
+    sender = jnp.sum(jnp.where(dests == device_id, senders, 0))
+    foreign = lax.dynamic_index_in_dim(every_query, sender, 0, keepdims=False)[:, :q_width]
     held_queries = jnp.stack([q_in[:tree_len], foreign]).reshape(
         2, tree_len, kv_local, GROUP, HEAD_DIM
     )
@@ -125,32 +138,31 @@
         jnp.zeros(stat_shape, jnp.float32),
         jnp.zeros(stat_shape + (HEAD_DIM,), jnp.float32),
     )
+    own_w = jnp.stack([w_in[0], w_in[1], w_down])
+    all_w = lax.all_gather(own_w, "a", axis=0, tiled=False)
     running, total, accum = lax.fori_loop(0, num_blocks, attend_block, start_state)
+    all_w, running, total, accum = lax.optimization_barrier((all_w, running, total, accum))
     cache_out = accum / total[..., None]
     sent_out = jnp.transpose(cache_out[1], (2, 0, 1, 3)).reshape(
         tree_len, kv_local * GROUP * HEAD_DIM
     )
     sent_max = jnp.transpose(running[1], (2, 0, 1)).reshape(tree_len, kv_local * GROUP)
     sent_total = jnp.transpose(total[1], (2, 0, 1)).reshape(tree_len, kv_local * GROUP)
-    back_out, back_max, back_total = (
-        lax.all_gather(sent_out.astype(jnp.bfloat16), "req", axis=0, tiled=True).astype(
-            sent_out.dtype
-        ),
-        lax.all_gather(sent_max.astype(jnp.bfloat16), "req", axis=0, tiled=True).astype(
-            sent_max.dtype
-        ),
-        lax.all_gather(sent_total.astype(jnp.bfloat16), "req", axis=0, tiled=True).astype(
-            sent_total.dtype
-        ),
-    )
-    first_row = prev_owner[0] * tree_len
-    recv_out = lax.dynamic_slice_in_dim(back_out, first_row, tree_len, 0).reshape(
-        tree_len, kv_local, GROUP, HEAD_DIM
-    )
-    recv_max = lax.dynamic_slice_in_dim(back_max, first_row, tree_len, 0).reshape(
+    stats = jnp.concatenate(
+        [split_hi_lo(sent_max), split_hi_lo(sent_total)], axis=1
+    )
+    pad = jnp.zeros((tree_len, TAG - stats.shape[1]), jnp.bfloat16)
+    r_packet = jnp.concatenate([sent_out.astype(jnp.bfloat16), stats, pad], axis=1)
+    back = lax.all_gather(r_packet, REQ, axis=0, tiled=False)
+    got = lax.dynamic_index_in_dim(back, prev_owner[0], 0, keepdims=False).astype(jnp.float32)
+    heads = kv_local * GROUP
+    o_w = heads * HEAD_DIM
+    recv_out = got[:, :o_w].reshape(tree_len, kv_local, GROUP, HEAD_DIM)
+    recv_max = (got[:, o_w : o_w + heads] + got[:, o_w + heads : o_w + 2 * heads]).reshape(
         tree_len, kv_local, GROUP
     )
-    recv_total = lax.dynamic_slice_in_dim(back_total, first_row, tree_len, 0).reshape(
+    t0 = o_w + 2 * heads
+    recv_total = (got[:, t0 : t0 + heads] + got[:, t0 + heads : t0 + 2 * heads]).reshape(
         tree_len, kv_local, GROUP
     )
     part_out = jnp.stack([cache_out[0], jnp.transpose(recv_out, (1, 2, 0, 3))])
@@ -192,10 +204,16 @@
     normed = rms_scale(mixed, gain_mid)
     column = lax.axis_index("mlp")
     half_count = normed.shape[0] // lax.axis_size("mlp")
-    every_row = lax.all_gather(normed, "req", axis=0, tiled=True)
-    mlp_half = lax.psum_scatter(
-        swiglu_rows(every_row, w_in, w_down), ("req", "mlp"), scatter_dimension=0, tiled=True
-    )
+    group_rows = lax.all_gather(normed, "b", axis=0, tiled=True)
+    dims = (((1,), (2,)), ((), ()))
+    gate = lax.dot_general(group_rows, all_w[:, 0], dims, preferred_element_type=jnp.float32)
+    up_part = lax.dot_general(group_rows, all_w[:, 1], dims, preferred_element_type=jnp.float32)
+    hidden = (jax.nn.silu(gate) * up_part).astype(jnp.bfloat16)
+    down_dims = (((1, 2), (0, 1)), ((), ()))
+    partial = lax.dot_general(
+        hidden, all_w[:, 2], down_dims, preferred_element_type=jnp.float32
+    )
+    mlp_half = lax.psum_scatter(partial, ("b", "mlp"), scatter_dimension=0, tiled=True)
     base_half = lax.dynamic_slice_in_dim(mixed, column * half_count, half_count, 0)
     out_half = (base_half.astype(jnp.float32) + mlp_half).astype(jnp.bfloat16)
     hidden_out = lax.all_gather(out_half, "mlp", axis=0, tiled=True)
@@ -207,28 +225,34 @@
 
 
 def solution(mesh):
+    devices = mesh.devices
+    owners = devices.shape[0]
+    sub_mesh = Mesh(
+        devices.reshape(owners // GROUP_SPLIT, GROUP_SPLIT, devices.shape[1]), ("a", "b", "mlp")
+    )
+    R = REQ
     placed = (
-        P("req", None),
-        P("req", "mlp"),
-        P("req", None, "mlp"),
-        P("req", None),
-        P("req"),
-        P("req"),
-        P("req", None, None, "mlp"),
-        P("req", None),
-        P("req"),
-        P("req"),
+        P(R, None),
+        P(R, "mlp"),
+        P(R, None, "mlp"),
+        P(R, None),
+        P(R),
+        P(R),
+        P(R, None, None, "mlp"),
+        P(R, None),
+        P(R),
+        P(R),
         P("mlp", None),
         P(),
-        P(None, ("req", "mlp"), None),
-        P(("req", "mlp"), None),
+        P(None, R + ("mlp",), None),
+        P(R + ("mlp",), None),
         P(),
         P(None, "mlp"),
     )
     return jax.shard_map(
         per_device,
-        mesh=mesh,
+        mesh=sub_mesh,
         in_specs=placed,
-        out_specs=(P("req", None), P("req", "mlp"), P("req", None, "mlp")),
+        out_specs=(P(R, None), P(R, "mlp"), P(R, None, "mlp")),
         check_vma=False,
     )

time: 1360 us -> 341 us (0.25)
  waiting for transfers between devices: 860 us -> 183 us
  blocking collectives: 320 us -> 16.3 us
  other arithmetic: 28.5 us -> 12.5 us
  matrix products: 59.4 us -> 45.5 us
    reduce_scatter x1, waiting for transfers between devices: 658 us -> 30.8 us  [per_device(): lax.psum_scatter(partial, ('b', 'mlp'), scatter_dimension=0, tiled=True)]
    all_gather x2 -> x1, blocking collectives: 289 us -> 11.3 us  [per_device(): group_rows = lax.all_gather(normed, 'b', axis=0, tiled=True)]
    psum x1, waiting for transfers between devices: 75.8 us -> 22.7 us  [per_device(): projected = lax.psum(partial_proj, 'mlp')]
    unnamed x1 -> x0, blocking collectives: 21.2 us -> none
  transfers between devices with their start and end apart: 5 -> 5, of which waited for: 4 -> 4; matrix products, arithmetic and copies ran while one was open for 1% -> 28% of each run, Pallas kernels for 0% -> 0%
where the time goes in v1:
time: 341 us; the launch traced here: 340 us
  waiting for transfers between devices  183 us (54%)
  local copies, waits for them, and re-layouts  66 us (19%)
  matrix products  45.5 us (13%)
  between operations  16.7 us (5%)
  blocking collectives  16.3 us (5%)
  other arithmetic  12.5 us (4%)
    all_gather x1, waiting for transfers between devices, per_device(): every_query = lax.all_gather(q_packet, REQ, axis=0, tiled=False)  68 us
    all_gather x1, waiting for transfers between devices, per_device(): back = lax.all_gather(r_packet, REQ, axis=0, tiled=False)  61.1 us
    reduce_scatter x1, waiting for transfers between devices, per_device(): lax.psum_scatter(partial, ('b', 'mlp'), scatter_dimension=0, tiled=True)  30.8 us
    gather x6, local copies, waits for them, and re-layouts, attend_block(): gathered = cache[page_ids]  25.6 us
    psum x1, waiting for transfers between devices, per_device(): projected = lax.psum(partial_proj, 'mlp')  22.7 us
    dot_general x6, matrix products, attend_block(): jnp.einsum('sghqk,skge->sghqe', weights, value_rows.astype(jnp.float32),...  21 us
    while x18, local copies, waits for them, and re-layouts  14.8 us
    all_gather x1, blocking collectives, per_device(): group_rows = lax.all_gather(normed, 'b', axis=0, tiled=True)  11.3 us
  transfers between devices with their start and end apart: 5, of which 4 were waited for; matrix products, arithmetic and copies ran while one was open for 28% of the time, Pallas kernels for 0%

profile of v1, /device:TPU:1, one launch (start us, length us, event | category | flops | bytes accessed | tf_op | source)
XLA Modules:
  0.0 340.2 jit_solution(6118323654761980903)
XLA Ops:
  7.9 0.8 fusion.82
  9.4 2.1 pad_maximum_fusion
  11.7 68.0 %all-gather.9.cloned.1.call-done = bf16[1024,1152]{1,0:T(8,128)(2,1)} async-done(((bf16[16,1152]{1,0:T(8,128)(2,1)}), bf16[1024,1152]{1,0:T(8,128)(2,1)}) %all-gather.9.cloned.1.call-update) | async-done | bytes 2359312 | tf_op jit(solution)/shard_map/all_gather | solution.py:93
  79.7 0.9 slice.104
  83.3 0.8 dynamic-slice_bitcast_fusion
  84.4 88.6 %while.18 = (s32[]{:T(128)}, f32[2,4,4,16]{3,2,1,0:T(4,128)S(1)}, f32[2,4,4,16]{3,2,1,0:T(4,128)S(1)}, f32[2,4,4,16,64]{4,3,2,1,0:T(8,128)}, s32[2]{0:T(128)S(1)...) while((s32[]{:T(128)}, f32[2,4,4,16]{3,2,1,0:T(4,128)S(1)}, ...), condition=%wide.region_4.5_spmd.clone, body=%wide.region_1.4_spmd.clone.sunk | while | flops 476158528 | bytes 25547344 | solution.py:143
  84.6 4.1 %gather_fusion = bf16[16,2,128,256]{3,2,1,0:T(8,128)(2,1)S(1)} fusion(bf16[64,2,128,256]{3,2,1,0:T(8,128)(2,1)} %get-tuple-element.363, s32[1024]{0:T(1024)S(1)} %pad_clamp_fusion.2), kind=kCustom, calls=%fused_computation.clone.clone.1 | custom fusion | bytes 4194368 | tf_op jit(solution)/shard_map/while/body/eval_jaxpr/gather | solution.py:110
  88.6 1.2 fusion.114
  92.4 1.7 copy.129
  94.1 1.3 reshape.273
  95.4 3.5 %fusion.117 = f32[2,4,4,16,64]{4,3,2,1,0:T(8,128)} fusion(f32[2,4,1024,16,4]{2,3,4,1,0:T(8,128)S(1)} %get-tuple-element.327, bf16[2,1024,4,64,1]{1,3,2,0,4:T(8,128)(2,1)} %reshape.273, f32[2,4,4,16]{3,2,1,0:T(4,128)S(1)} %select_maximum_fusion.2, pred[2,1024]{1,0:T(4,128)(4,1)S(1)} %broadcast_compare_fusion.2, ...), kind=kOutput, calls=%fused_computation.9.clone.1 | convolution fusion | flops 404848640 | bytes 3414017 | tf_op jit(solution)/shard_map/while/body/eval_jaxpr/sghqk,skge->sghqe/dot_general | solution.py:126
  99.1 4.2 %gather_fusion = bf16[16,2,128,256]{3,2,1,0:T(8,128)(2,1)S(1)} fusion(bf16[64,2,128,256]{3,2,1,0:T(8,128)(2,1)} %get-tuple-element.363, s32[1024]{0:T(1024)S(1)} %pad_clamp_fusion.2), kind=kCustom, calls=%fused_computation.clone.clone.1 | custom fusion | bytes 4194368 | tf_op jit(solution)/shard_map/while/body/eval_jaxpr/gather | solution.py:110
  103.3 1.2 fusion.114
  107.1 1.7 copy.129
  108.8 1.3 reshape.273
  110.1 3.5 %fusion.117 = f32[2,4,4,16,64]{4,3,2,1,0:T(8,128)} fusion(f32[2,4,1024,16,4]{2,3,4,1,0:T(8,128)S(1)} %get-tuple-element.327, bf16[2,1024,4,64,1]{1,3,2,0,4:T(8,128)(2,1)} %reshape.273, f32[2,4,4,16]{3,2,1,0:T(4,128)S(1)} %select_maximum_fusion.2, pred[2,1024]{1,0:T(4,128)(4,1)S(1)} %broadcast_compare_fusion.2, ...), kind=kOutput, calls=%fused_computation.9.clone.1 | convolution fusion | flops 404848640 | bytes 3414017 | tf_op jit(solution)/shard_map/while/body/eval_jaxpr/sghqk,skge->sghqe/dot_general | solution.py:126
  113.8 4.8 %gather_fusion = bf16[16,2,128,256]{3,2,1,0:T(8,128)(2,1)S(1)} fusion(bf16[64,2,128,256]{3,2,1,0:T(8,128)(2,1)} %get-tuple-element.363, s32[1024]{0:T(1024)S(1)} %pad_clamp_fusion.2), kind=kCustom, calls=%fused_computation.clone.clone.1 | custom fusion | bytes 4194368 | tf_op jit(solution)/shard_map/while/body/eval_jaxpr/gather | solution.py:110
  118.6 1.2 fusion.114
  122.3 1.7 copy.129
  124.1 1.3 reshape.273
  125.4 3.5 %fusion.117 = f32[2,4,4,16,64]{4,3,2,1,0:T(8,128)} fusion(f32[2,4,1024,16,4]{2,3,4,1,0:T(8,128)S(1)} %get-tuple-element.327, bf16[2,1024,4,64,1]{1,3,2,0,4:T(8,128)(2,1)} %reshape.273, f32[2,4,4,16]{3,2,1,0:T(4,128)S(1)} %select_maximum_fusion.2, pred[2,1024]{1,0:T(4,128)(4,1)S(1)} %broadcast_compare_fusion.2, ...), kind=kOutput, calls=%fused_computation.9.clone.1 | convolution fusion | flops 404848640 | bytes 3414017 | tf_op jit(solution)/shard_map/while/body/eval_jaxpr/sghqk,skge->sghqe/dot_general | solution.py:126
  129.1 4.2 %gather_fusion = bf16[16,2,128,256]{3,2,1,0:T(8,128)(2,1)S(1)} fusion(bf16[64,2,128,256]{3,2,1,0:T(8,128)(2,1)} %get-tuple-element.363, s32[1024]{0:T(1024)S(1)} %pad_clamp_fusion.2), kind=kCustom, calls=%fused_computation.clone.clone.1 | custom fusion | bytes 4194368 | tf_op jit(solution)/shard_map/while/body/eval_jaxpr/gather | solution.py:110
  133.3 1.2 fusion.114
  137.1 1.7 copy.129
  138.8 1.3 reshape.273
  140.1 3.5 %fusion.117 = f32[2,4,4,16,64]{4,3,2,1,0:T(8,128)} fusion(f32[2,4,1024,16,4]{2,3,4,1,0:T(8,128)S(1)} %get-tuple-element.327, bf16[2,1024,4,64,1]{1,3,2,0,4:T(8,128)(2,1)} %reshape.273, f32[2,4,4,16]{3,2,1,0:T(4,128)S(1)} %select_maximum_fusion.2, pred[2,1024]{1,0:T(4,128)(4,1)S(1)} %broadcast_compare_fusion.2, ...), kind=kOutput, calls=%fused_computation.9.clone.1 | convolution fusion | flops 404848640 | bytes 3414017 | tf_op jit(solution)/shard_map/while/body/eval_jaxpr/sghqk,skge->sghqe/dot_general | solution.py:126
  143.8 4.2 %gather_fusion = bf16[16,2,128,256]{3,2,1,0:T(8,128)(2,1)S(1)} fusion(bf16[64,2,128,256]{3,2,1,0:T(8,128)(2,1)} %get-tuple-element.363, s32[1024]{0:T(1024)S(1)} %pad_clamp_fusion.2), kind=kCustom, calls=%fused_computation.clone.clone.1 | custom fusion | bytes 4194368 | tf_op jit(solution)/shard_map/while/body/eval_jaxpr/gather | solution.py:110
  148.0 1.2 fusion.114
  151.8 1.7 copy.129
  153.5 1.3 reshape.273
  154.8 3.5 %fusion.117 = f32[2,4,4,16,64]{4,3,2,1,0:T(8,128)} fusion(f32[2,4,1024,16,4]{2,3,4,1,0:T(8,128)S(1)} %get-tuple-element.327, bf16[2,1024,4,64,1]{1,3,2,0,4:T(8,128)(2,1)} %reshape.273, f32[2,4,4,16]{3,2,1,0:T(4,128)S(1)} %select_maximum_fusion.2, pred[2,1024]{1,0:T(4,128)(4,1)S(1)} %broadcast_compare_fusion.2, ...), kind=kOutput, calls=%fused_computation.9.clone.1 | convolution fusion | flops 404848640 | bytes 3414017 | tf_op jit(solution)/shard_map/while/body/eval_jaxpr/sghqk,skge->sghqe/dot_general | solution.py:126
  158.6 4.1 %gather_fusion = bf16[16,2,128,256]{3,2,1,0:T(8,128)(2,1)S(1)} fusion(bf16[64,2,128,256]{3,2,1,0:T(8,128)(2,1)} %get-tuple-element.363, s32[1024]{0:T(1024)S(1)} %pad_clamp_fusion.2), kind=kCustom, calls=%fused_computation.clone.clone.1 | custom fusion | bytes 4194368 | tf_op jit(solution)/shard_map/while/body/eval_jaxpr/gather | solution.py:110
  162.6 1.2 fusion.114
  166.4 1.7 copy.129
  168.1 1.3 reshape.273
  169.4 3.5 %fusion.117 = f32[2,4,4,16,64]{4,3,2,1,0:T(8,128)} fusion(f32[2,4,1024,16,4]{2,3,4,1,0:T(8,128)S(1)} %get-tuple-element.327, bf16[2,1024,4,64,1]{1,3,2,0,4:T(8,128)(2,1)} %reshape.273, f32[2,4,4,16]{3,2,1,0:T(4,128)S(1)} %select_maximum_fusion.2, pred[2,1024]{1,0:T(4,128)(4,1)S(1)} %broadcast_compare_fusion.2, ...), kind=kOutput, calls=%fused_computation.9.clone.1 | convolution fusion | flops 404848640 | bytes 3414017 | tf_op jit(solution)/shard_map/while/body/eval_jaxpr/sghqk,skge->sghqe/dot_general | solution.py:126
  173.1 1.1 broadcast_divide_fusion
  177.2 61.1 %all-gather.11.cloned.1.call-done = bf16[1024,1152]{1,0:T(8,128)(2,1)} async-done(((bf16[16,1152]{1,0:T(8,128)(2,1)}), bf16[1024,1152]{1,0:T(8,128)(2,1)}) %all-gather.11.cloned.1.call-update) | async-done | bytes 2359312 | tf_op jit(solution)/shard_map/all_gather | solution.py:156
  240.2 3.8 %fusion.86 = f32[32,2048]{1,0:T(8,128)} fusion(bf16[32,1024]{1,0:T(8,128)(2,1)S(1)} %convert_element_type.133, bf16[1024,2048]{1,0:T(8,128)(2,1)} %param.28), kind=kOutput, calls=%fused_computation.137 | convolution fusion | flops 134217728 | bytes 4521984 | tf_op jit(solution)/shard_map/dot_general | solution.py:201
  244.1 22.7 %all-reduce.3.cloned.1.call-done = f32[32,2048]{1,0:T(8,128)} async-done(((f32[32,2048]{1,0:T(8,128)}), f32[32,2048]{1,0:T(8,128)}) %all-reduce.3.cloned.1.call-update) | async-done | bytes 262160 | tf_op jit(solution)/shard_map/psum | solution.py:202
  266.8 1.1 fusion.43
  268.0 11.3 %all_gather.30 = bf16[128,2048]{1,0:T(8,128)(2,1)S(1)} all-gather(bf16[32,2048]{1,0:T(8,128)(2,1)S(1)} %fusion.45), channel_id=1, replica_groups=mesh['a'=16,'b'=4,'mlp'=2] {'b'}, dimensions={0}, use_global_device_ids=true | all-gather | bytes 655360 | tf_op jit(solution)/shard_map/all_gather | solution.py:207
  279.3 3.4 %fusion.25 = f32[128,16,64]{0,2,1:T(8,128)S(1)} fusion(bf16[128,2048]{1,0:T(8,128)(2,1)S(1)} %all_gather.30, bf16[16,3,64,2048]{3,2,1,0:T(8,128)(2,1)} %bitcast.156), kind=kOutput, calls=%fused_computation.36 | convolution fusion | flops 536870912 | bytes 5242880 | tf_op jit(solution)/shard_map/dot_general | solution.py:209
  282.8 7.3 %fusion.26 = f32[128,2048]{1,0:T(8,128)} fusion(bf16[128,2048]{1,0:T(8,128)(2,1)S(1)} %all_gather.30, f32[128,16,64]{0,2,1:T(8,128)S(1)} %fusion.25, bf16[16,3,64,2048]{3,2,1,0:T(8,128)(2,1)} %bitcast.157), kind=kOutput, calls=%fused_computation.37 | convolution fusion | flops 1074528256 | bytes 10485760 | tf_op jit(solution)/shard_map/dot_general | solution.py:213
  291.4 30.8 %reduce-scatter.2.cloned.1.call-done = f32[16,2048]{1,0:T(8,128)} async-done(((f32[128,2048]{1,0:T(8,128)}), f32[16,2048]{1,0:T(8,128)}) %reduce-scatter.2.cloned.1.call-update) | async-done | bytes 131088 | tf_op jit(solution)/shard_map/reduce_scatter | solution.py:216
  322.3 0.9 add_convert_fusion.1
  323.2 5.0 %all_gather.31 = bf16[32,2048]{1,0:T(8,128)(2,1)S(1)} all-gather(bf16[16,2048]{1,0:T(8,128)(2,1)S(1)} %add_convert_fusion.1), channel_id=1, replica_groups=mesh['a'=16,'b'=4,'mlp'=2] {'mlp'}, dimensions={0}, use_global_device_ids=true | all-gather | bytes 196608 | tf_op jit(solution)/shard_map/all_gather | solution.py:219
  328.4 4.7 %convolution_convert_fusion = bf16[32,1536]{1,0:T(8,128)(2,1)} fusion(bf16[2048,1536]{1,0:T(8,128)(2,1)} %param.33, bf16[32,2048]{1,0:T(8,128)(2,1)S(1)} %all_gather.31, f32[2048]{0:T(1024)S(1)} %convert_element_type.142, f32[32]{0:T(128)S(1)} %add_rsqrt_fusion), kind=kOutput, calls=%fused_computation.38 | convolution fusion | flops 201637888 | bytes 6529152 | tf_op jit(solution)/shard_map/dot_general | solution.py:221
  (165 shorter events, 25.2 us)
Async XLA Ops:
  7.2 77.2 %copy-start.3 = (s32[2,48]{1,0:T(2,128)S(1)}, s32[2,48]{1,0:T(2,128)}, u32[]{:S(2)}) copy-start(s32[2,48]{1,0:T(2,128)} %param.25) | copy-start | bytes 1156
  7.2 77.2 %copy-start.4 = (s32[2]{0:T(128)S(1)}, s32[2]{0:T(128)}, u32[]{:S(2)}) copy-start(s32[2]{0:T(128)} %param.26) | copy-start | bytes 28
  7.2 72.5 %all-gather.9.cloned.1.call-start = ((), (), s32[]{:S(2)}) async-start(), calls=%async_computation.4 | async-start | bytes 2396160 | tf_op jit(solution)/shard_map/all_gather | solution.py:93
  9.3 163.6 %all-gather.7.cloned.1.call-start = ((), (), s32[]{:S(2)}) async-start(), calls=%async_computation.3 | async-start | bytes 13369344 | tf_op jit(solution)/shard_map/all_gather | solution.py:142
  11.5 226.8 %all-gather.11.cloned.1.call-start = ((), (), s32[]{:S(2)}) async-start(), calls=%async_computation.5 | async-start | bytes 2396160 | tf_op jit(solution)/shard_map/all_gather | solution.py:156
  84.3 90.8 %copy-start.1 = (bf16[32,1024]{1,0:T(8,128)(2,1)S(1)}, bf16[32,1024]{1,0:T(8,128)(2,1)}, u32[]{:S(2)}) copy-start(bf16[32,1024]{1,0:T(8,128)(2,1)} %param.19) | copy-start | bytes 196612
  84.3 91.0 %copy-start.8 = (s32[2]{0:T(128)S(1)}, s32[2]{0:T(128)}, u32[]{:S(2)}) copy-start(s32[2]{0:T(128)} %param.22) | copy-start | bytes 28
  84.4 91.1 %copy-start.7 = (s32[2,16]{1,0:T(2,128)S(1)}, s32[2,16]{1,0:T(2,128)}, u32[]{:S(2)}) copy-start(s32[2,16]{1,0:T(2,128)} %param.21) | copy-start | bytes 388
  84.4 92.0 %copy-start = (bf16[32,2,256]{2,1,0:T(2,128)(2,1)S(1)}, bf16[32,2,256]{2,1,0:T(2,128)(2,1)}, u32[]{:S(2)}) copy-start(bf16[32,2,256]{2,1,0:T(2,128)(2,1)} %param.20) | copy-start | bytes 98308
  175.1 91.7 %all-reduce.3.cloned.1.call-start = ((), (), s32[]{:S(2)}) async-start(), calls=%async_computation.1 | async-start | bytes 524288 | tf_op jit(solution)/shard_map/psum | solution.py:202
  240.2 3.9 %copy-start.5 = (bf16[2048]{0:T(1024)(128)(2,1)S(1)}, bf16[2048]{0:T(1024)(128)(2,1)}, u32[]{:S(2)}) copy-start(bf16[2048]{0:T(1024)(128)(2,1)} %param.29) | copy-start | bytes 12292
  240.2 26.6 %copy-start.2 = (bf16[32,2048]{1,0:T(8,128)(2,1)S(1)}, bf16[32,2048]{1,0:T(8,128)(2,1)}, u32[]{:S(2)}) copy-start(bf16[32,2048]{1,0:T(8,128)(2,1)} %param.18) | copy-start | bytes 393220
  244.0 78.2 %reduce-scatter.2.cloned.1.call-start = ((), (), s32[]{:S(2)}) async-start(), calls=%async_computation.2 | async-start | bytes 1179648 | tf_op jit(solution)/shard_map/reduce_scatter | solution.py:216
  282.8 7.4 %copy-start.6 = (bf16[2048]{0:T(1024)(128)(2,1)S(1)}, bf16[2048]{0:T(1024)(128)(2,1)}, u32[]{:S(2)}) copy-start(bf16[2048]{0:T(1024)(128)(2,1)} %param.32) | copy-start | bytes 12292
  282.8 7.4 %copy-start.9 = (s32[2]{0:T(128)S(1)}, s32[2]{0:T(128)}, u32[]{:S(2)}) copy-start(s32[2]{0:T(128)} %param.23) | copy-start | bytes 28
Sparse Core Ops, SparseCore 0:
  11.3 68.2 all-gather.8
  81.8 88.4 all-gather.6
  175.2 63.0 all-gather.10
  244.2 22.5 all-reduce.2
  290.2 31.9 reduce-scatter.1

commit v2 on v1

--- a/solution.py
+++ b/solution.py
@@ -10,8 +10,7 @@
 
 
 TAG = 128
-REQ = ("a", "b")
-GROUP_SPLIT = 4
+REQ = ("z", "x", "y")
 
 norm_eps = 1e-05
 masked_score = -1e30
@@ -21,6 +20,19 @@
     high = values.astype(jnp.bfloat16)
     low = (values - high.astype(jnp.float32)).astype(jnp.bfloat16)
     return jnp.concatenate([high, low], axis=1)
+
+
+def ring_gather(parts, axis, size):
+    pieces = [parts]
+    for shift in range(1, size):
+        perm = [(i, (i + shift) % size) for i in range(size)]
+        pieces.append(lax.ppermute(parts, axis, perm))
+    return jnp.concatenate(pieces, axis=0)
+
+
+def gather_weights(own_w):
+    line = ring_gather(own_w[None], "x", lax.axis_size("x"))
+    return ring_gather(line, "z", lax.axis_size("z"))
 
 
 def ancestors(parents):
@@ -91,69 +103,79 @@
     dest_col = jnp.broadcast_to(prev_owner[0].astype(q_in.dtype), (tree_len, TAG))
     q_packet = jnp.concatenate([q_in[tree_len:], dest_col], axis=1)
     every_query = lax.all_gather(q_packet, REQ, axis=0, tiled=False)
-    dests = every_query[:, 0, q_width].astype(jnp.int32)
-    senders = jnp.arange(dests.shape[0], dtype=jnp.int32)
-    sender = jnp.sum(jnp.where(dests == device_id, senders, 0))
-    foreign = lax.dynamic_index_in_dim(every_query, sender, 0, keepdims=False)[:, :q_width]
-    held_queries = jnp.stack([q_in[:tree_len], foreign]).reshape(
-        2, tree_len, kv_local, GROUP, HEAD_DIM
-    )
+    own_w = jnp.stack([w_in[0], w_in[1], w_down])
+    all_w = gather_weights(own_w)
     page_len = cache.shape[2]
     block_pages = math.gcd(held_table.shape[1], max(1, 1024 // page_len))
     block_keys = block_pages * page_len
     num_blocks = held_table.shape[1] // block_pages
     positions = jnp.arange(block_keys, dtype=jnp.int32)
 
-    def attend_block(block, state):
-        running, total, accum = state
-        page_ids = lax.dynamic_slice_in_dim(held_table, block * block_pages, block_pages, 1)
-        gathered = cache[page_ids]
-        key_rows = gathered[:, :, 0].reshape(2, block_keys, kv_local, HEAD_DIM)
-        value_rows = gathered[:, :, 1].reshape(2, block_keys, kv_local, HEAD_DIM)
-        scores = (
-            jnp.einsum(
-                "sqghe,skge->sghqk", held_queries, key_rows, preferred_element_type=jnp.float32
+    def attend(slot, slot_queries, first, last, state):
+        table = held_table[slot]
+        length = held_len[slot]
+
+        def attend_block(block, state):
+            running, total, accum = state
+            page_ids = lax.dynamic_slice_in_dim(table, block * block_pages, block_pages, 0)
+            gathered = cache[page_ids]
+            key_rows = gathered[:, 0].reshape(block_keys, kv_local, HEAD_DIM)
+            value_rows = gathered[:, 1].reshape(block_keys, kv_local, HEAD_DIM)
+            scores = (
+                jnp.einsum(
+                    "qghe,kge->ghqk", slot_queries, key_rows, preferred_element_type=jnp.float32
+                )
+                * scale
             )
-            * scale
-        )
-        visible = (block * block_keys + positions)[None, :] < held_len[:, None]
-        visible = visible[:, None, None, None, :]
-        scores = jnp.where(visible, scores, masked_score)
-        newest = jnp.maximum(running, jnp.max(scores, axis=-1))
-        weights = jnp.where(visible, jnp.exp(scores - newest[..., None]), 0.0)
-        factor = jnp.exp(running - newest)
-        total = total * factor + jnp.sum(weights, axis=-1)
-        update = jnp.einsum(
-            "sghqk,skge->sghqe",
-            weights,
-            value_rows.astype(jnp.float32),
-            precision=lax.Precision.HIGHEST,
-        )
-        accum = accum * factor[..., None] + update
-        return (newest, total, accum)
-
-    stat_shape = (2, kv_local, GROUP, tree_len)
+            visible = (block * block_keys + positions) < length
+            scores = jnp.where(visible, scores, masked_score)
+            newest = jnp.maximum(running, jnp.max(scores, axis=-1))
+            weights = jnp.where(visible, jnp.exp(scores - newest[..., None]), 0.0)
+            factor = jnp.exp(running - newest)
+            total = total * factor + jnp.sum(weights, axis=-1)
+            update = jnp.einsum(
+                "ghqk,kge->ghqe",
+                weights,
+                value_rows.astype(jnp.float32),
+                precision=lax.Precision.HIGHEST,
+            )
+            accum = accum * factor[..., None] + update
+            return (newest, total, accum)
+
+        return lax.fori_loop(first, last, attend_block, state)
+
+    stat_shape = (kv_local, GROUP, tree_len)
     start_state = (
         jnp.full(stat_shape, masked_score, jnp.float32),
         jnp.zeros(stat_shape, jnp.float32),
         jnp.zeros(stat_shape + (HEAD_DIM,), jnp.float32),
     )
-    own_w = jnp.stack([w_in[0], w_in[1], w_down])
-    all_w = lax.all_gather(own_w, "a", axis=0, tiled=False)
-    running, total, accum = lax.fori_loop(0, num_blocks, attend_block, start_state)
+    own_queries = queries[0]
+    split = num_blocks // 2
+    own_state = attend(0, own_queries, 0, split, start_state)
+    own_state, every_query = lax.optimization_barrier((own_state, every_query))
+    dests = every_query[:, 0, q_width].astype(jnp.int32)
+    senders = jnp.arange(dests.shape[0], dtype=jnp.int32)
+    sender = jnp.sum(jnp.where(dests == device_id, senders, 0))
+    foreign = lax.dynamic_index_in_dim(every_query, sender, 0, keepdims=False)[:, :q_width]
+    foreign = foreign.reshape(tree_len, kv_local, GROUP, HEAD_DIM)
+    f_running, f_total, f_accum = attend(1, foreign, 0, num_blocks, start_state)
+    f_out = f_accum / f_total[..., None]
+    sent_out = jnp.transpose(f_out, (2, 0, 1, 3)).reshape(
+        tree_len, kv_local * GROUP * HEAD_DIM
+    )
+    sent_max = jnp.transpose(f_running, (2, 0, 1)).reshape(tree_len, kv_local * GROUP)
+    sent_total = jnp.transpose(f_total, (2, 0, 1)).reshape(tree_len, kv_local * GROUP)
+    stats = jnp.concatenate(
+        [split_hi_lo(sent_max), split_hi_lo(sent_total)], axis=1
+    )
+    pad = jnp.zeros((tree_len, TAG - stats.shape[1]), jnp.bfloat16)
+    r_packet = jnp.concatenate([sent_out.astype(jnp.bfloat16), stats, pad], axis=1)
+    r_packet, own_state = lax.optimization_barrier((r_packet, own_state))
+    back = lax.all_gather(r_packet, REQ, axis=0, tiled=False)
+    running, total, accum = attend(0, own_queries, split, num_blocks, own_state)
     all_w, running, total, accum = lax.optimization_barrier((all_w, running, total, accum))
     cache_out = accum / total[..., None]
-    sent_out = jnp.transpose(cache_out[1], (2, 0, 1, 3)).reshape(
-        tree_len, kv_local * GROUP * HEAD_DIM
-    )
-    sent_max = jnp.transpose(running[1], (2, 0, 1)).reshape(tree_len, kv_local * GROUP)
-    sent_total = jnp.transpose(total[1], (2, 0, 1)).reshape(tree_len, kv_local * GROUP)
-    stats = jnp.concatenate(
-        [split_hi_lo(sent_max), split_hi_lo(sent_total)], axis=1
-    )
-    pad = jnp.zeros((tree_len, TAG - stats.shape[1]), jnp.bfloat16)
-    r_packet = jnp.concatenate([sent_out.astype(jnp.bfloat16), stats, pad], axis=1)
-    back = lax.all_gather(r_packet, REQ, axis=0, tiled=False)
     got = lax.dynamic_index_in_dim(back, prev_owner[0], 0, keepdims=False).astype(jnp.float32)
     heads = kv_local * GROUP
     o_w = heads * HEAD_DIM
@@ -165,9 +187,9 @@
     recv_total = (got[:, t0 : t0 + heads] + got[:, t0 + heads : t0 + 2 * heads]).reshape(
         tree_len, kv_local, GROUP
     )
-    part_out = jnp.stack([cache_out[0], jnp.transpose(recv_out, (1, 2, 0, 3))])
-    part_max = jnp.stack([running[0], jnp.transpose(recv_max, (1, 2, 0))])
-    part_total = jnp.stack([total[0], jnp.transpose(recv_total, (1, 2, 0))])
+    part_out = jnp.stack([cache_out, jnp.transpose(recv_out, (1, 2, 0, 3))])
+    part_max = jnp.stack([running, jnp.transpose(recv_max, (1, 2, 0))])
+    part_total = jnp.stack([total, jnp.transpose(recv_total, (1, 2, 0))])
     reach = ancestors(parents)
     live = jnp.arange(tree_len, dtype=jnp.int32)[None, :] < counts[:, None]
     allowed = ((reach > 0.5) & live[:, None, :])[:, None, None, :, :]
@@ -199,12 +221,12 @@
         .astype(jnp.bfloat16)
     )
     partial_proj = jnp.dot(attended, w_out, preferred_element_type=jnp.float32)
-    projected = lax.psum(partial_proj, "mlp")
+    projected = partial_proj + lax.ppermute(partial_proj, "mlp", [(0, 1), (1, 0)])
     mixed = (resid.astype(jnp.float32) + projected).astype(jnp.bfloat16)
     normed = rms_scale(mixed, gain_mid)
     column = lax.axis_index("mlp")
     half_count = normed.shape[0] // lax.axis_size("mlp")
-    group_rows = lax.all_gather(normed, "b", axis=0, tiled=True)
+    group_rows = lax.all_gather(normed, "y", axis=0, tiled=True)
     dims = (((1,), (2,)), ((), ()))
     gate = lax.dot_general(group_rows, all_w[:, 0], dims, preferred_element_type=jnp.float32)
     up_part = lax.dot_general(group_rows, all_w[:, 1], dims, preferred_element_type=jnp.float32)
@@ -213,7 +235,7 @@
     partial = lax.dot_general(
         hidden, all_w[:, 2], down_dims, preferred_element_type=jnp.float32
     )
-    mlp_half = lax.psum_scatter(partial, ("b", "mlp"), scatter_dimension=0, tiled=True)
+    mlp_half = lax.psum_scatter(partial, ("y", "mlp"), scatter_dimension=0, tiled=True)
     base_half = lax.dynamic_slice_in_dim(mixed, column * half_count, half_count, 0)
     out_half = (base_half.astype(jnp.float32) + mlp_half).astype(jnp.bfloat16)
     hidden_out = lax.all_gather(out_half, "mlp", axis=0, tiled=True)
@@ -227,8 +249,10 @@
 def solution(mesh):
     devices = mesh.devices
     owners = devices.shape[0]
+    lines = round(owners ** (1 / 3))
     sub_mesh = Mesh(
-        devices.reshape(owners // GROUP_SPLIT, GROUP_SPLIT, devices.shape[1]), ("a", "b", "mlp")
+        devices.reshape(owners // (lines * lines), lines, lines, devices.shape[1]),
+        ("z", "x", "y", "mlp"),
     )
     R = REQ
     placed = (

time: 341 us -> 420 us (1.23)
  waiting for transfers between devices: 183 us -> 222 us
  local copies, waits for them, and re-layouts: 66 us -> 92.1 us
  starting transfers between devices: 0.21 us -> 13.2 us
  other arithmetic: 12.5 us -> 23.9 us
  matrix products: 45.5 us -> 34.5 us
    ppermute x0 -> x7, waiting for transfers between devices: none -> 149 us  [the longest x6 148 us: ring_gather(): pieces.append(lax.ppermute(parts, axis, perm))]
    all_gather x1, waiting for transfers between devices: 68 us -> 0.01 us  [per_device(): every_query = lax.all_gather(q_packet, REQ, axis=0, tiled=False)]
    psum x1 -> x0, waiting for transfers between devices: 22.7 us -> none  [per_device(): projected = lax.psum(partial_proj, 'mlp')]
    gather x6 -> x12, local copies, waits for them, and re-layouts: 25.6 us -> 47.9 us  [attend_block(): gathered = cache[page_ids]]
    all_gather x1, waiting for transfers between devices: 61.1 us -> 44.6 us  [per_device(): back = lax.all_gather(r_packet, REQ, axis=0, tiled=False)]
    while x18 -> x12, local copies, waits for them, and re-layouts: 14.8 us -> 0.03 us
    ppermute x0 -> x7, starting transfers between devices: none -> 12.9 us  [the longest x6 11.4 us: ring_gather(): pieces.append(lax.ppermute(parts, axis, perm))]
    unnamed x23 -> x32, local copies, waits for them, and re-layouts: 0.84 us -> 12.8 us
  transfers between devices with their start and end apart: 5 -> 10, of which waited for: 4 -> 8; matrix products, arithmetic and copies ran while one was open for 28% -> 17% of each run, Pallas kernels for 0% -> 0%
where the time goes in v2:
time: 420 us; the launch traced here: 419 us
  waiting for transfers between devices  222 us (53%)
  local copies, waits for them, and re-layouts  92.1 us (22%)
  matrix products  34.5 us (8%)
  other arithmetic  23.9 us (6%)
  between operations  16.7 us (4%)
  blocking collectives  14.9 us (4%)
  starting transfers between devices  13.2 us (3%)
    ppermute x6, waiting for transfers between devices, ring_gather(): pieces.append(lax.ppermute(parts, axis, perm))  148 us
    gather x12, local copies, waits for them, and re-layouts, attend_block(): gathered = cache[page_ids]  47.9 us
    all_gather x1, waiting for transfers between devices, per_device(): back = lax.all_gather(r_packet, REQ, axis=0, tiled=False)  44.6 us
    reduce_scatter x1, waiting for transfers between devices, per_device(): lax.psum_scatter(partial, ('y', 'mlp'), scatter_dimension=0, tiled=True)  28.1 us
    unnamed x32, local copies, waits for them, and re-layouts  12.8 us
    ppermute x6, starting transfers between devices, ring_gather(): pieces.append(lax.ppermute(parts, axis, perm))  11.4 us
    all_gather x1, blocking collectives, per_device(): group_rows = lax.all_gather(normed, 'y', axis=0, tiled=True)  9.9 us
    dot_general x12, matrix products, attend_block(): jnp.einsum('ghqk,kge->ghqe', weights, value_rows.astype(jnp.float32), pre...  9.62 us
  transfers between devices with their start and end apart: 10, of which 8 were waited for; matrix products, arithmetic and copies ran while one was open for 17% of the time, Pallas kernels for 0%

profile of v2, /device:TPU:1, one launch (start us, length us, event | category | flops | bytes accessed | tf_op | source)
XLA Modules:
  0.0 418.7 jit_solution(10923962942070283096)
XLA Ops:
  7.2 2.1 maximum_bitcast_fusion
  9.3 2.0 collective-permute-start
  11.3 2.5 collective-permute-start.1
  13.8 1.2 collective-permute-start.2
  17.2 1.3 fusion.117
  19.3 10.3 %collective-permute-done = bf16[1,3,64,2048]{3,2,0,1:T(8,128)(2,1)S(1)} collective-permute-done((bf16[1,3,64,2048]{3,2,0,1:T(8,128)(2,1)}, bf16[1,3,64,2048]{3,2,0,1:T(8,128)(2,1)S(1)}, u32[]{:S(2)}, u32[]{:S(2)}) %collective-permute-start) | collective-permute-done | bytes 786464 | tf_op jit(solution)/shard_map/ppermute | solution.py:29
  29.6 18.6 %collective-permute-done.1 = bf16[1,3,64,2048]{3,2,0,1:T(8,128)(2,1)S(1)} collective-permute-done((bf16[1,3,64,2048]{3,2,0,1:T(8,128)(2,1)}, bf16[1,3,64,2048]{3,2,0,1:T(8,128)(2,1)S(1)}, u32[]{:S(2)}, u32[]{:S(2)}) %collective-permute-start.1) | collective-permute-done | bytes 786464 | tf_op jit(solution)/shard_map/ppermute | solution.py:29
  48.2 3.2 pad_maximum_fusion
  51.4 1.6 collective-permute-start.3
  53.0 22.3 %while.55 = (s32[]{:T(128)}, f32[4,4,16]{2,1,0:T(4,128)S(1)}, f32[4,4,16]{2,1,0:T(4,128)S(1)}, f32[4,4,16,64]{3,2,1,0:T(8,128)S(1)}, s32[]{:T(128)}, /*index=5*/...) while((s32[]{:T(128)}, f32[4,4,16]{2,1,0:T(4,128)S(1)}, ...), condition=%wide.region_3.4_spmd.clone, body=%wide.region_0.3_spmd.clone.sunk | while | flops 237031712 | bytes 12771671 | solution.py:145
  53.1 4.0 gather_fusion.1
  60.6 4.0 gather_fusion.1
  68.0 4.0 gather_fusion.1
  75.4 3.4 collective-permute-start.4
  81.6 2.1 constant_dynamic-update-slice_fusion.6
  83.7 1.0 constant_dynamic-update-slice_fusion.5
  84.7 2.1 constant_dynamic-update-slice_fusion.4
  86.8 1.0 constant_dynamic-update-slice_fusion.3
  87.8 41.9 %collective-permute-done.3 = bf16[4,3,64,2048]{3,2,0,1:T(8,128)(2,1)} collective-permute-done((bf16[4,3,64,2048]{3,2,0,1:T(8,128)(2,1)}, bf16[4,3,64,2048]{3,2,0,1:T(8,128)(2,1)}, u32[]{:S(2)}, u32[]{:S(2)}) %collective-permute-start.3) | collective-permute-done | bytes 3145760 | tf_op jit(solution)/shard_map/ppermute | solution.py:29
  129.7 4.0 constant_dynamic-update-slice_fusion.2
  133.7 63.9 %collective-permute-done.4 = bf16[4,3,64,2048]{3,2,0,1:T(8,128)(2,1)} collective-permute-done((bf16[4,3,64,2048]{3,2,0,1:T(8,128)(2,1)}, bf16[4,3,64,2048]{3,2,0,1:T(8,128)(2,1)}, u32[]{:S(2)}, u32[]{:S(2)}) %collective-permute-start.4) | collective-permute-done | bytes 3145760 | tf_op jit(solution)/shard_map/ppermute | solution.py:29
  197.7 4.0 constant_dynamic-update-slice_fusion.1
  201.7 13.3 %collective-permute-done.5 = bf16[4,3,64,2048]{3,2,0,1:T(8,128)(2,1)} collective-permute-done((bf16[4,3,64,2048]{3,2,0,1:T(8,128)(2,1)}, bf16[4,3,64,2048]{3,2,0,1:T(8,128)(2,1)}, u32[]{:S(2)}, u32[]{:S(2)}) %collective-permute-start.5) | collective-permute-done | bytes 3145760 | tf_op jit(solution)/shard_map/ppermute | solution.py:29
  215.0 3.9 constant_dynamic-update-slice_fusion
  218.9 6.2 %copy.62 = bf16[64,16,1152]{0,2,1:T(8,128)(2,1)} copy(bf16[64,16,1152]{2,1,0:T(8,128)(2,1)} %bitcast.200) | data formatting | bytes 4718592 | tf_op jit(solution)/shard_map/optimization_barrier | solution.py:156
  225.1 1.3 fusion.104
  229.2 45.0 %while.56 = (s32[]{:T(128)}, f32[4,4,16]{2,1,0:T(4,128)S(1)}, f32[4,4,16]{2,1,0:T(4,128)S(1)}, f32[4,4,16,64]{3,2,1,0:T(8,128)S(1)}, s32[]{:T(128)}, /*index=5*/...) while((s32[]{:T(128)}, f32[4,4,16]{2,1,0:T(4,128)S(1)}, ...), condition=%wide.region_8.9_spmd.clone, body=%wide.region_5.8_spmd.clone.sunk | while | flops 237031712 | bytes 12771671 | solution.py:145
  229.4 4.0 gather_fusion.2
  236.9 4.0 gather_fusion.2
  244.4 4.0 gather_fusion.2
  251.9 4.0 gather_fusion.2
  259.4 4.0 gather_fusion.2
  266.9 4.0 gather_fusion.2
  275.6 22.3 %while.54 = (s32[]{:T(128)}, f32[4,4,16]{2,1,0:T(4,128)S(1)}, f32[4,4,16]{2,1,0:T(4,128)S(1)}, f32[4,4,16,64]{3,2,1,0:T(8,128)S(1)}, s32[]{:T(128)}, /*index=5*/...) while((s32[]{:T(128)}, f32[4,4,16]{2,1,0:T(4,128)S(1)}, ...), condition=%wide.region_12.13_spmd.clone, body=%wide.region_9.12_spmd.clone.sunk | while | flops 237014560 | bytes 12771679 | solution.py:145
  275.8 4.0 gather_fusion
  283.2 4.0 gather_fusion
  290.6 4.0 gather_fusion
  298.1 44.6 %all-gather.7.cloned.1.call-done = bf16[1024,1152]{1,0:T(8,128)(2,1)} async-done(((bf16[16,1152]{1,0:T(8,128)(2,1)}), bf16[1024,1152]{1,0:T(8,128)(2,1)}) %all-gather.7.cloned.1.call-update) | async-done | bytes 2359312 | tf_op jit(solution)/shard_map/all_gather | solution.py:175
  344.6 3.0 fusion.119
  347.7 1.6 collective-permute-start.6
  349.2 1.2 collective-permute-done.6
  350.7 9.9 %all_gather.22 = bf16[128,2048]{1,0:T(8,128)(2,1)S(1)} all-gather(bf16[32,2048]{1,0:T(8,128)(2,1)S(1)} %fusion.74), channel_id=1, replica_groups=mesh['z'=4,'x'=4,'y'=4,'mlp'=2] {'y'}, dimensions={0}, use_global_device_ids=true | all-gather | bytes 655360 | tf_op jit(solution)/shard_map/all_gather | solution.py:229
  360.6 3.4 fusion.42
  364.0 7.3 %fusion.47 = f32[128,2048]{1,0:T(8,128)} fusion(bf16[16,3,64,2048]{3,2,0,1:T(8,128)(2,1)} %constant_dynamic-update-slice_fusion, bf16[128,2048]{1,0:T(8,128)(2,1)S(1)} %all_gather.22, f32[128,16,64]{0,2,1:T(8,128)S(1)} %fusion.42), kind=kOutput, calls=%fused_computation.76 | convolution fusion | flops 1074528256 | bytes 10485760 | tf_op jit(solution)/shard_map/dot_general | solution.py:235
  372.7 28.1 %reduce-scatter.2.cloned.1.call-done = f32[16,2048]{1,0:T(8,128)} async-done(((f32[128,2048]{1,0:T(8,128)}), f32[16,2048]{1,0:T(8,128)}) %reduce-scatter.2.cloned.1.call-update) | async-done | bytes 131088 | tf_op jit(solution)/shard_map/reduce_scatter | solution.py:238
  400.8 0.9 add_convert_fusion.1
  401.7 5.0 %all_gather.23 = bf16[32,2048]{1,0:T(8,128)(2,1)S(1)} all-gather(bf16[16,2048]{1,0:T(8,128)(2,1)S(1)} %add_convert_fusion.1), channel_id=1, replica_groups=mesh['z'=4,'x'=4,'y'=4,'mlp'=2] {'mlp'}, dimensions={0}, use_global_device_ids=true | all-gather | bytes 196608 | tf_op jit(solution)/shard_map/all_gather | solution.py:241
  406.9 4.7 %convolution_convert_fusion = bf16[32,1536]{1,0:T(8,128)(2,1)} fusion(bf16[2048,1536]{1,0:T(8,128)(2,1)} %param.37, bf16[32,2048]{1,0:T(8,128)(2,1)S(1)} %all_gather.23, f32[2048]{0:T(1024)S(1)} %convert_element_type.147, f32[32]{0:T(128)S(1)} %add_rsqrt_fusion), kind=kOutput, calls=%fused_computation.77 | convolution fusion | flops 201637888 | bytes 6529152 | tf_op jit(solution)/shard_map/dot_general | solution.py:243
  (266 shorter events, 52.2 us)
Async XLA Ops:
  7.2 211.8 %all-gather.5.cloned.1.call-start = ((), (), s32[]{:S(2)}) async-start(), calls=%async_computation.2 | async-start | bytes 2396160 | tf_op jit(solution)/shard_map/all_gather | solution.py:105
  9.3 20.3 %collective-permute-start = (bf16[1,3,64,2048]{3,2,0,1:T(8,128)(2,1)}, bf16[1,3,64,2048]{3,2,0,1:T(8,128)(2,1)S(1)}, u32[]{:S(2)}, u32[]{:S(2)}) collective-permute-start(bf16[1,3,64,2048]{3,2,0,1:T(8,128)(2,1)} %maximum_bitcast_fusion), channel_id=1, source_target_pairs={{0,8},{8,16},{16,24},{24,0},{1,9},{9,17},{17,25},{25,1},{2,10},{10... | collective-permute-start | bytes 2359304 | tf_op jit(solution)/shard_map/ppermute | solution.py:29
  11.3 36.9 %collective-permute-start.1 = (bf16[1,3,64,2048]{3,2,0,1:T(8,128)(2,1)}, bf16[1,3,64,2048]{3,2,0,1:T(8,128)(2,1)S(1)}, u32[]{:S(2)}, u32[]{:S(2)}) collective-permute-start(bf16[1,3,64,2048]{3,2,0,1:T(8,128)(2,1)} %maximum_bitcast_fusion), channel_id=1, source_target_pairs={{0,16},{8,24},{16,0},{24,8},{1,17},{9,25},{17,1},{25,9},{2,18},{10... | collective-permute-start | bytes 2359304 | tf_op jit(solution)/shard_map/ppermute | solution.py:29
  13.8 34.4 %collective-permute-start.2 = (bf16[1,3,64,2048]{3,2,0,1:T(8,128)(2,1)}, bf16[1,3,64,2048]{3,2,0,1:T(8,128)(2,1)S(1)}, u32[]{:S(2)}, u32[]{:S(2)}) collective-permute-start(bf16[1,3,64,2048]{3,2,0,1:T(8,128)(2,1)} %maximum_bitcast_fusion), channel_id=1, source_target_pairs={{0,24},{8,0},{16,8},{24,16},{1,25},{9,1},{17,9},{25,17},{2,26},{10... | collective-permute-start | bytes 2359304 | tf_op jit(solution)/shard_map/ppermute | solution.py:29
  17.0 325.7 %all-gather.7.cloned.1.call-start = ((), (), s32[]{:S(2)}) async-start(), calls=%async_computation.3 | async-start | bytes 2396160 | tf_op jit(solution)/shard_map/all_gather | solution.py:175
  48.2 4.8 %copy-start = (bf16[1,3,64,2048]{3,2,0,1:T(8,128)(2,1)}, bf16[1,3,64,2048]{3,2,0,1:T(8,128)(2,1)S(1)}, u32[]{:S(2)}) copy-start(bf16[1,3,64,2048]{3,2,0,1:T(8,128)(2,1)S(1)} %collective-permute-done.1) | copy-start | bytes 2359300
  48.2 4.8 %copy-start.1 = (bf16[1,3,64,2048]{3,2,0,1:T(8,128)(2,1)}, bf16[1,3,64,2048]{3,2,0,1:T(8,128)(2,1)S(1)}, u32[]{:S(2)}) copy-start(bf16[1,3,64,2048]{3,2,0,1:T(8,128)(2,1)S(1)} %collective-permute-done.2) | copy-start | bytes 2359300
  51.4 78.4 %collective-permute-start.3 = (bf16[4,3,64,2048]{3,2,0,1:T(8,128)(2,1)}, bf16[4,3,64,2048]{3,2,0,1:T(8,128)(2,1)}, u32[]{:S(2)}, u32[]{:S(2)}) collective-permute-start(bf16[4,3,64,2048]{3,2,0,1:T(8,128)(2,1)} %pad_maximum_fusion), channel_id=1, source_target_pairs={{0,32},{32,64},{64,96},{96,0},{1,33},{33,65},{65,97},{97,1},{2,34}... | collective-permute-start | bytes 9437192 | tf_op jit(solution)/shard_map/ppermute | solution.py:29
  53.0 25.8 %copy-start.3 = (bf16[32,2,256]{2,1,0:T(2,128)(2,1)S(1)}, bf16[32,2,256]{2,1,0:T(2,128)(2,1)}, u32[]{:S(2)}) copy-start(bf16[32,2,256]{2,1,0:T(2,128)(2,1)} %param.24) | copy-start | bytes 98308
  53.0 25.9 %copy-start.4 = (bf16[32,1024]{1,0:T(8,128)(2,1)S(1)}, bf16[32,1024]{1,0:T(8,128)(2,1)}, u32[]{:S(2)}) copy-start(bf16[32,1024]{1,0:T(8,128)(2,1)} %param.23) | copy-start | bytes 196612
  53.0 26.2 %copy-start.10 = (s32[2]{0:T(128)S(1)}, s32[2]{0:T(128)}, u32[]{:S(2)}) copy-start(s32[2]{0:T(128)} %param.26) | copy-start | bytes 28
  53.0 27.0 %copy-start.9 = (s32[2,16]{1,0:T(2,128)S(1)}, s32[2,16]{1,0:T(2,128)}, u32[]{:S(2)}) copy-start(s32[2,16]{1,0:T(2,128)} %param.25) | copy-start | bytes 388
  75.3 11.5 %copy-start.2 = (bf16[1,3,64,2048]{3,2,0,1:T(8,128)(2,1)S(1)}, bf16[1,3,64,2048]{3,2,0,1:T(8,128)(2,1)}, u32[]{:S(2)}) copy-start(bf16[1,3,64,2048]{3,2,0,1:T(8,128)(2,1)} %copy-done.1) | copy-start | bytes 2359300
  75.4 122.3 %collective-permute-start.4 = (bf16[4,3,64,2048]{3,2,0,1:T(8,128)(2,1)}, bf16[4,3,64,2048]{3,2,0,1:T(8,128)(2,1)}, u32[]{:S(2)}, u32[]{:S(2)}) collective-permute-start(bf16[4,3,64,2048]{3,2,0,1:T(8,128)(2,1)} %pad_maximum_fusion), channel_id=1, source_target_pairs={{0,64},{32,96},{64,0},{96,32},{1,65},{33,97},{65,1},{97,33},{2,66}... | collective-permute-start | bytes 9437192 | tf_op jit(solution)/shard_map/ppermute | solution.py:29
  79.3 135.7 %collective-permute-start.5 = (bf16[4,3,64,2048]{3,2,0,1:T(8,128)(2,1)}, bf16[4,3,64,2048]{3,2,0,1:T(8,128)(2,1)}, u32[]{:S(2)}, u32[]{:S(2)}) collective-permute-start(bf16[4,3,64,2048]{3,2,0,1:T(8,128)(2,1)} %pad_maximum_fusion), channel_id=1, source_target_pairs={{0,96},{32,0},{64,32},{96,64},{1,97},{33,1},{65,33},{97,65},{2,98}... | collective-permute-start | bytes 9437192 | tf_op jit(solution)/shard_map/ppermute | solution.py:29
  201.7 27.6 %copy-start.5 = (f32[4,4,16,64]{3,2,1,0:T(8,128)S(1)}, f32[4,4,16,64]{3,2,1,0:T(8,128)}, u32[]{:S(2)}) copy-start(f32[4,4,16,64]{3,2,1,0:T(8,128)} %custom-call.5) | copy-start | bytes 196612
  275.4 125.4 %reduce-scatter.2.cloned.1.call-start = ((), (), s32[]{:S(2)}) async-start(), calls=%async_computation.1 | async-start | bytes 1179648 | tf_op jit(solution)/shard_map/reduce_scatter | solution.py:238
  297.9 51.3 %copy-start.7 = (bf16[2048]{0:T(1024)(128)(2,1)S(1)}, bf16[2048]{0:T(1024)(128)(2,1)}, u32[]{:S(2)}) copy-start(bf16[2048]{0:T(1024)(128)(2,1)} %param.33) | copy-start | bytes 12292
  298.0 52.4 %copy-start.6 = (bf16[32,2048]{1,0:T(8,128)(2,1)S(1)}, bf16[32,2048]{1,0:T(8,128)(2,1)}, u32[]{:S(2)}) copy-start(bf16[32,2048]{1,0:T(8,128)(2,1)} %param.22) | copy-start | bytes 393220
  347.7 2.7 collective-permute-start.6
  364.0 7.4 %copy-start.8 = (bf16[2048]{0:T(1024)(128)(2,1)S(1)}, bf16[2048]{0:T(1024)(128)(2,1)}, u32[]{:S(2)}) copy-start(bf16[2048]{0:T(1024)(128)(2,1)} %param.36) | copy-start | bytes 12292
  364.0 7.4 %copy-start.11 = (s32[2]{0:T(128)S(1)}, s32[2]{0:T(128)}, u32[]{:S(2)}) copy-start(s32[2]{0:T(128)} %param.27) | copy-start | bytes 28
Sparse Core Ops, SparseCore 0:
  17.2 129.9 all-gather.4
  275.5 67.1 all-gather.6
  371.5 29.2 reduce-scatter.1

commit v3 on v2

--- a/solution.py
+++ b/solution.py
@@ -22,17 +22,11 @@
     return jnp.concatenate([high, low], axis=1)
 
 
-def ring_gather(parts, axis, size):
-    pieces = [parts]
-    for shift in range(1, size):
-        perm = [(i, (i + shift) % size) for i in range(size)]
-        pieces.append(lax.ppermute(parts, axis, perm))
-    return jnp.concatenate(pieces, axis=0)
-
-
-def gather_weights(own_w):
-    line = ring_gather(own_w[None], "x", lax.axis_size("x"))
-    return ring_gather(line, "z", lax.axis_size("z"))
+def gather_lines(packet):
+    lines = lax.all_gather(packet, "y", axis=0, tiled=False)
+    lines = lax.all_gather(lines, "x", axis=0, tiled=False)
+    lines = lax.all_gather(lines, "z", axis=0, tiled=False)
+    return lines.reshape((-1,) + packet.shape)
 
 
 def ancestors(parents):
@@ -102,9 +96,9 @@
     q_width = q_in.shape[1]
     dest_col = jnp.broadcast_to(prev_owner[0].astype(q_in.dtype), (tree_len, TAG))
     q_packet = jnp.concatenate([q_in[tree_len:], dest_col], axis=1)
-    every_query = lax.all_gather(q_packet, REQ, axis=0, tiled=False)
+    every_query = gather_lines(q_packet)
     own_w = jnp.stack([w_in[0], w_in[1], w_down])
-    all_w = gather_weights(own_w)
+    all_w = lax.all_gather(own_w, ("z", "x"), axis=0, tiled=False)
     page_len = cache.shape[2]
     block_pages = math.gcd(held_table.shape[1], max(1, 1024 // page_len))
     block_keys = block_pages * page_len
@@ -172,7 +166,7 @@
     pad = jnp.zeros((tree_len, TAG - stats.shape[1]), jnp.bfloat16)
     r_packet = jnp.concatenate([sent_out.astype(jnp.bfloat16), stats, pad], axis=1)
     r_packet, own_state = lax.optimization_barrier((r_packet, own_state))
-    back = lax.all_gather(r_packet, REQ, axis=0, tiled=False)
+    back = gather_lines(r_packet)
     running, total, accum = attend(0, own_queries, split, num_blocks, own_state)
     all_w, running, total, accum = lax.optimization_barrier((all_w, running, total, accum))
     cache_out = accum / total[..., None]

time: 420 us -> 350 us (0.83)
  waiting for transfers between devices: 222 us -> 148 us
  blocking collectives: 14.9 us -> 58.5 us
  local copies, waits for them, and re-layouts: 92.1 us -> 69.2 us
  starting transfers between devices: 13.2 us -> 1.03 us
    ppermute x6 -> x0, waiting for transfers between devices: 148 us -> none  [ring_gather(): pieces.append(lax.ppermute(parts, axis, perm))]
    all_gather x2 -> x3, waiting for transfers between devices: 44.6 us -> 118 us  [the longest x1 91.1 us: per_device(): all_w = lax.all_gather(own_w, ('z', 'x'), axis=0, tiled=False)]
    all_gather x0 -> x4, blocking collectives: none -> 42.3 us  [the longest x2 22.1 us: gather_lines(): lines = lax.all_gather(lines, 'x', axis=0, tiled=False)]
    unnamed x32 -> x23, local copies, waits for them, and re-layouts: 12.8 us -> 0.75 us
    ppermute x6 -> x0, starting transfers between devices: 11.4 us -> none  [ring_gather(): pieces.append(lax.ppermute(parts, axis, perm))]
    optimization_barrier x1 -> x0, local copies, waits for them, and re-layouts: 6.17 us -> none  [per_device(): own_state, every_query = lax.optimization_barrier((own_state, every_query))]
  transfers between devices with their start and end apart: 10 -> 5, of which waited for: 8 -> 5; matrix products, arithmetic and copies ran while one was open for 17% -> 15% of each run, Pallas kernels for 0% -> 0%
where the time goes in v3:
time: 350 us; the launch traced here: 349 us
  waiting for transfers between devices  148 us (42%)
  local copies, waits for them, and re-layouts  69.2 us (20%)
  blocking collectives  58.5 us (17%)
  matrix products  34.7 us (10%)
  other arithmetic  19.8 us (6%)
  between operations  16.5 us (5%)
    all_gather x1, waiting for transfers between devices, per_device(): all_w = lax.all_gather(own_w, ('z', 'x'), axis=0, tiled=False)  91.1 us
    gather x12, local copies, waits for them, and re-layouts, attend_block(): gathered = cache[page_ids]  48.4 us
    reduce_scatter x1, waiting for transfers between devices, per_device(): lax.psum_scatter(partial, ('y', 'mlp'), scatter_dimension=0, tiled=True)  29.2 us
    all_gather x2, waiting for transfers between devices, gather_lines(): lines = lax.all_gather(lines, 'z', axis=0, tiled=False)  26.6 us
    all_gather x2, blocking collectives, gather_lines(): lines = lax.all_gather(lines, 'x', axis=0, tiled=False)  22.1 us
    all_gather x2, blocking collectives, gather_lines(): lines = lax.all_gather(packet, 'y', axis=0, tiled=False)  20.2 us
    all_gather x1, blocking collectives, per_device(): group_rows = lax.all_gather(normed, 'y', axis=0, tiled=True)  11.2 us
    dot_general x12, matrix products, attend_block(): jnp.einsum('ghqk,kge->ghqe', weights, value_rows.astype(jnp.float32), pre...  9.76 us
  transfers between devices with their start and end apart: 5, of which 5 were waited for; matrix products, arithmetic and copies ran while one was open for 15% of the time, Pallas kernels for 0%

profile of v3, /device:TPU:1, one launch (start us, length us, event | category | flops | bytes accessed | tf_op | source)
XLA Modules:
  0.0 349.1 jit_solution(6265594295481610294)
XLA Ops:
  7.9 0.8 fusion.101
  8.7 10.6 %all-gather.1 = bf16[64,1152]{1,0:T(8,128)(2,1)S(1)} all-gather(bf16[16,1152]{1,0:T(8,128)(2,1)S(1)} %concatenate.28), channel_id=3, replica_groups=mesh['z'=4,'x'=4,'y'=4,'mlp'=2] {'y'}, dimensions={0}, use_global_device_ids=true | all-gather | bytes 184320 | tf_op jit(solution)/shard_map/all_gather | solution.py:26
  19.3 11.1 %all-gather.2 = bf16[16,16,1152]{2,1,0:T(8,128)(2,1)} all-gather(bf16[4,16,1152]{2,1,0:T(8,128)(2,1)S(1)} %bitcast.205), channel_id=4, replica_groups=mesh['z'=4,'x'=4,'y'=4,'mlp'=2] {'x'}, dimensions={0}, use_global_device_ids=true | all-gather | bytes 737280 | tf_op jit(solution)/shard_map/all_gather | solution.py:27
  31.3 1.3 fusion.102
  32.7 22.6 %while.55 = (s32[]{:T(128)}, f32[4,4,16]{2,1,0:T(4,128)S(1)}, f32[4,4,16]{2,1,0:T(4,128)S(1)}, f32[4,4,16,64]{3,2,1,0:T(8,128)S(1)}, s32[]{:T(128)}, /*index=5*/...) while((s32[]{:T(128)}, f32[4,4,16]{2,1,0:T(4,128)S(1)}, ...), condition=%wide.region_3.4_spmd.clone, body=%wide.region_0.3_spmd.clone.sunk | while | flops 237031712 | bytes 12771671 | solution.py:139
  33.5 4.0 %gather_fusion.1 = bf16[8,2,128,256]{3,2,1,0:T(8,128)(2,1)S(1)} fusion(bf16[64,2,128,256]{3,2,1,0:T(8,128)(2,1)} %get-tuple-element.962, s32[1024]{0:T(1024)S(1)} %pad_clamp_fusion.7), kind=kCustom, calls=%fused_computation.clone.clone.1 | custom fusion | bytes 2097184 | tf_op jit(solution)/shard_map/while/body/eval_jaxpr/gather | solution.py:115
  39.4 0.8 convolution_add_fusion.7
  41.0 4.0 %gather_fusion.1 = bf16[8,2,128,256]{3,2,1,0:T(8,128)(2,1)S(1)} fusion(bf16[64,2,128,256]{3,2,1,0:T(8,128)(2,1)} %get-tuple-element.962, s32[1024]{0:T(1024)S(1)} %pad_clamp_fusion.7), kind=kCustom, calls=%fused_computation.clone.clone.1 | custom fusion | bytes 2097184 | tf_op jit(solution)/shard_map/while/body/eval_jaxpr/gather | solution.py:115
  47.0 0.8 convolution_add_fusion.7
  48.6 4.0 %gather_fusion.1 = bf16[8,2,128,256]{3,2,1,0:T(8,128)(2,1)S(1)} fusion(bf16[64,2,128,256]{3,2,1,0:T(8,128)(2,1)} %get-tuple-element.962, s32[1024]{0:T(1024)S(1)} %pad_clamp_fusion.7), kind=kCustom, calls=%fused_computation.clone.clone.1 | custom fusion | bytes 2097184 | tf_op jit(solution)/shard_map/while/body/eval_jaxpr/gather | solution.py:115
  54.5 0.8 convolution_add_fusion.7
  55.3 15.2 %all-gather.13.cloned.1.call-done = bf16[16,4,16,1152]{3,2,1,0:T(8,128)(2,1)} async-done(((bf16[4,4,16,1152]{3,2,1,0:T(8,128)(2,1)}), bf16[16,4,16,1152]{3,2,1,0:T(8,128)(2,1)}) %all-gather.13.cloned.1.call-update) | async-done | bytes 2359312 | tf_op jit(solution)/shard_map/all_gather | solution.py:28
  70.5 2.2 compare_reduce_fusion
  75.0 0.8 dynamic-slice_bitcast_fusion
  76.0 45.4 %while.56 = (s32[]{:T(128)}, f32[4,4,16]{2,1,0:T(4,128)S(1)}, f32[4,4,16]{2,1,0:T(4,128)S(1)}, f32[4,4,16,64]{3,2,1,0:T(8,128)S(1)}, s32[]{:T(128)}, /*index=5*/...) while((s32[]{:T(128)}, f32[4,4,16]{2,1,0:T(4,128)S(1)}, ...), condition=%wide.region_8.9_spmd.clone, body=%wide.region_5.8_spmd.clone.sunk | while | flops 237031712 | bytes 12771671 | solution.py:139
  76.8 4.0 %gather_fusion.2 = bf16[8,2,128,256]{3,2,1,0:T(8,128)(2,1)S(1)} fusion(bf16[64,2,128,256]{3,2,1,0:T(8,128)(2,1)} %get-tuple-element.1001, s32[1024]{0:T(1024)S(1)} %pad_clamp_fusion.8), kind=kCustom, calls=%fused_computation.1.clone.clone.1 | custom fusion | bytes 2097184 | tf_op jit(solution)/shard_map/while/body/eval_jaxpr/gather | solution.py:115
  82.8 0.8 convolution_add_fusion.8
  84.4 4.0 %gather_fusion.2 = bf16[8,2,128,256]{3,2,1,0:T(8,128)(2,1)S(1)} fusion(bf16[64,2,128,256]{3,2,1,0:T(8,128)(2,1)} %get-tuple-element.1001, s32[1024]{0:T(1024)S(1)} %pad_clamp_fusion.8), kind=kCustom, calls=%fused_computation.1.clone.clone.1 | custom fusion | bytes 2097184 | tf_op jit(solution)/shard_map/while/body/eval_jaxpr/gather | solution.py:115
  90.3 0.8 convolution_add_fusion.8
  91.9 4.0 %gather_fusion.2 = bf16[8,2,128,256]{3,2,1,0:T(8,128)(2,1)S(1)} fusion(bf16[64,2,128,256]{3,2,1,0:T(8,128)(2,1)} %get-tuple-element.1001, s32[1024]{0:T(1024)S(1)} %pad_clamp_fusion.8), kind=kCustom, calls=%fused_computation.1.clone.clone.1 | custom fusion | bytes 2097184 | tf_op jit(solution)/shard_map/while/body/eval_jaxpr/gather | solution.py:115
  97.9 0.8 convolution_add_fusion.8
  99.5 4.0 %gather_fusion.2 = bf16[8,2,128,256]{3,2,1,0:T(8,128)(2,1)S(1)} fusion(bf16[64,2,128,256]{3,2,1,0:T(8,128)(2,1)} %get-tuple-element.1001, s32[1024]{0:T(1024)S(1)} %pad_clamp_fusion.8), kind=kCustom, calls=%fused_computation.1.clone.clone.1 | custom fusion | bytes 2097184 | tf_op jit(solution)/shard_map/while/body/eval_jaxpr/gather | solution.py:115
  105.4 0.8 convolution_add_fusion.8
  107.0 4.0 %gather_fusion.2 = bf16[8,2,128,256]{3,2,1,0:T(8,128)(2,1)S(1)} fusion(bf16[64,2,128,256]{3,2,1,0:T(8,128)(2,1)} %get-tuple-element.1001, s32[1024]{0:T(1024)S(1)} %pad_clamp_fusion.8), kind=kCustom, calls=%fused_computation.1.clone.clone.1 | custom fusion | bytes 2097184 | tf_op jit(solution)/shard_map/while/body/eval_jaxpr/gather | solution.py:115
  113.0 0.8 convolution_add_fusion.8
  114.6 4.0 %gather_fusion.2 = bf16[8,2,128,256]{3,2,1,0:T(8,128)(2,1)S(1)} fusion(bf16[64,2,128,256]{3,2,1,0:T(8,128)(2,1)} %get-tuple-element.1001, s32[1024]{0:T(1024)S(1)} %pad_clamp_fusion.8), kind=kCustom, calls=%fused_computation.1.clone.clone.1 | custom fusion | bytes 2097184 | tf_op jit(solution)/shard_map/while/body/eval_jaxpr/gather | solution.py:115
  120.5 0.8 convolution_add_fusion.8
  121.9 9.5 %all-gather.4 = bf16[64,1152]{1,0:T(8,128)(2,1)S(1)} all-gather(bf16[16,1152]{1,0:T(8,128)(2,1)S(1)} %concatenate.29), channel_id=6, replica_groups=mesh['z'=4,'x'=4,'y'=4,'mlp'=2] {'y'}, dimensions={0}, use_global_device_ids=true | all-gather | bytes 184320 | tf_op jit(solution)/shard_map/all_gather | solution.py:26
  131.4 11.0 %all-gather.5 = bf16[16,16,1152]{2,1,0:T(8,128)(2,1)} all-gather(bf16[4,16,1152]{2,1,0:T(8,128)(2,1)S(1)} %bitcast.206), channel_id=7, replica_groups=mesh['z'=4,'x'=4,'y'=4,'mlp'=2] {'x'}, dimensions={0}, use_global_device_ids=true | all-gather | bytes 737280 | tf_op jit(solution)/shard_map/all_gather | solution.py:27
  142.5 1.0 pad_maximum_fusion
  145.8 23.0 %while.54 = (s32[]{:T(128)}, f32[4,4,16]{2,1,0:T(4,128)S(1)}, f32[4,4,16]{2,1,0:T(4,128)S(1)}, f32[4,4,16,64]{3,2,1,0:T(8,128)S(1)}, s32[]{:T(128)}, /*index=5*/...) while((s32[]{:T(128)}, f32[4,4,16]{2,1,0:T(4,128)S(1)}, ...), condition=%wide.region_12.13_spmd.clone, body=%wide.region_9.12_spmd.clone.sunk | while | flops 237014560 | bytes 12771671 | solution.py:139
  146.6 4.0 %gather_fusion = bf16[8,2,128,256]{3,2,1,0:T(8,128)(2,1)S(1)} fusion(bf16[64,2,128,256]{3,2,1,0:T(8,128)(2,1)} %get-tuple-element.1042, s32[1024]{0:T(1024)S(1)} %pad_clamp_fusion.6), kind=kCustom, calls=%fused_computation.2.clone.clone.1 | custom fusion | bytes 2097184 | tf_op jit(solution)/shard_map/while/body/eval_jaxpr/gather | solution.py:115
  152.5 0.8 convolution_add_fusion.6
  154.1 4.4 %gather_fusion = bf16[8,2,128,256]{3,2,1,0:T(8,128)(2,1)S(1)} fusion(bf16[64,2,128,256]{3,2,1,0:T(8,128)(2,1)} %get-tuple-element.1042, s32[1024]{0:T(1024)S(1)} %pad_clamp_fusion.6), kind=kCustom, calls=%fused_computation.2.clone.clone.1 | custom fusion | bytes 2097184 | tf_op jit(solution)/shard_map/while/body/eval_jaxpr/gather | solution.py:115
  160.4 0.8 convolution_add_fusion.6
  162.0 4.0 %gather_fusion = bf16[8,2,128,256]{3,2,1,0:T(8,128)(2,1)S(1)} fusion(bf16[64,2,128,256]{3,2,1,0:T(8,128)(2,1)} %get-tuple-element.1042, s32[1024]{0:T(1024)S(1)} %pad_clamp_fusion.6), kind=kCustom, calls=%fused_computation.2.clone.clone.1 | custom fusion | bytes 2097184 | tf_op jit(solution)/shard_map/while/body/eval_jaxpr/gather | solution.py:115
  168.0 0.8 convolution_add_fusion.6
  168.8 11.4 %all-gather.15.cloned.1.call-done = bf16[16,4,16,1152]{3,2,1,0:T(8,128)(2,1)} async-done(((bf16[4,4,16,1152]{3,2,1,0:T(8,128)(2,1)}), bf16[16,4,16,1152]{3,2,1,0:T(8,128)(2,1)}) %all-gather.15.cloned.1.call-update) | async-done | bytes 2359312 | tf_op jit(solution)/shard_map/all_gather | solution.py:28
  181.5 91.1 %all-gather.11.cloned.1.call-done = bf16[48,64,2048]{2,1,0:T(8,128)(2,1)} async-done(((bf16[3,64,2048]{2,1,0:T(8,128)(2,1)}), bf16[48,64,2048]{2,1,0:T(8,128)(2,1)}) %all-gather.11.cloned.1.call-update) | async-done | bytes 12582928 | tf_op jit(solution)/shard_map/all_gather | solution.py:101
  273.4 3.0 fusion.104
  277.1 1.2 collective-permute-done
  278.5 11.2 %all_gather.62 = bf16[128,2048]{1,0:T(8,128)(2,1)S(1)} all-gather(bf16[32,2048]{1,0:T(8,128)(2,1)S(1)} %fusion.60), channel_id=1, replica_groups=mesh['z'=4,'x'=4,'y'=4,'mlp'=2] {'y'}, dimensions={0}, use_global_device_ids=true | all-gather | bytes 655360 | tf_op jit(solution)/shard_map/all_gather | solution.py:223
  289.7 3.4 fusion.40
  293.2 7.3 %fusion.41 = f32[128,2048]{1,0:T(8,128)} fusion(bf16[128,2048]{1,0:T(8,128)(2,1)S(1)} %all_gather.62, f32[128,16,64]{0,2,1:T(8,128)S(1)} %fusion.40, bf16[16,3,64,2048]{3,2,1,0:T(8,128)(2,1)} %bitcast.221), kind=kOutput, calls=%fused_computation.72 | convolution fusion | flops 1074528256 | bytes 10485760 | tf_op jit(solution)/shard_map/dot_general | solution.py:229
  301.9 29.2 %reduce-scatter.2.cloned.1.call-done = f32[16,2048]{1,0:T(8,128)} async-done(((f32[128,2048]{1,0:T(8,128)}), f32[16,2048]{1,0:T(8,128)}) %reduce-scatter.2.cloned.1.call-update) | async-done | bytes 131088 | tf_op jit(solution)/shard_map/reduce_scatter | solution.py:232
  331.1 0.9 add_convert_fusion.1
  332.0 5.1 %all_gather.63 = bf16[32,2048]{1,0:T(8,128)(2,1)S(1)} all-gather(bf16[16,2048]{1,0:T(8,128)(2,1)S(1)} %add_convert_fusion.1), channel_id=1, replica_groups=mesh['z'=4,'x'=4,'y'=4,'mlp'=2] {'mlp'}, dimensions={0}, use_global_device_ids=true | all-gather | bytes 196608 | tf_op jit(solution)/shard_map/all_gather | solution.py:235
  337.2 4.7 %convolution_convert_fusion = bf16[32,1536]{1,0:T(8,128)(2,1)} fusion(bf16[2048,1536]{1,0:T(8,128)(2,1)} %param.37, bf16[32,2048]{1,0:T(8,128)(2,1)S(1)} %all_gather.63, f32[2048]{0:T(1024)S(1)} %convert_element_type.147, f32[32]{0:T(128)S(1)} %add_rsqrt_fusion), kind=kOutput, calls=%fused_computation.73 | convolution fusion | flops 201637888 | bytes 6529152 | tf_op jit(solution)/shard_map/dot_general | solution.py:237
  (249 shorter events, 41.2 us)
Async XLA Ops:
  7.2 63.3 %all-gather.13.cloned.1.call-start = ((), (), s32[]{:S(2)}) async-start(), calls=%async_computation.3 | async-start | bytes 2949120 | tf_op jit(solution)/shard_map/all_gather | solution.py:28
  30.4 149.9 %all-gather.15.cloned.1.call-start = ((), (), s32[]{:S(2)}) async-start(), calls=%async_computation.4 | async-start | bytes 2949120 | tf_op jit(solution)/shard_map/all_gather | solution.py:28
  75.9 66.6 %copy-start = (bf16[2,64,2048]{2,1,0:T(8,128)(2,1)S(1)}, bf16[2,64,2048]{2,1,0:T(8,128)(2,1)}, u32[]{:S(2)}) copy-start(bf16[2,64,2048]{2,1,0:T(8,128)(2,1)} %param.34) | copy-start | bytes 1572868
  75.9 66.6 %copy-start.3 = (bf16[64,2048]{1,0:T(8,128)(2,1)S(1)}, bf16[64,2048]{1,0:T(8,128)(2,1)}, u32[]{:S(2)}) copy-start(bf16[64,2048]{1,0:T(8,128)(2,1)} %param.35) | copy-start | bytes 786436
  75.9 67.8 %copy-start.2 = (bf16[32,1024]{1,0:T(8,128)(2,1)S(1)}, bf16[32,1024]{1,0:T(8,128)(2,1)}, u32[]{:S(2)}) copy-start(bf16[32,1024]{1,0:T(8,128)(2,1)} %param.23) | copy-start | bytes 196612
  76.0 68.0 %copy-start.8 = (s32[2]{0:T(128)S(1)}, s32[2]{0:T(128)}, u32[]{:S(2)}) copy-start(s32[2]{0:T(128)} %param.26) | copy-start | bytes 28
  76.0 68.0 %copy-start.7 = (s32[2,16]{1,0:T(2,128)S(1)}, s32[2,16]{1,0:T(2,128)}, u32[]{:S(2)}) copy-start(s32[2,16]{1,0:T(2,128)} %param.25) | copy-start | bytes 388
  76.0 68.9 %copy-start.1 = (bf16[32,2,256]{2,1,0:T(2,128)(2,1)S(1)}, bf16[32,2,256]{2,1,0:T(2,128)(2,1)}, u32[]{:S(2)}) copy-start(bf16[32,2,256]{2,1,0:T(2,128)(2,1)} %param.24) | copy-start | bytes 98308
  142.4 130.1 %all-gather.11.cloned.1.call-start = ((), (), s32[]{:S(2)}) async-start(), calls=%async_computation.2 | async-start | bytes 13369344 | tf_op jit(solution)/shard_map/all_gather | solution.py:101
  143.5 187.6 %reduce-scatter.2.cloned.1.call-start = ((), (), s32[]{:S(2)}) async-start(), calls=%async_computation.1 | async-start | bytes 1179648 | tf_op jit(solution)/shard_map/reduce_scatter | solution.py:232
  145.8 131.3 %copy-start.5 = (bf16[2048]{0:T(1024)(128)(2,1)S(1)}, bf16[2048]{0:T(1024)(128)(2,1)}, u32[]{:S(2)}) copy-start(bf16[2048]{0:T(1024)(128)(2,1)} %param.33) | copy-start | bytes 12292
  145.8 132.4 %copy-start.4 = (bf16[32,2048]{1,0:T(8,128)(2,1)S(1)}, bf16[32,2048]{1,0:T(8,128)(2,1)}, u32[]{:S(2)}) copy-start(bf16[32,2048]{1,0:T(8,128)(2,1)} %param.22) | copy-start | bytes 393220
  276.4 1.8 collective-permute-start
  293.2 7.4 %copy-start.6 = (bf16[2048]{0:T(1024)(128)(2,1)S(1)}, bf16[2048]{0:T(1024)(128)(2,1)}, u32[]{:S(2)}) copy-start(bf16[2048]{0:T(1024)(128)(2,1)} %param.36) | copy-start | bytes 12292
  293.2 7.4 %copy-start.9 = (s32[2]{0:T(128)S(1)}, s32[2]{0:T(128)}, u32[]{:S(2)}) copy-start(s32[2]{0:T(128)} %param.27) | copy-start | bytes 28
Sparse Core Ops, SparseCore 0:
  30.5 39.9 all-gather.12
  142.6 37.6 all-gather.14
  182.4 90.0 all-gather.10
  300.7 30.3 reduce-scatter.1

commit v4 on v3

--- a/solution.py
+++ b/solution.py
@@ -20,13 +20,6 @@
     high = values.astype(jnp.bfloat16)
     low = (values - high.astype(jnp.float32)).astype(jnp.bfloat16)
     return jnp.concatenate([high, low], axis=1)
-
-
-def gather_lines(packet):
-    lines = lax.all_gather(packet, "y", axis=0, tiled=False)
-    lines = lax.all_gather(lines, "x", axis=0, tiled=False)
-    lines = lax.all_gather(lines, "z", axis=0, tiled=False)
-    return lines.reshape((-1,) + packet.shape)
 
 
 def ancestors(parents):
@@ -96,7 +89,7 @@
     q_width = q_in.shape[1]
     dest_col = jnp.broadcast_to(prev_owner[0].astype(q_in.dtype), (tree_len, TAG))
     q_packet = jnp.concatenate([q_in[tree_len:], dest_col], axis=1)
-    every_query = gather_lines(q_packet)
+    every_query = lax.all_gather(q_packet, REQ, axis=0, tiled=False)
     own_w = jnp.stack([w_in[0], w_in[1], w_down])
     all_w = lax.all_gather(own_w, ("z", "x"), axis=0, tiled=False)
     page_len = cache.shape[2]
@@ -145,8 +138,7 @@
         jnp.zeros(stat_shape + (HEAD_DIM,), jnp.float32),
     )
     own_queries = queries[0]
-    split = num_blocks // 2
-    own_state = attend(0, own_queries, 0, split, start_state)
+    own_state = attend(0, own_queries, 0, num_blocks, start_state)
     own_state, every_query = lax.optimization_barrier((own_state, every_query))
     dests = every_query[:, 0, q_width].astype(jnp.int32)
     senders = jnp.arange(dests.shape[0], dtype=jnp.int32)
@@ -154,6 +146,9 @@
     foreign = lax.dynamic_index_in_dim(every_query, sender, 0, keepdims=False)[:, :q_width]
     foreign = foreign.reshape(tree_len, kv_local, GROUP, HEAD_DIM)
     f_running, f_total, f_accum = attend(1, foreign, 0, num_blocks, start_state)
+    all_w, f_running, f_total, f_accum = lax.optimization_barrier(
+        (all_w, f_running, f_total, f_accum)
+    )
     f_out = f_accum / f_total[..., None]
     sent_out = jnp.transpose(f_out, (2, 0, 1, 3)).reshape(
         tree_len, kv_local * GROUP * HEAD_DIM
@@ -165,10 +160,8 @@
     )
     pad = jnp.zeros((tree_len, TAG - stats.shape[1]), jnp.bfloat16)
     r_packet = jnp.concatenate([sent_out.astype(jnp.bfloat16), stats, pad], axis=1)
-    r_packet, own_state = lax.optimization_barrier((r_packet, own_state))
-    back = gather_lines(r_packet)
-    running, total, accum = attend(0, own_queries, split, num_blocks, own_state)
-    all_w, running, total, accum = lax.optimization_barrier((all_w, running, total, accum))
+    back = lax.all_gather(r_packet, REQ, axis=0, tiled=False)
+    running, total, accum = own_state
     cache_out = accum / total[..., None]
     got = lax.dynamic_index_in_dim(back, prev_owner[0], 0, keepdims=False).astype(jnp.float32)
     heads = kv_local * GROUP

time: 350 us -> 316 us (0.903)
  blocking collectives: 58.5 us -> 15.1 us
  local copies, waits for them, and re-layouts: 69.2 us -> 77.3 us
    all_gather x2, waiting for transfers between devices: 26.6 us -> 85.2 us  [the longest x1 64.6 us: per_device(): back = lax.all_gather(r_packet, REQ, axis=0, tiled=False)]
    all_gather x1, waiting for transfers between devices: 91.1 us -> 34.1 us  [per_device(): all_w = lax.all_gather(own_w, ('z', 'x'), axis=0, tiled=False)]
    all_gather x4 -> x0, blocking collectives: 42.3 us -> none  [the longest x2 22.1 us: gather_lines(): lines = lax.all_gather(lines, 'x', axis=0, tiled=False)]
    optimization_barrier x0 -> x1, local copies, waits for them, and re-layouts: none -> 6.19 us  [per_device(): own_state, every_query = lax.optimization_barrier((own_state, every_query))]
  transfers between devices with their start and end apart: 5 -> 5, of which waited for: 5 -> 5; matrix products, arithmetic and copies ran while one was open for 15% -> 34% of each run, Pallas kernels for 0% -> 0%
where the time goes in v4:
time: 316 us; the launch traced here: 315 us
  waiting for transfers between devices  149 us (47%)
  local copies, waits for them, and re-layouts  77.3 us (24%)
  matrix products  34.6 us (11%)
  other arithmetic  19.1 us (6%)
  between operations  16.7 us (5%)
  blocking collectives  15.1 us (5%)
    all_gather x1, waiting for transfers between devices, per_device(): back = lax.all_gather(r_packet, REQ, axis=0, tiled=False)  64.6 us
    gather x12, local copies, waits for them, and re-layouts, attend_block(): gathered = cache[page_ids]  49.1 us
    all_gather x1, waiting for transfers between devices, per_device(): all_w = lax.all_gather(own_w, ('z', 'x'), axis=0, tiled=False)  34.1 us
    reduce_scatter x1, waiting for transfers between devices, per_device(): lax.psum_scatter(partial, ('y', 'mlp'), scatter_dimension=0, tiled=True)  28.1 us
    all_gather x1, waiting for transfers between devices, per_device(): every_query = lax.all_gather(q_packet, REQ, axis=0, tiled=False)  20.6 us
    all_gather x1, blocking collectives, per_device(): group_rows = lax.all_gather(normed, 'y', axis=0, tiled=True)  10.1 us
    dot_general x12, matrix products, attend_block(): jnp.einsum('ghqk,kge->ghqe', weights, value_rows.astype(jnp.float32), pre...  9.66 us
    lt x12, other arithmetic, attend_block(): visible = block * block_keys + positions < length  7.66 us
  transfers between devices with their start and end apart: 5, of which 5 were waited for; matrix products, arithmetic and copies ran while one was open for 34% of the time, Pallas kernels for 0%

profile of v4, /device:TPU:1, one launch (start us, length us, event | category | flops | bytes accessed | tf_op | source)
XLA Modules:
  0.0 314.5 jit_solution(1284628045455032757)
XLA Ops:
  7.2 0.8 fusion.88
  9.3 2.1 pad_maximum_fusion
  11.7 1.3 fusion.89
  13.0 0.8 slice_bitcast_fusion.15
  13.8 45.3 %while.36 = (s32[]{:T(128)}, f32[4,4,16]{2,1,0:T(4,128)S(1)}, f32[4,4,16]{2,1,0:T(4,128)S(1)}, f32[4,4,16,64]{3,2,1,0:T(8,128)S(1)}, s32[]{:T(128)}, /*index=5*/...) while((s32[]{:T(128)}, f32[4,4,16]{2,1,0:T(4,128)S(1)}, ...), condition=%wide.region_3.4_spmd.clone, body=%wide.region_0.3_spmd.clone.sunk | while | flops 237031712 | bytes 12771663 | solution.py:132
  13.9 4.0 %gather_fusion = bf16[8,2,128,256]{3,2,1,0:T(8,128)(2,1)S(1)} fusion(bf16[64,2,128,256]{3,2,1,0:T(8,128)(2,1)} %get-tuple-element.666, s32[1024]{0:T(1024)S(1)} %pad_clamp_fusion.4), kind=kCustom, calls=%fused_computation.clone.clone.1 | custom fusion | bytes 2097184 | tf_op jit(solution)/shard_map/while/body/eval_jaxpr/gather | solution.py:108
  20.5 0.8 convolution_add_fusion.4
  21.4 4.0 %gather_fusion = bf16[8,2,128,256]{3,2,1,0:T(8,128)(2,1)S(1)} fusion(bf16[64,2,128,256]{3,2,1,0:T(8,128)(2,1)} %get-tuple-element.666, s32[1024]{0:T(1024)S(1)} %pad_clamp_fusion.4), kind=kCustom, calls=%fused_computation.clone.clone.1 | custom fusion | bytes 2097184 | tf_op jit(solution)/shard_map/while/body/eval_jaxpr/gather | solution.py:108
  28.0 0.8 convolution_add_fusion.4
  28.9 4.0 %gather_fusion = bf16[8,2,128,256]{3,2,1,0:T(8,128)(2,1)S(1)} fusion(bf16[64,2,128,256]{3,2,1,0:T(8,128)(2,1)} %get-tuple-element.666, s32[1024]{0:T(1024)S(1)} %pad_clamp_fusion.4), kind=kCustom, calls=%fused_computation.clone.clone.1 | custom fusion | bytes 2097184 | tf_op jit(solution)/shard_map/while/body/eval_jaxpr/gather | solution.py:108
  35.6 0.8 convolution_add_fusion.4
  36.5 4.0 %gather_fusion = bf16[8,2,128,256]{3,2,1,0:T(8,128)(2,1)S(1)} fusion(bf16[64,2,128,256]{3,2,1,0:T(8,128)(2,1)} %get-tuple-element.666, s32[1024]{0:T(1024)S(1)} %pad_clamp_fusion.4), kind=kCustom, calls=%fused_computation.clone.clone.1 | custom fusion | bytes 2097184 | tf_op jit(solution)/shard_map/while/body/eval_jaxpr/gather | solution.py:108
  43.1 0.8 convolution_add_fusion.4
  44.0 4.0 %gather_fusion = bf16[8,2,128,256]{3,2,1,0:T(8,128)(2,1)S(1)} fusion(bf16[64,2,128,256]{3,2,1,0:T(8,128)(2,1)} %get-tuple-element.666, s32[1024]{0:T(1024)S(1)} %pad_clamp_fusion.4), kind=kCustom, calls=%fused_computation.clone.clone.1 | custom fusion | bytes 2097184 | tf_op jit(solution)/shard_map/while/body/eval_jaxpr/gather | solution.py:108
  50.7 0.8 convolution_add_fusion.4
  51.6 4.0 %gather_fusion = bf16[8,2,128,256]{3,2,1,0:T(8,128)(2,1)S(1)} fusion(bf16[64,2,128,256]{3,2,1,0:T(8,128)(2,1)} %get-tuple-element.666, s32[1024]{0:T(1024)S(1)} %pad_clamp_fusion.4), kind=kCustom, calls=%fused_computation.clone.clone.1 | custom fusion | bytes 2097184 | tf_op jit(solution)/shard_map/while/body/eval_jaxpr/gather | solution.py:108
  58.2 0.8 convolution_add_fusion.4
  59.1 20.6 %all-gather.7.cloned.1.call-done = bf16[1024,1152]{1,0:T(8,128)(2,1)} async-done(((bf16[16,1152]{1,0:T(8,128)(2,1)}), bf16[1024,1152]{1,0:T(8,128)(2,1)}) %all-gather.7.cloned.1.call-update) | async-done | bytes 2359312 | tf_op jit(solution)/shard_map/all_gather | solution.py:92
  79.7 6.2 %copy.81 = bf16[64,16,1152]{0,2,1:T(8,128)(2,1)} copy(bf16[64,16,1152]{2,1,0:T(8,128)(2,1)} %bitcast.151) | data formatting | bytes 4718592 | tf_op jit(solution)/shard_map/optimization_barrier | solution.py:142
  85.9 1.3 fusion.78
  89.1 0.8 dynamic-slice_bitcast_fusion
  90.1 46.1 %while.37 = (s32[]{:T(128)}, f32[4,4,16]{2,1,0:T(4,128)S(1)}, f32[4,4,16]{2,1,0:T(4,128)S(1)}, f32[4,4,16,64]{3,2,1,0:T(8,128)S(1)}, s32[]{:T(128)}, /*index=5*/...) while((s32[]{:T(128)}, f32[4,4,16]{2,1,0:T(4,128)S(1)}, ...), condition=%wide.region_8.9_spmd.clone, body=%wide.region_5.8_spmd.clone.sunk | while | flops 237031712 | bytes 12771663 | solution.py:132
  90.2 4.4 %gather_fusion.1 = bf16[8,2,128,256]{3,2,1,0:T(8,128)(2,1)S(1)} fusion(bf16[64,2,128,256]{3,2,1,0:T(8,128)(2,1)} %get-tuple-element.705, s32[1024]{0:T(1024)S(1)} %pad_clamp_fusion.5), kind=kCustom, calls=%fused_computation.1.clone.clone.1 | custom fusion | bytes 2097184 | tf_op jit(solution)/shard_map/while/body/eval_jaxpr/gather | solution.py:108
  97.2 0.8 convolution_add_fusion.5
  98.1 4.2 %gather_fusion.1 = bf16[8,2,128,256]{3,2,1,0:T(8,128)(2,1)S(1)} fusion(bf16[64,2,128,256]{3,2,1,0:T(8,128)(2,1)} %get-tuple-element.705, s32[1024]{0:T(1024)S(1)} %pad_clamp_fusion.5), kind=kCustom, calls=%fused_computation.1.clone.clone.1 | custom fusion | bytes 2097184 | tf_op jit(solution)/shard_map/while/body/eval_jaxpr/gather | solution.py:108
  104.9 0.8 convolution_add_fusion.5
  105.8 4.0 %gather_fusion.1 = bf16[8,2,128,256]{3,2,1,0:T(8,128)(2,1)S(1)} fusion(bf16[64,2,128,256]{3,2,1,0:T(8,128)(2,1)} %get-tuple-element.705, s32[1024]{0:T(1024)S(1)} %pad_clamp_fusion.5), kind=kCustom, calls=%fused_computation.1.clone.clone.1 | custom fusion | bytes 2097184 | tf_op jit(solution)/shard_map/while/body/eval_jaxpr/gather | solution.py:108
  112.4 0.8 convolution_add_fusion.5
  113.3 4.3 %gather_fusion.1 = bf16[8,2,128,256]{3,2,1,0:T(8,128)(2,1)S(1)} fusion(bf16[64,2,128,256]{3,2,1,0:T(8,128)(2,1)} %get-tuple-element.705, s32[1024]{0:T(1024)S(1)} %pad_clamp_fusion.5), kind=kCustom, calls=%fused_computation.1.clone.clone.1 | custom fusion | bytes 2097184 | tf_op jit(solution)/shard_map/while/body/eval_jaxpr/gather | solution.py:108
  120.1 0.8 convolution_add_fusion.5
  121.0 4.0 %gather_fusion.1 = bf16[8,2,128,256]{3,2,1,0:T(8,128)(2,1)S(1)} fusion(bf16[64,2,128,256]{3,2,1,0:T(8,128)(2,1)} %get-tuple-element.705, s32[1024]{0:T(1024)S(1)} %pad_clamp_fusion.5), kind=kCustom, calls=%fused_computation.1.clone.clone.1 | custom fusion | bytes 2097184 | tf_op jit(solution)/shard_map/while/body/eval_jaxpr/gather | solution.py:108
  127.6 0.8 convolution_add_fusion.5
  128.5 4.2 %gather_fusion.1 = bf16[8,2,128,256]{3,2,1,0:T(8,128)(2,1)S(1)} fusion(bf16[64,2,128,256]{3,2,1,0:T(8,128)(2,1)} %get-tuple-element.705, s32[1024]{0:T(1024)S(1)} %pad_clamp_fusion.5), kind=kCustom, calls=%fused_computation.1.clone.clone.1 | custom fusion | bytes 2097184 | tf_op jit(solution)/shard_map/while/body/eval_jaxpr/gather | solution.py:108
  135.3 0.8 convolution_add_fusion.5
  136.2 34.1 %all-gather.9.cloned.1.call-done = bf16[48,64,2048]{2,1,0:T(8,128)(2,1)} async-done(((bf16[3,64,2048]{2,1,0:T(8,128)(2,1)}), bf16[48,64,2048]{2,1,0:T(8,128)(2,1)}) %all-gather.9.cloned.1.call-update) | async-done | bytes 12582928 | tf_op jit(solution)/shard_map/all_gather | solution.py:94
  170.7 0.7 concatenate.29
  173.7 64.6 %all-gather.11.cloned.1.call-done = bf16[1024,1152]{1,0:T(8,128)(2,1)} async-done(((bf16[16,1152]{1,0:T(8,128)(2,1)}), bf16[1024,1152]{1,0:T(8,128)(2,1)}) %all-gather.11.cloned.1.call-update) | async-done | bytes 2359312 | tf_op jit(solution)/shard_map/all_gather | solution.py:163
  238.3 0.8 bitcast_convert_fusion
  240.2 3.0 fusion.91
  243.2 1.6 collective-permute-start
  244.8 1.2 collective-permute-done
  246.2 10.1 %all_gather.30 = bf16[128,2048]{1,0:T(8,128)(2,1)S(1)} all-gather(bf16[32,2048]{1,0:T(8,128)(2,1)S(1)} %fusion.48), channel_id=1, replica_groups=mesh['z'=4,'x'=4,'y'=4,'mlp'=2] {'y'}, dimensions={0}, use_global_device_ids=true | all-gather | bytes 655360 | tf_op jit(solution)/shard_map/all_gather | solution.py:216
  256.3 3.4 %fusion.28 = f32[128,16,64]{0,2,1:T(8,128)S(1)} fusion(bf16[128,2048]{1,0:T(8,128)(2,1)S(1)} %all_gather.30, bf16[16,3,64,2048]{3,2,1,0:T(8,128)(2,1)} %bitcast.167), kind=kOutput, calls=%fused_computation.51 | convolution fusion | flops 536870912 | bytes 5242880 | tf_op jit(solution)/shard_map/dot_general | solution.py:218
  259.8 7.3 %fusion.29 = f32[128,2048]{1,0:T(8,128)} fusion(bf16[128,2048]{1,0:T(8,128)(2,1)S(1)} %all_gather.30, f32[128,16,64]{0,2,1:T(8,128)S(1)} %fusion.28, bf16[16,3,64,2048]{3,2,1,0:T(8,128)(2,1)} %bitcast.168), kind=kOutput, calls=%fused_computation.52 | convolution fusion | flops 1074528256 | bytes 10485760 | tf_op jit(solution)/shard_map/dot_general | solution.py:222
  268.4 28.1 %reduce-scatter.2.cloned.1.call-done = f32[16,2048]{1,0:T(8,128)} async-done(((f32[128,2048]{1,0:T(8,128)}), f32[16,2048]{1,0:T(8,128)}) %reduce-scatter.2.cloned.1.call-update) | async-done | bytes 131088 | tf_op jit(solution)/shard_map/reduce_scatter | solution.py:225
  296.6 0.9 add_convert_fusion.1
  297.5 5.0 %all_gather.31 = bf16[32,2048]{1,0:T(8,128)(2,1)S(1)} all-gather(bf16[16,2048]{1,0:T(8,128)(2,1)S(1)} %add_convert_fusion.1), channel_id=1, replica_groups=mesh['z'=4,'x'=4,'y'=4,'mlp'=2] {'mlp'}, dimensions={0}, use_global_device_ids=true | all-gather | bytes 196608 | tf_op jit(solution)/shard_map/all_gather | solution.py:228
  302.7 4.7 %convolution_convert_fusion = bf16[32,1536]{1,0:T(8,128)(2,1)} fusion(bf16[2048,1536]{1,0:T(8,128)(2,1)} %param.35, bf16[32,2048]{1,0:T(8,128)(2,1)S(1)} %all_gather.31, f32[2048]{0:T(1024)S(1)} %convert_element_type.144, f32[32]{0:T(128)S(1)} %add_rsqrt_fusion), kind=kOutput, calls=%fused_computation.53 | convolution fusion | flops 201637888 | bytes 6529152 | tf_op jit(solution)/shard_map/dot_general | solution.py:230
  (240 shorter events, 38.4 us)
Async XLA Ops:
  7.2 72.5 %all-gather.7.cloned.1.call-start = ((), (), s32[]{:S(2)}) async-start(), calls=%async_computation.2 | async-start | bytes 2396160 | tf_op jit(solution)/shard_map/all_gather | solution.py:92
  9.3 161.0 %all-gather.9.cloned.1.call-start = ((), (), s32[]{:S(2)}) async-start(), calls=%async_computation.3 | async-start | bytes 13369344 | tf_op jit(solution)/shard_map/all_gather | solution.py:94
  11.4 226.8 %all-gather.11.cloned.1.call-start = ((), (), s32[]{:S(2)}) async-start(), calls=%async_computation.4 | async-start | bytes 2396160 | tf_op jit(solution)/shard_map/all_gather | solution.py:163
  90.0 81.5 %copy-start.1 = (bf16[32,1024]{1,0:T(8,128)(2,1)S(1)}, bf16[32,1024]{1,0:T(8,128)(2,1)}, u32[]{:S(2)}) copy-start(bf16[32,1024]{1,0:T(8,128)(2,1)} %param.21) | copy-start | bytes 196612
  90.1 81.6 %copy-start.6 = (s32[2]{0:T(128)S(1)}, s32[2]{0:T(128)}, u32[]{:S(2)}) copy-start(s32[2]{0:T(128)} %param.24) | copy-start | bytes 28
  90.1 81.7 %copy-start.5 = (s32[2,16]{1,0:T(2,128)S(1)}, s32[2,16]{1,0:T(2,128)}, u32[]{:S(2)}) copy-start(s32[2,16]{1,0:T(2,128)} %param.23) | copy-start | bytes 388
  90.1 82.6 %copy-start = (bf16[32,2,256]{2,1,0:T(2,128)(2,1)S(1)}, bf16[32,2,256]{2,1,0:T(2,128)(2,1)}, u32[]{:S(2)}) copy-start(bf16[32,2,256]{2,1,0:T(2,128)(2,1)} %param.22) | copy-start | bytes 98308
  136.2 108.6 %copy-start.3 = (bf16[2048]{0:T(1024)(128)(2,1)S(1)}, bf16[2048]{0:T(1024)(128)(2,1)}, u32[]{:S(2)}) copy-start(bf16[2048]{0:T(1024)(128)(2,1)} %param.31) | copy-start | bytes 12292
  136.2 109.8 %copy-start.2 = (bf16[32,2048]{1,0:T(8,128)(2,1)S(1)}, bf16[32,2048]{1,0:T(8,128)(2,1)}, u32[]{:S(2)}) copy-start(bf16[32,2048]{1,0:T(8,128)(2,1)} %param.20) | copy-start | bytes 393220
  171.5 125.1 %reduce-scatter.2.cloned.1.call-start = ((), (), s32[]{:S(2)}) async-start(), calls=%async_computation.1 | async-start | bytes 1179648 | tf_op jit(solution)/shard_map/reduce_scatter | solution.py:225
  243.2 2.7 collective-permute-start
  259.8 7.4 %copy-start.4 = (bf16[2048]{0:T(1024)(128)(2,1)S(1)}, bf16[2048]{0:T(1024)(128)(2,1)}, u32[]{:S(2)}) copy-start(bf16[2048]{0:T(1024)(128)(2,1)} %param.34) | copy-start | bytes 12292
  259.8 7.4 %copy-start.7 = (s32[2]{0:T(128)S(1)}, s32[2]{0:T(128)}, u32[]{:S(2)}) copy-start(s32[2]{0:T(128)} %param.25) | copy-start | bytes 28
Sparse Core Ops, SparseCore 0:
  11.3 68.2 all-gather.6
  81.8 88.4 all-gather.8
  173.6 64.6 all-gather.10
  267.2 29.2 reduce-scatter.1

commit v5 on v4

--- a/solution.py
+++ b/solution.py
@@ -90,62 +90,47 @@
     dest_col = jnp.broadcast_to(prev_owner[0].astype(q_in.dtype), (tree_len, TAG))
     q_packet = jnp.concatenate([q_in[tree_len:], dest_col], axis=1)
     every_query = lax.all_gather(q_packet, REQ, axis=0, tiled=False)
-    own_w = jnp.stack([w_in[0], w_in[1], w_down])
-    all_w = lax.all_gather(own_w, ("z", "x"), axis=0, tiled=False)
+    all_w = lax.all_gather(w_in, ("z", "x"), axis=1, tiled=False)
     page_len = cache.shape[2]
-    block_pages = math.gcd(held_table.shape[1], max(1, 1024 // page_len))
-    block_keys = block_pages * page_len
-    num_blocks = held_table.shape[1] // block_pages
-    positions = jnp.arange(block_keys, dtype=jnp.int32)
-
-    def attend(slot, slot_queries, first, last, state):
+    pool_pages = cache.shape[0]
+    pool_keys = cache[:, 0].reshape(pool_pages * page_len, kv_local, HEAD_DIM)
+    pool_values = cache[:, 1].reshape(pool_pages * page_len, kv_local, HEAD_DIM)
+    entries = held_table.shape[1]
+    page_ids = jnp.arange(pool_pages, dtype=jnp.int32)
+    entry_start = jnp.arange(entries, dtype=jnp.int32)[:, None] * page_len
+    in_page = jnp.arange(page_len, dtype=jnp.int32)[None, :]
+
+    def attend(slot, slot_queries, state):
         table = held_table[slot]
         length = held_len[slot]
-
-        def attend_block(block, state):
-            running, total, accum = state
-            page_ids = lax.dynamic_slice_in_dim(table, block * block_pages, block_pages, 0)
-            gathered = cache[page_ids]
-            key_rows = gathered[:, 0].reshape(block_keys, kv_local, HEAD_DIM)
-            value_rows = gathered[:, 1].reshape(block_keys, kv_local, HEAD_DIM)
-            scores = (
-                jnp.einsum(
-                    "qghe,kge->ghqk", slot_queries, key_rows, preferred_element_type=jnp.float32
-                )
-                * scale
-            )
-            visible = (block * block_keys + positions) < length
-            scores = jnp.where(visible, scores, masked_score)
-            newest = jnp.maximum(running, jnp.max(scores, axis=-1))
-            weights = jnp.where(visible, jnp.exp(scores - newest[..., None]), 0.0)
-            factor = jnp.exp(running - newest)
-            total = total * factor + jnp.sum(weights, axis=-1)
-            update = jnp.einsum(
-                "ghqk,kge->ghqe",
-                weights,
-                value_rows.astype(jnp.float32),
-                precision=lax.Precision.HIGHEST,
-            )
-            accum = accum * factor[..., None] + update
-            return (newest, total, accum)
-
-        return lax.fori_loop(first, last, attend_block, state)
-
-    stat_shape = (kv_local, GROUP, tree_len)
-    start_state = (
-        jnp.full(stat_shape, masked_score, jnp.float32),
-        jnp.zeros(stat_shape, jnp.float32),
-        jnp.zeros(stat_shape + (HEAD_DIM,), jnp.float32),
-    )
+        match = table[:, None] == page_ids[None, :]
+        valid = (entry_start + in_page) < length
+        visible = jnp.any(match[:, :, None] & valid[:, None, :], axis=0).reshape(-1)
+        scores = (
+            jnp.einsum("qghe,kge->ghqk", slot_queries, pool_keys, preferred_element_type=jnp.float32)
+            * scale
+        )
+        scores = jnp.where(visible, scores, masked_score)
+        running = jnp.max(scores, axis=-1)
+        weights = jnp.where(visible, jnp.exp(scores - running[..., None]), 0.0)
+        total = jnp.sum(weights, axis=-1)
+        accum = jnp.einsum(
+            "ghqk,kge->ghqe",
+            weights,
+            pool_values.astype(jnp.float32),
+            precision=lax.Precision.HIGHEST,
+        )
+        return (running, total, accum)
+
     own_queries = queries[0]
-    own_state = attend(0, own_queries, 0, num_blocks, start_state)
+    own_state = attend(0, own_queries, None)
     own_state, every_query = lax.optimization_barrier((own_state, every_query))
     dests = every_query[:, 0, q_width].astype(jnp.int32)
     senders = jnp.arange(dests.shape[0], dtype=jnp.int32)
     sender = jnp.sum(jnp.where(dests == device_id, senders, 0))
     foreign = lax.dynamic_index_in_dim(every_query, sender, 0, keepdims=False)[:, :q_width]
     foreign = foreign.reshape(tree_len, kv_local, GROUP, HEAD_DIM)
-    f_running, f_total, f_accum = attend(1, foreign, 0, num_blocks, start_state)
+    f_running, f_total, f_accum = attend(1, foreign, None)
     all_w, f_running, f_total, f_accum = lax.optimization_barrier(
         (all_w, f_running, f_total, f_accum)
     )
@@ -161,6 +146,8 @@
     pad = jnp.zeros((tree_len, TAG - stats.shape[1]), jnp.bfloat16)
     r_packet = jnp.concatenate([sent_out.astype(jnp.bfloat16), stats, pad], axis=1)
     back = lax.all_gather(r_packet, REQ, axis=0, tiled=False)
+    back, w_down = lax.optimization_barrier((back, w_down))
+    all_down = lax.all_gather(w_down, ("z", "x"), axis=0, tiled=False)
     running, total, accum = own_state
     cache_out = accum / total[..., None]
     got = lax.dynamic_index_in_dim(back, prev_owner[0], 0, keepdims=False).astype(jnp.float32)
@@ -215,13 +202,11 @@
     half_count = normed.shape[0] // lax.axis_size("mlp")
     group_rows = lax.all_gather(normed, "y", axis=0, tiled=True)
     dims = (((1,), (2,)), ((), ()))
-    gate = lax.dot_general(group_rows, all_w[:, 0], dims, preferred_element_type=jnp.float32)
-    up_part = lax.dot_general(group_rows, all_w[:, 1], dims, preferred_element_type=jnp.float32)
+    gate = lax.dot_general(group_rows, all_w[0], dims, preferred_element_type=jnp.float32)
+    up_part = lax.dot_general(group_rows, all_w[1], dims, preferred_element_type=jnp.float32)
     hidden = (jax.nn.silu(gate) * up_part).astype(jnp.bfloat16)
     down_dims = (((1, 2), (0, 1)), ((), ()))
-    partial = lax.dot_general(
-        hidden, all_w[:, 2], down_dims, preferred_element_type=jnp.float32
-    )
+    partial = lax.dot_general(hidden, all_down, down_dims, preferred_element_type=jnp.float32)
     mlp_half = lax.psum_scatter(partial, ("y", "mlp"), scatter_dimension=0, tiled=True)
     base_half = lax.dynamic_slice_in_dim(mixed, column * half_count, half_count, 0)
     out_half = (base_half.astype(jnp.float32) + mlp_half).astype(jnp.bfloat16)

time: 316 us -> 326 us (1.032)
  waiting for transfers between devices: 149 us -> 195 us
  local copies, waits for them, and re-layouts: 77.3 us -> 46.9 us
  other arithmetic: 19.1 us -> 10.6 us
  matrix products: 34.6 us -> 38.5 us
    gather x12 -> x0, local copies, waits for them, and re-layouts: 49.1 us -> none  [attend_block(): gathered = cache[page_ids]]
    all_gather x1 -> x2, waiting for transfers between devices: 34.1 us -> 77.4 us  [the longest x1 50 us: per_device(): all_w = lax.all_gather(w_in, ('z', 'x'), axis=1, tiled=False)]
    another operation x0 -> x2, local copies, waits for them, and re-layouts: none -> 14.6 us  [the longest x1 7.33 us: per_device(): pool_keys = cache[:, 0].reshape(pool_pages * page_len, kv_local, HEAD_DIM)]
    slice x36 -> x3, local copies, waits for them, and re-layouts: 8.65 us -> 19.3 us  [the longest x2 12.7 us: per_device(): pool_values = cache[:, 1].reshape(pool_pages * page_len, kv_local, HEAD_DIM)]
    lt x12 -> x1, other arithmetic: 7.66 us -> 1.35 us  [attend(): valid = entry_start + in_page < length]
    squeeze x25 -> x0, local copies, waits for them, and re-layouts: 6.15 us -> none  [the longest x12 2.7 us: attend_block(): key_rows = gathered[:, 0].reshape(block_keys, kv_local, HEAD_DIM)]
    dot_general x26 -> x6, matrix products: 24.8 us -> 28.7 us  [the longest x2 10.1 us: attend(): jnp.einsum('ghqk,kge->ghqe', weights, pool_values.astype(jnp.float32), pr...]
  transfers between devices with their start and end apart: 5 -> 6, of which waited for: 5 -> 6; matrix products, arithmetic and copies ran while one was open for 34% -> 24% of each run, Pallas kernels for 0% -> 0%
where the time goes in v5:
time: 326 us; the launch traced here: 325 us
  waiting for transfers between devices  195 us (60%)
  local copies, waits for them, and re-layouts  46.9 us (14%)
  matrix products  38.5 us (12%)
  between operations  16.7 us (5%)
  blocking collectives  16 us (5%)
  other arithmetic  10.6 us (3%)
    all_gather x1, waiting for transfers between devices, per_device(): back = lax.all_gather(r_packet, REQ, axis=0, tiled=False)  66.8 us
    all_gather x1, waiting for transfers between devices, per_device(): all_w = lax.all_gather(w_in, ('z', 'x'), axis=1, tiled=False)  50 us
    reduce_scatter x1, waiting for transfers between devices, per_device(): lax.psum_scatter(partial, ('y', 'mlp'), scatter_dimension=0, tiled=True)  27.5 us
    all_gather x1, waiting for transfers between devices, per_device(): all_down = lax.all_gather(w_down, ('z', 'x'), axis=0, tiled=False)  27.4 us
    all_gather x1, waiting for transfers between devices, per_device(): every_query = lax.all_gather(q_packet, REQ, axis=0, tiled=False)  21.1 us
    slice x2, local copies, waits for them, and re-layouts, per_device(): pool_values = cache[:, 1].reshape(pool_pages * page_len, kv_local, HEAD_DIM)  12.7 us
    all_gather x1, blocking collectives, per_device(): group_rows = lax.all_gather(normed, 'y', axis=0, tiled=True)  10.9 us
    dot_general x2, matrix products, attend(): jnp.einsum('ghqk,kge->ghqe', weights, pool_values.astype(jnp.float32), pr...  10.1 us
  transfers between devices with their start and end apart: 6, of which 6 were waited for; matrix products, arithmetic and copies ran while one was open for 24% of the time, Pallas kernels for 0%

profile of v5, /device:TPU:1, one launch (start us, length us, event | category | flops | bytes accessed | tf_op | source)
XLA Modules:
  0.0 325.1 jit_solution(10415423325515324926)
XLA Ops:
  7.2 0.8 fusion.91
  8.7 0.6 concatenate.28
  9.3 0.7 all-gather.11.cloned.1.call-update
  10.1 6.1 %fusion.90 = (bf16[64,1,128,256]{3,2,1,0:T(8,128)(2,1)}, bf16[64,1,128,256]{3,2,1,0:T(8,128)(2,1)}) fusion(bf16[64,2,128,256]{3,2,1,0:T(8,128)(2,1)} %param.22), kind=kLoop, calls=%fused_computation.136 | loop fusion | bytes 16777216 | tf_op jit(solution)/shard_map/slice | solution.py:97
  16.2 6.6 %copy.65 = bf16[64,1,128,256]{2,0,3,1:T(8,128)(2,1)} copy(bf16[64,1,128,256]{3,2,1,0:T(8,128)(2,1)} %get-tuple-element.35) | data formatting | bytes 8388608 | tf_op jit(solution)/shard_map/slice | solution.py:96
  22.8 7.3 %reshape.314 = bf16[8192,4,64,1]{0,2,1,3:T(8,128)(2,1)} reshape(bf16[64,1,128,256]{2,0,3,1:T(8,128)(2,1)} %copy.65) | data formatting | bytes 8388608 | tf_op jit(solution)/shard_map/reshape;squeeze | solution.py:96
  30.3 6.6 %copy.67 = bf16[64,1,128,256]{2,0,3,1:T(8,128)(2,1)} copy(bf16[64,1,128,256]{3,2,1,0:T(8,128)(2,1)} %get-tuple-element.34) | data formatting | bytes 8388608 | tf_op jit(solution)/shard_map/slice | solution.py:97
  36.9 7.3 %reshape.315 = bf16[8192,4,64,1]{0,2,1,3:T(8,128)(2,1)} reshape(bf16[64,1,128,256]{2,0,3,1:T(8,128)(2,1)} %copy.67) | data formatting | bytes 8388608 | tf_op jit(solution)/shard_map/reshape;squeeze | solution.py:97
  44.2 0.6 fusion.92
  45.0 1.4 fusion.67
  46.3 1.3 and_reduce_fusion
  47.6 3.7 %fusion.93 = (f32[4,4,16]{2,1,0:T(4,128)S(1)}, f32[4,4,16,8192]{3,2,1,0:T(8,128)S(1)}) fusion(bf16[16,4,4,64]{3,2,1,0:T(4,128)(2,1)S(1)} %squeeze.26, bf16[8192,4,64,1]{0,2,1,3:T(8,128)(2,1)} %reshape.314, pred[8192]{0:T(1024)(128)(4,1)S(1)} %bitcast.130), kind=kOutput, calls=%fused_computation.139 | convolution fusion | flops 274726656 | bytes 12624896 | tf_op jit(solution)/shard_map/qghe,kge->ghqk/dot_general | solution.py:110
  51.3 1.8 fusion.5
  53.1 0.4 copy-done
  53.5 5.1 %fusion.4 = f32[4,4,16,64]{3,2,1,0:T(8,128)S(1)} fusion(f32[4,4,16,8192]{3,2,1,0:T(8,128)S(1)} %get-tuple-element.47, bf16[8192,4,64,1]{0,2,1,3:T(8,128)(2,1)S(1)} %copy-done, f32[4,4,16]{2,1,0:T(4,128)S(1)} %get-tuple-element.20, pred[8192]{0:T(1024)(128)(4,1)S(1)} %bitcast.132), kind=kOutput, calls=%fused_computation.8 | convolution fusion | flops 1614807040 | bytes 12657664 | tf_op jit(solution)/shard_map/ghqk,kge->ghqe/dot_general | solution.py:117
  58.6 21.1 %all-gather.9.cloned.1.call-done = bf16[1024,1152]{1,0:T(8,128)(2,1)} async-done(((bf16[16,1152]{1,0:T(8,128)(2,1)}), bf16[1024,1152]{1,0:T(8,128)(2,1)}) %all-gather.9.cloned.1.call-update) | async-done | bytes 2359312 | tf_op jit(solution)/shard_map/all_gather | solution.py:92
  79.6 6.2 %copy.68 = bf16[64,16,1152]{0,2,1:T(8,128)(2,1)} copy(bf16[64,16,1152]{2,1,0:T(8,128)(2,1)} %bitcast.125) | data formatting | bytes 4718592 | tf_op jit(solution)/shard_map/optimization_barrier | solution.py:127
  85.8 1.3 fusion.82
  89.0 0.8 dynamic-slice_bitcast_fusion
  90.0 4.1 %fusion.94 = (f32[4,4,16]{2,1,0:T(4,128)S(1)}, f32[4,4,16,8192]{3,2,1,0:T(8,128)S(1)}) fusion(bf16[8192,4,64,1]{0,2,1,3:T(8,128)(2,1)} %reshape.314, bf16[16,4,4,64]{3,2,1,0:T(4,128)(2,1)S(1)} %reshape.300, pred[8192]{0:T(1024)(128)(4,1)S(1)} %bitcast.127), kind=kOutput, calls=%fused_computation.140 | convolution fusion | flops 274726656 | bytes 12624896 | tf_op jit(solution)/shard_map/qghe,kge->ghqk/dot_general | solution.py:110
  94.1 1.8 fusion.7
  95.9 5.1 %fusion.6 = f32[4,4,16,64]{3,2,1,0:T(8,128)S(1)} fusion(f32[4,4,16,8192]{3,2,1,0:T(8,128)S(1)} %get-tuple-element.49, bf16[8192,4,64,1]{0,2,1,3:T(8,128)(2,1)S(1)} %copy-done.1, f32[4,4,16]{2,1,0:T(4,128)S(1)} %get-tuple-element.18, pred[8192]{0:T(1024)(128)(4,1)S(1)} %bitcast.129), kind=kOutput, calls=%fused_computation.10 | convolution fusion | flops 1614807040 | bytes 12657664 | tf_op jit(solution)/shard_map/ghqk,kge->ghqe/dot_general | solution.py:117
  101.0 50.0 %all-gather.11.cloned.1.call-done = bf16[2,1024,2048]{2,1,0:T(8,128)(2,1)} async-done(((bf16[2,64,2048]{2,1,0:T(8,128)(2,1)}), bf16[2,1024,2048]{2,1,0:T(8,128)(2,1)}) %all-gather.11.cloned.1.call-update) | async-done | bytes 8388624 | tf_op jit(solution)/shard_map/all_gather | solution.py:93
  151.4 0.7 concatenate.29
  152.2 66.8 %all-gather.13.cloned.1.call-done = bf16[1024,1152]{1,0:T(8,128)(2,1)} async-done(((bf16[16,1152]{1,0:T(8,128)(2,1)}), bf16[1024,1152]{1,0:T(8,128)(2,1)}) %all-gather.13.cloned.1.call-update) | async-done | bytes 2359312 | tf_op jit(solution)/shard_map/all_gather | solution.py:148
  219.3 0.2 convolution_minimum_fusion.4
  219.5 0.1 convolution_minimum_fusion.3
  219.7 0.2 convolution_minimum_fusion.2
  220.0 0.2 compare_and_fusion
  220.6 0.4 fusion.95
  221.2 0.8 bitcast_convert_fusion
  222.5 0.5 fusion.35
  223.2 3.0 fusion.96
  226.2 1.6 collective-permute-start
  227.7 1.2 collective-permute-done
  228.9 0.2 fusion.46
  229.2 10.9 %all_gather.36 = bf16[128,2048]{1,0:T(8,128)(2,1)S(1)} all-gather(bf16[32,2048]{1,0:T(8,128)(2,1)S(1)} %fusion.48), channel_id=1, replica_groups=mesh['z'=4,'x'=4,'y'=4,'mlp'=2] {'y'}, dimensions={0}, use_global_device_ids=true | all-gather | bytes 655360 | tf_op jit(solution)/shard_map/all_gather | solution.py:203
  240.1 3.4 %fusion.10 = f32[128,16,64]{0,2,1:T(8,128)S(1)} fusion(bf16[2,16,64,2048]{3,2,1,0:T(8,128)(2,1)} %bitcast.146, bf16[128,2048]{1,0:T(8,128)(2,1)S(1)} %all_gather.36), kind=kOutput, calls=%fused_computation.14 | convolution fusion | flops 536870912 | bytes 5242880 | tf_op jit(solution)/shard_map/dot_general | solution.py:205
  243.6 27.4 %all-gather.15.cloned.1.call-done = bf16[1024,2048]{1,0:T(8,128)(2,1)} async-done(((bf16[64,2048]{1,0:T(8,128)(2,1)}), bf16[1024,2048]{1,0:T(8,128)(2,1)}) %all-gather.15.cloned.1.call-update) | async-done | bytes 4194320 | tf_op jit(solution)/shard_map/all_gather | solution.py:150
  271.0 7.3 %convolution_bitcast_fusion = f32[128,2048]{1,0:T(8,128)} fusion(bf16[16,64,2048]{2,1,0:T(8,128)(2,1)} %bitcast.148, bf16[2,16,64,2048]{3,2,1,0:T(8,128)(2,1)} %bitcast.147, bf16[128,2048]{1,0:T(8,128)(2,1)S(1)} %all_gather.36, f32[128,16,64]{0,2,1:T(8,128)S(1)} %fusion.10), kind=kOutput, calls=%fused_computation.28 | convolution fusion | flops 1074528256 | bytes 10485760 | tf_op jit(solution)/shard_map/dot_general | solution.py:209
  278.6 0.2 reduce_window_sum.11
  278.8 0.2 convolution_convert_fusion.1
  279.0 0.6 reshape.308
  279.7 27.5 %reduce-scatter.2.cloned.1.call-done = f32[16,2048]{1,0:T(8,128)} async-done(((f32[128,2048]{1,0:T(8,128)}), f32[16,2048]{1,0:T(8,128)}) %reduce-scatter.2.cloned.1.call-update) | async-done | bytes 131088 | tf_op jit(solution)/shard_map/reduce_scatter | solution.py:210
  307.2 0.9 add_convert_fusion.1
  308.1 5.1 %all_gather.39 = bf16[32,2048]{1,0:T(8,128)(2,1)S(1)} all-gather(bf16[16,2048]{1,0:T(8,128)(2,1)S(1)} %add_convert_fusion.1), channel_id=1, replica_groups=mesh['z'=4,'x'=4,'y'=4,'mlp'=2] {'mlp'}, dimensions={0}, use_global_device_ids=true | all-gather | bytes 196608 | tf_op jit(solution)/shard_map/all_gather | solution.py:213
  313.3 4.7 %convolution_convert_fusion = bf16[32,1536]{1,0:T(8,128)(2,1)} fusion(bf16[2048,1536]{1,0:T(8,128)(2,1)} %param.31, bf16[32,2048]{1,0:T(8,128)(2,1)S(1)} %all_gather.39, f32[2048]{0:T(1024)S(1)} %convert_element_type.140, f32[32]{0:T(128)S(1)} %add_rsqrt_fusion), kind=kOutput, calls=%fused_computation.29 | convolution fusion | flops 201637888 | bytes 6529152 | tf_op jit(solution)/shard_map/dot_general | solution.py:215
  317.9 0.7 copy.119
  (77 shorter events, 3.2 us)
Async XLA Ops:
  7.2 72.5 %all-gather.9.cloned.1.call-start = ((), (), s32[]{:S(2)}) async-start(), calls=%async_computation.2 | async-start | bytes 2396160 | tf_op jit(solution)/shard_map/all_gather | solution.py:92
  9.3 141.7 %all-gather.11.cloned.1.call-start = ((), (), s32[]{:S(2)}) async-start(), calls=%async_computation.3 | async-start | bytes 8912896 | tf_op jit(solution)/shard_map/all_gather | solution.py:93
  10.0 208.9 %all-gather.13.cloned.1.call-start = ((), (), s32[]{:S(2)}) async-start(), calls=%async_computation.4 | async-start | bytes 2396160 | tf_op jit(solution)/shard_map/all_gather | solution.py:148
  30.3 13.9 %copy-start.7 = (s32[2]{0:T(128)S(1)}, s32[2]{0:T(128)}, u32[]{:S(2)}) copy-start(s32[2]{0:T(128)} %param.24) | copy-start | bytes 28
  30.3 14.5 %copy-start.8 = (s32[2,48]{1,0:T(2,128)S(1)}, s32[2,48]{1,0:T(2,128)}, u32[]{:S(2)}) copy-start(s32[2,48]{1,0:T(2,128)} %param.23) | copy-start | bytes 1156
  51.3 2.2 copy-start
  90.0 5.9 %copy-start.1 = (bf16[8192,4,64,1]{0,2,1,3:T(8,128)(2,1)S(1)}, bf16[8192,4,64,1]{0,2,1,3:T(8,128)(2,1)}, u32[]{:S(2)}) copy-start(bf16[8192,4,64,1]{0,2,1,3:T(8,128)(2,1)} %reshape.315) | copy-start | bytes 12582916
  95.9 123.2 %copy-start.3 = (bf16[32,1024]{1,0:T(8,128)(2,1)S(1)}, bf16[32,1024]{1,0:T(8,128)(2,1)}, u32[]{:S(2)}) copy-start(bf16[32,1024]{1,0:T(8,128)(2,1)} %param.17) | copy-start | bytes 196612
  95.9 123.3 %copy-start.10 = (s32[2]{0:T(128)S(1)}, s32[2]{0:T(128)}, u32[]{:S(2)}) copy-start(s32[2]{0:T(128)} %param.20) | copy-start | bytes 28
  95.9 123.4 %copy-start.9 = (s32[2,16]{1,0:T(2,128)S(1)}, s32[2,16]{1,0:T(2,128)}, u32[]{:S(2)}) copy-start(s32[2,16]{1,0:T(2,128)} %param.19) | copy-start | bytes 388
  95.9 124.3 %copy-start.2 = (bf16[32,2,256]{2,1,0:T(2,128)(2,1)S(1)}, bf16[32,2,256]{2,1,0:T(2,128)(2,1)}, u32[]{:S(2)}) copy-start(bf16[32,2,256]{2,1,0:T(2,128)(2,1)} %param.18) | copy-start | bytes 98308
  101.0 126.7 %copy-start.5 = (bf16[2048]{0:T(1024)(128)(2,1)S(1)}, bf16[2048]{0:T(1024)(128)(2,1)}, u32[]{:S(2)}) copy-start(bf16[2048]{0:T(1024)(128)(2,1)} %param.27) | copy-start | bytes 12292
  101.0 127.9 %copy-start.4 = (bf16[32,2048]{1,0:T(8,128)(2,1)S(1)}, bf16[32,2048]{1,0:T(8,128)(2,1)}, u32[]{:S(2)}) copy-start(bf16[32,2048]{1,0:T(8,128)(2,1)} %param.16) | copy-start | bytes 393220
  152.1 118.9 %all-gather.15.cloned.1.call-start = ((), (), s32[]{:S(2)}) async-start(), calls=%async_computation.5 | async-start | bytes 4456448 | tf_op jit(solution)/shard_map/all_gather | solution.py:150
  219.0 88.1 %reduce-scatter.2.cloned.1.call-start = ((), (), s32[]{:S(2)}) async-start(), calls=%async_computation.1 | async-start | bytes 1179648 | tf_op jit(solution)/shard_map/reduce_scatter | solution.py:210
  226.2 2.7 collective-permute-start
  243.5 34.8 %copy-start.6 = (bf16[2048]{0:T(1024)(128)(2,1)S(1)}, bf16[2048]{0:T(1024)(128)(2,1)}, u32[]{:S(2)}) copy-start(bf16[2048]{0:T(1024)(128)(2,1)} %param.30) | copy-start | bytes 12292
  243.6 34.9 %copy-start.11 = (s32[2]{0:T(128)S(1)}, s32[2]{0:T(128)}, u32[]{:S(2)}) copy-start(s32[2]{0:T(128)} %param.21) | copy-start | bytes 28
Sparse Core Ops, SparseCore 0:
  11.3 68.2 all-gather.8
  81.8 69.1 all-gather.10
  154.3 64.6 all-gather.12
  221.0 49.9 all-gather.14
  278.5 28.6 reduce-scatter.1

commit v6 on v4

--- a/solution.py
+++ b/solution.py
@@ -213,7 +213,12 @@
     normed = rms_scale(mixed, gain_mid)
     column = lax.axis_index("mlp")
     half_count = normed.shape[0] // lax.axis_size("mlp")
-    group_rows = lax.all_gather(normed, "y", axis=0, tiled=True)
+    ring = lax.axis_size("y")
+    shifted = [normed]
+    for shift in range(1, ring):
+        perm = [(i, (i + shift) % ring) for i in range(ring)]
+        shifted.append(lax.ppermute(normed, "y", perm))
+    group_rows = jnp.concatenate(shifted, axis=0)
     dims = (((1,), (2,)), ((), ()))
     gate = lax.dot_general(group_rows, all_w[:, 0], dims, preferred_element_type=jnp.float32)
     up_part = lax.dot_general(group_rows, all_w[:, 1], dims, preferred_element_type=jnp.float32)
@@ -222,7 +227,14 @@
     partial = lax.dot_general(
         hidden, all_w[:, 2], down_dims, preferred_element_type=jnp.float32
     )
-    mlp_half = lax.psum_scatter(partial, ("y", "mlp"), scatter_dimension=0, tiled=True)
+    halves = partial.reshape(ring, 2, half_count, partial.shape[1])
+    mine = lax.dynamic_index_in_dim(halves, column, 1, keepdims=False)
+    theirs = lax.dynamic_index_in_dim(halves, 1 - column, 1, keepdims=False)
+    mine = mine + lax.ppermute(theirs, "mlp", [(0, 1), (1, 0)])
+    mlp_half = mine[0]
+    for shift in range(1, ring):
+        perm = [(i, (i - shift) % ring) for i in range(ring)]
+        mlp_half = mlp_half + lax.ppermute(mine[shift], "y", perm)
     base_half = lax.dynamic_slice_in_dim(mixed, column * half_count, half_count, 0)
     out_half = (base_half.astype(jnp.float32) + mlp_half).astype(jnp.bfloat16)
     hidden_out = lax.all_gather(out_half, "mlp", axis=0, tiled=True)

time: 316 us -> 296 us (0.937)
  waiting for transfers between devices: 149 us -> 135 us
  blocking collectives: 15.1 us -> 2.38 us
  starting transfers between devices: 1.72 us -> 9.73 us
    reduce_scatter x1 -> x0, waiting for transfers between devices: 28.1 us -> none  [per_device(): lax.psum_scatter(partial, ('y', 'mlp'), scatter_dimension=0, tiled=True)]
    ppermute x0 -> x7, waiting for transfers between devices: none -> 14.4 us  [the longest x3 7.6 us: per_device(): mlp_half = mlp_half + lax.ppermute(mine[shift], 'y', perm)]
    all_gather x1 -> x0, blocking collectives: 10.1 us -> none  [per_device(): group_rows = lax.all_gather(normed, 'y', axis=0, tiled=True)]
    ppermute x0 -> x7, starting transfers between devices: none -> 8.05 us  [the longest x3 3.32 us: per_device(): shifted.append(lax.ppermute(normed, 'y', perm))]
    dot_general x1, matrix products: 7.32 us -> 3.02 us  [per_device(): lax.dot_general(hidden, all_w[:, 2], down_dims, preferred_element_type=jn...]
    dot_general x0 -> x1, matrix products: none -> 3.45 us  [per_device(): lax.dot_general(group_rows, all_w[:, 1], dims, preferred_element_type=jnp...]
  transfers between devices with their start and end apart: 5 -> 11, of which waited for: 5 -> 11; matrix products, arithmetic and copies ran while one was open for 34% -> 36% of each run, Pallas kernels for 0% -> 0%
where the time goes in v6:
time: 296 us; the launch traced here: 295 us
  waiting for transfers between devices  135 us (46%)
  local copies, waits for them, and re-layouts  77.7 us (26%)
  matrix products  33.7 us (11%)
  other arithmetic  18.1 us (6%)
  between operations  16.7 us (6%)
  starting transfers between devices  9.73 us (3%)
    all_gather x1, waiting for transfers between devices, per_device(): back = lax.all_gather(r_packet, REQ, axis=0, tiled=False)  64.7 us
    gather x12, local copies, waits for them, and re-layouts, attend_block(): gathered = cache[page_ids]  49 us
    all_gather x1, waiting for transfers between devices, per_device(): all_w = lax.all_gather(own_w, ('z', 'x'), axis=0, tiled=False)  34.5 us
    all_gather x1, waiting for transfers between devices, per_device(): every_query = lax.all_gather(q_packet, REQ, axis=0, tiled=False)  20.6 us
    dot_general x12, matrix products, attend_block(): jnp.einsum('ghqk,kge->ghqe', weights, value_rows.astype(jnp.float32), pre...  9.67 us
    ppermute x3, waiting for transfers between devices, per_device(): mlp_half = mlp_half + lax.ppermute(mine[shift], 'y', perm)  7.6 us
    lt x12, other arithmetic, attend_block(): visible = block * block_keys + positions < length  7.4 us
    optimization_barrier x1, local copies, waits for them, and re-layouts, per_device(): own_state, every_query = lax.optimization_barrier((own_state, every_query))  6.17 us
  transfers between devices with their start and end apart: 11, of which 11 were waited for; matrix products, arithmetic and copies ran while one was open for 36% of the time, Pallas kernels for 0%

profile of v6, /device:TPU:1, one launch (start us, length us, event | category | flops | bytes accessed | tf_op | source)
XLA Modules:
  0.0 294.9 jit_solution(16650923499430487286)
XLA Ops:
  9.3 2.1 pad_maximum_fusion
  11.7 1.3 fusion.85
  13.8 45.3 %while.36 = (s32[]{:T(128)}, f32[4,4,16]{2,1,0:T(4,128)S(1)}, f32[4,4,16]{2,1,0:T(4,128)S(1)}, f32[4,4,16,64]{3,2,1,0:T(8,128)S(1)}, s32[]{:T(128)}, /*index=5*/...) while((s32[]{:T(128)}, f32[4,4,16]{2,1,0:T(4,128)S(1)}, ...), condition=%wide.region_3.4_spmd.clone, body=%wide.region_0.3_spmd.clone.sunk | while | flops 237031712 | bytes 12771663 | solution.py:132
  13.9 4.0 %gather_fusion = bf16[8,2,128,256]{3,2,1,0:T(8,128)(2,1)S(1)} fusion(bf16[64,2,128,256]{3,2,1,0:T(8,128)(2,1)} %get-tuple-element.669, s32[1024]{0:T(1024)S(1)} %pad_clamp_fusion.4), kind=kCustom, calls=%fused_computation.clone.clone.1 | custom fusion | bytes 2097184 | tf_op jit(solution)/shard_map/while/body/eval_jaxpr/gather | solution.py:108
  20.5 0.8 convolution_add_fusion.4
  21.4 4.0 %gather_fusion = bf16[8,2,128,256]{3,2,1,0:T(8,128)(2,1)S(1)} fusion(bf16[64,2,128,256]{3,2,1,0:T(8,128)(2,1)} %get-tuple-element.669, s32[1024]{0:T(1024)S(1)} %pad_clamp_fusion.4), kind=kCustom, calls=%fused_computation.clone.clone.1 | custom fusion | bytes 2097184 | tf_op jit(solution)/shard_map/while/body/eval_jaxpr/gather | solution.py:108
  28.0 0.8 convolution_add_fusion.4
  29.0 4.0 %gather_fusion = bf16[8,2,128,256]{3,2,1,0:T(8,128)(2,1)S(1)} fusion(bf16[64,2,128,256]{3,2,1,0:T(8,128)(2,1)} %get-tuple-element.669, s32[1024]{0:T(1024)S(1)} %pad_clamp_fusion.4), kind=kCustom, calls=%fused_computation.clone.clone.1 | custom fusion | bytes 2097184 | tf_op jit(solution)/shard_map/while/body/eval_jaxpr/gather | solution.py:108
  35.6 0.8 convolution_add_fusion.4
  36.5 4.0 %gather_fusion = bf16[8,2,128,256]{3,2,1,0:T(8,128)(2,1)S(1)} fusion(bf16[64,2,128,256]{3,2,1,0:T(8,128)(2,1)} %get-tuple-element.669, s32[1024]{0:T(1024)S(1)} %pad_clamp_fusion.4), kind=kCustom, calls=%fused_computation.clone.clone.1 | custom fusion | bytes 2097184 | tf_op jit(solution)/shard_map/while/body/eval_jaxpr/gather | solution.py:108
  43.1 0.8 convolution_add_fusion.4
  44.0 4.0 %gather_fusion = bf16[8,2,128,256]{3,2,1,0:T(8,128)(2,1)S(1)} fusion(bf16[64,2,128,256]{3,2,1,0:T(8,128)(2,1)} %get-tuple-element.669, s32[1024]{0:T(1024)S(1)} %pad_clamp_fusion.4), kind=kCustom, calls=%fused_computation.clone.clone.1 | custom fusion | bytes 2097184 | tf_op jit(solution)/shard_map/while/body/eval_jaxpr/gather | solution.py:108
  50.7 0.8 convolution_add_fusion.4
  51.6 4.0 %gather_fusion = bf16[8,2,128,256]{3,2,1,0:T(8,128)(2,1)S(1)} fusion(bf16[64,2,128,256]{3,2,1,0:T(8,128)(2,1)} %get-tuple-element.669, s32[1024]{0:T(1024)S(1)} %pad_clamp_fusion.4), kind=kCustom, calls=%fused_computation.clone.clone.1 | custom fusion | bytes 2097184 | tf_op jit(solution)/shard_map/while/body/eval_jaxpr/gather | solution.py:108
  59.1 20.6 %all-gather.7.cloned.1.call-done = bf16[1024,1152]{1,0:T(8,128)(2,1)} async-done(((bf16[16,1152]{1,0:T(8,128)(2,1)}), bf16[1024,1152]{1,0:T(8,128)(2,1)}) %all-gather.7.cloned.1.call-update) | async-done | bytes 2359312 | tf_op jit(solution)/shard_map/all_gather | solution.py:92
  79.6 6.2 %copy.87 = bf16[64,16,1152]{0,2,1:T(8,128)(2,1)} copy(bf16[64,16,1152]{2,1,0:T(8,128)(2,1)} %bitcast.175) | data formatting | bytes 4718592 | tf_op jit(solution)/shard_map/optimization_barrier | solution.py:142
  85.8 1.3 fusion.73
  90.0 45.7 %while.37 = (s32[]{:T(128)}, f32[4,4,16]{2,1,0:T(4,128)S(1)}, f32[4,4,16]{2,1,0:T(4,128)S(1)}, f32[4,4,16,64]{3,2,1,0:T(8,128)S(1)}, s32[]{:T(128)}, /*index=5*/...) while((s32[]{:T(128)}, f32[4,4,16]{2,1,0:T(4,128)S(1)}, ...), condition=%wide.region_8.9_spmd.clone, body=%wide.region_5.8_spmd.clone.sunk | while | flops 237031712 | bytes 12771663 | solution.py:132
  90.1 4.4 %gather_fusion.1 = bf16[8,2,128,256]{3,2,1,0:T(8,128)(2,1)S(1)} fusion(bf16[64,2,128,256]{3,2,1,0:T(8,128)(2,1)} %get-tuple-element.708, s32[1024]{0:T(1024)S(1)} %pad_clamp_fusion.5), kind=kCustom, calls=%fused_computation.1.clone.clone.1 | custom fusion | bytes 2097184 | tf_op jit(solution)/shard_map/while/body/eval_jaxpr/gather | solution.py:108
  97.1 0.8 convolution_add_fusion.5
  98.0 4.2 %gather_fusion.1 = bf16[8,2,128,256]{3,2,1,0:T(8,128)(2,1)S(1)} fusion(bf16[64,2,128,256]{3,2,1,0:T(8,128)(2,1)} %get-tuple-element.708, s32[1024]{0:T(1024)S(1)} %pad_clamp_fusion.5), kind=kCustom, calls=%fused_computation.1.clone.clone.1 | custom fusion | bytes 2097184 | tf_op jit(solution)/shard_map/while/body/eval_jaxpr/gather | solution.py:108
  104.7 0.8 convolution_add_fusion.5
  105.7 4.0 %gather_fusion.1 = bf16[8,2,128,256]{3,2,1,0:T(8,128)(2,1)S(1)} fusion(bf16[64,2,128,256]{3,2,1,0:T(8,128)(2,1)} %get-tuple-element.708, s32[1024]{0:T(1024)S(1)} %pad_clamp_fusion.5), kind=kCustom, calls=%fused_computation.1.clone.clone.1 | custom fusion | bytes 2097184 | tf_op jit(solution)/shard_map/while/body/eval_jaxpr/gather | solution.py:108
  113.1 4.1 %gather_fusion.1 = bf16[8,2,128,256]{3,2,1,0:T(8,128)(2,1)S(1)} fusion(bf16[64,2,128,256]{3,2,1,0:T(8,128)(2,1)} %get-tuple-element.708, s32[1024]{0:T(1024)S(1)} %pad_clamp_fusion.5), kind=kCustom, calls=%fused_computation.1.clone.clone.1 | custom fusion | bytes 2097184 | tf_op jit(solution)/shard_map/while/body/eval_jaxpr/gather | solution.py:108
  120.7 4.0 %gather_fusion.1 = bf16[8,2,128,256]{3,2,1,0:T(8,128)(2,1)S(1)} fusion(bf16[64,2,128,256]{3,2,1,0:T(8,128)(2,1)} %get-tuple-element.708, s32[1024]{0:T(1024)S(1)} %pad_clamp_fusion.5), kind=kCustom, calls=%fused_computation.1.clone.clone.1 | custom fusion | bytes 2097184 | tf_op jit(solution)/shard_map/while/body/eval_jaxpr/gather | solution.py:108
  128.1 4.2 %gather_fusion.1 = bf16[8,2,128,256]{3,2,1,0:T(8,128)(2,1)S(1)} fusion(bf16[64,2,128,256]{3,2,1,0:T(8,128)(2,1)} %get-tuple-element.708, s32[1024]{0:T(1024)S(1)} %pad_clamp_fusion.5), kind=kCustom, calls=%fused_computation.1.clone.clone.1 | custom fusion | bytes 2097184 | tf_op jit(solution)/shard_map/while/body/eval_jaxpr/gather | solution.py:108
  134.9 0.8 convolution_add_fusion.5
  135.8 34.5 %all-gather.9.cloned.1.call-done = bf16[48,64,2048]{2,1,0:T(8,128)(2,1)} async-done(((bf16[3,64,2048]{2,1,0:T(8,128)(2,1)}), bf16[48,64,2048]{2,1,0:T(8,128)(2,1)}) %all-gather.9.cloned.1.call-update) | async-done | bytes 12582928 | tf_op jit(solution)/shard_map/all_gather | solution.py:94
  173.6 64.7 %all-gather.11.cloned.1.call-done = bf16[1024,1152]{1,0:T(8,128)(2,1)} async-done(((bf16[16,1152]{1,0:T(8,128)(2,1)}), bf16[1024,1152]{1,0:T(8,128)(2,1)}) %all-gather.11.cloned.1.call-update) | async-done | bytes 2359312 | tf_op jit(solution)/shard_map/all_gather | solution.py:163
  240.2 3.0 %fusion.87 = f32[32,2048]{1,0:T(8,128)S(1)} fusion(bf16[32,1024]{1,0:T(8,128)(2,1)S(1)} %convert_element_type.135, bf16[1024,2048]{1,0:T(8,128)(2,1)} %param.30), kind=kOutput, calls=%fused_computation.160 | convolution fusion | flops 134217728 | bytes 4521984 | tf_op jit(solution)/shard_map/dot_general | solution.py:210
  243.2 1.6 collective-permute-start
  244.8 1.2 collective-permute-done
  246.3 1.8 collective-permute-start.2
  248.1 1.4 collective-permute-start.3
  249.6 3.4 %collective-permute-done.1 = bf16[32,2048]{1,0:T(8,128)(2,1)S(1)} collective-permute-done((bf16[32,2048]{1,0:T(8,128)(2,1)S(1)}, bf16[32,2048]{1,0:T(8,128)(2,1)S(1)}, u32[]{:S(2)}, u32[]{:S(2)}) %collective-permute-start.1) | collective-permute-done | bytes 131104 | tf_op jit(solution)/shard_map/ppermute | solution.py:220
  253.0 1.2 collective-permute-done.2
  254.2 1.1 collective-permute-done.3
  255.3 3.4 %fusion.28 = f32[128,16,64]{0,2,1:T(8,128)S(1)} fusion(bf16[32,2048]{1,0:T(8,128)(2,1)S(1)} %collective-permute-done.3, bf16[32,2048]{1,0:T(8,128)(2,1)S(1)} %collective-permute-done.2, bf16[32,2048]{1,0:T(8,128)(2,1)S(1)} %collective-permute-done.1, bf16[32,2048]{1,0:T(8,128)(2,1)S(1)} %fusion.39, bf16[16,3,64,2048]{3,2,1,0:T(8,128)(2,1)} %bitcast.192), kind=kOutput, calls=%fused_computation.51 | convolution fusion | flops 538968064 | bytes 5242880 | tf_op jit(solution)/shard_map/dot_general | solution.py:223
  258.7 3.5 %multiply_convert_fusion = bf16[128,16,64]{0,2,1:T(8,128)(2,1)S(1)} fusion(f32[128,16,64]{0,2,1:T(8,128)S(1)} %fusion.28, bf16[32,2048]{1,0:T(8,128)(2,1)S(1)} %collective-permute-done.3, bf16[32,2048]{1,0:T(8,128)(2,1)S(1)} %collective-permute-done.2, bf16[32,2048]{1,0:T(8,128)(2,1)S(1)} %collective-permute-done.1, bf16[32,2048]{1,0:T(8,128)(2,1)S(1)} %fusion.39, ...), kind=kOutput, calls=%fused_computation.73 | convolution fusion | flops 539754496 | bytes 5505024 | tf_op jit(solution)/shard_map/dot_general | solution.py:224
  262.6 3.0 %fusion.29 = f32[4,2,16,2048]{3,2,1,0:T(8,128)S(1)} fusion(bf16[4,2,16,16,64]{4,3,2,1,0:T(8,128)(2,1)S(1)} %bitcast.179, bf16[16,3,64,2048]{3,2,1,0:T(8,128)(2,1)} %bitcast.194), kind=kOutput, calls=%fused_computation.52 | convolution fusion | flops 536870912 | bytes 5505024 | tf_op jit(solution)/shard_map/dot_general | solution.py:227
  265.7 1.6 collective-permute-start.4
  267.7 1.1 collective-permute-done.4
  268.9 2.5 collective-permute-start.5
  272.9 1.7 collective-permute-done.5
  274.6 2.8 collective-permute-done.6
  277.4 3.1 %collective-permute-done.7 = f32[16,2048]{1,0:T(8,128)S(1)} collective-permute-done((f32[16,2048]{1,0:T(8,128)S(1)}, f32[16,2048]{1,0:T(8,128)S(1)}, u32[]{:S(2)}, u32[]{:S(2)}) %collective-permute-start.7) | collective-permute-done | bytes 131104 | tf_op jit(solution)/shard_map/ppermute | solution.py:237
  280.5 2.4 all_gather.27
  283.1 4.7 %convolution_convert_fusion = bf16[32,1536]{1,0:T(8,128)(2,1)} fusion(bf16[2048,1536]{1,0:T(8,128)(2,1)} %param.35, bf16[32,2048]{1,0:T(8,128)(2,1)S(1)} %all_gather.27, f32[2048]{0:T(1024)S(1)} %convert_element_type.144, f32[32]{0:T(128)S(1)} %add_rsqrt_fusion), kind=kOutput, calls=%fused_computation.53 | convolution fusion | flops 201637888 | bytes 6529152 | tf_op jit(solution)/shard_map/dot_general | solution.py:242
  (255 shorter events, 46.4 us)
Async XLA Ops:
  7.2 72.5 %all-gather.7.cloned.1.call-start = ((), (), s32[]{:S(2)}) async-start(), calls=%async_computation | async-start | bytes 2396160 | tf_op jit(solution)/shard_map/all_gather | solution.py:92
  9.3 161.0 %all-gather.9.cloned.1.call-start = ((), (), s32[]{:S(2)}) async-start(), calls=%async_computation.1 | async-start | bytes 13369344 | tf_op jit(solution)/shard_map/all_gather | solution.py:94
  11.5 226.8 %all-gather.11.cloned.1.call-start = ((), (), s32[]{:S(2)}) async-start(), calls=%async_computation.2 | async-start | bytes 2396160 | tf_op jit(solution)/shard_map/all_gather | solution.py:163
  90.0 81.4 %copy-start.1 = (bf16[32,1024]{1,0:T(8,128)(2,1)S(1)}, bf16[32,1024]{1,0:T(8,128)(2,1)}, u32[]{:S(2)}) copy-start(bf16[32,1024]{1,0:T(8,128)(2,1)} %param.21) | copy-start | bytes 196612
  90.0 81.6 %copy-start.6 = (s32[2]{0:T(128)S(1)}, s32[2]{0:T(128)}, u32[]{:S(2)}) copy-start(s32[2]{0:T(128)} %param.24) | copy-start | bytes 28
  90.0 81.7 %copy-start.5 = (s32[2,16]{1,0:T(2,128)S(1)}, s32[2,16]{1,0:T(2,128)}, u32[]{:S(2)}) copy-start(s32[2,16]{1,0:T(2,128)} %param.23) | copy-start | bytes 388
  90.0 82.6 %copy-start = (bf16[32,2,256]{2,1,0:T(2,128)(2,1)S(1)}, bf16[32,2,256]{2,1,0:T(2,128)(2,1)}, u32[]{:S(2)}) copy-start(bf16[32,2,256]{2,1,0:T(2,128)(2,1)} %param.22) | copy-start | bytes 98308
  135.8 109.0 %copy-start.3 = (bf16[2048]{0:T(1024)(128)(2,1)S(1)}, bf16[2048]{0:T(1024)(128)(2,1)}, u32[]{:S(2)}) copy-start(bf16[2048]{0:T(1024)(128)(2,1)} %param.31) | copy-start | bytes 12292
  135.8 110.2 %copy-start.2 = (bf16[32,2048]{1,0:T(8,128)(2,1)S(1)}, bf16[32,2048]{1,0:T(8,128)(2,1)}, u32[]{:S(2)}) copy-start(bf16[32,2048]{1,0:T(8,128)(2,1)} %param.20) | copy-start | bytes 393220
  135.8 113.8 %copy-start.4 = (bf16[2048]{0:T(1024)(128)(2,1)S(1)}, bf16[2048]{0:T(1024)(128)(2,1)}, u32[]{:S(2)}) copy-start(bf16[2048]{0:T(1024)(128)(2,1)} %param.34) | copy-start | bytes 12292
  243.2 2.7 collective-permute-start
  246.2 6.8 %collective-permute-start.1 = (bf16[32,2048]{1,0:T(8,128)(2,1)S(1)}, bf16[32,2048]{1,0:T(8,128)(2,1)S(1)}, u32[]{:S(2)}, u32[]{:S(2)}) collective-permute-start(bf16[32,2048]{1,0:T(8,128)(2,1)S(1)} %fusion.39), channel_id=1, source_target_pairs={{0,2},{2,4},{4,6},{6,0},{1,3},{3,5},{5,7},{7,1},{8,10},{10,12},{12... | collective-permute-start | bytes 393224 | tf_op jit(solution)/shard_map/ppermute | solution.py:220
  246.3 7.9 %collective-permute-start.2 = (bf16[32,2048]{1,0:T(8,128)(2,1)S(1)}, bf16[32,2048]{1,0:T(8,128)(2,1)S(1)}, u32[]{:S(2)}, u32[]{:S(2)}) collective-permute-start(bf16[32,2048]{1,0:T(8,128)(2,1)S(1)} %fusion.39), channel_id=1, source_target_pairs={{0,4},{2,6},{4,0},{6,2},{1,5},{3,7},{5,1},{7,3},{8,12},{10,14},{12... | collective-permute-start | bytes 393224 | tf_op jit(solution)/shard_map/ppermute | solution.py:220
  248.1 7.2 %collective-permute-start.3 = (bf16[32,2048]{1,0:T(8,128)(2,1)S(1)}, bf16[32,2048]{1,0:T(8,128)(2,1)S(1)}, u32[]{:S(2)}, u32[]{:S(2)}) collective-permute-start(bf16[32,2048]{1,0:T(8,128)(2,1)S(1)} %fusion.39), channel_id=1, source_target_pairs={{0,6},{2,0},{4,2},{6,4},{1,7},{3,1},{5,3},{7,5},{8,14},{10,8},{12,... | collective-permute-start | bytes 393224 | tf_op jit(solution)/shard_map/ppermute | solution.py:220
  262.6 4.7 %copy-start.7 = (s32[2]{0:T(128)S(1)}, s32[2]{0:T(128)}, u32[]{:S(2)}) copy-start(s32[2]{0:T(128)} %param.25) | copy-start | bytes 28
  265.7 3.1 %collective-permute-start.4 = (f32[4,16,2048]{2,1,0:T(8,128)S(1)}, f32[4,16,2048]{2,1,0:T(8,128)S(1)}, u32[]{:S(2)}, u32[]{:S(2)}) collective-permute-start(f32[4,16,2048]{2,1,0:T(8,128)S(1)} %dynamic-slice_bitcast_fusion), channel_id=1, source_target_pairs={{0,1},{1,0},{2,3},{3,2},{4,5},{5,4},{6,7},{7,6},{8,9},{9,8},{10,11... | collective-permute-start | bytes 1572872 | tf_op jit(solution)/shard_map/ppermute | solution.py:233
  268.9 5.7 %collective-permute-start.5 = (f32[16,2048]{1,0:T(8,128)S(1)}, f32[16,2048]{1,0:T(8,128)S(1)}, u32[]{:S(2)}, u32[]{:S(2)}) collective-permute-start(f32[16,2048]{1,0:T(8,128)S(1)} %get-tuple-element.498), channel_id=1, source_target_pairs={{0,6},{2,0},{4,2},{6,4},{1,7},{3,1},{5,3},{7,5},{8,14},{10,8},{12,... | collective-permute-start | bytes 393224 | tf_op jit(solution)/shard_map/ppermute | solution.py:237
  271.4 6.0 %collective-permute-start.6 = (f32[16,2048]{1,0:T(8,128)S(1)}, f32[16,2048]{1,0:T(8,128)S(1)}, u32[]{:S(2)}, u32[]{:S(2)}) collective-permute-start(f32[16,2048]{1,0:T(8,128)S(1)} %get-tuple-element.500), channel_id=1, source_target_pairs={{0,4},{2,6},{4,0},{6,2},{1,5},{3,7},{5,1},{7,3},{8,12},{10,14},{12... | collective-permute-start | bytes 393224 | tf_op jit(solution)/shard_map/ppermute | solution.py:237
  271.4 9.1 %collective-permute-start.7 = (f32[16,2048]{1,0:T(8,128)S(1)}, f32[16,2048]{1,0:T(8,128)S(1)}, u32[]{:S(2)}, u32[]{:S(2)}) collective-permute-start(f32[16,2048]{1,0:T(8,128)S(1)} %get-tuple-element.499), channel_id=1, source_target_pairs={{0,2},{2,4},{4,6},{6,0},{1,3},{3,5},{5,7},{7,1},{8,10},{10,12},{12... | collective-permute-start | bytes 393224 | tf_op jit(solution)/shard_map/ppermute | solution.py:237
Sparse Core Ops, SparseCore 0:
  11.3 68.2 all-gather.6
  81.8 88.4 all-gather.8
  173.6 64.6 all-gather.10

commit v7 on v6

--- a/solution.py
+++ b/solution.py
@@ -87,9 +87,12 @@
     queries = q_in.reshape(2, tree_len, kv_local, GROUP, HEAD_DIM)
     device_id = lax.axis_index(REQ)
     q_width = q_in.shape[1]
-    dest_col = jnp.broadcast_to(prev_owner[0].astype(q_in.dtype), (tree_len, TAG))
-    q_packet = jnp.concatenate([q_in[tree_len:], dest_col], axis=1)
-    every_query = lax.all_gather(q_packet, REQ, axis=0, tiled=False)
+    owners = lax.axis_size(REQ)
+    marker = jnp.ones((tree_len, TAG), q_in.dtype)
+    q_packet = jnp.concatenate([q_in[tree_len:], marker], axis=1)
+    q_send = jnp.zeros((owners,) + q_packet.shape, q_packet.dtype)
+    q_send = lax.dynamic_update_index_in_dim(q_send, q_packet, prev_owner[0], 0)
+    every_query = lax.all_to_all(q_send, REQ, 0, 0, tiled=True)
     own_w = jnp.stack([w_in[0], w_in[1], w_down])
     all_w = lax.all_gather(own_w, ("z", "x"), axis=0, tiled=False)
     page_len = cache.shape[2]
@@ -140,9 +143,9 @@
     own_queries = queries[0]
     own_state = attend(0, own_queries, 0, num_blocks, start_state)
     own_state, every_query = lax.optimization_barrier((own_state, every_query))
-    dests = every_query[:, 0, q_width].astype(jnp.int32)
-    senders = jnp.arange(dests.shape[0], dtype=jnp.int32)
-    sender = jnp.sum(jnp.where(dests == device_id, senders, 0))
+    marks = every_query[:, 0, q_width]
+    senders = jnp.arange(marks.shape[0], dtype=jnp.int32)
+    sender = jnp.sum(jnp.where(marks > 0.5, senders, 0))
     foreign = lax.dynamic_index_in_dim(every_query, sender, 0, keepdims=False)[:, :q_width]
     foreign = foreign.reshape(tree_len, kv_local, GROUP, HEAD_DIM)
     f_running, f_total, f_accum = attend(1, foreign, 0, num_blocks, start_state)
@@ -160,7 +163,9 @@
     )
     pad = jnp.zeros((tree_len, TAG - stats.shape[1]), jnp.bfloat16)
     r_packet = jnp.concatenate([sent_out.astype(jnp.bfloat16), stats, pad], axis=1)
-    back = lax.all_gather(r_packet, REQ, axis=0, tiled=False)
+    r_send = jnp.zeros((owners,) + r_packet.shape, r_packet.dtype)
+    r_send = lax.dynamic_update_index_in_dim(r_send, r_packet, sender, 0)
+    back = lax.all_to_all(r_send, REQ, 0, 0, tiled=True)
     running, total, accum = own_state
     cache_out = accum / total[..., None]
     got = lax.dynamic_index_in_dim(back, prev_owner[0], 0, keepdims=False).astype(jnp.float32)

time: 296 us -> 231 us (0.78)
  waiting for transfers between devices: 135 us -> 51.1 us
  starting transfers between devices: 9.73 us -> 32.2 us
  local copies, waits for them, and re-layouts: 77.7 us -> 73.4 us
    all_gather x2 -> x0, waiting for transfers between devices: 85.2 us -> none  [the longest x1 64.7 us: per_device(): back = lax.all_gather(r_packet, REQ, axis=0, tiled=False)]
    all_to_all x0 -> x2, waiting for transfers between devices: none -> 28.3 us  [the longest x1 28.3 us: per_device(): back = lax.all_to_all(r_send, REQ, 0, 0, tiled=True)]
    all_gather x1, waiting for transfers between devices: 34.5 us -> 6.98 us  [per_device(): all_w = lax.all_gather(own_w, ('z', 'x'), axis=0, tiled=False)]
    all_to_all x0 -> x2, starting transfers between devices: none -> 20.7 us  [the longest x1 12.2 us: per_device(): every_query = lax.all_to_all(q_send, REQ, 0, 0, tiled=True)]
    optimization_barrier x1 -> x0, local copies, waits for them, and re-layouts: 6.17 us -> none  [per_device(): own_state, every_query = lax.optimization_barrier((own_state, every_query))]
    another operation x0 -> x2, local copies, waits for them, and re-layouts: none -> 3.14 us
  transfers between devices with their start and end apart: 11 -> 11, of which waited for: 11 -> 10; matrix products, arithmetic and copies ran while one was open for 36% -> 44% of each run, Pallas kernels for 0% -> 0%
where the time goes in v7:
time: 231 us; the launch traced here: 230 us
  local copies, waits for them, and re-layouts  73.4 us (32%)
  waiting for transfers between devices  51.1 us (22%)
  matrix products  33.8 us (15%)
  starting transfers between devices  32.2 us (14%)
  other arithmetic  19.2 us (8%)
  between operations  17 us (7%)
    gather x12, local copies, waits for them, and re-layouts, attend_block(): gathered = cache[page_ids]  49.2 us
    all_to_all x1, waiting for transfers between devices, per_device(): back = lax.all_to_all(r_send, REQ, 0, 0, tiled=True)  28.3 us
    all_to_all x1, starting transfers between devices, per_device(): every_query = lax.all_to_all(q_send, REQ, 0, 0, tiled=True)  12.2 us
    dot_general x12, matrix products, attend_block(): jnp.einsum('ghqk,kge->ghqe', weights, value_rows.astype(jnp.float32), pre...  9.71 us
    all_to_all x1, starting transfers between devices, per_device(): back = lax.all_to_all(r_send, REQ, 0, 0, tiled=True)  8.46 us
    ppermute x3, waiting for transfers between devices, per_device(): mlp_half = mlp_half + lax.ppermute(mine[shift], 'y', perm)  8.23 us
    lt x12, other arithmetic, attend_block(): visible = block * block_keys + positions < length  7.84 us
    all_gather x1, waiting for transfers between devices, per_device(): all_w = lax.all_gather(own_w, ('z', 'x'), axis=0, tiled=False)  6.98 us
  transfers between devices with their start and end apart: 11, of which 10 were waited for; matrix products, arithmetic and copies ran while one was open for 44% of the time, Pallas kernels for 0%

profile of v7, /device:TPU:1, one launch (start us, length us, event | category | flops | bytes accessed | tf_op | source)
XLA Modules:
  0.0 230.0 jit_solution(12701698807882818634)
XLA Ops:
  7.2 2.1 pad_maximum_fusion
  10.8 1.5 broadcast.120.clone
  12.9 12.2 %all-to-all-start = ((bf16[64,16,1152]{2,1,0:T(8,128)(2,1)}), bf16[64,16,1152]{2,1,0:T(8,128)(2,1)}, u32[]{:S(2)}, u32[]{:S(2)}) async-start(bf16[64,16,1152]{2,1,0:T(8,128)(2,1)} %bitcast_dynamic-update-slice_fusion.1), calls=%async_computation | async-start | bytes 4718592 | tf_op jit(solution)/shard_map/all_to_all | solution.py:95
  25.9 45.5 %while.36 = (s32[]{:T(128)}, f32[4,4,16]{2,1,0:T(4,128)S(1)}, f32[4,4,16]{2,1,0:T(4,128)S(1)}, f32[4,4,16,64]{3,2,1,0:T(8,128)S(1)}, s32[]{:T(128)}, /*index=5*/...) while((s32[]{:T(128)}, f32[4,4,16]{2,1,0:T(4,128)S(1)}, ...), condition=%wide.region_3.4_spmd.clone, body=%wide.region_0.3_spmd.clone.sunk | while | flops 237031712 | bytes 12771663 | solution.py:135
  26.0 4.0 %gather_fusion = bf16[8,2,128,256]{3,2,1,0:T(8,128)(2,1)S(1)} fusion(bf16[64,2,128,256]{3,2,1,0:T(8,128)(2,1)} %get-tuple-element.669, s32[1024]{0:T(1024)S(1)} %pad_clamp_fusion.4), kind=kCustom, calls=%fused_computation.clone.clone.1 | custom fusion | bytes 2097184 | tf_op jit(solution)/shard_map/while/body/eval_jaxpr/gather | solution.py:111
  32.6 0.8 convolution_add_fusion.4
  33.5 4.0 %gather_fusion = bf16[8,2,128,256]{3,2,1,0:T(8,128)(2,1)S(1)} fusion(bf16[64,2,128,256]{3,2,1,0:T(8,128)(2,1)} %get-tuple-element.669, s32[1024]{0:T(1024)S(1)} %pad_clamp_fusion.4), kind=kCustom, calls=%fused_computation.clone.clone.1 | custom fusion | bytes 2097184 | tf_op jit(solution)/shard_map/while/body/eval_jaxpr/gather | solution.py:111
  40.2 0.8 convolution_add_fusion.4
  41.1 4.1 %gather_fusion = bf16[8,2,128,256]{3,2,1,0:T(8,128)(2,1)S(1)} fusion(bf16[64,2,128,256]{3,2,1,0:T(8,128)(2,1)} %get-tuple-element.669, s32[1024]{0:T(1024)S(1)} %pad_clamp_fusion.4), kind=kCustom, calls=%fused_computation.clone.clone.1 | custom fusion | bytes 2097184 | tf_op jit(solution)/shard_map/while/body/eval_jaxpr/gather | solution.py:111
  47.8 0.8 convolution_add_fusion.4
  48.7 4.1 %gather_fusion = bf16[8,2,128,256]{3,2,1,0:T(8,128)(2,1)S(1)} fusion(bf16[64,2,128,256]{3,2,1,0:T(8,128)(2,1)} %get-tuple-element.669, s32[1024]{0:T(1024)S(1)} %pad_clamp_fusion.4), kind=kCustom, calls=%fused_computation.clone.clone.1 | custom fusion | bytes 2097184 | tf_op jit(solution)/shard_map/while/body/eval_jaxpr/gather | solution.py:111
  55.5 0.8 convolution_add_fusion.4
  56.4 4.0 %gather_fusion = bf16[8,2,128,256]{3,2,1,0:T(8,128)(2,1)S(1)} fusion(bf16[64,2,128,256]{3,2,1,0:T(8,128)(2,1)} %get-tuple-element.669, s32[1024]{0:T(1024)S(1)} %pad_clamp_fusion.4), kind=kCustom, calls=%fused_computation.clone.clone.1 | custom fusion | bytes 2097184 | tf_op jit(solution)/shard_map/while/body/eval_jaxpr/gather | solution.py:111
  63.0 0.8 convolution_add_fusion.4
  64.0 4.0 %gather_fusion = bf16[8,2,128,256]{3,2,1,0:T(8,128)(2,1)S(1)} fusion(bf16[64,2,128,256]{3,2,1,0:T(8,128)(2,1)} %get-tuple-element.669, s32[1024]{0:T(1024)S(1)} %pad_clamp_fusion.4), kind=kCustom, calls=%fused_computation.clone.clone.1 | custom fusion | bytes 2097184 | tf_op jit(solution)/shard_map/while/body/eval_jaxpr/gather | solution.py:111
  70.6 0.8 convolution_add_fusion.4
  71.5 2.1 compare_reduce_fusion
  77.1 46.2 %while.37 = (s32[]{:T(128)}, f32[4,4,16]{2,1,0:T(4,128)S(1)}, f32[4,4,16]{2,1,0:T(4,128)S(1)}, f32[4,4,16,64]{3,2,1,0:T(8,128)S(1)}, s32[]{:T(128)}, /*index=5*/...) while((s32[]{:T(128)}, f32[4,4,16]{2,1,0:T(4,128)S(1)}, ...), condition=%wide.region_8.9_spmd.clone, body=%wide.region_5.8_spmd.clone.sunk | while | flops 237031712 | bytes 12771663 | solution.py:135
  77.2 4.2 %gather_fusion.1 = bf16[8,2,128,256]{3,2,1,0:T(8,128)(2,1)S(1)} fusion(bf16[64,2,128,256]{3,2,1,0:T(8,128)(2,1)} %get-tuple-element.708, s32[1024]{0:T(1024)S(1)} %pad_clamp_fusion.5), kind=kCustom, calls=%fused_computation.1.clone.clone.1 | custom fusion | bytes 2097184 | tf_op jit(solution)/shard_map/while/body/eval_jaxpr/gather | solution.py:111
  84.9 4.1 %gather_fusion.1 = bf16[8,2,128,256]{3,2,1,0:T(8,128)(2,1)S(1)} fusion(bf16[64,2,128,256]{3,2,1,0:T(8,128)(2,1)} %get-tuple-element.708, s32[1024]{0:T(1024)S(1)} %pad_clamp_fusion.5), kind=kCustom, calls=%fused_computation.1.clone.clone.1 | custom fusion | bytes 2097184 | tf_op jit(solution)/shard_map/while/body/eval_jaxpr/gather | solution.py:111
  91.7 0.8 convolution_add_fusion.5
  92.6 4.2 %gather_fusion.1 = bf16[8,2,128,256]{3,2,1,0:T(8,128)(2,1)S(1)} fusion(bf16[64,2,128,256]{3,2,1,0:T(8,128)(2,1)} %get-tuple-element.708, s32[1024]{0:T(1024)S(1)} %pad_clamp_fusion.5), kind=kCustom, calls=%fused_computation.1.clone.clone.1 | custom fusion | bytes 2097184 | tf_op jit(solution)/shard_map/while/body/eval_jaxpr/gather | solution.py:111
  100.4 4.3 %gather_fusion.1 = bf16[8,2,128,256]{3,2,1,0:T(8,128)(2,1)S(1)} fusion(bf16[64,2,128,256]{3,2,1,0:T(8,128)(2,1)} %get-tuple-element.708, s32[1024]{0:T(1024)S(1)} %pad_clamp_fusion.5), kind=kCustom, calls=%fused_computation.1.clone.clone.1 | custom fusion | bytes 2097184 | tf_op jit(solution)/shard_map/while/body/eval_jaxpr/gather | solution.py:111
  108.2 4.2 %gather_fusion.1 = bf16[8,2,128,256]{3,2,1,0:T(8,128)(2,1)S(1)} fusion(bf16[64,2,128,256]{3,2,1,0:T(8,128)(2,1)} %get-tuple-element.708, s32[1024]{0:T(1024)S(1)} %pad_clamp_fusion.5), kind=kCustom, calls=%fused_computation.1.clone.clone.1 | custom fusion | bytes 2097184 | tf_op jit(solution)/shard_map/while/body/eval_jaxpr/gather | solution.py:111
  115.9 4.0 %gather_fusion.1 = bf16[8,2,128,256]{3,2,1,0:T(8,128)(2,1)S(1)} fusion(bf16[64,2,128,256]{3,2,1,0:T(8,128)(2,1)} %get-tuple-element.708, s32[1024]{0:T(1024)S(1)} %pad_clamp_fusion.5), kind=kCustom, calls=%fused_computation.1.clone.clone.1 | custom fusion | bytes 2097184 | tf_op jit(solution)/shard_map/while/body/eval_jaxpr/gather | solution.py:111
  123.4 7.0 %all-gather.3.cloned.1.call-done = bf16[48,64,2048]{2,1,0:T(8,128)(2,1)} async-done(((bf16[3,64,2048]{2,1,0:T(8,128)(2,1)}), bf16[48,64,2048]{2,1,0:T(8,128)(2,1)}) %all-gather.3.cloned.1.call-update) | async-done | bytes 12582928 | tf_op jit(solution)/shard_map/all_gather | solution.py:97
  130.9 1.6 broadcast.120
  133.1 8.5 %all-to-all-start.1 = ((bf16[64,16,1152]{2,1,0:T(8,128)(2,1)}), bf16[64,16,1152]{2,1,0:T(8,128)(2,1)S(1)}, u32[]{:S(2)}, u32[]{:S(2)}) async-start(bf16[64,16,1152]{2,1,0:T(8,128)(2,1)} %bitcast_dynamic-update-slice_fusion), calls=%async_computation.1 | async-start | bytes 4718592 | tf_op jit(solution)/shard_map/all_to_all | solution.py:168
  143.7 28.3 %all-to-all-done.1 = bf16[64,16,1152]{2,1,0:T(8,128)(2,1)S(1)} async-done(((bf16[64,16,1152]{2,1,0:T(8,128)(2,1)}), bf16[64,16,1152]{2,1,0:T(8,128)(2,1)S(1)}, u32[]{:S(2)}, u32[]{:S(2)}) %all-to-all-start.1) | async-done | bytes 2359328 | tf_op jit(solution)/shard_map/all_to_all | solution.py:168
  173.2 3.0 %fusion.86 = f32[32,2048]{1,0:T(8,128)S(1)} fusion(bf16[32,1024]{1,0:T(8,128)(2,1)S(1)} %convert_element_type.126, bf16[1024,2048]{1,0:T(8,128)(2,1)} %param.30), kind=kOutput, calls=%fused_computation.161 | convolution fusion | flops 134217728 | bytes 4521984 | tf_op jit(solution)/shard_map/dot_general | solution.py:215
  176.2 3.0 %collective-permute-start = (f32[32,2048]{1,0:T(8,128)S(1)}, f32[32,2048]{1,0:T(8,128)S(1)}, u32[]{:S(2)}, u32[]{:S(2)}) collective-permute-start(f32[32,2048]{1,0:T(8,128)S(1)} %fusion.86), channel_id=1, source_target_pairs={{0,1},{1,0},{2,3},{3,2},{4,5},{5,4},{6,7},{7,6},{8,9},{9,8},{10,11... | collective-permute-start | bytes 786440 | tf_op jit(solution)/shard_map/ppermute | solution.py:216
  179.2 1.2 collective-permute-done
  181.4 1.1 collective-permute-start.2
  182.5 1.9 collective-permute-start.3
  184.4 3.0 %collective-permute-done.1 = bf16[32,2048]{1,0:T(8,128)(2,1)S(1)} collective-permute-done((bf16[32,2048]{1,0:T(8,128)(2,1)S(1)}, bf16[32,2048]{1,0:T(8,128)(2,1)S(1)}, u32[]{:S(2)}, u32[]{:S(2)}) %collective-permute-start.1) | collective-permute-done | bytes 131104 | tf_op jit(solution)/shard_map/ppermute | solution.py:225
  187.4 1.2 collective-permute-done.2
  188.6 1.1 collective-permute-done.3
  189.7 3.4 %fusion.28 = f32[128,16,64]{0,2,1:T(8,128)S(1)} fusion(bf16[32,2048]{1,0:T(8,128)(2,1)S(1)} %collective-permute-done.3, bf16[32,2048]{1,0:T(8,128)(2,1)S(1)} %collective-permute-done.2, bf16[32,2048]{1,0:T(8,128)(2,1)S(1)} %collective-permute-done.1, bf16[32,2048]{1,0:T(8,128)(2,1)S(1)} %fusion.39, bf16[16,3,64,2048]{3,2,1,0:T(8,128)(2,1)} %bitcast.186), kind=kOutput, calls=%fused_computation.51 | convolution fusion | flops 538968064 | bytes 5242880 | tf_op jit(solution)/shard_map/dot_general | solution.py:228
  193.1 3.4 %multiply_convert_fusion = bf16[128,16,64]{0,2,1:T(8,128)(2,1)S(1)} fusion(f32[128,16,64]{0,2,1:T(8,128)S(1)} %fusion.28, bf16[32,2048]{1,0:T(8,128)(2,1)S(1)} %collective-permute-done.3, bf16[32,2048]{1,0:T(8,128)(2,1)S(1)} %collective-permute-done.2, bf16[32,2048]{1,0:T(8,128)(2,1)S(1)} %collective-permute-done.1, bf16[32,2048]{1,0:T(8,128)(2,1)S(1)} %fusion.39, ...), kind=kOutput, calls=%fused_computation.73 | convolution fusion | flops 539754496 | bytes 5505024 | tf_op jit(solution)/shard_map/dot_general | solution.py:229
  197.1 3.0 %fusion.29 = f32[4,2,16,2048]{3,2,1,0:T(8,128)S(1)} fusion(bf16[4,2,16,16,64]{4,3,2,1,0:T(8,128)(2,1)S(1)} %bitcast.174, bf16[16,3,64,2048]{3,2,1,0:T(8,128)(2,1)} %bitcast.188), kind=kOutput, calls=%fused_computation.52 | convolution fusion | flops 536870912 | bytes 5505024 | tf_op jit(solution)/shard_map/dot_general | solution.py:232
  200.1 1.6 collective-permute-start.4
  202.1 1.1 collective-permute-done.4
  203.4 2.5 %collective-permute-start.5 = (f32[16,2048]{1,0:T(8,128)S(1)}, f32[16,2048]{1,0:T(8,128)S(1)}, u32[]{:S(2)}, u32[]{:S(2)}) collective-permute-start(f32[16,2048]{1,0:T(8,128)S(1)} %get-tuple-element.498), channel_id=1, source_target_pairs={{0,6},{2,0},{4,2},{6,4},{1,7},{3,1},{5,3},{7,5},{8,14},{10,8},{12,... | collective-permute-start | bytes 393224 | tf_op jit(solution)/shard_map/ppermute | solution.py:242
  207.3 1.7 collective-permute-done.5
  209.0 2.7 %collective-permute-done.6 = f32[16,2048]{1,0:T(8,128)S(1)} collective-permute-done((f32[16,2048]{1,0:T(8,128)S(1)}, f32[16,2048]{1,0:T(8,128)S(1)}, u32[]{:S(2)}, u32[]{:S(2)}) %collective-permute-start.6) | collective-permute-done | bytes 131104 | tf_op jit(solution)/shard_map/ppermute | solution.py:242
  211.7 3.8 %collective-permute-done.7 = f32[16,2048]{1,0:T(8,128)S(1)} collective-permute-done((f32[16,2048]{1,0:T(8,128)S(1)}, f32[16,2048]{1,0:T(8,128)S(1)}, u32[]{:S(2)}, u32[]{:S(2)}) %collective-permute-start.7) | collective-permute-done | bytes 131104 | tf_op jit(solution)/shard_map/ppermute | solution.py:242
  215.6 2.0 all_gather.11
  217.8 4.7 %convolution_convert_fusion = bf16[32,1536]{1,0:T(8,128)(2,1)} fusion(bf16[2048,1536]{1,0:T(8,128)(2,1)} %param.35, bf16[32,2048]{1,0:T(8,128)(2,1)S(1)} %all_gather.11, f32[2048]{0:T(1024)S(1)} %convert_element_type.135, f32[32]{0:T(128)S(1)} %add_rsqrt_fusion), kind=kOutput, calls=%fused_computation.53 | convolution fusion | flops 201637888 | bytes 6529152 | tf_op jit(solution)/shard_map/dot_general | solution.py:247
  (260 shorter events, 48.0 us)
Async XLA Ops:
  7.2 18.1 %copy-start.5 = (s32[2]{0:T(128)S(1)}, s32[2]{0:T(128)}, u32[]{:S(2)}) copy-start(s32[2]{0:T(128)} %param.28) | copy-start | bytes 28
  7.2 18.7 %copy-start.6 = (s32[2,48]{1,0:T(2,128)S(1)}, s32[2,48]{1,0:T(2,128)}, u32[]{:S(2)}) copy-start(s32[2,48]{1,0:T(2,128)} %param.27) | copy-start | bytes 1156
  7.2 123.2 %all-gather.3.cloned.1.call-start = ((), (), s32[]{:S(2)}) async-start(), calls=%async_computation.2 | async-start | bytes 13369344 | tf_op jit(solution)/shard_map/all_gather | solution.py:97
  12.9 58.5 %all-to-all-start = ((bf16[64,16,1152]{2,1,0:T(8,128)(2,1)}), bf16[64,16,1152]{2,1,0:T(8,128)(2,1)}, u32[]{:S(2)}, u32[]{:S(2)}) async-start(bf16[64,16,1152]{2,1,0:T(8,128)(2,1)} %bitcast_dynamic-update-slice_fusion.1), calls=%async_computation | async-start | bytes 4718592 | tf_op jit(solution)/shard_map/all_to_all | solution.py:95
  123.3 18.2 %copy-start.1 = (bf16[32,1024]{1,0:T(8,128)(2,1)S(1)}, bf16[32,1024]{1,0:T(8,128)(2,1)}, u32[]{:S(2)}) copy-start(bf16[32,1024]{1,0:T(8,128)(2,1)} %param.21) | copy-start | bytes 196612
  123.3 18.4 %copy-start.8 = (s32[2]{0:T(128)S(1)}, s32[2]{0:T(128)}, u32[]{:S(2)}) copy-start(s32[2]{0:T(128)} %param.24) | copy-start | bytes 28
  123.4 18.5 %copy-start.7 = (s32[2,16]{1,0:T(2,128)S(1)}, s32[2,16]{1,0:T(2,128)}, u32[]{:S(2)}) copy-start(s32[2,16]{1,0:T(2,128)} %param.23) | copy-start | bytes 388
  123.4 19.4 %copy-start = (bf16[32,2,256]{2,1,0:T(2,128)(2,1)S(1)}, bf16[32,2,256]{2,1,0:T(2,128)(2,1)}, u32[]{:S(2)}) copy-start(bf16[32,2,256]{2,1,0:T(2,128)(2,1)} %param.22) | copy-start | bytes 98308
  133.1 46.1 %copy-start.3 = (bf16[2048]{0:T(1024)(128)(2,1)S(1)}, bf16[2048]{0:T(1024)(128)(2,1)}, u32[]{:S(2)}) copy-start(bf16[2048]{0:T(1024)(128)(2,1)} %param.31) | copy-start | bytes 12292
  133.1 47.2 %copy-start.2 = (bf16[32,2048]{1,0:T(8,128)(2,1)S(1)}, bf16[32,2048]{1,0:T(8,128)(2,1)}, u32[]{:S(2)}) copy-start(bf16[32,2048]{1,0:T(8,128)(2,1)} %param.20) | copy-start | bytes 393220
  133.1 38.9 %all-to-all-start.1 = ((bf16[64,16,1152]{2,1,0:T(8,128)(2,1)}), bf16[64,16,1152]{2,1,0:T(8,128)(2,1)S(1)}, u32[]{:S(2)}, u32[]{:S(2)}) async-start(bf16[64,16,1152]{2,1,0:T(8,128)(2,1)} %bitcast_dynamic-update-slice_fusion), calls=%async_computation.1 | async-start | bytes 4718592 | tf_op jit(solution)/shard_map/all_to_all | solution.py:168
  141.6 42.8 %copy-start.4 = (bf16[2048]{0:T(1024)(128)(2,1)S(1)}, bf16[2048]{0:T(1024)(128)(2,1)}, u32[]{:S(2)}) copy-start(bf16[2048]{0:T(1024)(128)(2,1)} %param.34) | copy-start | bytes 12292
  176.2 4.2 %collective-permute-start = (f32[32,2048]{1,0:T(8,128)S(1)}, f32[32,2048]{1,0:T(8,128)S(1)}, u32[]{:S(2)}, u32[]{:S(2)}) collective-permute-start(f32[32,2048]{1,0:T(8,128)S(1)} %fusion.86), channel_id=1, source_target_pairs={{0,1},{1,0},{2,3},{3,2},{4,5},{5,4},{6,7},{7,6},{8,9},{9,8},{10,11... | collective-permute-start | bytes 786440 | tf_op jit(solution)/shard_map/ppermute | solution.py:216
  180.6 6.8 %collective-permute-start.1 = (bf16[32,2048]{1,0:T(8,128)(2,1)S(1)}, bf16[32,2048]{1,0:T(8,128)(2,1)S(1)}, u32[]{:S(2)}, u32[]{:S(2)}) collective-permute-start(bf16[32,2048]{1,0:T(8,128)(2,1)S(1)} %fusion.39), channel_id=1, source_target_pairs={{0,2},{2,4},{4,6},{6,0},{1,3},{3,5},{5,7},{7,1},{8,10},{10,12},{12... | collective-permute-start | bytes 393224 | tf_op jit(solution)/shard_map/ppermute | solution.py:225
  181.4 7.2 %collective-permute-start.2 = (bf16[32,2048]{1,0:T(8,128)(2,1)S(1)}, bf16[32,2048]{1,0:T(8,128)(2,1)S(1)}, u32[]{:S(2)}, u32[]{:S(2)}) collective-permute-start(bf16[32,2048]{1,0:T(8,128)(2,1)S(1)} %fusion.39), channel_id=1, source_target_pairs={{0,4},{2,6},{4,0},{6,2},{1,5},{3,7},{5,1},{7,3},{8,12},{10,14},{12... | collective-permute-start | bytes 393224 | tf_op jit(solution)/shard_map/ppermute | solution.py:225
  182.5 7.2 %collective-permute-start.3 = (bf16[32,2048]{1,0:T(8,128)(2,1)S(1)}, bf16[32,2048]{1,0:T(8,128)(2,1)S(1)}, u32[]{:S(2)}, u32[]{:S(2)}) collective-permute-start(bf16[32,2048]{1,0:T(8,128)(2,1)S(1)} %fusion.39), channel_id=1, source_target_pairs={{0,6},{2,0},{4,2},{6,4},{1,7},{3,1},{5,3},{7,5},{8,14},{10,8},{12,... | collective-permute-start | bytes 393224 | tf_op jit(solution)/shard_map/ppermute | solution.py:225
  197.0 4.7 %copy-start.9 = (s32[2]{0:T(128)S(1)}, s32[2]{0:T(128)}, u32[]{:S(2)}) copy-start(s32[2]{0:T(128)} %param.25) | copy-start | bytes 28
  200.1 3.1 %collective-permute-start.4 = (f32[4,16,2048]{2,1,0:T(8,128)S(1)}, f32[4,16,2048]{2,1,0:T(8,128)S(1)}, u32[]{:S(2)}, u32[]{:S(2)}) collective-permute-start(f32[4,16,2048]{2,1,0:T(8,128)S(1)} %dynamic-slice_bitcast_fusion), channel_id=1, source_target_pairs={{0,1},{1,0},{2,3},{3,2},{4,5},{5,4},{6,7},{7,6},{8,9},{9,8},{10,11... | collective-permute-start | bytes 1572872 | tf_op jit(solution)/shard_map/ppermute | solution.py:238
  203.4 5.7 %collective-permute-start.5 = (f32[16,2048]{1,0:T(8,128)S(1)}, f32[16,2048]{1,0:T(8,128)S(1)}, u32[]{:S(2)}, u32[]{:S(2)}) collective-permute-start(f32[16,2048]{1,0:T(8,128)S(1)} %get-tuple-element.498), channel_id=1, source_target_pairs={{0,6},{2,0},{4,2},{6,4},{1,7},{3,1},{5,3},{7,5},{8,14},{10,8},{12,... | collective-permute-start | bytes 393224 | tf_op jit(solution)/shard_map/ppermute | solution.py:242
  205.8 5.9 %collective-permute-start.6 = (f32[16,2048]{1,0:T(8,128)S(1)}, f32[16,2048]{1,0:T(8,128)S(1)}, u32[]{:S(2)}, u32[]{:S(2)}) collective-permute-start(f32[16,2048]{1,0:T(8,128)S(1)} %get-tuple-element.500), channel_id=1, source_target_pairs={{0,4},{2,6},{4,0},{6,2},{1,5},{3,7},{5,1},{7,3},{8,12},{10,14},{12... | collective-permute-start | bytes 393224 | tf_op jit(solution)/shard_map/ppermute | solution.py:242
  206.2 9.3 %collective-permute-start.7 = (f32[16,2048]{1,0:T(8,128)S(1)}, f32[16,2048]{1,0:T(8,128)S(1)}, u32[]{:S(2)}, u32[]{:S(2)}) collective-permute-start(f32[16,2048]{1,0:T(8,128)S(1)} %get-tuple-element.499), channel_id=1, source_target_pairs={{0,2},{2,4},{4,6},{6,0},{1,3},{3,5},{5,7},{7,1},{8,10},{10,12},{12... | collective-permute-start | bytes 393224 | tf_op jit(solution)/shard_map/ppermute | solution.py:242
Sparse Core Ops, SparseCore 0:
  10.2 120.1 all-gather.2

commit v8 on v7

--- a/solution.py
+++ b/solution.py
@@ -141,7 +141,8 @@
         jnp.zeros(stat_shape + (HEAD_DIM,), jnp.float32),
     )
     own_queries = queries[0]
-    own_state = attend(0, own_queries, 0, num_blocks, start_state)
+    split = num_blocks // 2
+    own_state = attend(0, own_queries, 0, split, start_state)
     own_state, every_query = lax.optimization_barrier((own_state, every_query))
     marks = every_query[:, 0, q_width]
     senders = jnp.arange(marks.shape[0], dtype=jnp.int32)
@@ -149,9 +150,6 @@
     foreign = lax.dynamic_index_in_dim(every_query, sender, 0, keepdims=False)[:, :q_width]
     foreign = foreign.reshape(tree_len, kv_local, GROUP, HEAD_DIM)
     f_running, f_total, f_accum = attend(1, foreign, 0, num_blocks, start_state)
-    all_w, f_running, f_total, f_accum = lax.optimization_barrier(
-        (all_w, f_running, f_total, f_accum)
-    )
     f_out = f_accum / f_total[..., None]
     sent_out = jnp.transpose(f_out, (2, 0, 1, 3)).reshape(
         tree_len, kv_local * GROUP * HEAD_DIM
@@ -165,8 +163,10 @@
     r_packet = jnp.concatenate([sent_out.astype(jnp.bfloat16), stats, pad], axis=1)
     r_send = jnp.zeros((owners,) + r_packet.shape, r_packet.dtype)
     r_send = lax.dynamic_update_index_in_dim(r_send, r_packet, sender, 0)
+    r_send, own_state = lax.optimization_barrier((r_send, own_state))
     back = lax.all_to_all(r_send, REQ, 0, 0, tiled=True)
-    running, total, accum = own_state
+    running, total, accum = attend(0, own_queries, split, num_blocks, own_state)
+    all_w, running, total, accum = lax.optimization_barrier((all_w, running, total, accum))
     cache_out = accum / total[..., None]
     got = lax.dynamic_index_in_dim(back, prev_owner[0], 0, keepdims=False).astype(jnp.float32)
     heads = kv_local * GROUP

time: 231 us -> 213 us (0.922)
  waiting for transfers between devices: 51.1 us -> 34.2 us
    all_to_all x1, waiting for transfers between devices: 28.3 us -> 11.3 us  [per_device(): back = lax.all_to_all(r_send, REQ, 0, 0, tiled=True)]
    all_to_all x1, waiting for transfers between devices: 0.01 us -> 8.83 us  [per_device(): every_query = lax.all_to_all(q_send, REQ, 0, 0, tiled=True)]
    all_gather x1, waiting for transfers between devices: 6.98 us -> 0.01 us  [per_device(): all_w = lax.all_gather(own_w, ('z', 'x'), axis=0, tiled=False)]
    ppermute x3, waiting for transfers between devices: 8.23 us -> 4.62 us  [per_device(): mlp_half = mlp_half + lax.ppermute(mine[shift], 'y', perm)]
  transfers between devices with their start and end apart: 11 -> 11, of which waited for: 10 -> 9; matrix products, arithmetic and copies ran while one was open for 44% -> 49% of each run, Pallas kernels for 0% -> 0%
where the time goes in v8:
time: 213 us; the launch traced here: 212 us
  local copies, waits for them, and re-layouts  73.4 us (34%)
  waiting for transfers between devices  34.2 us (16%)
  matrix products  33.8 us (16%)
  starting transfers between devices  30.3 us (14%)
  other arithmetic  19 us (9%)
  between operations  17.1 us (8%)
  blocking collectives  3.07 us (1%)
    gather x12, local copies, waits for them, and re-layouts, attend_block(): gathered = cache[page_ids]  49.2 us
    all_to_all x1, starting transfers between devices, per_device(): every_query = lax.all_to_all(q_send, REQ, 0, 0, tiled=True)  12.2 us
    all_to_all x1, waiting for transfers between devices, per_device(): back = lax.all_to_all(r_send, REQ, 0, 0, tiled=True)  11.3 us
    dot_general x12, matrix products, attend_block(): jnp.einsum('ghqk,kge->ghqe', weights, value_rows.astype(jnp.float32), pre...  9.77 us
    all_to_all x1, waiting for transfers between devices, per_device(): every_query = lax.all_to_all(q_send, REQ, 0, 0, tiled=True)  8.83 us
    lt x12, other arithmetic, attend_block(): visible = block * block_keys + positions < length  7.97 us
    all_to_all x1, starting transfers between devices, per_device(): back = lax.all_to_all(r_send, REQ, 0, 0, tiled=True)  7.44 us
    ppermute x3, waiting for transfers between devices, per_device(): shifted.append(lax.ppermute(normed, 'y', perm))  7.06 us
  transfers between devices with their start and end apart: 11, of which 9 were waited for; matrix products, arithmetic and copies ran while one was open for 49% of the time, Pallas kernels for 0%

profile of v8, /device:TPU:1, one launch (start us, length us, event | category | flops | bytes accessed | tf_op | source)
XLA Modules:
  0.0 212.1 jit_solution(15303678811170208777)
XLA Ops:
  7.2 0.8 fusion.97
  8.7 1.5 broadcast.148.clone
  10.9 12.2 %all-to-all-start = ((bf16[64,16,1152]{2,1,0:T(8,128)(2,1)}), bf16[64,16,1152]{2,1,0:T(8,128)(2,1)}, u32[]{:S(2)}, u32[]{:S(2)}) async-start(bf16[64,16,1152]{2,1,0:T(8,128)(2,1)} %bitcast_dynamic-update-slice_fusion.1), calls=%async_computation | async-start | bytes 4718592 | tf_op jit(solution)/shard_map/all_to_all | solution.py:95
  23.1 1.0 pad_maximum_fusion
  24.9 22.7 %while.55 = (s32[]{:T(128)}, f32[4,4,16]{2,1,0:T(4,128)S(1)}, f32[4,4,16]{2,1,0:T(4,128)S(1)}, f32[4,4,16,64]{3,2,1,0:T(8,128)S(1)}, s32[]{:T(128)}, /*index=5*/...) while((s32[]{:T(128)}, f32[4,4,16]{2,1,0:T(4,128)S(1)}, ...), condition=%wide.region_3.4_spmd.clone, body=%wide.region_0.3_spmd.clone.sunk | while | flops 237031712 | bytes 12771671 | solution.py:135
  25.0 4.0 %gather_fusion.1 = bf16[8,2,128,256]{3,2,1,0:T(8,128)(2,1)S(1)} fusion(bf16[64,2,128,256]{3,2,1,0:T(8,128)(2,1)} %get-tuple-element.965, s32[1024]{0:T(1024)S(1)} %pad_clamp_fusion.7), kind=kCustom, calls=%fused_computation.clone.clone.1 | custom fusion | bytes 2097184 | tf_op jit(solution)/shard_map/while/body/eval_jaxpr/gather | solution.py:111
  32.6 4.0 %gather_fusion.1 = bf16[8,2,128,256]{3,2,1,0:T(8,128)(2,1)S(1)} fusion(bf16[64,2,128,256]{3,2,1,0:T(8,128)(2,1)} %get-tuple-element.965, s32[1024]{0:T(1024)S(1)} %pad_clamp_fusion.7), kind=kCustom, calls=%fused_computation.clone.clone.1 | custom fusion | bytes 2097184 | tf_op jit(solution)/shard_map/while/body/eval_jaxpr/gather | solution.py:111
  40.2 4.0 %gather_fusion.1 = bf16[8,2,128,256]{3,2,1,0:T(8,128)(2,1)S(1)} fusion(bf16[64,2,128,256]{3,2,1,0:T(8,128)(2,1)} %get-tuple-element.965, s32[1024]{0:T(1024)S(1)} %pad_clamp_fusion.7), kind=kCustom, calls=%fused_computation.clone.clone.1 | custom fusion | bytes 2097184 | tf_op jit(solution)/shard_map/while/body/eval_jaxpr/gather | solution.py:111
  49.7 8.8 %all-to-all-done = bf16[64,16,1152]{2,1,0:T(8,128)(2,1)} async-done(((bf16[64,16,1152]{2,1,0:T(8,128)(2,1)}), bf16[64,16,1152]{2,1,0:T(8,128)(2,1)}, u32[]{:S(2)}, u32[]{:S(2)}) %all-to-all-start) | async-done | bytes 2359328 | tf_op jit(solution)/shard_map/all_to_all | solution.py:95
  58.6 2.1 %compare_reduce_fusion = pred[64]{0:T(512)(128)(4,1)S(1)} fusion(bf16[64,16,1152]{2,1,0:T(8,128)(2,1)} %all-to-all-done), kind=kLoop, calls=%fused_computation.126 | loop fusion | flops 64 | bytes 192 | tf_op jit(solution)/shard_map/gt | solution.py:149
  64.2 46.5 %while.56 = (s32[]{:T(128)}, f32[4,4,16]{2,1,0:T(4,128)S(1)}, f32[4,4,16]{2,1,0:T(4,128)S(1)}, f32[4,4,16,64]{3,2,1,0:T(8,128)S(1)}, s32[]{:T(128)}, /*index=5*/...) while((s32[]{:T(128)}, f32[4,4,16]{2,1,0:T(4,128)S(1)}, ...), condition=%wide.region_8.9_spmd.clone, body=%wide.region_5.8_spmd.clone.sunk | while | flops 237031712 | bytes 12771671 | solution.py:135
  64.3 4.0 %gather_fusion.2 = bf16[8,2,128,256]{3,2,1,0:T(8,128)(2,1)S(1)} fusion(bf16[64,2,128,256]{3,2,1,0:T(8,128)(2,1)} %get-tuple-element.1004, s32[1024]{0:T(1024)S(1)} %pad_clamp_fusion.8), kind=kCustom, calls=%fused_computation.1.clone.clone.1 | custom fusion | bytes 2097184 | tf_op jit(solution)/shard_map/while/body/eval_jaxpr/gather | solution.py:111
  70.9 0.8 convolution_add_fusion.8
  71.8 4.7 %gather_fusion.2 = bf16[8,2,128,256]{3,2,1,0:T(8,128)(2,1)S(1)} fusion(bf16[64,2,128,256]{3,2,1,0:T(8,128)(2,1)} %get-tuple-element.1004, s32[1024]{0:T(1024)S(1)} %pad_clamp_fusion.8), kind=kCustom, calls=%fused_computation.1.clone.clone.1 | custom fusion | bytes 2097184 | tf_op jit(solution)/shard_map/while/body/eval_jaxpr/gather | solution.py:111
  79.1 0.8 convolution_add_fusion.8
  80.1 4.1 %gather_fusion.2 = bf16[8,2,128,256]{3,2,1,0:T(8,128)(2,1)S(1)} fusion(bf16[64,2,128,256]{3,2,1,0:T(8,128)(2,1)} %get-tuple-element.1004, s32[1024]{0:T(1024)S(1)} %pad_clamp_fusion.8), kind=kCustom, calls=%fused_computation.1.clone.clone.1 | custom fusion | bytes 2097184 | tf_op jit(solution)/shard_map/while/body/eval_jaxpr/gather | solution.py:111
  86.7 0.8 convolution_add_fusion.8
  87.7 4.1 %gather_fusion.2 = bf16[8,2,128,256]{3,2,1,0:T(8,128)(2,1)S(1)} fusion(bf16[64,2,128,256]{3,2,1,0:T(8,128)(2,1)} %get-tuple-element.1004, s32[1024]{0:T(1024)S(1)} %pad_clamp_fusion.8), kind=kCustom, calls=%fused_computation.1.clone.clone.1 | custom fusion | bytes 2097184 | tf_op jit(solution)/shard_map/while/body/eval_jaxpr/gather | solution.py:111
  94.4 0.8 convolution_add_fusion.8
  95.3 4.2 %gather_fusion.2 = bf16[8,2,128,256]{3,2,1,0:T(8,128)(2,1)S(1)} fusion(bf16[64,2,128,256]{3,2,1,0:T(8,128)(2,1)} %get-tuple-element.1004, s32[1024]{0:T(1024)S(1)} %pad_clamp_fusion.8), kind=kCustom, calls=%fused_computation.1.clone.clone.1 | custom fusion | bytes 2097184 | tf_op jit(solution)/shard_map/while/body/eval_jaxpr/gather | solution.py:111
  102.1 0.8 convolution_add_fusion.8
  103.0 4.3 %gather_fusion.2 = bf16[8,2,128,256]{3,2,1,0:T(8,128)(2,1)S(1)} fusion(bf16[64,2,128,256]{3,2,1,0:T(8,128)(2,1)} %get-tuple-element.1004, s32[1024]{0:T(1024)S(1)} %pad_clamp_fusion.8), kind=kCustom, calls=%fused_computation.1.clone.clone.1 | custom fusion | bytes 2097184 | tf_op jit(solution)/shard_map/while/body/eval_jaxpr/gather | solution.py:111
  109.9 0.8 convolution_add_fusion.8
  111.2 1.5 broadcast.148
  113.4 7.4 %all-to-all-start.1 = ((bf16[64,16,1152]{2,1,0:T(8,128)(2,1)}), bf16[64,16,1152]{2,1,0:T(8,128)(2,1)}, u32[]{:S(2)}, u32[]{:S(2)}) async-start(bf16[64,16,1152]{2,1,0:T(8,128)(2,1)} %bitcast_dynamic-update-slice_fusion), calls=%async_computation.1 | async-start | bytes 4718592 | tf_op jit(solution)/shard_map/all_to_all | solution.py:167
  120.8 22.7 %while.54 = (s32[]{:T(128)}, f32[4,4,16]{2,1,0:T(4,128)S(1)}, f32[4,4,16]{2,1,0:T(4,128)S(1)}, f32[4,4,16,64]{3,2,1,0:T(8,128)S(1)}, s32[]{:T(128)}, /*index=5*/...) while((s32[]{:T(128)}, f32[4,4,16]{2,1,0:T(4,128)S(1)}, ...), condition=%wide.region_12.13_spmd.clone, body=%wide.region_9.12_spmd.clone.sunk | while | flops 237014560 | bytes 12771679 | solution.py:135
  120.9 4.0 %gather_fusion = bf16[8,2,128,256]{3,2,1,0:T(8,128)(2,1)S(1)} fusion(bf16[64,2,128,256]{3,2,1,0:T(8,128)(2,1)} %get-tuple-element.1045, s32[1024]{0:T(1024)S(1)} %pad_clamp_fusion.6), kind=kCustom, calls=%fused_computation.2.clone.clone.1 | custom fusion | bytes 2097184 | tf_op jit(solution)/shard_map/while/body/eval_jaxpr/gather | solution.py:111
  127.6 0.8 convolution_add_fusion.6
  128.5 4.0 %gather_fusion = bf16[8,2,128,256]{3,2,1,0:T(8,128)(2,1)S(1)} fusion(bf16[64,2,128,256]{3,2,1,0:T(8,128)(2,1)} %get-tuple-element.1045, s32[1024]{0:T(1024)S(1)} %pad_clamp_fusion.6), kind=kCustom, calls=%fused_computation.2.clone.clone.1 | custom fusion | bytes 2097184 | tf_op jit(solution)/shard_map/while/body/eval_jaxpr/gather | solution.py:111
  136.1 4.0 %gather_fusion = bf16[8,2,128,256]{3,2,1,0:T(8,128)(2,1)S(1)} fusion(bf16[64,2,128,256]{3,2,1,0:T(8,128)(2,1)} %get-tuple-element.1045, s32[1024]{0:T(1024)S(1)} %pad_clamp_fusion.6), kind=kCustom, calls=%fused_computation.2.clone.clone.1 | custom fusion | bytes 2097184 | tf_op jit(solution)/shard_map/while/body/eval_jaxpr/gather | solution.py:111
  143.6 11.3 %all-to-all-done.1 = bf16[64,16,1152]{2,1,0:T(8,128)(2,1)} async-done(((bf16[64,16,1152]{2,1,0:T(8,128)(2,1)}), bf16[64,16,1152]{2,1,0:T(8,128)(2,1)}, u32[]{:S(2)}, u32[]{:S(2)}) %all-to-all-start.1) | async-done | bytes 2359328 | tf_op jit(solution)/shard_map/all_to_all | solution.py:167
  157.0 3.0 %fusion.100 = f32[32,2048]{1,0:T(8,128)S(1)} fusion(bf16[32,1024]{1,0:T(8,128)(2,1)S(1)} %convert_element_type.129, bf16[1024,2048]{1,0:T(8,128)(2,1)} %param.32), kind=kOutput, calls=%fused_computation.183 | convolution fusion | flops 134217728 | bytes 4521984 | tf_op jit(solution)/shard_map/dot_general | solution.py:215
  160.0 3.3 %collective-permute-start = (f32[32,2048]{1,0:T(8,128)S(1)}, f32[32,2048]{1,0:T(8,128)S(1)}, u32[]{:S(2)}, u32[]{:S(2)}) collective-permute-start(f32[32,2048]{1,0:T(8,128)S(1)} %fusion.100), channel_id=1, source_target_pairs={{0,1},{1,0},{2,3},{3,2},{4,5},{5,4},{6,7},{7,6},{8,9},{9,8},{10,11... | collective-permute-start | bytes 786440 | tf_op jit(solution)/shard_map/ppermute | solution.py:216
  163.2 1.2 collective-permute-done
  165.3 2.0 collective-permute-start.2
  167.3 2.2 %collective-permute-done.3 = bf16[32,2048]{1,0:T(8,128)(2,1)S(1)} collective-permute-done((bf16[32,2048]{1,0:T(8,128)(2,1)S(1)}, bf16[32,2048]{1,0:T(8,128)(2,1)S(1)}, u32[]{:S(2)}, u32[]{:S(2)}) %collective-permute-start.3) | collective-permute-done | bytes 131104 | tf_op jit(solution)/shard_map/ppermute | solution.py:225
  169.5 1.7 collective-permute-done.2
  171.2 3.2 %collective-permute-done.1 = bf16[32,2048]{1,0:T(8,128)(2,1)S(1)} collective-permute-done((bf16[32,2048]{1,0:T(8,128)(2,1)S(1)}, bf16[32,2048]{1,0:T(8,128)(2,1)S(1)}, u32[]{:S(2)}, u32[]{:S(2)}) %collective-permute-start.1) | collective-permute-done | bytes 131104 | tf_op jit(solution)/shard_map/ppermute | solution.py:225
  174.3 3.4 %fusion.40 = f32[128,16,64]{0,2,1:T(8,128)S(1)} fusion(bf16[32,2048]{1,0:T(8,128)(2,1)S(1)} %collective-permute-done.3, bf16[32,2048]{1,0:T(8,128)(2,1)S(1)} %collective-permute-done.2, bf16[32,2048]{1,0:T(8,128)(2,1)S(1)} %collective-permute-done.1, bf16[32,2048]{1,0:T(8,128)(2,1)S(1)} %fusion.51, bf16[16,3,64,2048]{3,2,1,0:T(8,128)(2,1)} %bitcast.235), kind=kOutput, calls=%fused_computation.71 | convolution fusion | flops 538968064 | bytes 5242880 | tf_op jit(solution)/shard_map/dot_general | solution.py:228
  177.8 3.5 %multiply_convert_fusion = bf16[128,16,64]{0,2,1:T(8,128)(2,1)S(1)} fusion(f32[128,16,64]{0,2,1:T(8,128)S(1)} %fusion.40, bf16[32,2048]{1,0:T(8,128)(2,1)S(1)} %collective-permute-done.3, bf16[32,2048]{1,0:T(8,128)(2,1)S(1)} %collective-permute-done.2, bf16[32,2048]{1,0:T(8,128)(2,1)S(1)} %collective-permute-done.1, bf16[32,2048]{1,0:T(8,128)(2,1)S(1)} %fusion.51, ...), kind=kOutput, calls=%fused_computation.93 | convolution fusion | flops 539754496 | bytes 5505024 | tf_op jit(solution)/shard_map/dot_general | solution.py:229
  181.7 3.0 %fusion.41 = f32[4,2,16,2048]{3,2,1,0:T(8,128)S(1)} fusion(bf16[4,2,16,16,64]{4,3,2,1,0:T(8,128)(2,1)S(1)} %bitcast.224, bf16[16,3,64,2048]{3,2,1,0:T(8,128)(2,1)} %bitcast.237), kind=kOutput, calls=%fused_computation.72 | convolution fusion | flops 536870912 | bytes 5505024 | tf_op jit(solution)/shard_map/dot_general | solution.py:232
  184.8 1.2 collective-permute-start.4
  186.4 1.1 collective-permute-done.4
  188.2 1.1 collective-permute-start.6
  189.3 2.0 collective-permute-start.5
  192.1 4.4 %collective-permute-done.7 = f32[16,2048]{1,0:T(8,128)S(1)} collective-permute-done((f32[16,2048]{1,0:T(8,128)S(1)}, f32[16,2048]{1,0:T(8,128)S(1)}, u32[]{:S(2)}, u32[]{:S(2)}) %collective-permute-start.7) | collective-permute-done | bytes 131104 | tf_op jit(solution)/shard_map/ppermute | solution.py:242
  196.7 3.1 %all_gather.11 = bf16[32,2048]{1,0:T(8,128)(2,1)S(1)} all-gather(bf16[16,2048]{1,0:T(8,128)(2,1)S(1)} %fusion.61), channel_id=1, replica_groups=mesh['z'=4,'x'=4,'y'=4,'mlp'=2] {'mlp'}, dimensions={0}, use_global_device_ids=true | all-gather | bytes 196608 | tf_op jit(solution)/shard_map/all_gather | solution.py:245
  200.0 4.7 %convolution_convert_fusion = bf16[32,1536]{1,0:T(8,128)(2,1)} fusion(bf16[2048,1536]{1,0:T(8,128)(2,1)} %param.37, bf16[32,2048]{1,0:T(8,128)(2,1)S(1)} %all_gather.11, f32[2048]{0:T(1024)S(1)} %convert_element_type.138, f32[32]{0:T(128)S(1)} %add_rsqrt_fusion), kind=kOutput, calls=%fused_computation.73 | convolution fusion | flops 201637888 | bytes 6529152 | tf_op jit(solution)/shard_map/dot_general | solution.py:247
  (265 shorter events, 48.2 us)
Async XLA Ops:
  7.2 16.0 %copy-start.3 = (bf16[64,2048]{1,0:T(8,128)(2,1)S(1)}, bf16[64,2048]{1,0:T(8,128)(2,1)}, u32[]{:S(2)}) copy-start(bf16[64,2048]{1,0:T(8,128)(2,1)} %param.35) | copy-start | bytes 786436
  7.2 16.0 %copy-start = (bf16[2,64,2048]{2,1,0:T(8,128)(2,1)S(1)}, bf16[2,64,2048]{2,1,0:T(8,128)(2,1)}, u32[]{:S(2)}) copy-start(bf16[2,64,2048]{2,1,0:T(8,128)(2,1)} %param.34) | copy-start | bytes 1572868
  7.2 17.0 %copy-start.7 = (s32[2]{0:T(128)S(1)}, s32[2]{0:T(128)}, u32[]{:S(2)}) copy-start(s32[2]{0:T(128)} %param.30) | copy-start | bytes 28
  7.2 17.6 %copy-start.8 = (s32[2,48]{1,0:T(2,128)S(1)}, s32[2,48]{1,0:T(2,128)}, u32[]{:S(2)}) copy-start(s32[2,48]{1,0:T(2,128)} %param.29) | copy-start | bytes 1156
  10.9 47.7 %all-to-all-start = ((bf16[64,16,1152]{2,1,0:T(8,128)(2,1)}), bf16[64,16,1152]{2,1,0:T(8,128)(2,1)}, u32[]{:S(2)}, u32[]{:S(2)}) async-start(bf16[64,16,1152]{2,1,0:T(8,128)(2,1)} %bitcast_dynamic-update-slice_fusion.1), calls=%async_computation | async-start | bytes 4718592 | tf_op jit(solution)/shard_map/all_to_all | solution.py:95
  23.1 133.0 %all-gather.3.cloned.1.call-start = ((), (), s32[]{:S(2)}) async-start(), calls=%async_computation.2 | async-start | bytes 13369344 | tf_op jit(solution)/shard_map/all_gather | solution.py:97
  24.9 22.8 %copy-start.2 = (bf16[32,1024]{1,0:T(8,128)(2,1)S(1)}, bf16[32,1024]{1,0:T(8,128)(2,1)}, u32[]{:S(2)}) copy-start(bf16[32,1024]{1,0:T(8,128)(2,1)} %param.23) | copy-start | bytes 196612
  24.9 22.9 %copy-start.1 = (bf16[32,2,256]{2,1,0:T(2,128)(2,1)S(1)}, bf16[32,2,256]{2,1,0:T(2,128)(2,1)}, u32[]{:S(2)}) copy-start(bf16[32,2,256]{2,1,0:T(2,128)(2,1)} %param.24) | copy-start | bytes 98308
  24.9 23.2 %copy-start.10 = (s32[2]{0:T(128)S(1)}, s32[2]{0:T(128)}, u32[]{:S(2)}) copy-start(s32[2]{0:T(128)} %param.26) | copy-start | bytes 28
  24.9 23.2 %copy-start.9 = (s32[2,16]{1,0:T(2,128)S(1)}, s32[2,16]{1,0:T(2,128)}, u32[]{:S(2)}) copy-start(s32[2,16]{1,0:T(2,128)} %param.25) | copy-start | bytes 388
  113.4 41.5 %all-to-all-start.1 = ((bf16[64,16,1152]{2,1,0:T(8,128)(2,1)}), bf16[64,16,1152]{2,1,0:T(8,128)(2,1)}, u32[]{:S(2)}, u32[]{:S(2)}) async-start(bf16[64,16,1152]{2,1,0:T(8,128)(2,1)} %bitcast_dynamic-update-slice_fusion), calls=%async_computation.1 | async-start | bytes 4718592 | tf_op jit(solution)/shard_map/all_to_all | solution.py:167
  143.5 19.7 %copy-start.5 = (bf16[2048]{0:T(1024)(128)(2,1)S(1)}, bf16[2048]{0:T(1024)(128)(2,1)}, u32[]{:S(2)}) copy-start(bf16[2048]{0:T(1024)(128)(2,1)} %param.33) | copy-start | bytes 12292
  143.5 20.9 %copy-start.4 = (bf16[32,2048]{1,0:T(8,128)(2,1)S(1)}, bf16[32,2048]{1,0:T(8,128)(2,1)}, u32[]{:S(2)}) copy-start(bf16[32,2048]{1,0:T(8,128)(2,1)} %param.22) | copy-start | bytes 393220
  143.6 23.7 %copy-start.6 = (bf16[2048]{0:T(1024)(128)(2,1)S(1)}, bf16[2048]{0:T(1024)(128)(2,1)}, u32[]{:S(2)}) copy-start(bf16[2048]{0:T(1024)(128)(2,1)} %param.36) | copy-start | bytes 12292
  160.0 4.4 %collective-permute-start = (f32[32,2048]{1,0:T(8,128)S(1)}, f32[32,2048]{1,0:T(8,128)S(1)}, u32[]{:S(2)}, u32[]{:S(2)}) collective-permute-start(f32[32,2048]{1,0:T(8,128)S(1)} %fusion.100), channel_id=1, source_target_pairs={{0,1},{1,0},{2,3},{3,2},{4,5},{5,4},{6,7},{7,6},{8,9},{9,8},{10,11... | collective-permute-start | bytes 786440 | tf_op jit(solution)/shard_map/ppermute | solution.py:216
  164.7 4.8 %collective-permute-start.3 = (bf16[32,2048]{1,0:T(8,128)(2,1)S(1)}, bf16[32,2048]{1,0:T(8,128)(2,1)S(1)}, u32[]{:S(2)}, u32[]{:S(2)}) collective-permute-start(bf16[32,2048]{1,0:T(8,128)(2,1)S(1)} %fusion.51), channel_id=1, source_target_pairs={{0,6},{2,0},{4,2},{6,4},{1,7},{3,1},{5,3},{7,5},{8,14},{10,8},{12,... | collective-permute-start | bytes 393224 | tf_op jit(solution)/shard_map/ppermute | solution.py:225
  165.3 5.9 %collective-permute-start.2 = (bf16[32,2048]{1,0:T(8,128)(2,1)S(1)}, bf16[32,2048]{1,0:T(8,128)(2,1)S(1)}, u32[]{:S(2)}, u32[]{:S(2)}) collective-permute-start(bf16[32,2048]{1,0:T(8,128)(2,1)S(1)} %fusion.51), channel_id=1, source_target_pairs={{0,4},{2,6},{4,0},{6,2},{1,5},{3,7},{5,1},{7,3},{8,12},{10,14},{12... | collective-permute-start | bytes 393224 | tf_op jit(solution)/shard_map/ppermute | solution.py:225
  167.2 7.1 %collective-permute-start.1 = (bf16[32,2048]{1,0:T(8,128)(2,1)S(1)}, bf16[32,2048]{1,0:T(8,128)(2,1)S(1)}, u32[]{:S(2)}, u32[]{:S(2)}) collective-permute-start(bf16[32,2048]{1,0:T(8,128)(2,1)S(1)} %fusion.51), channel_id=1, source_target_pairs={{0,2},{2,4},{4,6},{6,0},{1,3},{3,5},{5,7},{7,1},{8,10},{10,12},{12... | collective-permute-start | bytes 393224 | tf_op jit(solution)/shard_map/ppermute | solution.py:225
  181.7 4.3 %copy-start.11 = (s32[2]{0:T(128)S(1)}, s32[2]{0:T(128)}, u32[]{:S(2)}) copy-start(s32[2]{0:T(128)} %param.27) | copy-start | bytes 28
  184.8 2.8 %collective-permute-start.4 = (f32[4,16,2048]{2,1,0:T(8,128)S(1)}, f32[4,16,2048]{2,1,0:T(8,128)S(1)}, u32[]{:S(2)}, u32[]{:S(2)}) collective-permute-start(f32[4,16,2048]{2,1,0:T(8,128)S(1)} %dynamic-slice_bitcast_fusion), channel_id=1, source_target_pairs={{0,1},{1,0},{2,3},{3,2},{4,5},{5,4},{6,7},{7,6},{8,9},{9,8},{10,11... | collective-permute-start | bytes 1572872 | tf_op jit(solution)/shard_map/ppermute | solution.py:238
  187.7 8.8 %collective-permute-start.7 = (f32[16,2048]{1,0:T(8,128)S(1)}, f32[16,2048]{1,0:T(8,128)S(1)}, u32[]{:S(2)}, u32[]{:S(2)}) collective-permute-start(f32[16,2048]{1,0:T(8,128)S(1)} %get-tuple-element.730), channel_id=1, source_target_pairs={{0,2},{2,4},{4,6},{6,0},{1,3},{3,5},{5,7},{7,1},{8,10},{10,12},{12... | collective-permute-start | bytes 393224 | tf_op jit(solution)/shard_map/ppermute | solution.py:242
  188.2 8.2 %collective-permute-start.6 = (f32[16,2048]{1,0:T(8,128)S(1)}, f32[16,2048]{1,0:T(8,128)S(1)}, u32[]{:S(2)}, u32[]{:S(2)}) collective-permute-start(f32[16,2048]{1,0:T(8,128)S(1)} %get-tuple-element.731), channel_id=1, source_target_pairs={{0,4},{2,6},{4,0},{6,2},{1,5},{3,7},{5,1},{7,3},{8,12},{10,14},{12... | collective-permute-start | bytes 393224 | tf_op jit(solution)/shard_map/ppermute | solution.py:242
  189.3 7.4 %collective-permute-start.5 = (f32[16,2048]{1,0:T(8,128)S(1)}, f32[16,2048]{1,0:T(8,128)S(1)}, u32[]{:S(2)}, u32[]{:S(2)}) collective-permute-start(f32[16,2048]{1,0:T(8,128)S(1)} %get-tuple-element.729), channel_id=1, source_target_pairs={{0,6},{2,0},{4,2},{6,4},{1,7},{3,1},{5,3},{7,5},{8,14},{10,8},{12,... | collective-permute-start | bytes 393224 | tf_op jit(solution)/shard_map/ppermute | solution.py:242
Sparse Core Ops, SparseCore 0:
  26.0 108.6 all-gather.2

commit v9 on v8

--- a/solution.py
+++ b/solution.py
@@ -96,43 +96,56 @@
     own_w = jnp.stack([w_in[0], w_in[1], w_down])
     all_w = lax.all_gather(own_w, ("z", "x"), axis=0, tiled=False)
     page_len = cache.shape[2]
-    block_pages = math.gcd(held_table.shape[1], max(1, 1024 // page_len))
-    block_keys = block_pages * page_len
-    num_blocks = held_table.shape[1] // block_pages
-    positions = jnp.arange(block_keys, dtype=jnp.int32)
+    num_blocks = cache.shape[0]
+    width = kv_local * HEAD_DIM
+    entries = held_table.shape[1]
+    entry_start = jnp.arange(entries, dtype=jnp.int32)[:, None] * page_len
+    in_page = jnp.arange(page_len, dtype=jnp.int32)[None, :]
+    head_eye = jnp.eye(kv_local, dtype=jnp.float32)
+    rows = kv_local * GROUP * tree_len
 
     def attend(slot, slot_queries, first, last, state):
+        running, total, accum = state
         table = held_table[slot]
         length = held_len[slot]
-
-        def attend_block(block, state):
-            running, total, accum = state
-            page_ids = lax.dynamic_slice_in_dim(table, block * block_pages, block_pages, 0)
-            gathered = cache[page_ids]
-            key_rows = gathered[:, 0].reshape(block_keys, kv_local, HEAD_DIM)
-            value_rows = gathered[:, 1].reshape(block_keys, kv_local, HEAD_DIM)
-            scores = (
-                jnp.einsum(
-                    "qghe,kge->ghqk", slot_queries, key_rows, preferred_element_type=jnp.float32
-                )
-                * scale
+        page_ids = jnp.arange(first, last, dtype=jnp.int32)
+        match = table[:, None] == page_ids[None, :]
+        valid = (entry_start + in_page) < length
+        visible = jnp.any(match[:, :, None] & valid[:, None, :], axis=0).reshape(-1)
+        key_rows = cache[first:last, 0].reshape((last - first) * page_len, width)
+        value_rows = cache[first:last, 1].reshape((last - first) * page_len, width)
+        spread = jnp.einsum(
+            "qghe,gf->ghqfe", slot_queries, head_eye.astype(slot_queries.dtype)
+        ).reshape(rows, width)
+        scores = (
+            lax.dot_general(
+                spread, key_rows, (((1,), (1,)), ((), ())), preferred_element_type=jnp.float32
             )
-            visible = (block * block_keys + positions) < length
-            scores = jnp.where(visible, scores, masked_score)
-            newest = jnp.maximum(running, jnp.max(scores, axis=-1))
-            weights = jnp.where(visible, jnp.exp(scores - newest[..., None]), 0.0)
-            factor = jnp.exp(running - newest)
-            total = total * factor + jnp.sum(weights, axis=-1)
-            update = jnp.einsum(
-                "ghqk,kge->ghqe",
-                weights,
-                value_rows.astype(jnp.float32),
-                precision=lax.Precision.HIGHEST,
-            )
-            accum = accum * factor[..., None] + update
-            return (newest, total, accum)
-
-        return lax.fori_loop(first, last, attend_block, state)
+            * scale
+        )
+        scores = jnp.where(visible, scores, masked_score)
+        old = running.reshape(rows)
+        newest = jnp.maximum(old, jnp.max(scores, axis=-1))
+        weights = jnp.where(visible, jnp.exp(scores - newest[:, None]), 0.0)
+        factor = jnp.exp(old - newest)
+        total = total.reshape(rows) * factor + jnp.sum(weights, axis=-1)
+        high = weights.astype(jnp.bfloat16)
+        low = (weights - high.astype(jnp.float32)).astype(jnp.bfloat16)
+        full = jnp.dot(high, value_rows, preferred_element_type=jnp.float32) + jnp.dot(
+            low, value_rows, preferred_element_type=jnp.float32
+        )
+        update = jnp.einsum(
+            "ghqfe,gf->ghqe",
+            full.reshape(kv_local, GROUP, tree_len, kv_local, HEAD_DIM),
+            head_eye,
+            precision=lax.Precision.HIGHEST,
+        )
+        accum = accum * factor.reshape(kv_local, GROUP, tree_len)[..., None] + update
+        return (
+            newest.reshape(kv_local, GROUP, tree_len),
+            total.reshape(kv_local, GROUP, tree_len),
+            accum,
+        )
 
     stat_shape = (kv_local, GROUP, tree_len)
     start_state = (
@@ -141,9 +154,7 @@
         jnp.zeros(stat_shape + (HEAD_DIM,), jnp.float32),
     )
     own_queries = queries[0]
-    split = num_blocks // 2
-    own_state = attend(0, own_queries, 0, split, start_state)
-    own_state, every_query = lax.optimization_barrier((own_state, every_query))
+    own_state = start_state
     marks = every_query[:, 0, q_width]
     senders = jnp.arange(marks.shape[0], dtype=jnp.int32)
     sender = jnp.sum(jnp.where(marks > 0.5, senders, 0))
@@ -165,7 +176,7 @@
     r_send = lax.dynamic_update_index_in_dim(r_send, r_packet, sender, 0)
     r_send, own_state = lax.optimization_barrier((r_send, own_state))
     back = lax.all_to_all(r_send, REQ, 0, 0, tiled=True)
-    running, total, accum = attend(0, own_queries, split, num_blocks, own_state)
+    running, total, accum = attend(0, own_queries, 0, num_blocks, own_state)
     all_w, running, total, accum = lax.optimization_barrier((all_w, running, total, accum))
     cache_out = accum / total[..., None]
     got = lax.dynamic_index_in_dim(back, prev_owner[0], 0, keepdims=False).astype(jnp.float32)

time: 213 us -> 215 us (level)
  local copies, waits for them, and re-layouts: 73.4 us -> 22.3 us
  waiting for transfers between devices: 34.2 us -> 77.7 us
  matrix products: 33.8 us -> 47.2 us
    gather x12 -> x0, local copies, waits for them, and re-layouts: 49.2 us -> none  [attend_block(): gathered = cache[page_ids]]
    all_to_all x1, waiting for transfers between devices: 8.83 us -> 31.7 us  [per_device(): every_query = lax.all_to_all(q_send, REQ, 0, 0, tiled=True)]
    all_to_all x1, waiting for transfers between devices: 11.3 us -> 30.3 us  [per_device(): back = lax.all_to_all(r_send, REQ, 0, 0, tiled=True)]
    dot_general x24 -> x8, matrix products: 14.1 us -> 27.5 us  [the longest x2 10.9 us: attend(): lax.dot_general(spread, key_rows, (((1,), (1,)), ((), ())), preferred_ele...]
    lt x12 -> x1, other arithmetic: 7.97 us -> 1.37 us  [attend(): valid = entry_start + in_page < length]
    reduce_sum x12 -> x2, other arithmetic: 3.88 us -> 10.4 us  [attend(): total = total.reshape(rows) * factor + jnp.sum(weights, axis=-1)]
    squeeze x25 -> x0, local copies, waits for them, and re-layouts: 5.4 us -> none  [the longest x12 2.7 us: attend_block(): key_rows = gathered[:, 0].reshape(block_keys, kv_local, HEAD_DIM)]
    unnamed x27 -> x31, local copies, waits for them, and re-layouts: 0.76 us -> 5.86 us
  transfers between devices with their start and end apart: 11 -> 11, of which waited for: 9 -> 9; matrix products, arithmetic and copies ran while one was open for 49% -> 28% of each run, Pallas kernels for 0% -> 0%
where the time goes in v9:
time: 215 us
  waiting for transfers between devices  77.7 us (36%)
  matrix products  47.2 us (22%)
  starting transfers between devices  29 us (13%)
  local copies, waits for them, and re-layouts  22.3 us (10%)
  other arithmetic  19.1 us (9%)
  between operations  17.2 us (8%)
  blocking collectives  2.28 us (1%)
    all_to_all x1, waiting for transfers between devices, per_device(): every_query = lax.all_to_all(q_send, REQ, 0, 0, tiled=True)  31.7 us
    all_to_all x1, waiting for transfers between devices, per_device(): back = lax.all_to_all(r_send, REQ, 0, 0, tiled=True)  30.3 us
    all_to_all x1, starting transfers between devices, per_device(): every_query = lax.all_to_all(q_send, REQ, 0, 0, tiled=True)  12 us
    dot_general x2, matrix products, attend(): lax.dot_general(spread, key_rows, (((1,), (1,)), ((), ())), preferred_ele...  10.9 us
    reduce_sum x2, other arithmetic, attend(): total = total.reshape(rows) * factor + jnp.sum(weights, axis=-1)  10.4 us
    dot_general x2, matrix products, attend(): jnp.dot(low, value_rows, preferred_element_type=jnp.float32)  8.17 us
    ppermute x3, waiting for transfers between devices, per_device(): mlp_half = mlp_half + lax.ppermute(mine[shift], 'y', perm)  7.77 us
    dot_general x2, matrix products, attend(): jnp.dot(high, value_rows, preferred_element_type=jnp.float32)  7.19 us
  transfers between devices with their start and end apart: 11, of which 9 were waited for; matrix products, arithmetic and copies ran while one was open for 28% of the time, Pallas kernels for 0%

profile of v9, /device:TPU:1, one launch (start us, length us, event | category | flops | bytes accessed | tf_op | source)
XLA Modules:
  0.0 214.7 jit_solution(9287862148944135975)
XLA Ops:
  7.3 2.1 pad_maximum_fusion
  10.1 0.8 fusion.92
  10.9 1.6 broadcast.161.clone
  12.5 0.6 bitcast_dynamic-update-slice_fusion.1
  13.1 12.0 %all-to-all-start = ((bf16[64,16,1152]{2,1,0:T(8,128)(2,1)}), bf16[64,16,1152]{2,1,0:T(8,128)(2,1)S(1)}, u32[]{:S(2)}, u32[]{:S(2)}) async-start(bf16[64,16,1152]{2,1,0:T(8,128)(2,1)} %bitcast_dynamic-update-slice_fusion.1), calls=%async_computation | async-start | bytes 4718592 | tf_op jit(solution)/shard_map/all_to_all | solution.py:95
  28.1 1.4 fusion.59
  29.4 1.3 and_reduce_fusion
  30.7 6.1 %fusion.91 = (bf16[64,1,128,256]{3,2,1,0:T(8,128)(2,1)}, bf16[64,1,128,256]{3,2,1,0:T(8,128)(2,1)}) fusion(bf16[64,2,128,256]{3,2,1,0:T(8,128)(2,1)} %param.22), kind=kLoop, calls=%fused_computation.161 | loop fusion | bytes 16777216 | tf_op jit(solution)/shard_map/slice | solution.py:116
  36.8 31.7 %all-to-all-done = bf16[64,16,1152]{2,1,0:T(8,128)(2,1)S(1)} async-done(((bf16[64,16,1152]{2,1,0:T(8,128)(2,1)}), bf16[64,16,1152]{2,1,0:T(8,128)(2,1)S(1)}, u32[]{:S(2)}, u32[]{:S(2)}) %all-to-all-start) | async-done | bytes 2359328 | tf_op jit(solution)/shard_map/all_to_all | solution.py:95
  68.4 1.2 compare_reduce_fusion
  69.7 0.6 select_reduce_fusion
  72.9 7.0 %fusion.94 = (f32[256]{0:T(256)S(1)}, f32[256,8192]{1,0:T(8,128)}) fusion(bf16[256,256]{1,0:T(8,128)(2,1)S(1)} %reshape.369, bf16[8192,256]{1,0:T(8,128)(2,1)} %bitcast.161, pred[8192]{0:T(1024)(128)(4,1)S(1)} %bitcast.178), kind=kOutput, calls=%fused_computation.164 | convolution fusion | flops 1080033024 | bytes 12723200 | tf_op jit(solution)/shard_map/dot_general | solution.py:121
  80.0 6.4 %fusion.19 = f32[256,256]{1,0:T(8,128)S(1)} fusion(bf16[8192,256]{1,0:T(8,128)(2,1)} %bitcast.163, f32[256,8192]{1,0:T(8,128)} %get-tuple-element.53, f32[256]{0:T(256)S(1)} %broadcast_maximum_fusion, pred[8192]{0:T(1024)(128)(4,1)S(1)} %bitcast.179), kind=kOutput, calls=%fused_computation.26 | convolution fusion | flops 1086324736 | bytes 12854272 | tf_op jit(solution)/shard_map/dot_general | solution.py:134
  86.5 0.8 copy-done.1
  87.2 1.2 copy-done.2
  88.4 1.3 fusion.26
  90.0 5.2 %fusion.2 = f32[256]{0:T(256)S(1)} fusion(f32[256,8192]{1,0:T(8,128)} %get-tuple-element.53, f32[256]{0:T(256)S(1)} %broadcast_maximum_fusion, pred[8192]{0:T(1024)(128)(4,1)S(1)} %bitcast.181), kind=kLoop, calls=%fused_computation.8 | loop fusion | flops 6291200 | bytes 8398848 | tf_op jit(solution)/shard_map/reduce_sum | solution.py:131
  95.5 0.6 fusion.74
  96.9 1.6 broadcast.161
  98.5 0.6 bitcast_dynamic-update-slice_fusion
  99.4 6.9 %all-to-all-start.1 = ((bf16[64,16,1152]{2,1,0:T(8,128)(2,1)}), bf16[64,16,1152]{2,1,0:T(8,128)(2,1)S(1)}, u32[]{:S(2)}, u32[]{:S(2)}) async-start(bf16[64,16,1152]{2,1,0:T(8,128)(2,1)} %bitcast_dynamic-update-slice_fusion), calls=%async_computation.1 | async-start | bytes 4718592 | tf_op jit(solution)/shard_map/all_to_all | solution.py:178
  106.3 3.9 %fusion.95 = (f32[256]{0:T(256)S(1)}, f32[256,8192]{1,0:T(8,128)S(1)}) fusion(bf16[256,256]{1,0:T(8,128)(2,1)S(1)} %reshape.375, bf16[8192,256]{1,0:T(8,128)(2,1)} %bitcast.162, pred[8192]{0:T(1024)(128)(4,1)S(1)} %bitcast.174), kind=kOutput, calls=%fused_computation.165 | convolution fusion | flops 1080033024 | bytes 12723200 | tf_op jit(solution)/shard_map/dot_general | solution.py:121
  110.3 3.2 %copy-done = f32[256,8192]{1,0:T(8,128)} copy-done((f32[256,8192]{1,0:T(8,128)}, f32[256,8192]{1,0:T(8,128)S(1)}, u32[]{:S(2)}) %copy-start) | copy-done | bytes 8388632
  113.5 1.7 fusion.20
  115.3 5.9 %fusion.29 = f32[256,256]{1,0:T(8,128)S(1)} fusion(f32[256,256]{1,0:T(8,128)S(1)} %fusion.20, bf16[8192,256]{1,0:T(8,128)(2,1)} %bitcast.164, f32[256,8192]{1,0:T(8,128)} %copy-done, f32[256]{0:T(256)S(1)} %max.27, pred[8192]{0:T(1024)(128)(4,1)S(1)} %bitcast.176), kind=kOutput, calls=%fused_computation.39 | convolution fusion | flops 1080098816 | bytes 13116416 | tf_op jit(solution)/shard_map/dot_general | solution.py:134
  121.5 5.3 %fusion.5 = f32[256]{0:T(256)S(1)} fusion(f32[256,8192]{1,0:T(8,128)} %copy-done, f32[256]{0:T(256)} %copy-done.9, pred[8192]{0:T(1024)(128)(4,1)S(1)} %bitcast.177), kind=kLoop, calls=%fused_computation.11 | loop fusion | flops 6291200 | bytes 8398848 | tf_op jit(solution)/shard_map/reduce_sum | solution.py:131
  126.8 0.6 fusion.72
  127.6 30.3 %all-to-all-done.1 = bf16[64,16,1152]{2,1,0:T(8,128)(2,1)S(1)} async-done(((bf16[64,16,1152]{2,1,0:T(8,128)(2,1)}), bf16[64,16,1152]{2,1,0:T(8,128)(2,1)S(1)}, u32[]{:S(2)}, u32[]{:S(2)}) %all-to-all-start.1) | async-done | bytes 2359328 | tf_op jit(solution)/shard_map/all_to_all | solution.py:178
  159.2 3.0 %fusion.97 = f32[32,2048]{1,0:T(8,128)S(1)} fusion(bf16[32,1024]{1,0:T(8,128)(2,1)S(1)} %convert_element_type.153, bf16[1024,2048]{1,0:T(8,128)(2,1)} %param.26), kind=kOutput, calls=%fused_computation.167 | convolution fusion | flops 134217728 | bytes 4521984 | tf_op jit(solution)/shard_map/dot_general | solution.py:226
  162.2 1.9 collective-permute-start
  164.2 1.2 collective-permute-done
  165.6 0.9 collective-permute-start.1
  166.6 2.5 %collective-permute-start.3 = (bf16[32,2048]{1,0:T(8,128)(2,1)S(1)}, bf16[32,2048]{1,0:T(8,128)(2,1)S(1)}, u32[]{:S(2)}, u32[]{:S(2)}) collective-permute-start(bf16[32,2048]{1,0:T(8,128)(2,1)S(1)} %fusion.37), channel_id=1, source_target_pairs={{0,6},{2,0},{4,2},{6,4},{1,7},{3,1},{5,3},{7,5},{8,14},{10,8},{12,... | collective-permute-start | bytes 393224 | tf_op jit(solution)/shard_map/ppermute | solution.py:236
  169.1 5.3 %collective-permute-done.1 = bf16[32,2048]{1,0:T(8,128)(2,1)S(1)} collective-permute-done((bf16[32,2048]{1,0:T(8,128)(2,1)S(1)}, bf16[32,2048]{1,0:T(8,128)(2,1)S(1)}, u32[]{:S(2)}, u32[]{:S(2)}) %collective-permute-start.1) | collective-permute-done | bytes 131104 | tf_op jit(solution)/shard_map/ppermute | solution.py:236
  174.7 3.4 %fusion.12 = f32[128,16,64]{0,2,1:T(8,128)S(1)} fusion(bf16[32,2048]{1,0:T(8,128)(2,1)S(1)} %collective-permute-done.3, bf16[32,2048]{1,0:T(8,128)(2,1)S(1)} %collective-permute-done.2, bf16[32,2048]{1,0:T(8,128)(2,1)S(1)} %collective-permute-done.1, bf16[32,2048]{1,0:T(8,128)(2,1)S(1)} %fusion.37, bf16[16,3,64,2048]{3,2,1,0:T(8,128)(2,1)} %bitcast.199), kind=kOutput, calls=%fused_computation.19 | convolution fusion | flops 538968064 | bytes 5242880 | tf_op jit(solution)/shard_map/dot_general | solution.py:239
  178.1 3.4 %multiply_convert_fusion = bf16[128,16,64]{0,2,1:T(8,128)(2,1)S(1)} fusion(f32[128,16,64]{0,2,1:T(8,128)S(1)} %fusion.12, bf16[32,2048]{1,0:T(8,128)(2,1)S(1)} %collective-permute-done.3, bf16[32,2048]{1,0:T(8,128)(2,1)S(1)} %collective-permute-done.2, bf16[32,2048]{1,0:T(8,128)(2,1)S(1)} %collective-permute-done.1, bf16[32,2048]{1,0:T(8,128)(2,1)S(1)} %fusion.37, ...), kind=kOutput, calls=%fused_computation.53 | convolution fusion | flops 539754496 | bytes 5505024 | tf_op jit(solution)/shard_map/dot_general | solution.py:240
  182.0 3.0 %fusion.21 = f32[4,2,16,2048]{3,2,1,0:T(8,128)S(1)} fusion(bf16[4,2,16,16,64]{4,3,2,1,0:T(8,128)(2,1)S(1)} %bitcast.168, bf16[16,3,64,2048]{3,2,1,0:T(8,128)(2,1)} %bitcast.201), kind=kOutput, calls=%fused_computation.28 | convolution fusion | flops 536870912 | bytes 5505024 | tf_op jit(solution)/shard_map/dot_general | solution.py:243
  185.1 1.6 collective-permute-start.4
  187.1 1.1 collective-permute-done.4
  188.3 2.5 %collective-permute-start.5 = (f32[16,2048]{1,0:T(8,128)S(1)}, f32[16,2048]{1,0:T(8,128)S(1)}, u32[]{:S(2)}, u32[]{:S(2)}) collective-permute-start(f32[16,2048]{1,0:T(8,128)S(1)} %get-tuple-element.35), channel_id=1, source_target_pairs={{0,6},{2,0},{4,2},{6,4},{1,7},{3,1},{5,3},{7,5},{8,14},{10,8},{12,... | collective-permute-start | bytes 393224 | tf_op jit(solution)/shard_map/ppermute | solution.py:253
  190.9 0.6 collective-permute-start.7
  191.7 0.6 reshape.383
  192.3 1.7 collective-permute-done.5
  194.0 2.8 %collective-permute-done.6 = f32[16,2048]{1,0:T(8,128)S(1)} collective-permute-done((f32[16,2048]{1,0:T(8,128)S(1)}, f32[16,2048]{1,0:T(8,128)S(1)}, u32[]{:S(2)}, u32[]{:S(2)}) %collective-permute-start.6) | collective-permute-done | bytes 131104 | tf_op jit(solution)/shard_map/ppermute | solution.py:253
  196.8 3.3 %collective-permute-done.7 = f32[16,2048]{1,0:T(8,128)S(1)} collective-permute-done((f32[16,2048]{1,0:T(8,128)S(1)}, f32[16,2048]{1,0:T(8,128)S(1)}, u32[]{:S(2)}, u32[]{:S(2)}) %collective-permute-start.7) | collective-permute-done | bytes 131104 | tf_op jit(solution)/shard_map/ppermute | solution.py:253
  200.1 2.3 %all_gather.11 = bf16[32,2048]{1,0:T(8,128)(2,1)S(1)} all-gather(bf16[16,2048]{1,0:T(8,128)(2,1)S(1)} %fusion.47), channel_id=1, replica_groups=mesh['z'=4,'x'=4,'y'=4,'mlp'=2] {'mlp'}, dimensions={0}, use_global_device_ids=true | all-gather | bytes 196608 | tf_op jit(solution)/shard_map/all_gather | solution.py:256
  202.5 4.7 %convolution_convert_fusion = bf16[32,1536]{1,0:T(8,128)(2,1)} fusion(bf16[2048,1536]{1,0:T(8,128)(2,1)} %param.31, bf16[32,2048]{1,0:T(8,128)(2,1)S(1)} %all_gather.11, f32[2048]{0:T(1024)S(1)} %convert_element_type.162, f32[32]{0:T(128)S(1)} %add_rsqrt_fusion), kind=kOutput, calls=%fused_computation.29 | convolution fusion | flops 201637888 | bytes 6529152 | tf_op jit(solution)/shard_map/dot_general | solution.py:258
  207.2 0.7 copy.169
  (122 shorter events, 9.1 us)
Async XLA Ops:
  7.2 19.0 %copy-start.5 = (bf16[32,1024]{1,0:T(8,128)(2,1)S(1)}, bf16[32,1024]{1,0:T(8,128)(2,1)}, u32[]{:S(2)}) copy-start(bf16[32,1024]{1,0:T(8,128)(2,1)} %param.17) | copy-start | bytes 196612
  7.2 17.9 %copy-start.4 = (bf16[32,2,256]{2,1,0:T(2,128)(2,1)S(1)}, bf16[32,2,256]{2,1,0:T(2,128)(2,1)}, u32[]{:S(2)}) copy-start(bf16[32,2,256]{2,1,0:T(2,128)(2,1)} %param.18) | copy-start | bytes 98308
  7.2 18.0 %copy-start.13 = (s32[2]{0:T(128)S(1)}, s32[2]{0:T(128)}, u32[]{:S(2)}) copy-start(s32[2]{0:T(128)} %param.20) | copy-start | bytes 28
  7.2 18.1 %copy-start.12 = (s32[2,16]{1,0:T(2,128)S(1)}, s32[2,16]{1,0:T(2,128)}, u32[]{:S(2)}) copy-start(s32[2,16]{1,0:T(2,128)} %param.19) | copy-start | bytes 388
  7.2 19.5 %copy-start.10 = (s32[2]{0:T(128)S(1)}, s32[2]{0:T(128)}, u32[]{:S(2)}) copy-start(s32[2]{0:T(128)} %param.24) | copy-start | bytes 28
  7.2 20.7 %copy-start.11 = (s32[2,48]{1,0:T(2,128)S(1)}, s32[2,48]{1,0:T(2,128)}, u32[]{:S(2)}) copy-start(s32[2,48]{1,0:T(2,128)} %param.23) | copy-start | bytes 1156
  7.2 151.1 %all-gather.3.cloned.1.call-start = ((), (), s32[]{:S(2)}) async-start(), calls=%async_computation.2 | async-start | bytes 13369344 | tf_op jit(solution)/shard_map/all_gather | solution.py:97
  13.1 55.3 %all-to-all-start = ((bf16[64,16,1152]{2,1,0:T(8,128)(2,1)}), bf16[64,16,1152]{2,1,0:T(8,128)(2,1)S(1)}, u32[]{:S(2)}, u32[]{:S(2)}) async-start(bf16[64,16,1152]{2,1,0:T(8,128)(2,1)} %bitcast_dynamic-update-slice_fusion.1), calls=%async_computation | async-start | bytes 4718592 | tf_op jit(solution)/shard_map/all_to_all | solution.py:95
  80.0 7.2 %copy-start.1 = (f32[256,8192]{1,0:T(8,128)S(1)}, f32[256,8192]{1,0:T(8,128)}, u32[]{:S(2)}) copy-start(f32[256,8192]{1,0:T(8,128)} %get-tuple-element.53) | copy-start | bytes 25165828
  80.0 8.4 %copy-start.2 = (bf16[64,1,128,256]{3,2,1,0:T(8,128)(2,1)S(1)}, bf16[64,1,128,256]{3,2,1,0:T(8,128)(2,1)}, u32[]{:S(2)}) copy-start(bf16[64,1,128,256]{3,2,1,0:T(8,128)(2,1)} %get-tuple-element.33) | copy-start | bytes 12582916
  99.4 58.5 %all-to-all-start.1 = ((bf16[64,16,1152]{2,1,0:T(8,128)(2,1)}), bf16[64,16,1152]{2,1,0:T(8,128)(2,1)S(1)}, u32[]{:S(2)}, u32[]{:S(2)}) async-start(bf16[64,16,1152]{2,1,0:T(8,128)(2,1)} %bitcast_dynamic-update-slice_fusion), calls=%async_computation.1 | async-start | bytes 4718592 | tf_op jit(solution)/shard_map/all_to_all | solution.py:178
  106.3 7.1 %copy-start.3 = (bf16[64,1,128,256]{3,2,1,0:T(8,128)(2,1)S(1)}, bf16[64,1,128,256]{3,2,1,0:T(8,128)(2,1)}, u32[]{:S(2)}) copy-start(bf16[64,1,128,256]{3,2,1,0:T(8,128)(2,1)} %get-tuple-element.33) | copy-start | bytes 12582916
  110.3 3.2 %copy-start = (f32[256,8192]{1,0:T(8,128)}, f32[256,8192]{1,0:T(8,128)S(1)}, u32[]{:S(2)}) copy-start(f32[256,8192]{1,0:T(8,128)S(1)} %get-tuple-element.55) | copy-start | bytes 25165828
  110.3 5.0 %copy-start.9 = (f32[256]{0:T(256)}, f32[256]{0:T(256)S(1)}, u32[]{:S(2)}) copy-start(f32[256]{0:T(256)S(1)} %max.27) | copy-start | bytes 3076
  121.4 42.8 %copy-start.7 = (bf16[2048]{0:T(1024)(128)(2,1)S(1)}, bf16[2048]{0:T(1024)(128)(2,1)}, u32[]{:S(2)}) copy-start(bf16[2048]{0:T(1024)(128)(2,1)} %param.27) | copy-start | bytes 12292
  121.4 43.9 %copy-start.6 = (bf16[32,2048]{1,0:T(8,128)(2,1)S(1)}, bf16[32,2048]{1,0:T(8,128)(2,1)}, u32[]{:S(2)}) copy-start(bf16[32,2048]{1,0:T(8,128)(2,1)} %param.16) | copy-start | bytes 393220
  121.4 47.6 %copy-start.8 = (bf16[2048]{0:T(1024)(128)(2,1)S(1)}, bf16[2048]{0:T(1024)(128)(2,1)}, u32[]{:S(2)}) copy-start(bf16[2048]{0:T(1024)(128)(2,1)} %param.30) | copy-start | bytes 12292
  162.2 3.1 %collective-permute-start = (f32[32,2048]{1,0:T(8,128)S(1)}, f32[32,2048]{1,0:T(8,128)S(1)}, u32[]{:S(2)}, u32[]{:S(2)}) collective-permute-start(f32[32,2048]{1,0:T(8,128)S(1)} %fusion.97), channel_id=1, source_target_pairs={{0,1},{1,0},{2,3},{3,2},{4,5},{5,4},{6,7},{7,6},{8,9},{9,8},{10,11... | collective-permute-start | bytes 786440 | tf_op jit(solution)/shard_map/ppermute | solution.py:227
  165.6 8.8 %collective-permute-start.1 = (bf16[32,2048]{1,0:T(8,128)(2,1)S(1)}, bf16[32,2048]{1,0:T(8,128)(2,1)S(1)}, u32[]{:S(2)}, u32[]{:S(2)}) collective-permute-start(bf16[32,2048]{1,0:T(8,128)(2,1)S(1)} %fusion.37), channel_id=1, source_target_pairs={{0,2},{2,4},{4,6},{6,0},{1,3},{3,5},{5,7},{7,1},{8,10},{10,12},{12... | collective-permute-start | bytes 393224 | tf_op jit(solution)/shard_map/ppermute | solution.py:236
  166.6 7.9 %collective-permute-start.2 = (bf16[32,2048]{1,0:T(8,128)(2,1)S(1)}, bf16[32,2048]{1,0:T(8,128)(2,1)S(1)}, u32[]{:S(2)}, u32[]{:S(2)}) collective-permute-start(bf16[32,2048]{1,0:T(8,128)(2,1)S(1)} %fusion.37), channel_id=1, source_target_pairs={{0,4},{2,6},{4,0},{6,2},{1,5},{3,7},{5,1},{7,3},{8,12},{10,14},{12... | collective-permute-start | bytes 393224 | tf_op jit(solution)/shard_map/ppermute | solution.py:236
  166.6 8.1 %collective-permute-start.3 = (bf16[32,2048]{1,0:T(8,128)(2,1)S(1)}, bf16[32,2048]{1,0:T(8,128)(2,1)S(1)}, u32[]{:S(2)}, u32[]{:S(2)}) collective-permute-start(bf16[32,2048]{1,0:T(8,128)(2,1)S(1)} %fusion.37), channel_id=1, source_target_pairs={{0,6},{2,0},{4,2},{6,4},{1,7},{3,1},{5,3},{7,5},{8,14},{10,8},{12,... | collective-permute-start | bytes 393224 | tf_op jit(solution)/shard_map/ppermute | solution.py:236
  182.0 4.7 %copy-start.14 = (s32[2]{0:T(128)S(1)}, s32[2]{0:T(128)}, u32[]{:S(2)}) copy-start(s32[2]{0:T(128)} %param.21) | copy-start | bytes 28
  185.1 3.1 %collective-permute-start.4 = (f32[4,16,2048]{2,1,0:T(8,128)S(1)}, f32[4,16,2048]{2,1,0:T(8,128)S(1)}, u32[]{:S(2)}, u32[]{:S(2)}) collective-permute-start(f32[4,16,2048]{2,1,0:T(8,128)S(1)} %dynamic-slice_bitcast_fusion), channel_id=1, source_target_pairs={{0,1},{1,0},{2,3},{3,2},{4,5},{5,4},{6,7},{7,6},{8,9},{9,8},{10,11... | collective-permute-start | bytes 1572872 | tf_op jit(solution)/shard_map/ppermute | solution.py:249
  188.3 5.7 %collective-permute-start.5 = (f32[16,2048]{1,0:T(8,128)S(1)}, f32[16,2048]{1,0:T(8,128)S(1)}, u32[]{:S(2)}, u32[]{:S(2)}) collective-permute-start(f32[16,2048]{1,0:T(8,128)S(1)} %get-tuple-element.35), channel_id=1, source_target_pairs={{0,6},{2,0},{4,2},{6,4},{1,7},{3,1},{5,3},{7,5},{8,14},{10,8},{12,... | collective-permute-start | bytes 393224 | tf_op jit(solution)/shard_map/ppermute | solution.py:253
  190.8 6.0 %collective-permute-start.6 = (f32[16,2048]{1,0:T(8,128)S(1)}, f32[16,2048]{1,0:T(8,128)S(1)}, u32[]{:S(2)}, u32[]{:S(2)}) collective-permute-start(f32[16,2048]{1,0:T(8,128)S(1)} %get-tuple-element.37), channel_id=1, source_target_pairs={{0,4},{2,6},{4,0},{6,2},{1,5},{3,7},{5,1},{7,3},{8,12},{10,14},{12... | collective-permute-start | bytes 393224 | tf_op jit(solution)/shard_map/ppermute | solution.py:253
  190.9 9.2 %collective-permute-start.7 = (f32[16,2048]{1,0:T(8,128)S(1)}, f32[16,2048]{1,0:T(8,128)S(1)}, u32[]{:S(2)}, u32[]{:S(2)}) collective-permute-start(f32[16,2048]{1,0:T(8,128)S(1)} %get-tuple-element.36), channel_id=1, source_target_pairs={{0,2},{2,4},{4,6},{6,0},{1,3},{3,5},{5,7},{7,1},{8,10},{10,12},{12... | collective-permute-start | bytes 393224 | tf_op jit(solution)/shard_map/ppermute | solution.py:253
Sparse Core Ops, SparseCore 0:
  10.2 144.1 all-gather.2

commit v10 on v9

--- a/solution.py
+++ b/solution.py
@@ -14,6 +14,21 @@
 
 norm_eps = 1e-05
 masked_score = -1e30
+
+
+def route(packet, dest, mark):
+    plane = lax.axis_size("x") * lax.axis_size("y")
+    first = jnp.zeros((lax.axis_size("z"),) + packet.shape, packet.dtype)
+    first = lax.dynamic_update_index_in_dim(first, packet, dest // plane, 0)
+    middle = lax.all_to_all(first, "z", 0, 0, tiled=True)
+    real = middle[:, 0, mark] > 0.5
+    target = middle[:, 0, mark + 1].astype(jnp.int32) % plane
+    spots = jnp.arange(plane, dtype=jnp.int32)
+    pick = (target[None, :] == spots[:, None]) & real[None, :]
+    second = jnp.sum(jnp.where(pick[:, :, None, None], middle[None], 0), axis=1)
+    second = second.astype(packet.dtype)
+    arrived = lax.all_to_all(second, ("x", "y"), 0, 0, tiled=True)
+    return jnp.sum(arrived.astype(jnp.float32), axis=0).astype(packet.dtype)
 
 
 def split_hi_lo(values):
@@ -87,12 +102,10 @@
     queries = q_in.reshape(2, tree_len, kv_local, GROUP, HEAD_DIM)
     device_id = lax.axis_index(REQ)
     q_width = q_in.shape[1]
-    owners = lax.axis_size(REQ)
-    marker = jnp.ones((tree_len, TAG), q_in.dtype)
-    q_packet = jnp.concatenate([q_in[tree_len:], marker], axis=1)
-    q_send = jnp.zeros((owners,) + q_packet.shape, q_packet.dtype)
-    q_send = lax.dynamic_update_index_in_dim(q_send, q_packet, prev_owner[0], 0)
-    every_query = lax.all_to_all(q_send, REQ, 0, 0, tiled=True)
+    q_tags = jnp.zeros((tree_len, TAG), jnp.float32)
+    q_tags = q_tags.at[:, 0].set(1.0).at[:, 1].set(prev_owner[0]).at[:, 2].set(device_id)
+    q_packet = jnp.concatenate([q_in[tree_len:], q_tags.astype(q_in.dtype)], axis=1)
+    every_query = route(q_packet, prev_owner[0], q_width)
     own_w = jnp.stack([w_in[0], w_in[1], w_down])
     all_w = lax.all_gather(own_w, ("z", "x"), axis=0, tiled=False)
     page_len = cache.shape[2]
@@ -155,10 +168,8 @@
     )
     own_queries = queries[0]
     own_state = start_state
-    marks = every_query[:, 0, q_width]
-    senders = jnp.arange(marks.shape[0], dtype=jnp.int32)
-    sender = jnp.sum(jnp.where(marks > 0.5, senders, 0))
-    foreign = lax.dynamic_index_in_dim(every_query, sender, 0, keepdims=False)[:, :q_width]
+    sender = every_query[0, q_width + 2].astype(jnp.int32)
+    foreign = every_query[:, :q_width]
     foreign = foreign.reshape(tree_len, kv_local, GROUP, HEAD_DIM)
     f_running, f_total, f_accum = attend(1, foreign, 0, num_blocks, start_state)
     f_out = f_accum / f_total[..., None]
@@ -170,16 +181,16 @@
     stats = jnp.concatenate(
         [split_hi_lo(sent_max), split_hi_lo(sent_total)], axis=1
     )
-    pad = jnp.zeros((tree_len, TAG - stats.shape[1]), jnp.bfloat16)
-    r_packet = jnp.concatenate([sent_out.astype(jnp.bfloat16), stats, pad], axis=1)
-    r_send = jnp.zeros((owners,) + r_packet.shape, r_packet.dtype)
-    r_send = lax.dynamic_update_index_in_dim(r_send, r_packet, sender, 0)
-    r_send, own_state = lax.optimization_barrier((r_send, own_state))
-    back = lax.all_to_all(r_send, REQ, 0, 0, tiled=True)
+    r_tags = jnp.zeros((tree_len, TAG - stats.shape[1]), jnp.float32)
+    r_tags = r_tags.at[:, 0].set(1.0).at[:, 1].set(sender)
+    r_packet = jnp.concatenate(
+        [sent_out.astype(jnp.bfloat16), stats, r_tags.astype(jnp.bfloat16)], axis=1
+    )
+    r_packet, own_state = lax.optimization_barrier((r_packet, own_state))
+    got = route(r_packet, sender, sent_out.shape[1] + stats.shape[1]).astype(jnp.float32)
     running, total, accum = attend(0, own_queries, 0, num_blocks, own_state)
     all_w, running, total, accum = lax.optimization_barrier((all_w, running, total, accum))
     cache_out = accum / total[..., None]
-    got = lax.dynamic_index_in_dim(back, prev_owner[0], 0, keepdims=False).astype(jnp.float32)
     heads = kv_local * GROUP
     o_w = heads * HEAD_DIM
     recv_out = got[:, :o_w].reshape(tree_len, kv_local, GROUP, HEAD_DIM)

time: 215 us -> 168 us (0.78)
  waiting for transfers between devices: 77.7 us -> 28.4 us
  matrix products: 47.2 us -> 43.7 us
  other arithmetic: 19.1 us -> 22.2 us
  starting transfers between devices: 29 us -> 31.3 us
    all_to_all x2 -> x4, waiting for transfers between devices: 62 us -> 12.3 us  [the longest x2 12.3 us: route(): arrived = lax.all_to_all(second, ('x', 'y'), 0, 0, tiled=True)]
    dot_general x2, matrix products: 7.19 us -> 2.78 us  [attend(): jnp.dot(high, value_rows, preferred_element_type=jnp.float32)]
    reduce_sum x2, other arithmetic: 10.4 us -> 7.12 us  [attend(): total = total.reshape(rows) * factor + jnp.sum(weights, axis=-1)]
    another operation x0 -> x5, other arithmetic: none -> 3.28 us
    unnamed x31 -> x17, local copies, waits for them, and re-layouts: 5.86 us -> 2.65 us
    all_to_all x2 -> x4, starting transfers between devices: 18.9 us -> 20.3 us  [the longest x2 10.9 us: route(): arrived = lax.all_to_all(second, ('x', 'y'), 0, 0, tiled=True)]
  transfers between devices with their start and end apart: 11 -> 13, of which waited for: 9 -> 9; matrix products, arithmetic and copies ran while one was open for 28% -> 37% of each run, Pallas kernels for 0% -> 0%
where the time goes in v10:
time: 168 us; the launch traced here: 167 us
  matrix products  43.7 us (26%)
  starting transfers between devices  31.3 us (19%)
  waiting for transfers between devices  28.4 us (17%)
  other arithmetic  22.2 us (13%)
  local copies, waits for them, and re-layouts  20.8 us (12%)
  between operations  18.6 us (11%)
  blocking collectives  2.34 us (1%)
    all_to_all x2, waiting for transfers between devices, route(): arrived = lax.all_to_all(second, ('x', 'y'), 0, 0, tiled=True)  12.3 us
    all_to_all x2, starting transfers between devices, route(): arrived = lax.all_to_all(second, ('x', 'y'), 0, 0, tiled=True)  10.9 us
    dot_general x2, matrix products, attend(): lax.dot_general(spread, key_rows, (((1,), (1,)), ((), ())), preferred_ele...  10.7 us
    all_to_all x2, starting transfers between devices, route(): middle = lax.all_to_all(first, 'z', 0, 0, tiled=True)  9.41 us
    dot_general x2, matrix products, attend(): jnp.dot(low, value_rows, preferred_element_type=jnp.float32)  8.52 us
    ppermute x3, waiting for transfers between devices, per_device(): mlp_half = mlp_half + lax.ppermute(mine[shift], 'y', perm)  7.64 us
    reduce_sum x2, other arithmetic, attend(): total = total.reshape(rows) * factor + jnp.sum(weights, axis=-1)  7.12 us
    ppermute x3, waiting for transfers between devices, per_device(): shifted.append(lax.ppermute(normed, 'y', perm))  6.14 us
  transfers between devices with their start and end apart: 13, of which 9 were waited for; matrix products, arithmetic and copies ran while one was open for 37% of the time, Pallas kernels for 0%

profile of v10, /device:TPU:1, one launch (start us, length us, event | category | flops | bytes accessed | tf_op | source)
XLA Modules:
  0.0 167.3 jit_solution(3512064763320856056)
XLA Ops:
  7.2 2.1 %pad_maximum_fusion = bf16[3,64,2048]{2,1,0:T(8,128)(2,1)} fusion(bf16[1,64,2048]{2,1,0:T(8,128)(2,1)} %bitcast.174, bf16[2,64,2048]{2,1,0:T(8,128)(2,1)} %param.38), kind=kLoop, calls=%fused_computation.50 | loop fusion | flops 393216 | bytes 1572864 | tf_op jit(solution)/shard_map/stack | solution.py:109
  13.4 0.7 slice_select_fusion
  14.3 0.8 fusion.99
  16.3 5.9 %all-to-all-start = ((bf16[4,16,1152]{2,1,0:T(8,128)(2,1)}), bf16[4,16,1152]{2,1,0:T(8,128)(2,1)S(1)}, u32[]{:S(2)}, u32[]{:S(2)}) async-start(bf16[4,16,1152]{2,1,0:T(8,128)(2,1)} %fusion.56), calls=%async_computation | async-start | bytes 294912 | tf_op jit(solution)/shard_map/all_to_all | solution.py:23
  22.2 1.0 reshape.605
  23.2 0.7 iota_compare_fusion.8
  24.0 1.0 convolution_minimum_fusion.4
  25.6 1.0 slice_reduce_fusion
  26.7 1.3 fusion.100
  28.6 0.8 slice_bitcast_fusion.15
  29.5 1.4 fusion.60
  30.9 1.3 and_reduce_fusion
  32.6 1.3 select_reduce_fusion.1
  33.9 6.8 %all-to-all-start.1 = ((bf16[16,16,1152]{2,1,0:T(8,128)(2,1)}), bf16[16,16,1152]{2,1,0:T(8,128)(2,1)S(1)}, u32[]{:S(2)}, u32[]{:S(2)}) async-start(bf16[16,16,1152]{2,1,0:T(8,128)(2,1)} %select_reduce_fusion.1), calls=%async_computation.1 | async-start | bytes 1179648 | tf_op jit(solution)/shard_map/all_to_all | solution.py:30
  42.2 6.0 %fusion.98 = (bf16[64,1,128,256]{3,2,1,0:T(8,128)(2,1)}, bf16[64,1,128,256]{3,2,1,0:T(8,128)(2,1)}) fusion(bf16[64,2,128,256]{3,2,1,0:T(8,128)(2,1)} %param.32), kind=kLoop, calls=%fused_computation.186 | loop fusion | bytes 16777216 | tf_op jit(solution)/shard_map/slice | solution.py:129
  48.2 3.4 %all-to-all-done.1 = bf16[16,16,1152]{2,1,0:T(8,128)(2,1)S(1)} async-done(((bf16[16,16,1152]{2,1,0:T(8,128)(2,1)}), bf16[16,16,1152]{2,1,0:T(8,128)(2,1)S(1)}, u32[]{:S(2)}, u32[]{:S(2)}) %all-to-all-start.1) | async-done | bytes 589856 | tf_op jit(solution)/shard_map/all_to_all | solution.py:30
  53.7 6.8 %fusion.101 = (f32[256]{0:T(256)S(1)}, f32[256,8192]{1,0:T(8,128)}) fusion(bf16[256,256]{1,0:T(8,128)(2,1)S(1)} %reshape.592, bf16[8192,256]{1,0:T(8,128)(2,1)} %bitcast.164, pred[8192]{0:T(1024)(128)(4,1)S(1)} %bitcast.181), kind=kOutput, calls=%fused_computation.189 | convolution fusion | flops 1080033024 | bytes 12723200 | tf_op jit(solution)/shard_map/dot_general | solution.py:134
  60.6 5.3 %fusion.2 = f32[256]{0:T(256)S(1)} fusion(f32[256,8192]{1,0:T(8,128)} %get-tuple-element.113, f32[256]{0:T(256)S(1)} %broadcast_maximum_fusion, pred[8192]{0:T(1024)(128)(4,1)S(1)} %bitcast.182), kind=kLoop, calls=%fused_computation.8 | loop fusion | flops 6291200 | bytes 8398848 | tf_op jit(solution)/shard_map/reduce_sum | solution.py:144
  66.2 6.7 %fusion.19 = f32[256,256]{1,0:T(8,128)S(1)} fusion(bf16[8192,256]{1,0:T(8,128)(2,1)} %bitcast.166, f32[256,8192]{1,0:T(8,128)} %get-tuple-element.113, f32[256]{0:T(256)S(1)} %broadcast_maximum_fusion, pred[8192]{0:T(1024)(128)(4,1)S(1)} %bitcast.183), kind=kOutput, calls=%fused_computation.26 | convolution fusion | flops 1086324736 | bytes 12854272 | tf_op jit(solution)/shard_map/dot_general | solution.py:147
  72.9 0.8 copy-done
  73.7 1.2 copy-done.1
  74.8 1.3 fusion.26
  78.9 0.7 broadcast.395
  80.2 3.6 %all-to-all-start.2 = ((bf16[4,16,1152]{2,1,0:T(8,128)(2,1)}), bf16[4,16,1152]{2,1,0:T(8,128)(2,1)S(1)}, u32[]{:S(2)}, u32[]{:S(2)}) async-start(bf16[4,16,1152]{2,1,0:T(8,128)(2,1)} %bitcast_dynamic-update-slice_fusion), calls=%async_computation.2 | async-start | bytes 294912 | tf_op jit(solution)/shard_map/all_to_all | solution.py:23
  83.8 3.9 %fusion.102 = (f32[256]{0:T(256)S(1)}, f32[256,8192]{1,0:T(8,128)S(1)}) fusion(bf16[256,256]{1,0:T(8,128)(2,1)S(1)} %reshape.599, bf16[8192,256]{1,0:T(8,128)(2,1)} %bitcast.165, pred[8192]{0:T(1024)(128)(4,1)S(1)} %bitcast.177), kind=kOutput, calls=%fused_computation.190 | convolution fusion | flops 1080033024 | bytes 12723200 | tf_op jit(solution)/shard_map/dot_general | solution.py:134
  87.8 1.9 %fusion.20 = f32[256,256]{1,0:T(8,128)S(1)} fusion(bf16[8192,256]{1,0:T(8,128)(2,1)S(1)} %bitcast.168, f32[256,8192]{1,0:T(8,128)S(1)} %get-tuple-element.115, f32[256]{0:T(256)S(1)} %max.27, pred[8192]{0:T(1024)(128)(4,1)S(1)} %bitcast.178), kind=kOutput, calls=%fused_computation.27 | convolution fusion | flops 1086324736 | bytes 12854272 | tf_op jit(solution)/shard_map/dot_general | solution.py:147
  89.6 1.5 fusion.29
  91.1 1.8 %fusion.5 = f32[256]{0:T(256)S(1)} fusion(f32[256,8192]{1,0:T(8,128)S(1)} %get-tuple-element.115, f32[256]{0:T(256)S(1)} %max.27, pred[8192]{0:T(1024)(128)(4,1)S(1)} %bitcast.180), kind=kLoop, calls=%fused_computation.11 | loop fusion | flops 6291200 | bytes 8398848 | tf_op jit(solution)/shard_map/reduce_sum | solution.py:144
  93.7 1.3 select_reduce_fusion
  95.0 4.2 %all-to-all-start.3 = ((bf16[16,16,1152]{2,1,0:T(8,128)(2,1)}), bf16[16,16,1152]{2,1,0:T(8,128)(2,1)S(1)}, u32[]{:S(2)}, u32[]{:S(2)}) async-start(bf16[16,16,1152]{2,1,0:T(8,128)(2,1)} %select_reduce_fusion), calls=%async_computation.3 | async-start | bytes 1179648 | tf_op jit(solution)/shard_map/all_to_all | solution.py:30
  100.2 8.9 %all-to-all-done.3 = bf16[16,16,1152]{2,1,0:T(8,128)(2,1)S(1)} async-done(((bf16[16,16,1152]{2,1,0:T(8,128)(2,1)}), bf16[16,16,1152]{2,1,0:T(8,128)(2,1)S(1)}, u32[]{:S(2)}, u32[]{:S(2)}) %all-to-all-start.3) | async-done | bytes 589856 | tf_op jit(solution)/shard_map/all_to_all | solution.py:30
  110.5 3.0 %fusion.104 = f32[32,2048]{1,0:T(8,128)S(1)} fusion(bf16[32,1024]{1,0:T(8,128)(2,1)S(1)} %convert_element_type.212, bf16[1024,2048]{1,0:T(8,128)(2,1)} %param.36), kind=kOutput, calls=%fused_computation.192 | convolution fusion | flops 134217728 | bytes 4521984 | tf_op jit(solution)/shard_map/dot_general | solution.py:237
  113.5 3.4 %collective-permute-start = (f32[32,2048]{1,0:T(8,128)S(1)}, f32[32,2048]{1,0:T(8,128)S(1)}, u32[]{:S(2)}, u32[]{:S(2)}) collective-permute-start(f32[32,2048]{1,0:T(8,128)S(1)} %fusion.104), channel_id=1, source_target_pairs={{0,1},{1,0},{2,3},{3,2},{4,5},{5,4},{6,7},{7,6},{8,9},{9,8},{10,11... | collective-permute-start | bytes 786440 | tf_op jit(solution)/shard_map/ppermute | solution.py:238
  116.9 1.2 collective-permute-done
  118.7 1.2 collective-permute-start.2
  119.9 1.4 collective-permute-start.3
  121.4 5.8 %collective-permute-done.1 = bf16[32,2048]{1,0:T(8,128)(2,1)S(1)} collective-permute-done((bf16[32,2048]{1,0:T(8,128)(2,1)S(1)}, bf16[32,2048]{1,0:T(8,128)(2,1)S(1)}, u32[]{:S(2)}, u32[]{:S(2)}) %collective-permute-start.1) | collective-permute-done | bytes 131104 | tf_op jit(solution)/shard_map/ppermute | solution.py:247
  127.5 3.4 %fusion.12 = f32[128,16,64]{0,2,1:T(8,128)S(1)} fusion(bf16[32,2048]{1,0:T(8,128)(2,1)S(1)} %collective-permute-done.3, bf16[32,2048]{1,0:T(8,128)(2,1)S(1)} %collective-permute-done.2, bf16[32,2048]{1,0:T(8,128)(2,1)S(1)} %collective-permute-done.1, bf16[32,2048]{1,0:T(8,128)(2,1)S(1)} %fusion.37, bf16[16,3,64,2048]{3,2,1,0:T(8,128)(2,1)} %bitcast.202), kind=kOutput, calls=%fused_computation.19 | convolution fusion | flops 538968064 | bytes 5242880 | tf_op jit(solution)/shard_map/dot_general | solution.py:250
  131.0 3.5 %multiply_convert_fusion = bf16[128,16,64]{0,2,1:T(8,128)(2,1)S(1)} fusion(f32[128,16,64]{0,2,1:T(8,128)S(1)} %fusion.12, bf16[32,2048]{1,0:T(8,128)(2,1)S(1)} %collective-permute-done.3, bf16[32,2048]{1,0:T(8,128)(2,1)S(1)} %collective-permute-done.2, bf16[32,2048]{1,0:T(8,128)(2,1)S(1)} %collective-permute-done.1, bf16[32,2048]{1,0:T(8,128)(2,1)S(1)} %fusion.37, ...), kind=kOutput, calls=%fused_computation.55 | convolution fusion | flops 539754496 | bytes 5505024 | tf_op jit(solution)/shard_map/dot_general | solution.py:251
  134.9 3.0 %fusion.21 = f32[4,2,16,2048]{3,2,1,0:T(8,128)S(1)} fusion(bf16[4,2,16,16,64]{4,3,2,1,0:T(8,128)(2,1)S(1)} %bitcast.171, bf16[16,3,64,2048]{3,2,1,0:T(8,128)(2,1)} %bitcast.204), kind=kOutput, calls=%fused_computation.28 | convolution fusion | flops 536870912 | bytes 5505024 | tf_op jit(solution)/shard_map/dot_general | solution.py:254
  137.9 1.6 collective-permute-start.4
  139.9 1.1 collective-permute-done.4
  141.1 2.3 %collective-permute-start.5 = (f32[16,2048]{1,0:T(8,128)S(1)}, f32[16,2048]{1,0:T(8,128)S(1)}, u32[]{:S(2)}, u32[]{:S(2)}) collective-permute-start(f32[16,2048]{1,0:T(8,128)S(1)} %get-tuple-element.95), channel_id=1, source_target_pairs={{0,6},{2,0},{4,2},{6,4},{1,7},{3,1},{5,3},{7,5},{8,14},{10,8},{12,... | collective-permute-start | bytes 393224 | tf_op jit(solution)/shard_map/ppermute | solution.py:264
  145.0 1.6 collective-permute-done.5
  146.5 2.9 %collective-permute-done.6 = f32[16,2048]{1,0:T(8,128)S(1)} collective-permute-done((f32[16,2048]{1,0:T(8,128)S(1)}, f32[16,2048]{1,0:T(8,128)S(1)}, u32[]{:S(2)}, u32[]{:S(2)}) %collective-permute-start.6) | collective-permute-done | bytes 131104 | tf_op jit(solution)/shard_map/ppermute | solution.py:264
  149.4 3.2 %collective-permute-done.7 = f32[16,2048]{1,0:T(8,128)S(1)} collective-permute-done((f32[16,2048]{1,0:T(8,128)S(1)}, f32[16,2048]{1,0:T(8,128)S(1)}, u32[]{:S(2)}, u32[]{:S(2)}) %collective-permute-start.7) | collective-permute-done | bytes 131104 | tf_op jit(solution)/shard_map/ppermute | solution.py:264
  152.6 2.3 %all_gather.11 = bf16[32,2048]{1,0:T(8,128)(2,1)S(1)} all-gather(bf16[16,2048]{1,0:T(8,128)(2,1)S(1)} %fusion.47), channel_id=1, replica_groups=mesh['z'=4,'x'=4,'y'=4,'mlp'=2] {'mlp'}, dimensions={0}, use_global_device_ids=true | all-gather | bytes 196608 | tf_op jit(solution)/shard_map/all_gather | solution.py:267
  155.1 4.7 %convolution_convert_fusion = bf16[32,1536]{1,0:T(8,128)(2,1)} fusion(bf16[2048,1536]{1,0:T(8,128)(2,1)} %param.41, bf16[32,2048]{1,0:T(8,128)(2,1)S(1)} %all_gather.11, f32[2048]{0:T(1024)S(1)} %convert_element_type.221, f32[32]{0:T(128)S(1)} %add_rsqrt_fusion), kind=kOutput, calls=%fused_computation.31 | convolution fusion | flops 201637888 | bytes 6529152 | tf_op jit(solution)/shard_map/dot_general | solution.py:269
  (135 shorter events, 18.0 us)
Async XLA Ops:
  7.2 102.5 %all-gather.3.cloned.1.call-start = ((), (), s32[]{:S(2)}) async-start(), calls=%async_computation.4 | async-start | bytes 13369344 | tf_op jit(solution)/shard_map/all_gather | solution.py:110
  16.3 15.8 %all-to-all-start = ((bf16[4,16,1152]{2,1,0:T(8,128)(2,1)}), bf16[4,16,1152]{2,1,0:T(8,128)(2,1)S(1)}, u32[]{:S(2)}, u32[]{:S(2)}) async-start(bf16[4,16,1152]{2,1,0:T(8,128)(2,1)} %fusion.56), calls=%async_computation | async-start | bytes 294912 | tf_op jit(solution)/shard_map/all_to_all | solution.py:23
  33.9 17.7 %all-to-all-start.1 = ((bf16[16,16,1152]{2,1,0:T(8,128)(2,1)}), bf16[16,16,1152]{2,1,0:T(8,128)(2,1)S(1)}, u32[]{:S(2)}, u32[]{:S(2)}) async-start(bf16[16,16,1152]{2,1,0:T(8,128)(2,1)} %select_reduce_fusion.1), calls=%async_computation.1 | async-start | bytes 1179648 | tf_op jit(solution)/shard_map/all_to_all | solution.py:30
  66.2 7.4 %copy-start = (f32[256,8192]{1,0:T(8,128)S(1)}, f32[256,8192]{1,0:T(8,128)}, u32[]{:S(2)}) copy-start(f32[256,8192]{1,0:T(8,128)} %get-tuple-element.113) | copy-start | bytes 25165828
  66.2 8.6 %copy-start.1 = (bf16[64,1,128,256]{3,2,1,0:T(8,128)(2,1)S(1)}, bf16[64,1,128,256]{3,2,1,0:T(8,128)(2,1)}, u32[]{:S(2)}) copy-start(bf16[64,1,128,256]{3,2,1,0:T(8,128)(2,1)} %get-tuple-element.93) | copy-start | bytes 12582916
  80.2 12.9 %all-to-all-start.2 = ((bf16[4,16,1152]{2,1,0:T(8,128)(2,1)}), bf16[4,16,1152]{2,1,0:T(8,128)(2,1)S(1)}, u32[]{:S(2)}, u32[]{:S(2)}) async-start(bf16[4,16,1152]{2,1,0:T(8,128)(2,1)} %bitcast_dynamic-update-slice_fusion), calls=%async_computation.2 | async-start | bytes 294912 | tf_op jit(solution)/shard_map/all_to_all | solution.py:23
  83.8 4.0 %copy-start.2 = (bf16[64,1,128,256]{3,2,1,0:T(8,128)(2,1)S(1)}, bf16[64,1,128,256]{3,2,1,0:T(8,128)(2,1)}, u32[]{:S(2)}) copy-start(bf16[64,1,128,256]{3,2,1,0:T(8,128)(2,1)} %get-tuple-element.93) | copy-start | bytes 12582916
  92.9 24.0 %copy-start.5 = (bf16[2048]{0:T(1024)(128)(2,1)S(1)}, bf16[2048]{0:T(1024)(128)(2,1)}, u32[]{:S(2)}) copy-start(bf16[2048]{0:T(1024)(128)(2,1)} %param.37) | copy-start | bytes 12292
  92.9 25.1 %copy-start.4 = (bf16[32,2048]{1,0:T(8,128)(2,1)S(1)}, bf16[32,2048]{1,0:T(8,128)(2,1)}, u32[]{:S(2)}) copy-start(bf16[32,2048]{1,0:T(8,128)(2,1)} %param.26) | copy-start | bytes 393220
  92.9 28.4 %copy-start.3 = (bf16[32,2,256]{2,1,0:T(2,128)(2,1)S(1)}, bf16[32,2,256]{2,1,0:T(2,128)(2,1)}, u32[]{:S(2)}) copy-start(bf16[32,2,256]{2,1,0:T(2,128)(2,1)} %param.28) | copy-start | bytes 98308
  93.0 28.4 %copy-start.6 = (bf16[2048]{0:T(1024)(128)(2,1)S(1)}, bf16[2048]{0:T(1024)(128)(2,1)}, u32[]{:S(2)}) copy-start(bf16[2048]{0:T(1024)(128)(2,1)} %param.40) | copy-start | bytes 12292
  95.0 14.1 %all-to-all-start.3 = ((bf16[16,16,1152]{2,1,0:T(8,128)(2,1)}), bf16[16,16,1152]{2,1,0:T(8,128)(2,1)S(1)}, u32[]{:S(2)}, u32[]{:S(2)}) async-start(bf16[16,16,1152]{2,1,0:T(8,128)(2,1)} %select_reduce_fusion), calls=%async_computation.3 | async-start | bytes 1179648 | tf_op jit(solution)/shard_map/all_to_all | solution.py:30
  113.5 4.6 %collective-permute-start = (f32[32,2048]{1,0:T(8,128)S(1)}, f32[32,2048]{1,0:T(8,128)S(1)}, u32[]{:S(2)}, u32[]{:S(2)}) collective-permute-start(f32[32,2048]{1,0:T(8,128)S(1)} %fusion.104), channel_id=1, source_target_pairs={{0,1},{1,0},{2,3},{3,2},{4,5},{5,4},{6,7},{7,6},{8,9},{9,8},{10,11... | collective-permute-start | bytes 786440 | tf_op jit(solution)/shard_map/ppermute | solution.py:238
  118.4 8.8 %collective-permute-start.1 = (bf16[32,2048]{1,0:T(8,128)(2,1)S(1)}, bf16[32,2048]{1,0:T(8,128)(2,1)S(1)}, u32[]{:S(2)}, u32[]{:S(2)}) collective-permute-start(bf16[32,2048]{1,0:T(8,128)(2,1)S(1)} %fusion.37), channel_id=1, source_target_pairs={{0,2},{2,4},{4,6},{6,0},{1,3},{3,5},{5,7},{7,1},{8,10},{10,12},{12... | collective-permute-start | bytes 393224 | tf_op jit(solution)/shard_map/ppermute | solution.py:247
  118.7 8.4 %collective-permute-start.2 = (bf16[32,2048]{1,0:T(8,128)(2,1)S(1)}, bf16[32,2048]{1,0:T(8,128)(2,1)S(1)}, u32[]{:S(2)}, u32[]{:S(2)}) collective-permute-start(bf16[32,2048]{1,0:T(8,128)(2,1)S(1)} %fusion.37), channel_id=1, source_target_pairs={{0,4},{2,6},{4,0},{6,2},{1,5},{3,7},{5,1},{7,3},{8,12},{10,14},{12... | collective-permute-start | bytes 393224 | tf_op jit(solution)/shard_map/ppermute | solution.py:247
  119.9 7.6 %collective-permute-start.3 = (bf16[32,2048]{1,0:T(8,128)(2,1)S(1)}, bf16[32,2048]{1,0:T(8,128)(2,1)S(1)}, u32[]{:S(2)}, u32[]{:S(2)}) collective-permute-start(bf16[32,2048]{1,0:T(8,128)(2,1)S(1)} %fusion.37), channel_id=1, source_target_pairs={{0,6},{2,0},{4,2},{6,4},{1,7},{3,1},{5,3},{7,5},{8,14},{10,8},{12,... | collective-permute-start | bytes 393224 | tf_op jit(solution)/shard_map/ppermute | solution.py:247
  134.8 4.7 %copy-start.7 = (s32[2]{0:T(128)S(1)}, s32[2]{0:T(128)}, u32[]{:S(2)}) copy-start(s32[2]{0:T(128)} %param.31) | copy-start | bytes 28
  137.9 3.1 %collective-permute-start.4 = (f32[4,16,2048]{2,1,0:T(8,128)S(1)}, f32[4,16,2048]{2,1,0:T(8,128)S(1)}, u32[]{:S(2)}, u32[]{:S(2)}) collective-permute-start(f32[4,16,2048]{2,1,0:T(8,128)S(1)} %dynamic-slice_bitcast_fusion), channel_id=1, source_target_pairs={{0,1},{1,0},{2,3},{3,2},{4,5},{5,4},{6,7},{7,6},{8,9},{9,8},{10,11... | collective-permute-start | bytes 1572872 | tf_op jit(solution)/shard_map/ppermute | solution.py:260
  141.1 5.4 %collective-permute-start.5 = (f32[16,2048]{1,0:T(8,128)S(1)}, f32[16,2048]{1,0:T(8,128)S(1)}, u32[]{:S(2)}, u32[]{:S(2)}) collective-permute-start(f32[16,2048]{1,0:T(8,128)S(1)} %get-tuple-element.95), channel_id=1, source_target_pairs={{0,6},{2,0},{4,2},{6,4},{1,7},{3,1},{5,3},{7,5},{8,14},{10,8},{12,... | collective-permute-start | bytes 393224 | tf_op jit(solution)/shard_map/ppermute | solution.py:264
  143.5 6.0 %collective-permute-start.6 = (f32[16,2048]{1,0:T(8,128)S(1)}, f32[16,2048]{1,0:T(8,128)S(1)}, u32[]{:S(2)}, u32[]{:S(2)}) collective-permute-start(f32[16,2048]{1,0:T(8,128)S(1)} %get-tuple-element.97), channel_id=1, source_target_pairs={{0,4},{2,6},{4,0},{6,2},{1,5},{3,7},{5,1},{7,3},{8,12},{10,14},{12... | collective-permute-start | bytes 393224 | tf_op jit(solution)/shard_map/ppermute | solution.py:264
  143.5 9.1 %collective-permute-start.7 = (f32[16,2048]{1,0:T(8,128)S(1)}, f32[16,2048]{1,0:T(8,128)S(1)}, u32[]{:S(2)}, u32[]{:S(2)}) collective-permute-start(f32[16,2048]{1,0:T(8,128)S(1)} %get-tuple-element.96), channel_id=1, source_target_pairs={{0,2},{2,4},{4,6},{6,0},{1,3},{3,5},{5,7},{7,1},{8,10},{10,12},{12... | collective-permute-start | bytes 393224 | tf_op jit(solution)/shard_map/ppermute | solution.py:264
Sparse Core Ops, SparseCore 0:
  10.1 95.1 all-gather.2

commit v11 on v10

--- a/solution.py
+++ b/solution.py
@@ -45,7 +45,13 @@
     )
     for step in range(count_nodes.bit_length()):
         reach = jnp.minimum(
-            jnp.einsum("sij,sjk->sik", reach, reach, precision=lax.Precision.HIGHEST), 1.0
+            jnp.einsum(
+                "sij,sjk->sik",
+                reach.astype(jnp.bfloat16),
+                reach.astype(jnp.bfloat16),
+                preferred_element_type=jnp.float32,
+            ),
+            1.0,
         )
     return reach
 
@@ -68,7 +74,12 @@
     count_nodes = reach.shape[-1]
     nodes = jnp.arange(count_nodes, dtype=jnp.int32)
     leaf_hot = (nodes[None, :] == leaves[:, None]).astype(jnp.float32)
-    path = jnp.einsum("si,sij->sj", leaf_hot, reach, precision=lax.Precision.HIGHEST)
+    path = jnp.einsum(
+        "si,sij->sj",
+        leaf_hot.astype(jnp.bfloat16),
+        reach.astype(jnp.bfloat16),
+        preferred_element_type=jnp.float32,
+    )
     ranks = jnp.cumsum(path, axis=1) - path
     places = nodes.astype(jnp.float32)
     select = path[:, None, :] * (ranks[:, None, :] == places[None, :, None]).astype(jnp.float32)
@@ -147,12 +158,8 @@
         full = jnp.dot(high, value_rows, preferred_element_type=jnp.float32) + jnp.dot(
             low, value_rows, preferred_element_type=jnp.float32
         )
-        update = jnp.einsum(
-            "ghqfe,gf->ghqe",
-            full.reshape(kv_local, GROUP, tree_len, kv_local, HEAD_DIM),
-            head_eye,
-            precision=lax.Precision.HIGHEST,
-        )
+        blocks = full.reshape(kv_local, GROUP, tree_len, kv_local, HEAD_DIM)
+        update = jnp.stack([blocks[g, :, :, g] for g in range(kv_local)])
         accum = accum * factor.reshape(kv_local, GROUP, tree_len)[..., None] + update
         return (
             newest.reshape(kv_local, GROUP, tree_len),
@@ -217,11 +224,12 @@
     tree_max = jnp.max(tree_scores, axis=-1)
     tree_weights = jnp.where(allowed, jnp.exp(tree_scores - tree_max[..., None]), 0.0)
     tree_total = jnp.sum(tree_weights, axis=-1)
+    tree_high = tree_weights.astype(jnp.bfloat16)
+    tree_low = (tree_weights - tree_high.astype(jnp.float32)).astype(jnp.bfloat16)
     tree_accum = jnp.einsum(
-        "sghqk,skge->sghqe",
-        tree_weights,
-        draft_values.astype(jnp.float32),
-        precision=lax.Precision.HIGHEST,
+        "sghqk,skge->sghqe", tree_high, draft_values, preferred_element_type=jnp.float32
+    ) + jnp.einsum(
+        "sghqk,skge->sghqe", tree_low, draft_values, preferred_element_type=jnp.float32
     )
     overall = jnp.maximum(part_max, tree_max)
     cache_weight = part_total * jnp.exp(part_max - overall)

time: 168 us -> 168 us (level)
    dot_general x9 -> x6, matrix products: 3.44 us -> 2.23 us  [the longest x3 1.51 us: ancestors(): jnp.einsum('sij,sjk->sik', reach.astype(jnp.bfloat16), reach.astype(jnp.b...]
where the time goes in v11:
time: 168 us; the launch traced here: 167 us
  matrix products  42.6 us (25%)
  starting transfers between devices  31.7 us (19%)
  waiting for transfers between devices  29.2 us (17%)
  other arithmetic  22 us (13%)
  local copies, waits for them, and re-layouts  20.9 us (12%)
  between operations  18.6 us (11%)
  blocking collectives  2.34 us (1%)
    all_to_all x2, waiting for transfers between devices, route(): arrived = lax.all_to_all(second, ('x', 'y'), 0, 0, tiled=True)  13 us
    all_to_all x2, starting transfers between devices, route(): arrived = lax.all_to_all(second, ('x', 'y'), 0, 0, tiled=True)  10.9 us
    dot_general x2, matrix products, attend(): lax.dot_general(spread, key_rows, (((1,), (1,)), ((), ())), preferred_ele...  10.8 us
    all_to_all x2, starting transfers between devices, route(): middle = lax.all_to_all(first, 'z', 0, 0, tiled=True)  9.54 us
    dot_general x2, matrix products, attend(): jnp.dot(low, value_rows, preferred_element_type=jnp.float32)  8.58 us
    ppermute x3, waiting for transfers between devices, per_device(): mlp_half = mlp_half + lax.ppermute(mine[shift], 'y', perm)  7.64 us
    reduce_sum x2, other arithmetic, attend(): total = total.reshape(rows) * factor + jnp.sum(weights, axis=-1)  7.07 us
    ppermute x3, waiting for transfers between devices, per_device(): shifted.append(lax.ppermute(normed, 'y', perm))  6.15 us
  transfers between devices with their start and end apart: 13, of which 9 were waited for; matrix products, arithmetic and copies ran while one was open for 37% of the time, Pallas kernels for 0%

profile of v11, /device:TPU:1, one launch (start us, length us, event | category | flops | bytes accessed | tf_op | source)
XLA Modules:
  0.0 167.3 jit_solution(588380765995941854)
XLA Ops:
  7.2 2.1 %pad_maximum_fusion = bf16[3,64,2048]{2,1,0:T(8,128)(2,1)} fusion(bf16[1,64,2048]{2,1,0:T(8,128)(2,1)} %bitcast.178, bf16[2,64,2048]{2,1,0:T(8,128)(2,1)} %param.38), kind=kLoop, calls=%fused_computation.55 | loop fusion | flops 393216 | bytes 1572864 | tf_op jit(solution)/shard_map/stack | solution.py:120
  13.4 0.7 slice_select_fusion
  14.3 0.8 fusion.116
  15.0 0.7 broadcast.393.clone
  16.3 5.9 %all-to-all-start = ((bf16[4,16,1152]{2,1,0:T(8,128)(2,1)}), bf16[4,16,1152]{2,1,0:T(8,128)(2,1)S(1)}, u32[]{:S(2)}, u32[]{:S(2)}) async-start(bf16[4,16,1152]{2,1,0:T(8,128)(2,1)} %fusion.68), calls=%async_computation | async-start | bytes 294912 | tf_op jit(solution)/shard_map/all_to_all | solution.py:23
  22.2 1.0 reshape.605
  23.2 0.7 iota_compare_fusion.7
  24.0 1.1 fusion.36
  25.6 1.0 slice_reduce_fusion
  26.7 1.3 fusion.117
  28.1 0.8 slice_bitcast_fusion.15
  29.0 1.4 fusion.73
  30.4 1.3 and_reduce_fusion
  32.8 1.3 select_reduce_fusion.1
  34.2 6.8 %all-to-all-start.1 = ((bf16[16,16,1152]{2,1,0:T(8,128)(2,1)}), bf16[16,16,1152]{2,1,0:T(8,128)(2,1)S(1)}, u32[]{:S(2)}, u32[]{:S(2)}) async-start(bf16[16,16,1152]{2,1,0:T(8,128)(2,1)} %select_reduce_fusion.1), calls=%async_computation.1 | async-start | bytes 1179648 | tf_op jit(solution)/shard_map/all_to_all | solution.py:30
  42.4 6.0 %fusion.113 = (bf16[64,1,128,256]{3,2,1,0:T(8,128)(2,1)}, bf16[64,1,128,256]{3,2,1,0:T(8,128)(2,1)}) fusion(bf16[64,2,128,256]{3,2,1,0:T(8,128)(2,1)} %param.32), kind=kLoop, calls=%fused_computation.200 | loop fusion | bytes 16777216 | tf_op jit(solution)/shard_map/slice | solution.py:140
  48.4 3.5 %all-to-all-done.1 = bf16[16,16,1152]{2,1,0:T(8,128)(2,1)S(1)} async-done(((bf16[16,16,1152]{2,1,0:T(8,128)(2,1)}), bf16[16,16,1152]{2,1,0:T(8,128)(2,1)S(1)}, u32[]{:S(2)}, u32[]{:S(2)}) %all-to-all-start.1) | async-done | bytes 589856 | tf_op jit(solution)/shard_map/all_to_all | solution.py:30
  53.9 6.8 %fusion.118 = (f32[256]{0:T(256)S(1)}, f32[256,8192]{1,0:T(8,128)}) fusion(bf16[256,256]{1,0:T(8,128)(2,1)S(1)} %reshape.592, bf16[8192,256]{1,0:T(8,128)(2,1)} %bitcast.169, pred[8192]{0:T(1024)(128)(4,1)S(1)} %bitcast.195), kind=kOutput, calls=%fused_computation.205 | convolution fusion | flops 1080033024 | bytes 12723200 | tf_op jit(solution)/shard_map/dot_general | solution.py:145
  60.8 6.7 %fusion.19 = f32[256,256]{1,0:T(8,128)S(1)} fusion(bf16[8192,256]{1,0:T(8,128)(2,1)} %bitcast.171, f32[256,8192]{1,0:T(8,128)} %get-tuple-element.121, f32[256]{0:T(256)S(1)} %broadcast_maximum_fusion, pred[8192]{0:T(1024)(128)(4,1)S(1)} %bitcast.196), kind=kOutput, calls=%fused_computation.26 | convolution fusion | flops 1086324736 | bytes 12854272 | tf_op jit(solution)/shard_map/dot_general | solution.py:158
  68.2 1.3 copy-done.1
  69.5 1.3 fusion.27
  71.1 5.3 %fusion.2 = f32[256]{0:T(256)S(1)} fusion(f32[256,8192]{1,0:T(8,128)} %get-tuple-element.121, f32[256]{0:T(256)S(1)} %broadcast_maximum_fusion, pred[8192]{0:T(1024)(128)(4,1)S(1)} %bitcast.198), kind=kLoop, calls=%fused_computation.8 | loop fusion | flops 6291200 | bytes 8398848 | tf_op jit(solution)/shard_map/reduce_sum | solution.py:155
  78.5 0.7 broadcast.393
  79.8 3.7 %all-to-all-start.2 = ((bf16[4,16,1152]{2,1,0:T(8,128)(2,1)}), bf16[4,16,1152]{2,1,0:T(8,128)(2,1)S(1)}, u32[]{:S(2)}, u32[]{:S(2)}) async-start(bf16[4,16,1152]{2,1,0:T(8,128)(2,1)} %bitcast_dynamic-update-slice_fusion), calls=%async_computation.2 | async-start | bytes 294912 | tf_op jit(solution)/shard_map/all_to_all | solution.py:23
  83.5 4.0 %fusion.119 = (f32[256]{0:T(256)S(1)}, f32[256,8192]{1,0:T(8,128)S(1)}) fusion(bf16[256,256]{1,0:T(8,128)(2,1)S(1)} %reshape.599, bf16[8192,256]{1,0:T(8,128)(2,1)} %bitcast.170, pred[8192]{0:T(1024)(128)(4,1)S(1)} %bitcast.191), kind=kOutput, calls=%fused_computation.206 | convolution fusion | flops 1080033024 | bytes 12723200 | tf_op jit(solution)/shard_map/dot_general | solution.py:145
  87.5 1.9 %fusion.20 = f32[256,256]{1,0:T(8,128)S(1)} fusion(bf16[8192,256]{1,0:T(8,128)(2,1)S(1)} %bitcast.173, f32[256,8192]{1,0:T(8,128)S(1)} %get-tuple-element.123, f32[256]{0:T(256)S(1)} %max.27, pred[8192]{0:T(1024)(128)(4,1)S(1)} %bitcast.192), kind=kOutput, calls=%fused_computation.27 | convolution fusion | flops 1086324736 | bytes 12854272 | tf_op jit(solution)/shard_map/dot_general | solution.py:158
  89.3 1.5 fusion.30
  90.8 1.8 %fusion.5 = f32[256]{0:T(256)S(1)} fusion(f32[256,8192]{1,0:T(8,128)S(1)} %get-tuple-element.123, f32[256]{0:T(256)S(1)} %max.27, pred[8192]{0:T(1024)(128)(4,1)S(1)} %bitcast.194), kind=kLoop, calls=%fused_computation.11 | loop fusion | flops 6291200 | bytes 8398848 | tf_op jit(solution)/shard_map/reduce_sum | solution.py:155
  93.4 1.3 select_reduce_fusion
  94.7 4.1 %all-to-all-start.3 = ((bf16[16,16,1152]{2,1,0:T(8,128)(2,1)}), bf16[16,16,1152]{2,1,0:T(8,128)(2,1)S(1)}, u32[]{:S(2)}, u32[]{:S(2)}) async-start(bf16[16,16,1152]{2,1,0:T(8,128)(2,1)} %select_reduce_fusion), calls=%async_computation.3 | async-start | bytes 1179648 | tf_op jit(solution)/shard_map/all_to_all | solution.py:30
  99.3 9.5 %all-to-all-done.3 = bf16[16,16,1152]{2,1,0:T(8,128)(2,1)S(1)} async-done(((bf16[16,16,1152]{2,1,0:T(8,128)(2,1)}), bf16[16,16,1152]{2,1,0:T(8,128)(2,1)S(1)}, u32[]{:S(2)}, u32[]{:S(2)}) %all-to-all-start.3) | async-done | bytes 589856 | tf_op jit(solution)/shard_map/all_to_all | solution.py:30
  110.1 3.0 %fusion.121 = f32[32,2048]{1,0:T(8,128)S(1)} fusion(bf16[32,1024]{1,0:T(8,128)(2,1)S(1)} %convert_element_type.260, bf16[1024,2048]{1,0:T(8,128)(2,1)} %param.36), kind=kOutput, calls=%fused_computation.208 | convolution fusion | flops 134217728 | bytes 4521984 | tf_op jit(solution)/shard_map/dot_general | solution.py:245
  113.1 3.8 %collective-permute-start = (f32[32,2048]{1,0:T(8,128)S(1)}, f32[32,2048]{1,0:T(8,128)S(1)}, u32[]{:S(2)}, u32[]{:S(2)}) collective-permute-start(f32[32,2048]{1,0:T(8,128)S(1)} %fusion.121), channel_id=1, source_target_pairs={{0,1},{1,0},{2,3},{3,2},{4,5},{5,4},{6,7},{7,6},{8,9},{9,8},{10,11... | collective-permute-start | bytes 786440 | tf_op jit(solution)/shard_map/ppermute | solution.py:246
  116.9 1.2 collective-permute-done
  118.7 1.1 collective-permute-start.2
  119.8 1.5 collective-permute-start.3
  121.3 5.8 %collective-permute-done.1 = bf16[32,2048]{1,0:T(8,128)(2,1)S(1)} collective-permute-done((bf16[32,2048]{1,0:T(8,128)(2,1)S(1)}, bf16[32,2048]{1,0:T(8,128)(2,1)S(1)}, u32[]{:S(2)}, u32[]{:S(2)}) %collective-permute-start.1) | collective-permute-done | bytes 131104 | tf_op jit(solution)/shard_map/ppermute | solution.py:255
  127.5 3.4 %fusion.12 = f32[128,16,64]{0,2,1:T(8,128)S(1)} fusion(bf16[32,2048]{1,0:T(8,128)(2,1)S(1)} %collective-permute-done.3, bf16[32,2048]{1,0:T(8,128)(2,1)S(1)} %collective-permute-done.2, bf16[32,2048]{1,0:T(8,128)(2,1)S(1)} %collective-permute-done.1, bf16[32,2048]{1,0:T(8,128)(2,1)S(1)} %fusion.42, bf16[16,3,64,2048]{3,2,1,0:T(8,128)(2,1)} %bitcast.214), kind=kOutput, calls=%fused_computation.19 | convolution fusion | flops 538968064 | bytes 5242880 | tf_op jit(solution)/shard_map/dot_general | solution.py:258
  130.9 3.4 %multiply_convert_fusion = bf16[128,16,64]{0,2,1:T(8,128)(2,1)S(1)} fusion(f32[128,16,64]{0,2,1:T(8,128)S(1)} %fusion.12, bf16[32,2048]{1,0:T(8,128)(2,1)S(1)} %collective-permute-done.3, bf16[32,2048]{1,0:T(8,128)(2,1)S(1)} %collective-permute-done.2, bf16[32,2048]{1,0:T(8,128)(2,1)S(1)} %collective-permute-done.1, bf16[32,2048]{1,0:T(8,128)(2,1)S(1)} %fusion.42, ...), kind=kOutput, calls=%fused_computation.60 | convolution fusion | flops 539754496 | bytes 5505024 | tf_op jit(solution)/shard_map/dot_general | solution.py:259
  134.8 3.0 %fusion.21 = f32[4,2,16,2048]{3,2,1,0:T(8,128)S(1)} fusion(bf16[4,2,16,16,64]{4,3,2,1,0:T(8,128)(2,1)S(1)} %bitcast.175, bf16[16,3,64,2048]{3,2,1,0:T(8,128)(2,1)} %bitcast.216), kind=kOutput, calls=%fused_computation.28 | convolution fusion | flops 536870912 | bytes 5505024 | tf_op jit(solution)/shard_map/dot_general | solution.py:262
  137.9 1.6 collective-permute-start.4
  139.9 1.1 collective-permute-done.4
  141.1 2.3 %collective-permute-start.5 = (f32[16,2048]{1,0:T(8,128)S(1)}, f32[16,2048]{1,0:T(8,128)S(1)}, u32[]{:S(2)}, u32[]{:S(2)}) collective-permute-start(f32[16,2048]{1,0:T(8,128)S(1)} %get-tuple-element.95), channel_id=1, source_target_pairs={{0,6},{2,0},{4,2},{6,4},{1,7},{3,1},{5,3},{7,5},{8,14},{10,8},{12,... | collective-permute-start | bytes 393224 | tf_op jit(solution)/shard_map/ppermute | solution.py:272
  144.9 1.6 collective-permute-done.5
  146.5 2.9 %collective-permute-done.6 = f32[16,2048]{1,0:T(8,128)S(1)} collective-permute-done((f32[16,2048]{1,0:T(8,128)S(1)}, f32[16,2048]{1,0:T(8,128)S(1)}, u32[]{:S(2)}, u32[]{:S(2)}) %collective-permute-start.6) | collective-permute-done | bytes 131104 | tf_op jit(solution)/shard_map/ppermute | solution.py:272
  149.4 3.2 %collective-permute-done.7 = f32[16,2048]{1,0:T(8,128)S(1)} collective-permute-done((f32[16,2048]{1,0:T(8,128)S(1)}, f32[16,2048]{1,0:T(8,128)S(1)}, u32[]{:S(2)}, u32[]{:S(2)}) %collective-permute-start.7) | collective-permute-done | bytes 131104 | tf_op jit(solution)/shard_map/ppermute | solution.py:272
  152.6 2.3 %all_gather.11 = bf16[32,2048]{1,0:T(8,128)(2,1)S(1)} all-gather(bf16[16,2048]{1,0:T(8,128)(2,1)S(1)} %fusion.55), channel_id=1, replica_groups=mesh['z'=4,'x'=4,'y'=4,'mlp'=2] {'mlp'}, dimensions={0}, use_global_device_ids=true | all-gather | bytes 196608 | tf_op jit(solution)/shard_map/all_gather | solution.py:275
  155.1 4.7 %convolution_convert_fusion = bf16[32,1536]{1,0:T(8,128)(2,1)} fusion(bf16[2048,1536]{1,0:T(8,128)(2,1)} %param.41, bf16[32,2048]{1,0:T(8,128)(2,1)S(1)} %all_gather.11, f32[2048]{0:T(1024)S(1)} %convert_element_type.269, f32[32]{0:T(128)S(1)} %add_rsqrt_fusion), kind=kOutput, calls=%fused_computation.31 | convolution fusion | flops 201637888 | bytes 6529152 | tf_op jit(solution)/shard_map/dot_general | solution.py:277
  (132 shorter events, 16.6 us)
Async XLA Ops:
  7.2 102.2 %all-gather.3.cloned.1.call-start = ((), (), s32[]{:S(2)}) async-start(), calls=%async_computation.4 | async-start | bytes 13369344 | tf_op jit(solution)/shard_map/all_gather | solution.py:121
  16.3 16.1 %all-to-all-start = ((bf16[4,16,1152]{2,1,0:T(8,128)(2,1)}), bf16[4,16,1152]{2,1,0:T(8,128)(2,1)S(1)}, u32[]{:S(2)}, u32[]{:S(2)}) async-start(bf16[4,16,1152]{2,1,0:T(8,128)(2,1)} %fusion.68), calls=%async_computation | async-start | bytes 294912 | tf_op jit(solution)/shard_map/all_to_all | solution.py:23
  34.2 17.7 %all-to-all-start.1 = ((bf16[16,16,1152]{2,1,0:T(8,128)(2,1)}), bf16[16,16,1152]{2,1,0:T(8,128)(2,1)S(1)}, u32[]{:S(2)}, u32[]{:S(2)}) async-start(bf16[16,16,1152]{2,1,0:T(8,128)(2,1)} %select_reduce_fusion.1), calls=%async_computation.1 | async-start | bytes 1179648 | tf_op jit(solution)/shard_map/all_to_all | solution.py:30
  60.8 7.4 %copy-start = (f32[256,8192]{1,0:T(8,128)S(1)}, f32[256,8192]{1,0:T(8,128)}, u32[]{:S(2)}) copy-start(f32[256,8192]{1,0:T(8,128)} %get-tuple-element.121) | copy-start | bytes 25165828
  60.8 8.7 %copy-start.1 = (bf16[64,1,128,256]{3,2,1,0:T(8,128)(2,1)S(1)}, bf16[64,1,128,256]{3,2,1,0:T(8,128)(2,1)}, u32[]{:S(2)}) copy-start(bf16[64,1,128,256]{3,2,1,0:T(8,128)(2,1)} %get-tuple-element.93) | copy-start | bytes 12582916
  79.8 13.1 %all-to-all-start.2 = ((bf16[4,16,1152]{2,1,0:T(8,128)(2,1)}), bf16[4,16,1152]{2,1,0:T(8,128)(2,1)S(1)}, u32[]{:S(2)}, u32[]{:S(2)}) async-start(bf16[4,16,1152]{2,1,0:T(8,128)(2,1)} %bitcast_dynamic-update-slice_fusion), calls=%async_computation.2 | async-start | bytes 294912 | tf_op jit(solution)/shard_map/all_to_all | solution.py:23
  83.5 4.0 %copy-start.2 = (bf16[64,1,128,256]{3,2,1,0:T(8,128)(2,1)S(1)}, bf16[64,1,128,256]{3,2,1,0:T(8,128)(2,1)}, u32[]{:S(2)}) copy-start(bf16[64,1,128,256]{3,2,1,0:T(8,128)(2,1)} %get-tuple-element.93) | copy-start | bytes 12582916
  90.8 26.1 %copy-start.5 = (bf16[2048]{0:T(1024)(128)(2,1)S(1)}, bf16[2048]{0:T(1024)(128)(2,1)}, u32[]{:S(2)}) copy-start(bf16[2048]{0:T(1024)(128)(2,1)} %param.37) | copy-start | bytes 12292
  90.8 27.2 %copy-start.4 = (bf16[32,2048]{1,0:T(8,128)(2,1)S(1)}, bf16[32,2048]{1,0:T(8,128)(2,1)}, u32[]{:S(2)}) copy-start(bf16[32,2048]{1,0:T(8,128)(2,1)} %param.26) | copy-start | bytes 393220
  92.7 28.6 %copy-start.3 = (bf16[32,2,256]{2,1,0:T(2,128)(2,1)S(1)}, bf16[32,2,256]{2,1,0:T(2,128)(2,1)}, u32[]{:S(2)}) copy-start(bf16[32,2,256]{2,1,0:T(2,128)(2,1)} %param.28) | copy-start | bytes 98308
  92.7 28.7 %copy-start.6 = (bf16[2048]{0:T(1024)(128)(2,1)S(1)}, bf16[2048]{0:T(1024)(128)(2,1)}, u32[]{:S(2)}) copy-start(bf16[2048]{0:T(1024)(128)(2,1)} %param.40) | copy-start | bytes 12292
  94.7 14.2 %all-to-all-start.3 = ((bf16[16,16,1152]{2,1,0:T(8,128)(2,1)}), bf16[16,16,1152]{2,1,0:T(8,128)(2,1)S(1)}, u32[]{:S(2)}, u32[]{:S(2)}) async-start(bf16[16,16,1152]{2,1,0:T(8,128)(2,1)} %select_reduce_fusion), calls=%async_computation.3 | async-start | bytes 1179648 | tf_op jit(solution)/shard_map/all_to_all | solution.py:30
  113.1 4.9 %collective-permute-start = (f32[32,2048]{1,0:T(8,128)S(1)}, f32[32,2048]{1,0:T(8,128)S(1)}, u32[]{:S(2)}, u32[]{:S(2)}) collective-permute-start(f32[32,2048]{1,0:T(8,128)S(1)} %fusion.121), channel_id=1, source_target_pairs={{0,1},{1,0},{2,3},{3,2},{4,5},{5,4},{6,7},{7,6},{8,9},{9,8},{10,11... | collective-permute-start | bytes 786440 | tf_op jit(solution)/shard_map/ppermute | solution.py:246
  118.3 8.8 %collective-permute-start.1 = (bf16[32,2048]{1,0:T(8,128)(2,1)S(1)}, bf16[32,2048]{1,0:T(8,128)(2,1)S(1)}, u32[]{:S(2)}, u32[]{:S(2)}) collective-permute-start(bf16[32,2048]{1,0:T(8,128)(2,1)S(1)} %fusion.42), channel_id=1, source_target_pairs={{0,2},{2,4},{4,6},{6,0},{1,3},{3,5},{5,7},{7,1},{8,10},{10,12},{12... | collective-permute-start | bytes 393224 | tf_op jit(solution)/shard_map/ppermute | solution.py:255
  118.7 8.5 %collective-permute-start.2 = (bf16[32,2048]{1,0:T(8,128)(2,1)S(1)}, bf16[32,2048]{1,0:T(8,128)(2,1)S(1)}, u32[]{:S(2)}, u32[]{:S(2)}) collective-permute-start(bf16[32,2048]{1,0:T(8,128)(2,1)S(1)} %fusion.42), channel_id=1, source_target_pairs={{0,4},{2,6},{4,0},{6,2},{1,5},{3,7},{5,1},{7,3},{8,12},{10,14},{12... | collective-permute-start | bytes 393224 | tf_op jit(solution)/shard_map/ppermute | solution.py:255
  119.8 7.7 %collective-permute-start.3 = (bf16[32,2048]{1,0:T(8,128)(2,1)S(1)}, bf16[32,2048]{1,0:T(8,128)(2,1)S(1)}, u32[]{:S(2)}, u32[]{:S(2)}) collective-permute-start(bf16[32,2048]{1,0:T(8,128)(2,1)S(1)} %fusion.42), channel_id=1, source_target_pairs={{0,6},{2,0},{4,2},{6,4},{1,7},{3,1},{5,3},{7,5},{8,14},{10,8},{12,... | collective-permute-start | bytes 393224 | tf_op jit(solution)/shard_map/ppermute | solution.py:255
  134.8 4.6 %copy-start.7 = (s32[2]{0:T(128)S(1)}, s32[2]{0:T(128)}, u32[]{:S(2)}) copy-start(s32[2]{0:T(128)} %param.31) | copy-start | bytes 28
  137.9 3.1 %collective-permute-start.4 = (f32[4,16,2048]{2,1,0:T(8,128)S(1)}, f32[4,16,2048]{2,1,0:T(8,128)S(1)}, u32[]{:S(2)}, u32[]{:S(2)}) collective-permute-start(f32[4,16,2048]{2,1,0:T(8,128)S(1)} %dynamic-slice_bitcast_fusion), channel_id=1, source_target_pairs={{0,1},{1,0},{2,3},{3,2},{4,5},{5,4},{6,7},{7,6},{8,9},{9,8},{10,11... | collective-permute-start | bytes 1572872 | tf_op jit(solution)/shard_map/ppermute | solution.py:268
  141.1 5.4 %collective-permute-start.5 = (f32[16,2048]{1,0:T(8,128)S(1)}, f32[16,2048]{1,0:T(8,128)S(1)}, u32[]{:S(2)}, u32[]{:S(2)}) collective-permute-start(f32[16,2048]{1,0:T(8,128)S(1)} %get-tuple-element.95), channel_id=1, source_target_pairs={{0,6},{2,0},{4,2},{6,4},{1,7},{3,1},{5,3},{7,5},{8,14},{10,8},{12,... | collective-permute-start | bytes 393224 | tf_op jit(solution)/shard_map/ppermute | solution.py:272
  143.4 6.0 %collective-permute-start.6 = (f32[16,2048]{1,0:T(8,128)S(1)}, f32[16,2048]{1,0:T(8,128)S(1)}, u32[]{:S(2)}, u32[]{:S(2)}) collective-permute-start(f32[16,2048]{1,0:T(8,128)S(1)} %get-tuple-element.97), channel_id=1, source_target_pairs={{0,4},{2,6},{4,0},{6,2},{1,5},{3,7},{5,1},{7,3},{8,12},{10,14},{12... | collective-permute-start | bytes 393224 | tf_op jit(solution)/shard_map/ppermute | solution.py:272
  143.4 9.1 %collective-permute-start.7 = (f32[16,2048]{1,0:T(8,128)S(1)}, f32[16,2048]{1,0:T(8,128)S(1)}, u32[]{:S(2)}, u32[]{:S(2)}) collective-permute-start(f32[16,2048]{1,0:T(8,128)S(1)} %get-tuple-element.96), channel_id=1, source_target_pairs={{0,2},{2,4},{4,6},{6,0},{1,3},{3,5},{5,7},{7,1},{8,10},{10,12},{12... | collective-permute-start | bytes 393224 | tf_op jit(solution)/shard_map/ppermute | solution.py:272
Sparse Core Ops, SparseCore 0:
  10.1 95.3 all-gather.2

commit v12 on v11

--- a/solution.py
+++ b/solution.py
@@ -153,10 +153,8 @@
         weights = jnp.where(visible, jnp.exp(scores - newest[:, None]), 0.0)
         factor = jnp.exp(old - newest)
         total = total.reshape(rows) * factor + jnp.sum(weights, axis=-1)
-        high = weights.astype(jnp.bfloat16)
-        low = (weights - high.astype(jnp.float32)).astype(jnp.bfloat16)
-        full = jnp.dot(high, value_rows, preferred_element_type=jnp.float32) + jnp.dot(
-            low, value_rows, preferred_element_type=jnp.float32
+        full = jnp.dot(
+            weights.astype(jnp.bfloat16), value_rows, preferred_element_type=jnp.float32
         )
         blocks = full.reshape(kv_local, GROUP, tree_len, kv_local, HEAD_DIM)
         update = jnp.stack([blocks[g, :, :, g] for g in range(kv_local)])

time: 168 us -> 172 us (1.024)
  local copies, waits for them, and re-layouts: 20.9 us -> 24.8 us
  matrix products: 42.6 us -> 38.9 us
  starting transfers between devices: 31.7 us -> 34.6 us
    convert_element_type x0 -> x2, other arithmetic: none -> 8.51 us  [attend(): weights.astype(jnp.bfloat16)]
    reduce_sum x2 -> x0, other arithmetic: 7.07 us -> none  [attend(): total = total.reshape(rows) * factor + jnp.sum(weights, axis=-1)]
    another operation x4 -> x7, local copies, waits for them, and re-layouts: 1.37 us -> 8.01 us  [the longest x1 6.62 us: attend(): value_rows = cache[first:last, 1].reshape((last - first) * page_len, width)]
    dot_general x4 -> x2, matrix products: 11.4 us -> 7.84 us  [attend(): jnp.dot(weights.astype(jnp.bfloat16), value_rows, preferred_element_type=...]
    all_to_all x2, starting transfers between devices: 10.9 us -> 12.8 us  [route(): arrived = lax.all_to_all(second, ('x', 'y'), 0, 0, tiled=True)]
    unnamed x17 -> x13, local copies, waits for them, and re-layouts: 2.65 us -> 0.69 us
  transfers between devices with their start and end apart: 13 -> 13, of which waited for: 9 -> 9; matrix products, arithmetic and copies ran while one was open for 37% -> 38% of each run, Pallas kernels for 0% -> 0%
where the time goes in v12:
time: 172 us; the launch traced here: 171 us
  matrix products  38.9 us (23%)
  starting transfers between devices  34.6 us (20%)
  waiting for transfers between devices  28.2 us (16%)
  local copies, waits for them, and re-layouts  24.8 us (14%)
  other arithmetic  23.4 us (14%)
  between operations  18.6 us (11%)
  blocking collectives  2.34 us (1%)
    all_to_all x2, starting transfers between devices, route(): arrived = lax.all_to_all(second, ('x', 'y'), 0, 0, tiled=True)  12.8 us
    all_to_all x2, waiting for transfers between devices, route(): arrived = lax.all_to_all(second, ('x', 'y'), 0, 0, tiled=True)  12.1 us
    dot_general x2, matrix products, attend(): lax.dot_general(spread, key_rows, (((1,), (1,)), ((), ())), preferred_ele...  10.6 us
    all_to_all x2, starting transfers between devices, route(): middle = lax.all_to_all(first, 'z', 0, 0, tiled=True)  9.66 us
    convert_element_type x2, other arithmetic, attend(): weights.astype(jnp.bfloat16)  8.51 us
    dot_general x2, matrix products, attend(): jnp.dot(weights.astype(jnp.bfloat16), value_rows, preferred_element_type=...  7.84 us
    ppermute x3, waiting for transfers between devices, per_device(): mlp_half = mlp_half + lax.ppermute(mine[shift], 'y', perm)  7.64 us
    another operation x1, local copies, waits for them, and re-layouts, attend(): value_rows = cache[first:last, 1].reshape((last - first) * page_len, width)  6.62 us
  transfers between devices with their start and end apart: 13, of which 9 were waited for; matrix products, arithmetic and copies ran while one was open for 38% of the time, Pallas kernels for 0%

profile of v12, /device:TPU:1, one launch (start us, length us, event | category | flops | bytes accessed | tf_op | source)
XLA Modules:
  0.0 170.7 jit_solution(7037093113917409594)
XLA Ops:
  7.2 2.1 %pad_maximum_fusion = bf16[3,64,2048]{2,1,0:T(8,128)(2,1)} fusion(bf16[1,64,2048]{2,1,0:T(8,128)(2,1)} %bitcast.202, bf16[2,64,2048]{2,1,0:T(8,128)(2,1)} %param.38), kind=kLoop, calls=%fused_computation.41 | loop fusion | flops 393216 | bytes 1572864 | tf_op jit(solution)/shard_map/stack | solution.py:120
  13.4 0.7 slice_select_fusion
  14.2 0.8 fusion.92
  15.0 0.7 broadcast.393.clone
  16.3 5.9 %all-to-all-start = ((bf16[4,16,1152]{2,1,0:T(8,128)(2,1)}), bf16[4,16,1152]{2,1,0:T(8,128)(2,1)S(1)}, u32[]{:S(2)}, u32[]{:S(2)}) async-start(bf16[4,16,1152]{2,1,0:T(8,128)(2,1)} %fusion.50), calls=%async_computation | async-start | bytes 294912 | tf_op jit(solution)/shard_map/all_to_all | solution.py:23
  22.2 1.0 reshape.603
  23.2 0.7 iota_compare_fusion.7
  23.9 1.1 fusion.18
  25.5 1.0 slice_reduce_fusion
  26.6 1.3 fusion.93
  27.9 0.8 slice_bitcast_fusion.23
  28.8 1.4 fusion.55
  30.6 6.2 %fusion.91 = (bf16[64,1,128,256]{3,2,1,0:T(8,128)(2,1)}, bf16[64,1,128,256]{3,2,1,0:T(8,128)(2,1)}) fusion(bf16[64,2,128,256]{3,2,1,0:T(8,128)(2,1)} %param.32), kind=kLoop, calls=%fused_computation.190 | loop fusion | bytes 16777216 | tf_op jit(solution)/shard_map/slice | solution.py:140
  37.3 1.3 select_reduce_fusion.1
  38.5 6.7 %all-to-all-start.1 = ((bf16[16,16,1152]{2,1,0:T(8,128)(2,1)}), bf16[16,16,1152]{2,1,0:T(8,128)(2,1)S(1)}, u32[]{:S(2)}, u32[]{:S(2)}) async-start(bf16[16,16,1152]{2,1,0:T(8,128)(2,1)} %select_reduce_fusion.1), calls=%async_computation.1 | async-start | bytes 1179648 | tf_op jit(solution)/shard_map/all_to_all | solution.py:30
  45.5 6.6 %copy.163 = bf16[8192,256]{0,1:T(8,128)(2,1)} copy(bf16[8192,256]{1,0:T(8,128)(2,1)} %bitcast.194) | data formatting | bytes 8388608 | tf_op jit(solution)/shard_map/reshape;squeeze | solution.py:140
  53.6 1.3 and_reduce_fusion
  55.1 1.0 all-to-all-done.1
  58.1 6.9 %fusion.94 = (f32[256]{0:T(256)S(1)}, f32[256,8192]{1,0:T(8,128)}) fusion(bf16[256,256]{1,0:T(8,128)(2,1)S(1)} %reshape.592, bf16[8192,256]{1,0:T(8,128)(2,1)} %bitcast.192, pred[8192]{0:T(1024)(128)(4,1)S(1)} %bitcast.205), kind=kOutput, calls=%fused_computation.193 | convolution fusion | flops 1080033024 | bytes 12723200 | tf_op jit(solution)/shard_map/dot_general | solution.py:145
  65.1 6.1 %fusion.3 = (bf16[256,8192]{1,0:T(8,128)(2,1)}, f32[256]{0:T(256)S(1)}) fusion(f32[256,8192]{1,0:T(8,128)} %get-tuple-element.125, f32[256]{0:T(256)S(1)} %broadcast_maximum_fusion, pred[8192]{0:T(1024)(128)(4,1)S(1)} %bitcast.206), kind=kLoop, calls=%fused_computation.7 | loop fusion | flops 8388352 | bytes 12593152 | tf_op jit(solution)/shard_map/convert_element_type | solution.py:157
  71.3 5.5 %fusion.97 = f32[4,4,16,4,64]{4,2,3,1,0:T(8,128)S(1)} fusion(bf16[4,4,16,8192,1]{3,2,4,1,0:T(8,128)(2,1)} %bitcast.195, bf16[4,64,8192,1,1]{2,1,0,4,3:T(8,128)(2,1)} %bitcast.197), kind=kOutput, calls=%fused_computation.196 | convolution fusion | flops 1073741824 | bytes 8650752 | tf_op jit(solution)/shard_map/dot_general | solution.py:156
  78.5 0.7 broadcast.393
  79.8 3.8 %all-to-all-start.2 = ((bf16[4,16,1152]{2,1,0:T(8,128)(2,1)}), bf16[4,16,1152]{2,1,0:T(8,128)(2,1)S(1)}, u32[]{:S(2)}, u32[]{:S(2)}) async-start(bf16[4,16,1152]{2,1,0:T(8,128)(2,1)} %bitcast_dynamic-update-slice_fusion), calls=%async_computation.2 | async-start | bytes 294912 | tf_op jit(solution)/shard_map/all_to_all | solution.py:23
  83.6 3.7 %fusion.95 = (f32[256]{0:T(256)S(1)}, f32[256,8192]{1,0:T(8,128)S(1)}) fusion(bf16[256,256]{1,0:T(8,128)(2,1)S(1)} %reshape.598, bf16[8192,256]{1,0:T(8,128)(2,1)} %bitcast.193, pred[8192]{0:T(1024)(128)(4,1)S(1)} %bitcast.203), kind=kOutput, calls=%fused_computation.194 | convolution fusion | flops 1080033024 | bytes 12723200 | tf_op jit(solution)/shard_map/dot_general | solution.py:145
  87.4 2.4 %fusion.4 = (bf16[256,8192]{1,0:T(8,128)(2,1)S(1)}, f32[256]{0:T(256)S(1)}) fusion(f32[256,8192]{1,0:T(8,128)S(1)} %get-tuple-element.127, f32[256]{0:T(256)S(1)} %max.27, pred[8192]{0:T(1024)(128)(4,1)S(1)} %bitcast.204), kind=kLoop, calls=%fused_computation.8 | loop fusion | flops 8388352 | bytes 12593152 | tf_op jit(solution)/shard_map/convert_element_type | solution.py:157
  89.8 2.3 %fusion.98 = f32[4,4,16,4,64]{4,2,3,1,0:T(8,128)S(1)} fusion(bf16[4,4,16,8192,1]{3,2,4,1,0:T(8,128)(2,1)S(1)} %bitcast.196, bf16[4,64,8192,1,1]{2,1,0,4,3:T(8,128)(2,1)S(1)} %bitcast.198), kind=kOutput, calls=%fused_computation.197 | convolution fusion | flops 1073741824 | bytes 8650752 | tf_op jit(solution)/shard_map/dot_general | solution.py:156
  92.8 1.3 select_reduce_fusion
  94.1 6.1 %all-to-all-start.3 = ((bf16[16,16,1152]{2,1,0:T(8,128)(2,1)}), bf16[16,16,1152]{2,1,0:T(8,128)(2,1)S(1)}, u32[]{:S(2)}, u32[]{:S(2)}) async-start(bf16[16,16,1152]{2,1,0:T(8,128)(2,1)} %select_reduce_fusion), calls=%async_computation.3 | async-start | bytes 1179648 | tf_op jit(solution)/shard_map/all_to_all | solution.py:30
  100.4 11.1 %all-to-all-done.3 = bf16[16,16,1152]{2,1,0:T(8,128)(2,1)S(1)} async-done(((bf16[16,16,1152]{2,1,0:T(8,128)(2,1)}), bf16[16,16,1152]{2,1,0:T(8,128)(2,1)S(1)}, u32[]{:S(2)}, u32[]{:S(2)}) %all-to-all-start.3) | async-done | bytes 589856 | tf_op jit(solution)/shard_map/all_to_all | solution.py:30
  112.8 3.0 %fusion.99 = f32[32,2048]{1,0:T(8,128)S(1)} fusion(bf16[32,1024]{1,0:T(8,128)(2,1)S(1)} %convert_element_type.244, bf16[1024,2048]{1,0:T(8,128)(2,1)} %param.36), kind=kOutput, calls=%fused_computation.198 | convolution fusion | flops 134217728 | bytes 4521984 | tf_op jit(solution)/shard_map/dot_general | solution.py:243
  115.8 4.6 %collective-permute-start = (f32[32,2048]{1,0:T(8,128)S(1)}, f32[32,2048]{1,0:T(8,128)S(1)}, u32[]{:S(2)}, u32[]{:S(2)}) collective-permute-start(f32[32,2048]{1,0:T(8,128)S(1)} %fusion.99), channel_id=1, source_target_pairs={{0,1},{1,0},{2,3},{3,2},{4,5},{5,4},{6,7},{7,6},{8,9},{9,8},{10,11... | collective-permute-start | bytes 786440 | tf_op jit(solution)/shard_map/ppermute | solution.py:244
  120.4 1.2 collective-permute-done
  122.2 1.2 collective-permute-start.2
  123.4 1.4 collective-permute-start.3
  124.8 5.8 %collective-permute-done.1 = bf16[32,2048]{1,0:T(8,128)(2,1)S(1)} collective-permute-done((bf16[32,2048]{1,0:T(8,128)(2,1)S(1)}, bf16[32,2048]{1,0:T(8,128)(2,1)S(1)}, u32[]{:S(2)}, u32[]{:S(2)}) %collective-permute-start.1) | collective-permute-done | bytes 131104 | tf_op jit(solution)/shard_map/ppermute | solution.py:253
  131.0 3.4 %fusion.8 = f32[128,16,64]{0,2,1:T(8,128)S(1)} fusion(bf16[32,2048]{1,0:T(8,128)(2,1)S(1)} %collective-permute-done.3, bf16[32,2048]{1,0:T(8,128)(2,1)S(1)} %collective-permute-done.2, bf16[32,2048]{1,0:T(8,128)(2,1)S(1)} %collective-permute-done.1, bf16[32,2048]{1,0:T(8,128)(2,1)S(1)} %fusion.24, bf16[16,3,64,2048]{3,2,1,0:T(8,128)(2,1)} %bitcast.226), kind=kOutput, calls=%fused_computation.15 | convolution fusion | flops 538968064 | bytes 5242880 | tf_op jit(solution)/shard_map/dot_general | solution.py:256
  134.4 3.5 %multiply_convert_fusion = bf16[128,16,64]{0,2,1:T(8,128)(2,1)S(1)} fusion(f32[128,16,64]{0,2,1:T(8,128)S(1)} %fusion.8, bf16[32,2048]{1,0:T(8,128)(2,1)S(1)} %collective-permute-done.3, bf16[32,2048]{1,0:T(8,128)(2,1)S(1)} %collective-permute-done.2, bf16[32,2048]{1,0:T(8,128)(2,1)S(1)} %collective-permute-done.1, bf16[32,2048]{1,0:T(8,128)(2,1)S(1)} %fusion.24, ...), kind=kOutput, calls=%fused_computation.46 | convolution fusion | flops 539754496 | bytes 5505024 | tf_op jit(solution)/shard_map/dot_general | solution.py:257
  138.3 3.0 %fusion.9 = f32[4,2,16,2048]{3,2,1,0:T(8,128)S(1)} fusion(bf16[4,2,16,16,64]{4,3,2,1,0:T(8,128)(2,1)S(1)} %bitcast.199, bf16[16,3,64,2048]{3,2,1,0:T(8,128)(2,1)} %bitcast.228), kind=kOutput, calls=%fused_computation.16 | convolution fusion | flops 536870912 | bytes 5505024 | tf_op jit(solution)/shard_map/dot_general | solution.py:260
  141.4 1.6 collective-permute-start.4
  143.4 1.1 collective-permute-done.4
  144.6 2.3 %collective-permute-start.5 = (f32[16,2048]{1,0:T(8,128)S(1)}, f32[16,2048]{1,0:T(8,128)S(1)}, u32[]{:S(2)}, u32[]{:S(2)}) collective-permute-start(f32[16,2048]{1,0:T(8,128)S(1)} %get-tuple-element.99), channel_id=1, source_target_pairs={{0,6},{2,0},{4,2},{6,4},{1,7},{3,1},{5,3},{7,5},{8,14},{10,8},{12,... | collective-permute-start | bytes 393224 | tf_op jit(solution)/shard_map/ppermute | solution.py:270
  146.9 0.7 collective-permute-start.7
  148.4 1.6 collective-permute-done.5
  150.0 2.9 %collective-permute-done.6 = f32[16,2048]{1,0:T(8,128)S(1)} collective-permute-done((f32[16,2048]{1,0:T(8,128)S(1)}, f32[16,2048]{1,0:T(8,128)S(1)}, u32[]{:S(2)}, u32[]{:S(2)}) %collective-permute-start.6) | collective-permute-done | bytes 131104 | tf_op jit(solution)/shard_map/ppermute | solution.py:270
  152.9 3.2 %collective-permute-done.7 = f32[16,2048]{1,0:T(8,128)S(1)} collective-permute-done((f32[16,2048]{1,0:T(8,128)S(1)}, f32[16,2048]{1,0:T(8,128)S(1)}, u32[]{:S(2)}, u32[]{:S(2)}) %collective-permute-start.7) | collective-permute-done | bytes 131104 | tf_op jit(solution)/shard_map/ppermute | solution.py:270
  156.1 2.3 %all_gather.11 = bf16[32,2048]{1,0:T(8,128)(2,1)S(1)} all-gather(bf16[16,2048]{1,0:T(8,128)(2,1)S(1)} %fusion.37), channel_id=1, replica_groups=mesh['z'=4,'x'=4,'y'=4,'mlp'=2] {'mlp'}, dimensions={0}, use_global_device_ids=true | all-gather | bytes 196608 | tf_op jit(solution)/shard_map/all_gather | solution.py:273
  158.6 4.7 %convolution_convert_fusion = bf16[32,1536]{1,0:T(8,128)(2,1)} fusion(bf16[2048,1536]{1,0:T(8,128)(2,1)} %param.41, bf16[32,2048]{1,0:T(8,128)(2,1)S(1)} %all_gather.11, f32[2048]{0:T(1024)S(1)} %convert_element_type.253, f32[32]{0:T(128)S(1)} %add_rsqrt_fusion), kind=kOutput, calls=%fused_computation.19 | convolution fusion | flops 201637888 | bytes 6529152 | tf_op jit(solution)/shard_map/dot_general | solution.py:275
  163.2 0.7 copy.252
  (123 shorter events, 13.7 us)
Async XLA Ops:
  7.2 104.9 %all-gather.3.cloned.1.call-start = ((), (), s32[]{:S(2)}) async-start(), calls=%async_computation.4 | async-start | bytes 13369344 | tf_op jit(solution)/shard_map/all_gather | solution.py:121
  16.3 20.5 %all-to-all-start = ((bf16[4,16,1152]{2,1,0:T(8,128)(2,1)}), bf16[4,16,1152]{2,1,0:T(8,128)(2,1)S(1)}, u32[]{:S(2)}, u32[]{:S(2)}) async-start(bf16[4,16,1152]{2,1,0:T(8,128)(2,1)} %fusion.50), calls=%async_computation | async-start | bytes 294912 | tf_op jit(solution)/shard_map/all_to_all | solution.py:23
  38.5 17.5 %all-to-all-start.1 = ((bf16[16,16,1152]{2,1,0:T(8,128)(2,1)}), bf16[16,16,1152]{2,1,0:T(8,128)(2,1)S(1)}, u32[]{:S(2)}, u32[]{:S(2)}) async-start(bf16[16,16,1152]{2,1,0:T(8,128)(2,1)} %select_reduce_fusion.1), calls=%async_computation.1 | async-start | bytes 1179648 | tf_op jit(solution)/shard_map/all_to_all | solution.py:30
  79.8 12.5 %all-to-all-start.2 = ((bf16[4,16,1152]{2,1,0:T(8,128)(2,1)}), bf16[4,16,1152]{2,1,0:T(8,128)(2,1)S(1)}, u32[]{:S(2)}, u32[]{:S(2)}) async-start(bf16[4,16,1152]{2,1,0:T(8,128)(2,1)} %bitcast_dynamic-update-slice_fusion), calls=%async_computation.2 | async-start | bytes 294912 | tf_op jit(solution)/shard_map/all_to_all | solution.py:23
  87.4 2.4 %copy-start = (bf16[8192,256]{0,1:T(8,128)(2,1)S(1)}, bf16[8192,256]{0,1:T(8,128)(2,1)}, u32[]{:S(2)}) copy-start(bf16[8192,256]{0,1:T(8,128)(2,1)} %copy.163) | copy-start | bytes 12582916
  94.1 17.3 %all-to-all-start.3 = ((bf16[16,16,1152]{2,1,0:T(8,128)(2,1)}), bf16[16,16,1152]{2,1,0:T(8,128)(2,1)S(1)}, u32[]{:S(2)}, u32[]{:S(2)}) async-start(bf16[16,16,1152]{2,1,0:T(8,128)(2,1)} %select_reduce_fusion), calls=%async_computation.3 | async-start | bytes 1179648 | tf_op jit(solution)/shard_map/all_to_all | solution.py:30
  111.6 8.8 %copy-start.3 = (bf16[2048]{0:T(1024)(128)(2,1)S(1)}, bf16[2048]{0:T(1024)(128)(2,1)}, u32[]{:S(2)}) copy-start(bf16[2048]{0:T(1024)(128)(2,1)} %param.37) | copy-start | bytes 12292
  111.6 10.0 %copy-start.2 = (bf16[32,2048]{1,0:T(8,128)(2,1)S(1)}, bf16[32,2048]{1,0:T(8,128)(2,1)}, u32[]{:S(2)}) copy-start(bf16[32,2048]{1,0:T(8,128)(2,1)} %param.26) | copy-start | bytes 393220
  112.2 12.6 %copy-start.1 = (bf16[32,2,256]{2,1,0:T(2,128)(2,1)S(1)}, bf16[32,2,256]{2,1,0:T(2,128)(2,1)}, u32[]{:S(2)}) copy-start(bf16[32,2,256]{2,1,0:T(2,128)(2,1)} %param.28) | copy-start | bytes 98308
  112.2 12.6 %copy-start.4 = (bf16[2048]{0:T(1024)(128)(2,1)S(1)}, bf16[2048]{0:T(1024)(128)(2,1)}, u32[]{:S(2)}) copy-start(bf16[2048]{0:T(1024)(128)(2,1)} %param.40) | copy-start | bytes 12292
  115.8 5.7 %collective-permute-start = (f32[32,2048]{1,0:T(8,128)S(1)}, f32[32,2048]{1,0:T(8,128)S(1)}, u32[]{:S(2)}, u32[]{:S(2)}) collective-permute-start(f32[32,2048]{1,0:T(8,128)S(1)} %fusion.99), channel_id=1, source_target_pairs={{0,1},{1,0},{2,3},{3,2},{4,5},{5,4},{6,7},{7,6},{8,9},{9,8},{10,11... | collective-permute-start | bytes 786440 | tf_op jit(solution)/shard_map/ppermute | solution.py:244
  121.8 8.8 %collective-permute-start.1 = (bf16[32,2048]{1,0:T(8,128)(2,1)S(1)}, bf16[32,2048]{1,0:T(8,128)(2,1)S(1)}, u32[]{:S(2)}, u32[]{:S(2)}) collective-permute-start(bf16[32,2048]{1,0:T(8,128)(2,1)S(1)} %fusion.24), channel_id=1, source_target_pairs={{0,2},{2,4},{4,6},{6,0},{1,3},{3,5},{5,7},{7,1},{8,10},{10,12},{12... | collective-permute-start | bytes 393224 | tf_op jit(solution)/shard_map/ppermute | solution.py:253
  122.2 8.5 %collective-permute-start.2 = (bf16[32,2048]{1,0:T(8,128)(2,1)S(1)}, bf16[32,2048]{1,0:T(8,128)(2,1)S(1)}, u32[]{:S(2)}, u32[]{:S(2)}) collective-permute-start(bf16[32,2048]{1,0:T(8,128)(2,1)S(1)} %fusion.24), channel_id=1, source_target_pairs={{0,4},{2,6},{4,0},{6,2},{1,5},{3,7},{5,1},{7,3},{8,12},{10,14},{12... | collective-permute-start | bytes 393224 | tf_op jit(solution)/shard_map/ppermute | solution.py:253
  123.4 7.6 %collective-permute-start.3 = (bf16[32,2048]{1,0:T(8,128)(2,1)S(1)}, bf16[32,2048]{1,0:T(8,128)(2,1)S(1)}, u32[]{:S(2)}, u32[]{:S(2)}) collective-permute-start(bf16[32,2048]{1,0:T(8,128)(2,1)S(1)} %fusion.24), channel_id=1, source_target_pairs={{0,6},{2,0},{4,2},{6,4},{1,7},{3,1},{5,3},{7,5},{8,14},{10,8},{12,... | collective-permute-start | bytes 393224 | tf_op jit(solution)/shard_map/ppermute | solution.py:253
  138.3 4.6 %copy-start.5 = (s32[2]{0:T(128)S(1)}, s32[2]{0:T(128)}, u32[]{:S(2)}) copy-start(s32[2]{0:T(128)} %param.31) | copy-start | bytes 28
  141.4 3.1 %collective-permute-start.4 = (f32[4,16,2048]{2,1,0:T(8,128)S(1)}, f32[4,16,2048]{2,1,0:T(8,128)S(1)}, u32[]{:S(2)}, u32[]{:S(2)}) collective-permute-start(f32[4,16,2048]{2,1,0:T(8,128)S(1)} %dynamic-slice_bitcast_fusion), channel_id=1, source_target_pairs={{0,1},{1,0},{2,3},{3,2},{4,5},{5,4},{6,7},{7,6},{8,9},{9,8},{10,11... | collective-permute-start | bytes 1572872 | tf_op jit(solution)/shard_map/ppermute | solution.py:266
  144.6 5.4 %collective-permute-start.5 = (f32[16,2048]{1,0:T(8,128)S(1)}, f32[16,2048]{1,0:T(8,128)S(1)}, u32[]{:S(2)}, u32[]{:S(2)}) collective-permute-start(f32[16,2048]{1,0:T(8,128)S(1)} %get-tuple-element.99), channel_id=1, source_target_pairs={{0,6},{2,0},{4,2},{6,4},{1,7},{3,1},{5,3},{7,5},{8,14},{10,8},{12,... | collective-permute-start | bytes 393224 | tf_op jit(solution)/shard_map/ppermute | solution.py:270
  146.9 6.0 %collective-permute-start.6 = (f32[16,2048]{1,0:T(8,128)S(1)}, f32[16,2048]{1,0:T(8,128)S(1)}, u32[]{:S(2)}, u32[]{:S(2)}) collective-permute-start(f32[16,2048]{1,0:T(8,128)S(1)} %get-tuple-element.101), channel_id=1, source_target_pairs={{0,4},{2,6},{4,0},{6,2},{1,5},{3,7},{5,1},{7,3},{8,12},{10,14},{12... | collective-permute-start | bytes 393224 | tf_op jit(solution)/shard_map/ppermute | solution.py:270
  146.9 9.1 %collective-permute-start.7 = (f32[16,2048]{1,0:T(8,128)S(1)}, f32[16,2048]{1,0:T(8,128)S(1)}, u32[]{:S(2)}, u32[]{:S(2)}) collective-permute-start(f32[16,2048]{1,0:T(8,128)S(1)} %get-tuple-element.100), channel_id=1, source_target_pairs={{0,2},{2,4},{4,6},{6,0},{1,3},{3,5},{5,7},{7,1},{8,10},{10,12},{12... | collective-permute-start | bytes 393224 | tf_op jit(solution)/shard_map/ppermute | solution.py:270
Sparse Core Ops, SparseCore 0:
  10.1 97.5 all-gather.2

commit v13 on v11

--- a/solution.py
+++ b/solution.py
@@ -16,11 +16,12 @@
 masked_score = -1e30
 
 
-def route(packet, dest, mark):
+def route(packet, dest, mark, carry):
     plane = lax.axis_size("x") * lax.axis_size("y")
     first = jnp.zeros((lax.axis_size("z"),) + packet.shape, packet.dtype)
     first = lax.dynamic_update_index_in_dim(first, packet, dest // plane, 0)
     middle = lax.all_to_all(first, "z", 0, 0, tiled=True)
+    middle, carry = lax.optimization_barrier((middle, carry))
     real = middle[:, 0, mark] > 0.5
     target = middle[:, 0, mark + 1].astype(jnp.int32) % plane
     spots = jnp.arange(plane, dtype=jnp.int32)
@@ -28,7 +29,7 @@
     second = jnp.sum(jnp.where(pick[:, :, None, None], middle[None], 0), axis=1)
     second = second.astype(packet.dtype)
     arrived = lax.all_to_all(second, ("x", "y"), 0, 0, tiled=True)
-    return jnp.sum(arrived.astype(jnp.float32), axis=0).astype(packet.dtype)
+    return jnp.sum(arrived.astype(jnp.float32), axis=0).astype(packet.dtype), carry
 
 
 def split_hi_lo(values):
@@ -116,7 +117,7 @@
     q_tags = jnp.zeros((tree_len, TAG), jnp.float32)
     q_tags = q_tags.at[:, 0].set(1.0).at[:, 1].set(prev_owner[0]).at[:, 2].set(device_id)
     q_packet = jnp.concatenate([q_in[tree_len:], q_tags.astype(q_in.dtype)], axis=1)
-    every_query = route(q_packet, prev_owner[0], q_width)
+    every_query, _ = route(q_packet, prev_owner[0], q_width, q_width)
     own_w = jnp.stack([w_in[0], w_in[1], w_down])
     all_w = lax.all_gather(own_w, ("z", "x"), axis=0, tiled=False)
     page_len = cache.shape[2]
@@ -194,8 +195,11 @@
         [sent_out.astype(jnp.bfloat16), stats, r_tags.astype(jnp.bfloat16)], axis=1
     )
     r_packet, own_state = lax.optimization_barrier((r_packet, own_state))
-    got = route(r_packet, sender, sent_out.shape[1] + stats.shape[1]).astype(jnp.float32)
-    running, total, accum = attend(0, own_queries, 0, num_blocks, own_state)
+    half = num_blocks // 2
+    own_state = attend(0, own_queries, 0, half, own_state)
+    got, own_state = route(r_packet, sender, sent_out.shape[1] + stats.shape[1], own_state)
+    got = got.astype(jnp.float32)
+    running, total, accum = attend(0, own_queries, half, num_blocks, own_state)
     all_w, running, total, accum = lax.optimization_barrier((all_w, running, total, accum))
     cache_out = accum / total[..., None]
     heads = kv_local * GROUP

time: 168 us -> 198 us (1.18)
  matrix products: 42.6 us -> 53.1 us
  local copies, waits for them, and re-layouts: 20.9 us -> 29.7 us
  other arithmetic: 22 us -> 28.5 us
  starting transfers between devices: 31.7 us -> 35.3 us
    dot_general x2 -> x3, matrix products: 8.58 us -> 14.6 us  [attend(): jnp.dot(low, value_rows, preferred_element_type=jnp.float32)]
    slice x1 -> x2, local copies, waits for them, and re-layouts: 6.01 us -> 12 us  [attend(): value_rows = cache[first:last, 1].reshape((last - first) * page_len, width)]
    reduce_sum x2 -> x3, other arithmetic: 7.07 us -> 11.5 us  [attend(): total = total.reshape(rows) * factor + jnp.sum(weights, axis=-1)]
    dot_general x2 -> x3, matrix products: 10.8 us -> 13.9 us  [attend(): lax.dot_general(spread, key_rows, (((1,), (1,)), ((), ())), preferred_ele...]
    all_to_all x2, waiting for transfers between devices: 13 us -> 10.6 us  [route(): arrived = lax.all_to_all(second, ('x', 'y'), 0, 0, tiled=True)]
    all_to_all x2, starting transfers between devices: 10.9 us -> 13 us  [route(): arrived = lax.all_to_all(second, ('x', 'y'), 0, 0, tiled=True)]
    unnamed x17 -> x47, local copies, waits for them, and re-layouts: 2.65 us -> 4.14 us
  transfers between devices with their start and end apart: 13 -> 13, of which waited for: 9 -> 10; matrix products, arithmetic and copies ran while one was open for 37% -> 44% of each run, Pallas kernels for 0% -> 0%
where the time goes in v13:
time: 198 us; the launch traced here: 196 us
  matrix products  53.1 us (27%)
  starting transfers between devices  35.3 us (18%)
  local copies, waits for them, and re-layouts  29.7 us (15%)
  other arithmetic  28.5 us (14%)
  waiting for transfers between devices  28.5 us (14%)
  between operations  18.8 us (9%)
  blocking collectives  2.34 us (1%)
    dot_general x3, matrix products, attend(): jnp.dot(low, value_rows, preferred_element_type=jnp.float32)  14.6 us
    dot_general x3, matrix products, attend(): lax.dot_general(spread, key_rows, (((1,), (1,)), ((), ())), preferred_ele...  13.9 us
    all_to_all x2, starting transfers between devices, route(): arrived = lax.all_to_all(second, ('x', 'y'), 0, 0, tiled=True)  13 us
    slice x2, local copies, waits for them, and re-layouts, attend(): value_rows = cache[first:last, 1].reshape((last - first) * page_len, width)  12 us
    reduce_sum x3, other arithmetic, attend(): total = total.reshape(rows) * factor + jnp.sum(weights, axis=-1)  11.5 us
    all_to_all x2, waiting for transfers between devices, route(): arrived = lax.all_to_all(second, ('x', 'y'), 0, 0, tiled=True)  10.6 us
    all_to_all x2, starting transfers between devices, route(): middle = lax.all_to_all(first, 'z', 0, 0, tiled=True)  9.76 us
    ppermute x3, waiting for transfers between devices, per_device(): mlp_half = mlp_half + lax.ppermute(mine[shift], 'y', perm)  7.64 us
  transfers between devices with their start and end apart: 13, of which 10 were waited for; matrix products, arithmetic and copies ran while one was open for 44% of the time, Pallas kernels for 0%

profile of v13, /device:TPU:1, one launch (start us, length us, event | category | flops | bytes accessed | tf_op | source)
XLA Modules:
  0.0 196.4 jit_solution(3401837567038423219)
XLA Ops:
  7.2 2.1 %pad_maximum_fusion = bf16[3,64,2048]{2,1,0:T(8,128)(2,1)} fusion(bf16[1,64,2048]{2,1,0:T(8,128)(2,1)} %bitcast.209, bf16[2,64,2048]{2,1,0:T(8,128)(2,1)} %param.38), kind=kLoop, calls=%fused_computation.68 | loop fusion | flops 393216 | bytes 1572864 | tf_op jit(solution)/shard_map/stack | solution.py:121
  16.4 5.9 %all-to-all-start = ((bf16[4,16,1152]{2,1,0:T(8,128)(2,1)}), bf16[4,16,1152]{2,1,0:T(8,128)(2,1)S(1)}, u32[]{:S(2)}, u32[]{:S(2)}) async-start(bf16[4,16,1152]{2,1,0:T(8,128)(2,1)} %fusion.82), calls=%async_computation | async-start | bytes 294912 | tf_op jit(solution)/shard_map/all_to_all | solution.py:23
  22.2 1.0 reshape.672
  24.0 1.1 fusion.50
  26.2 1.0 slice_reduce_fusion
  27.4 1.3 fusion.134
  29.6 1.3 fusion.87
  31.6 1.2 and_reduce_fusion.1
  33.2 0.9 fusion.62
  34.1 6.0 %fusion.128 = (bf16[32,1,128,256]{3,2,1,0:T(8,128)(2,1)}, bf16[32,1,128,256]{3,2,1,0:T(8,128)(2,1)}, bf16[32,1,128,256]{3,2,1,0:T(8,128)(2,1)}, bf16[32,1,128,256]{3,2,1,0:T(8,128)(2,1)S(1)}) fusion(bf16[64,2,128,256]{3,2,1,0:T(8,128)(2,1)} %param.32), kind=kLoop, calls=%fused_computation.221 | loop fusion | bytes 16777216 | tf_op jit(solution)/shard_map/slice | solution.py:141
  41.2 1.3 select_reduce_fusion.1
  42.5 6.8 %all-to-all-start.1 = ((bf16[16,16,1152]{2,1,0:T(8,128)(2,1)}), bf16[16,16,1152]{2,1,0:T(8,128)(2,1)S(1)}, u32[]{:S(2)}, u32[]{:S(2)}) async-start(bf16[16,16,1152]{2,1,0:T(8,128)(2,1)} %select_reduce_fusion.1), calls=%async_computation.1 | async-start | bytes 1179648 | tf_op jit(solution)/shard_map/all_to_all | solution.py:31
  51.5 6.0 %fusion.129 = (bf16[64,1,128,256]{3,2,1,0:T(8,128)(2,1)}, bf16[64,1,128,256]{3,2,1,0:T(8,128)(2,1)}) fusion(bf16[64,2,128,256]{3,2,1,0:T(8,128)(2,1)} %param.32), kind=kLoop, calls=%fused_computation.222 | loop fusion | bytes 16777216 | tf_op jit(solution)/shard_map/slice | solution.py:141
  57.5 7.3 %all-to-all-done.1 = bf16[16,16,1152]{2,1,0:T(8,128)(2,1)S(1)} async-done(((bf16[16,16,1152]{2,1,0:T(8,128)(2,1)}), bf16[16,16,1152]{2,1,0:T(8,128)(2,1)S(1)}, u32[]{:S(2)}, u32[]{:S(2)}) %all-to-all-start.1) | async-done | bytes 589856 | tf_op jit(solution)/shard_map/all_to_all | solution.py:31
  66.8 6.8 %fusion.135 = (f32[256]{0:T(256)S(1)}, f32[256,8192]{1,0:T(8,128)}) fusion(bf16[256,256]{1,0:T(8,128)(2,1)S(1)} %reshape.656, bf16[8192,256]{1,0:T(8,128)(2,1)} %bitcast.197, pred[8192]{0:T(1024)(128)(4,1)S(1)} %bitcast.226), kind=kOutput, calls=%fused_computation.228 | convolution fusion | flops 1080033024 | bytes 12723200 | tf_op jit(solution)/shard_map/dot_general | solution.py:146
  73.8 6.7 %fusion.13 = f32[256,256]{1,0:T(8,128)S(1)} fusion(bf16[8192,256]{1,0:T(8,128)(2,1)} %bitcast.200, f32[256,8192]{1,0:T(8,128)} %get-tuple-element.144, f32[256]{0:T(256)S(1)} %broadcast_maximum_fusion, pred[8192]{0:T(1024)(128)(4,1)S(1)} %bitcast.227), kind=kOutput, calls=%fused_computation.24 | convolution fusion | flops 1086324736 | bytes 12854272 | tf_op jit(solution)/shard_map/dot_general | solution.py:159
  81.1 1.3 copy-done.3
  82.4 1.3 fusion.38
  83.9 5.3 %fusion.3 = f32[256]{0:T(256)S(1)} fusion(f32[256,8192]{1,0:T(8,128)} %get-tuple-element.144, f32[256]{0:T(256)S(1)} %broadcast_maximum_fusion, pred[8192]{0:T(1024)(128)(4,1)} %bitcast.229), kind=kLoop, calls=%fused_computation.8 | loop fusion | flops 6291200 | bytes 8398848 | tf_op jit(solution)/shard_map/reduce_sum | solution.py:156
  90.0 0.8 subtract_convert_fusion.9
  92.4 4.3 %fusion.136 = (f32[256]{0:T(256)S(1)}, f32[256,4096]{1,0:T(8,128)}) fusion(bf16[256,256]{1,0:T(8,128)(2,1)S(1)} %reshape.663, bf16[4096,256]{1,0:T(8,128)(2,1)} %bitcast.199, pred[4096]{0:T(1024)(128)(4,1)S(1)} %bitcast.240), kind=kOutput, calls=%fused_computation.229 | convolution fusion | flops 540016384 | bytes 6427648 | tf_op jit(solution)/shard_map/dot_general | solution.py:146
  96.9 4.0 %fusion.27 = f32[256,256]{1,0:T(8,128)S(1)} fusion(bf16[4096,256]{1,0:T(8,128)(2,1)} %bitcast.204, f32[256,4096]{1,0:T(8,128)} %get-tuple-element.146, f32[256]{0:T(256)S(1)} %max.40, pred[4096]{0:T(1024)(128)(4,1)S(1)} %bitcast.241), kind=kOutput, calls=%fused_computation.39 | convolution fusion | flops 543162368 | bytes 6558720 | tf_op jit(solution)/shard_map/dot_general | solution.py:159
  102.6 3.1 %fusion.15 = f32[256]{0:T(256)S(1)} fusion(f32[256,4096]{1,0:T(8,128)} %get-tuple-element.146, f32[256]{0:T(256)S(1)} %max.40, pred[4096]{0:T(1024)(128)(4,1)S(1)} %bitcast.243), kind=kLoop, calls=%fused_computation.26 | loop fusion | flops 3145472 | bytes 4200448 | tf_op jit(solution)/shard_map/reduce_sum | solution.py:156
  107.1 3.9 %all-to-all-start.2 = ((bf16[4,16,1152]{2,1,0:T(8,128)(2,1)}), bf16[4,16,1152]{2,1,0:T(8,128)(2,1)S(1)}, u32[]{:S(2)}, u32[]{:S(2)}) async-start(bf16[4,16,1152]{2,1,0:T(8,128)(2,1)} %bitcast_dynamic-update-slice_fusion), calls=%async_computation.2 | async-start | bytes 294912 | tf_op jit(solution)/shard_map/all_to_all | solution.py:23
  111.2 2.8 %fusion.137 = (f32[256]{0:T(256)S(1)}, f32[256,4096]{1,0:T(8,128)}) fusion(bf16[256,256]{1,0:T(8,128)(2,1)S(1)} %reshape.663, bf16[4096,256]{1,0:T(8,128)(2,1)S(1)} %bitcast.198, pred[4096]{0:T(1024)(128)(4,1)S(1)} %bitcast.236), kind=kOutput, calls=%fused_computation.230 | convolution fusion | flops 540016384 | bytes 6427648 | tf_op jit(solution)/shard_map/dot_general | solution.py:146
  114.1 1.8 all-to-all-done.2
  116.0 3.1 %fusion.17 = f32[256]{0:T(256)S(1)} fusion(f32[256,4096]{1,0:T(8,128)} %get-tuple-element.148, f32[256]{0:T(256)S(1)} %max.42, pred[4096]{0:T(1024)(128)(4,1)S(1)} %bitcast.237), kind=kLoop, calls=%fused_computation.28 | loop fusion | flops 3145472 | bytes 4200448 | tf_op jit(solution)/shard_map/reduce_sum | solution.py:156
  119.7 1.3 select_reduce_fusion
  121.0 6.2 %all-to-all-start.3 = ((bf16[16,16,1152]{2,1,0:T(8,128)(2,1)}), bf16[16,16,1152]{2,1,0:T(8,128)(2,1)S(1)}, u32[]{:S(2)}, u32[]{:S(2)}) async-start(bf16[16,16,1152]{2,1,0:T(8,128)(2,1)} %select_reduce_fusion), calls=%async_computation.3 | async-start | bytes 1179648 | tf_op jit(solution)/shard_map/all_to_all | solution.py:31
  127.3 4.0 %fusion.28 = f32[256,256]{1,0:T(8,128)S(1)} fusion(bf16[4096,256]{1,0:T(8,128)(2,1)} %bitcast.202, f32[256,4096]{1,0:T(8,128)} %get-tuple-element.148, f32[256]{0:T(256)S(1)} %max.42, pred[4096]{0:T(1024)(128)(4,1)S(1)} %bitcast.238), kind=kOutput, calls=%fused_computation.40 | convolution fusion | flops 543162368 | bytes 6558720 | tf_op jit(solution)/shard_map/dot_general | solution.py:159
  133.3 3.3 %all-to-all-done.3 = bf16[16,16,1152]{2,1,0:T(8,128)(2,1)S(1)} async-done(((bf16[16,16,1152]{2,1,0:T(8,128)(2,1)}), bf16[16,16,1152]{2,1,0:T(8,128)(2,1)S(1)}, u32[]{:S(2)}, u32[]{:S(2)}) %all-to-all-start.3) | async-done | bytes 589856 | tf_op jit(solution)/shard_map/all_to_all | solution.py:31
  138.0 3.0 %fusion.139 = f32[32,2048]{1,0:T(8,128)S(1)} fusion(bf16[32,1024]{1,0:T(8,128)(2,1)S(1)} %convert_element_type.273, bf16[1024,2048]{1,0:T(8,128)(2,1)} %param.36), kind=kOutput, calls=%fused_computation.232 | convolution fusion | flops 134217728 | bytes 4521984 | tf_op jit(solution)/shard_map/dot_general | solution.py:249
  141.0 5.0 %collective-permute-start = (f32[32,2048]{1,0:T(8,128)S(1)}, f32[32,2048]{1,0:T(8,128)S(1)}, u32[]{:S(2)}, u32[]{:S(2)}) collective-permute-start(f32[32,2048]{1,0:T(8,128)S(1)} %fusion.139), channel_id=1, source_target_pairs={{0,1},{1,0},{2,3},{3,2},{4,5},{5,4},{6,7},{7,6},{8,9},{9,8},{10,11... | collective-permute-start | bytes 786440 | tf_op jit(solution)/shard_map/ppermute | solution.py:250
  146.0 1.2 collective-permute-done
  147.8 1.2 collective-permute-start.2
  149.0 1.4 collective-permute-start.3
  150.4 5.8 %collective-permute-done.1 = bf16[32,2048]{1,0:T(8,128)(2,1)S(1)} collective-permute-done((bf16[32,2048]{1,0:T(8,128)(2,1)S(1)}, bf16[32,2048]{1,0:T(8,128)(2,1)S(1)}, u32[]{:S(2)}, u32[]{:S(2)}) %collective-permute-start.1) | collective-permute-done | bytes 131104 | tf_op jit(solution)/shard_map/ppermute | solution.py:259
  156.6 3.4 %fusion.9 = f32[128,16,64]{0,2,1:T(8,128)S(1)} fusion(bf16[32,2048]{1,0:T(8,128)(2,1)S(1)} %collective-permute-done.3, bf16[32,2048]{1,0:T(8,128)(2,1)S(1)} %collective-permute-done.2, bf16[32,2048]{1,0:T(8,128)(2,1)S(1)} %collective-permute-done.1, bf16[32,2048]{1,0:T(8,128)(2,1)S(1)} %fusion.56, bf16[16,3,64,2048]{3,2,1,0:T(8,128)(2,1)} %bitcast.257), kind=kOutput, calls=%fused_computation.16 | convolution fusion | flops 538968064 | bytes 5242880 | tf_op jit(solution)/shard_map/dot_general | solution.py:262
  160.0 3.4 %multiply_convert_fusion = bf16[128,16,64]{0,2,1:T(8,128)(2,1)S(1)} fusion(f32[128,16,64]{0,2,1:T(8,128)S(1)} %fusion.9, bf16[32,2048]{1,0:T(8,128)(2,1)S(1)} %collective-permute-done.3, bf16[32,2048]{1,0:T(8,128)(2,1)S(1)} %collective-permute-done.2, bf16[32,2048]{1,0:T(8,128)(2,1)S(1)} %collective-permute-done.1, bf16[32,2048]{1,0:T(8,128)(2,1)S(1)} %fusion.56, ...), kind=kOutput, calls=%fused_computation.75 | convolution fusion | flops 539754496 | bytes 5505024 | tf_op jit(solution)/shard_map/dot_general | solution.py:263
  163.9 3.0 %fusion.18 = f32[4,2,16,2048]{3,2,1,0:T(8,128)S(1)} fusion(bf16[4,2,16,16,64]{4,3,2,1,0:T(8,128)(2,1)S(1)} %bitcast.206, bf16[16,3,64,2048]{3,2,1,0:T(8,128)(2,1)} %bitcast.259), kind=kOutput, calls=%fused_computation.29 | convolution fusion | flops 536870912 | bytes 5505024 | tf_op jit(solution)/shard_map/dot_general | solution.py:266
  167.0 1.6 collective-permute-start.4
  169.0 1.1 collective-permute-done.4
  170.2 2.3 %collective-permute-start.5 = (f32[16,2048]{1,0:T(8,128)S(1)}, f32[16,2048]{1,0:T(8,128)S(1)}, u32[]{:S(2)}, u32[]{:S(2)}) collective-permute-start(f32[16,2048]{1,0:T(8,128)S(1)} %get-tuple-element.112), channel_id=1, source_target_pairs={{0,6},{2,0},{4,2},{6,4},{1,7},{3,1},{5,3},{7,5},{8,14},{10,8},{12,... | collective-permute-start | bytes 393224 | tf_op jit(solution)/shard_map/ppermute | solution.py:276
  174.0 1.6 collective-permute-done.5
  175.6 2.9 %collective-permute-done.6 = f32[16,2048]{1,0:T(8,128)S(1)} collective-permute-done((f32[16,2048]{1,0:T(8,128)S(1)}, f32[16,2048]{1,0:T(8,128)S(1)}, u32[]{:S(2)}, u32[]{:S(2)}) %collective-permute-start.6) | collective-permute-done | bytes 131104 | tf_op jit(solution)/shard_map/ppermute | solution.py:276
  178.5 3.2 %collective-permute-done.7 = f32[16,2048]{1,0:T(8,128)S(1)} collective-permute-done((f32[16,2048]{1,0:T(8,128)S(1)}, f32[16,2048]{1,0:T(8,128)S(1)}, u32[]{:S(2)}, u32[]{:S(2)}) %collective-permute-start.7) | collective-permute-done | bytes 131104 | tf_op jit(solution)/shard_map/ppermute | solution.py:276
  181.7 2.3 %all_gather.11 = bf16[32,2048]{1,0:T(8,128)(2,1)S(1)} all-gather(bf16[16,2048]{1,0:T(8,128)(2,1)S(1)} %fusion.69), channel_id=1, replica_groups=mesh['z'=4,'x'=4,'y'=4,'mlp'=2] {'mlp'}, dimensions={0}, use_global_device_ids=true | all-gather | bytes 196608 | tf_op jit(solution)/shard_map/all_gather | solution.py:279
  184.2 4.7 %convolution_convert_fusion = bf16[32,1536]{1,0:T(8,128)(2,1)} fusion(bf16[2048,1536]{1,0:T(8,128)(2,1)} %param.41, bf16[32,2048]{1,0:T(8,128)(2,1)S(1)} %all_gather.11, f32[2048]{0:T(1024)S(1)} %convert_element_type.282, f32[32]{0:T(128)S(1)} %add_rsqrt_fusion), kind=kOutput, calls=%fused_computation.34 | convolution fusion | flops 201637888 | bytes 6529152 | tf_op jit(solution)/shard_map/dot_general | solution.py:281
  (177 shorter events, 27.2 us)
Async XLA Ops:
  7.2 130.0 %all-gather.3.cloned.1.call-start = ((), (), s32[]{:S(2)}) async-start(), calls=%async_computation.4 | async-start | bytes 13369344 | tf_op jit(solution)/shard_map/all_gather | solution.py:122
  16.4 24.4 %all-to-all-start = ((bf16[4,16,1152]{2,1,0:T(8,128)(2,1)}), bf16[4,16,1152]{2,1,0:T(8,128)(2,1)S(1)}, u32[]{:S(2)}, u32[]{:S(2)}) async-start(bf16[4,16,1152]{2,1,0:T(8,128)(2,1)} %fusion.82), calls=%async_computation | async-start | bytes 294912 | tf_op jit(solution)/shard_map/all_to_all | solution.py:23
  26.2 13.9 %copy-start.13 = (pred[2,16,16]{1,2,0:T(8,128)(4,1)}, pred[2,16,16]{1,2,0:T(8,128)(4,1)S(1)}, u32[]{:S(2)}) copy-start(pred[2,16,16]{1,2,0:T(8,128)(4,1)S(1)} %copy.204) | copy-start | bytes 1540
  27.4 12.7 %copy-start.8 = (bf16[2,16,4,64]{3,2,1,0:T(4,128)(2,1)}, bf16[2,16,4,64]{3,2,1,0:T(4,128)(2,1)S(1)}, u32[]{:S(2)}) copy-start(bf16[2,16,4,64]{3,2,1,0:T(4,128)(2,1)S(1)} %reshape_squeeze.31) | copy-start | bytes 49156
  31.5 49.0 %copy-start.11 = (pred[64,128]{1,0:T(8,128)(4,1)}, pred[64,128]{1,0:T(8,128)(4,1)S(1)}, u32[]{:S(2)}) copy-start(pred[64,128]{1,0:T(8,128)(4,1)S(1)} %and_reduce_fusion) | copy-start | bytes 24580
  42.5 22.3 %all-to-all-start.1 = ((bf16[16,16,1152]{2,1,0:T(8,128)(2,1)}), bf16[16,16,1152]{2,1,0:T(8,128)(2,1)S(1)}, u32[]{:S(2)}, u32[]{:S(2)}) async-start(bf16[16,16,1152]{2,1,0:T(8,128)(2,1)} %select_reduce_fusion.1), calls=%async_computation.1 | async-start | bytes 1179648 | tf_op jit(solution)/shard_map/all_to_all | solution.py:31
  73.8 15.6 %copy-start.12 = (f32[4,4,16]{2,1,0:T(4,128)}, f32[4,4,16]{2,1,0:T(4,128)S(1)}, u32[]{:S(2)}) copy-start(f32[4,4,16]{2,1,0:T(4,128)S(1)} %max_reshape.20) | copy-start | bytes 3076
  73.8 7.3 %copy-start = (f32[256,8192]{1,0:T(8,128)S(1)}, f32[256,8192]{1,0:T(8,128)}, u32[]{:S(2)}) copy-start(f32[256,8192]{1,0:T(8,128)} %get-tuple-element.144) | copy-start | bytes 25165828
  73.8 8.6 %copy-start.3 = (bf16[64,1,128,256]{3,2,1,0:T(8,128)(2,1)S(1)}, bf16[64,1,128,256]{3,2,1,0:T(8,128)(2,1)}, u32[]{:S(2)}) copy-start(bf16[64,1,128,256]{3,2,1,0:T(8,128)(2,1)} %get-tuple-element.110) | copy-start | bytes 12582916
  83.9 7.8 %copy-start.20 = (bf16[64]{0:T(256)(128)(2,1)S(1)}, bf16[64]{0:T(256)(128)(2,1)}, u32[]{:S(2)}) copy-start(bf16[64]{0:T(256)(128)(2,1)} %scatter.33) | copy-start | bytes 388
  83.9 8.5 %copy-start.16 = (pred[32,128]{1,0:T(8,128)(4,1)S(1)}, pred[32,128]{1,0:T(8,128)(4,1)}, u32[]{:S(2)}) copy-start(pred[32,128]{1,0:T(8,128)(4,1)} %get-tuple-element.90) | copy-start | bytes 12292
  96.9 4.1 %copy-start.2 = (f32[256,4096]{1,0:T(8,128)S(1)}, f32[256,4096]{1,0:T(8,128)}, u32[]{:S(2)}) copy-start(f32[256,4096]{1,0:T(8,128)} %get-tuple-element.146) | copy-start | bytes 12582916
  96.9 4.7 %copy-start.5 = (bf16[32,1,128,256]{3,2,1,0:T(8,128)(2,1)S(1)}, bf16[32,1,128,256]{3,2,1,0:T(8,128)(2,1)}, u32[]{:S(2)}) copy-start(bf16[32,1,128,256]{3,2,1,0:T(8,128)(2,1)} %get-tuple-element.107) | copy-start | bytes 6291460
  102.4 8.8 %copy-start.15 = (pred[32,128]{1,0:T(8,128)(4,1)S(1)}, pred[32,128]{1,0:T(8,128)(4,1)}, u32[]{:S(2)}) copy-start(pred[32,128]{1,0:T(8,128)(4,1)} %get-tuple-element.89) | copy-start | bytes 12292
  107.1 8.8 %all-to-all-start.2 = ((bf16[4,16,1152]{2,1,0:T(8,128)(2,1)}), bf16[4,16,1152]{2,1,0:T(8,128)(2,1)S(1)}, u32[]{:S(2)}, u32[]{:S(2)}) async-start(bf16[4,16,1152]{2,1,0:T(8,128)(2,1)} %bitcast_dynamic-update-slice_fusion), calls=%async_computation.2 | async-start | bytes 294912 | tf_op jit(solution)/shard_map/all_to_all | solution.py:23
  121.0 15.6 %all-to-all-start.3 = ((bf16[16,16,1152]{2,1,0:T(8,128)(2,1)}), bf16[16,16,1152]{2,1,0:T(8,128)(2,1)S(1)}, u32[]{:S(2)}, u32[]{:S(2)}) async-start(bf16[16,16,1152]{2,1,0:T(8,128)(2,1)} %select_reduce_fusion), calls=%async_computation.3 | async-start | bytes 1179648 | tf_op jit(solution)/shard_map/all_to_all | solution.py:31
  127.2 4.1 %copy-start.1 = (f32[256,4096]{1,0:T(8,128)S(1)}, f32[256,4096]{1,0:T(8,128)}, u32[]{:S(2)}) copy-start(f32[256,4096]{1,0:T(8,128)} %get-tuple-element.148) | copy-start | bytes 12582916
  127.3 4.7 %copy-start.4 = (bf16[32,1,128,256]{3,2,1,0:T(8,128)(2,1)S(1)}, bf16[32,1,128,256]{3,2,1,0:T(8,128)(2,1)}, u32[]{:S(2)}) copy-start(bf16[32,1,128,256]{3,2,1,0:T(8,128)(2,1)} %get-tuple-element.106) | copy-start | bytes 6291460
  132.0 5.3 %copy-start.17 = (f32[2,4,4,16]{3,2,1,0:T(4,128)S(1)}, f32[2,4,4,16]{3,2,1,0:T(4,128)}, u32[]{:S(2)}) copy-start(f32[2,4,4,16]{3,2,1,0:T(4,128)} %fusion.60) | copy-start | bytes 6148
  132.0 5.4 %copy-start.7 = (f32[2,4,4,16,64]{4,3,2,1,0:T(8,128)S(1)}, f32[2,4,4,16,64]{4,3,2,1,0:T(8,128)}, u32[]{:S(2)}) copy-start(f32[2,4,4,16,64]{4,3,2,1,0:T(8,128)} %fusion.62) | copy-start | bytes 393220
  132.0 5.4 %copy-start.9 = (bf16[2,16,4,64]{3,2,1,0:T(4,128)(2,1)S(1)}, bf16[2,16,4,64]{3,2,1,0:T(4,128)(2,1)}, u32[]{:S(2)}) copy-start(bf16[2,16,4,64]{3,2,1,0:T(4,128)(2,1)} %copy-done.8) | copy-start | bytes 49156
  132.0 5.4 %copy-start.14 = (pred[2,16,16]{1,2,0:T(8,128)(4,1)S(1)}, pred[2,16,16]{1,2,0:T(8,128)(4,1)}, u32[]{:S(2)}) copy-start(pred[2,16,16]{1,2,0:T(8,128)(4,1)} %copy-done.13) | copy-start | bytes 1540
  136.7 9.3 %copy-start.18 = (bf16[2048]{0:T(1024)(128)(2,1)S(1)}, bf16[2048]{0:T(1024)(128)(2,1)}, u32[]{:S(2)}) copy-start(bf16[2048]{0:T(1024)(128)(2,1)} %param.37) | copy-start | bytes 12292
  136.7 10.4 %copy-start.10 = (bf16[32,2048]{1,0:T(8,128)(2,1)S(1)}, bf16[32,2048]{1,0:T(8,128)(2,1)}, u32[]{:S(2)}) copy-start(bf16[32,2048]{1,0:T(8,128)(2,1)} %param.26) | copy-start | bytes 393220
  137.3 13.1 %copy-start.6 = (bf16[32,2,256]{2,1,0:T(2,128)(2,1)S(1)}, bf16[32,2,256]{2,1,0:T(2,128)(2,1)}, u32[]{:S(2)}) copy-start(bf16[32,2,256]{2,1,0:T(2,128)(2,1)} %param.28) | copy-start | bytes 98308
  137.3 13.1 %copy-start.19 = (bf16[2048]{0:T(1024)(128)(2,1)S(1)}, bf16[2048]{0:T(1024)(128)(2,1)}, u32[]{:S(2)}) copy-start(bf16[2048]{0:T(1024)(128)(2,1)} %param.40) | copy-start | bytes 12292
  141.0 6.2 %collective-permute-start = (f32[32,2048]{1,0:T(8,128)S(1)}, f32[32,2048]{1,0:T(8,128)S(1)}, u32[]{:S(2)}, u32[]{:S(2)}) collective-permute-start(f32[32,2048]{1,0:T(8,128)S(1)} %fusion.139), channel_id=1, source_target_pairs={{0,1},{1,0},{2,3},{3,2},{4,5},{5,4},{6,7},{7,6},{8,9},{9,8},{10,11... | collective-permute-start | bytes 786440 | tf_op jit(solution)/shard_map/ppermute | solution.py:250
  147.4 8.8 %collective-permute-start.1 = (bf16[32,2048]{1,0:T(8,128)(2,1)S(1)}, bf16[32,2048]{1,0:T(8,128)(2,1)S(1)}, u32[]{:S(2)}, u32[]{:S(2)}) collective-permute-start(bf16[32,2048]{1,0:T(8,128)(2,1)S(1)} %fusion.56), channel_id=1, source_target_pairs={{0,2},{2,4},{4,6},{6,0},{1,3},{3,5},{5,7},{7,1},{8,10},{10,12},{12... | collective-permute-start | bytes 393224 | tf_op jit(solution)/shard_map/ppermute | solution.py:259
  147.8 8.5 %collective-permute-start.2 = (bf16[32,2048]{1,0:T(8,128)(2,1)S(1)}, bf16[32,2048]{1,0:T(8,128)(2,1)S(1)}, u32[]{:S(2)}, u32[]{:S(2)}) collective-permute-start(bf16[32,2048]{1,0:T(8,128)(2,1)S(1)} %fusion.56), channel_id=1, source_target_pairs={{0,4},{2,6},{4,0},{6,2},{1,5},{3,7},{5,1},{7,3},{8,12},{10,14},{12... | collective-permute-start | bytes 393224 | tf_op jit(solution)/shard_map/ppermute | solution.py:259
  149.0 7.6 %collective-permute-start.3 = (bf16[32,2048]{1,0:T(8,128)(2,1)S(1)}, bf16[32,2048]{1,0:T(8,128)(2,1)S(1)}, u32[]{:S(2)}, u32[]{:S(2)}) collective-permute-start(bf16[32,2048]{1,0:T(8,128)(2,1)S(1)} %fusion.56), channel_id=1, source_target_pairs={{0,6},{2,0},{4,2},{6,4},{1,7},{3,1},{5,3},{7,5},{8,14},{10,8},{12,... | collective-permute-start | bytes 393224 | tf_op jit(solution)/shard_map/ppermute | solution.py:259
  163.9 4.7 %copy-start.21 = (s32[2]{0:T(128)S(1)}, s32[2]{0:T(128)}, u32[]{:S(2)}) copy-start(s32[2]{0:T(128)} %param.31) | copy-start | bytes 28
  163.9 4.7 %copy-start.22 = (bf16[2,16,16]{2,1,0:T(8,128)(2,1)S(1)}, bf16[2,16,16]{2,1,0:T(8,128)(2,1)}, u32[]{:S(2)}) copy-start(bf16[2,16,16]{2,1,0:T(8,128)(2,1)} %get-tuple-element.150) | copy-start | bytes 3076
  167.0 3.1 %collective-permute-start.4 = (f32[4,16,2048]{2,1,0:T(8,128)S(1)}, f32[4,16,2048]{2,1,0:T(8,128)S(1)}, u32[]{:S(2)}, u32[]{:S(2)}) collective-permute-start(f32[4,16,2048]{2,1,0:T(8,128)S(1)} %dynamic-slice_bitcast_fusion), channel_id=1, source_target_pairs={{0,1},{1,0},{2,3},{3,2},{4,5},{5,4},{6,7},{7,6},{8,9},{9,8},{10,11... | collective-permute-start | bytes 1572872 | tf_op jit(solution)/shard_map/ppermute | solution.py:272
  170.2 5.4 %collective-permute-start.5 = (f32[16,2048]{1,0:T(8,128)S(1)}, f32[16,2048]{1,0:T(8,128)S(1)}, u32[]{:S(2)}, u32[]{:S(2)}) collective-permute-start(f32[16,2048]{1,0:T(8,128)S(1)} %get-tuple-element.112), channel_id=1, source_target_pairs={{0,6},{2,0},{4,2},{6,4},{1,7},{3,1},{5,3},{7,5},{8,14},{10,8},{12,... | collective-permute-start | bytes 393224 | tf_op jit(solution)/shard_map/ppermute | solution.py:276
  172.5 6.0 %collective-permute-start.6 = (f32[16,2048]{1,0:T(8,128)S(1)}, f32[16,2048]{1,0:T(8,128)S(1)}, u32[]{:S(2)}, u32[]{:S(2)}) collective-permute-start(f32[16,2048]{1,0:T(8,128)S(1)} %get-tuple-element.114), channel_id=1, source_target_pairs={{0,4},{2,6},{4,0},{6,2},{1,5},{3,7},{5,1},{7,3},{8,12},{10,14},{12... | collective-permute-start | bytes 393224 | tf_op jit(solution)/shard_map/ppermute | solution.py:276
  172.5 9.1 %collective-permute-start.7 = (f32[16,2048]{1,0:T(8,128)S(1)}, f32[16,2048]{1,0:T(8,128)S(1)}, u32[]{:S(2)}, u32[]{:S(2)}) collective-permute-start(f32[16,2048]{1,0:T(8,128)S(1)} %get-tuple-element.113), channel_id=1, source_target_pairs={{0,2},{2,4},{4,6},{6,0},{1,3},{3,5},{5,7},{7,1},{8,10},{10,12},{12... | collective-permute-start | bytes 393224 | tf_op jit(solution)/shard_map/ppermute | solution.py:276
Sparse Core Ops, SparseCore 0:
  10.1 99.8 all-gather.2

commit v14 on v11

--- a/solution.py
+++ b/solution.py
@@ -150,7 +150,7 @@
         scores = jnp.where(visible, scores, masked_score)
         old = running.reshape(rows)
         newest = jnp.maximum(old, jnp.max(scores, axis=-1))
-        weights = jnp.where(visible, jnp.exp(scores - newest[:, None]), 0.0)
+        weights = jnp.exp(scores - newest[:, None])
         factor = jnp.exp(old - newest)
         total = total.reshape(rows) * factor + jnp.sum(weights, axis=-1)
         high = weights.astype(jnp.bfloat16)

time: 168 us -> 168 us (level)
  waiting for transfers between devices: 29.2 us -> 31.9 us
    dot_general x2, matrix products: 8.58 us -> 3.03 us  [attend(): jnp.dot(low, value_rows, preferred_element_type=jnp.float32)]
    dot_general x2, matrix products: 2.78 us -> 7.72 us  [attend(): jnp.dot(high, value_rows, preferred_element_type=jnp.float32)]
    all_to_all x2, waiting for transfers between devices: 13 us -> 15.8 us  [route(): arrived = lax.all_to_all(second, ('x', 'y'), 0, 0, tiled=True)]
  transfers between devices with their start and end apart: 13 -> 13, of which waited for: 9 -> 9; matrix products, arithmetic and copies ran while one was open for 37% -> 36% of each run, Pallas kernels for 0% -> 0%
where the time goes in v14:
time: 168 us; the launch traced here: 167 us
  matrix products  42 us (25%)
  waiting for transfers between devices  31.9 us (19%)
  starting transfers between devices  30.1 us (18%)
  local copies, waits for them, and re-layouts  21.3 us (13%)
  other arithmetic  21.1 us (13%)
  between operations  18.6 us (11%)
  blocking collectives  2.34 us (1%)
    all_to_all x2, waiting for transfers between devices, route(): arrived = lax.all_to_all(second, ('x', 'y'), 0, 0, tiled=True)  15.8 us
    all_to_all x2, starting transfers between devices, route(): arrived = lax.all_to_all(second, ('x', 'y'), 0, 0, tiled=True)  10.8 us
    dot_general x2, matrix products, attend(): lax.dot_general(spread, key_rows, (((1,), (1,)), ((), ())), preferred_ele...  10.8 us
    all_to_all x2, starting transfers between devices, route(): middle = lax.all_to_all(first, 'z', 0, 0, tiled=True)  9.37 us
    dot_general x2, matrix products, attend(): jnp.dot(high, value_rows, preferred_element_type=jnp.float32)  7.72 us
    ppermute x3, waiting for transfers between devices, per_device(): mlp_half = mlp_half + lax.ppermute(mine[shift], 'y', perm)  7.64 us
    ppermute x3, waiting for transfers between devices, per_device(): shifted.append(lax.ppermute(normed, 'y', perm))  6.15 us
    reduce_sum x2, other arithmetic, attend(): total = total.reshape(rows) * factor + jnp.sum(weights, axis=-1)  6.12 us
  transfers between devices with their start and end apart: 13, of which 9 were waited for; matrix products, arithmetic and copies ran while one was open for 36% of the time, Pallas kernels for 0%

profile of v14, /device:TPU:1, one launch (start us, length us, event | category | flops | bytes accessed | tf_op | source)
XLA Modules:
  0.0 167.3 jit_solution(310430471406341069)
XLA Ops:
  7.2 2.1 %pad_maximum_fusion = bf16[3,64,2048]{2,1,0:T(8,128)(2,1)} fusion(bf16[1,64,2048]{2,1,0:T(8,128)(2,1)} %bitcast.178, bf16[2,64,2048]{2,1,0:T(8,128)(2,1)} %param.38), kind=kLoop, calls=%fused_computation.51 | loop fusion | flops 393216 | bytes 1572864 | tf_op jit(solution)/shard_map/stack | solution.py:120
  13.4 0.7 slice_select_fusion
  14.3 0.8 fusion.104
  16.3 5.9 %all-to-all-start = ((bf16[4,16,1152]{2,1,0:T(8,128)(2,1)}), bf16[4,16,1152]{2,1,0:T(8,128)(2,1)S(1)}, u32[]{:S(2)}, u32[]{:S(2)}) async-start(bf16[4,16,1152]{2,1,0:T(8,128)(2,1)} %fusion.60), calls=%async_computation | async-start | bytes 294912 | tf_op jit(solution)/shard_map/all_to_all | solution.py:23
  22.2 1.0 reshape.605
  23.2 0.7 iota_compare_fusion.7
  24.0 1.1 fusion.28
  25.6 1.0 slice_reduce_fusion
  26.7 1.3 fusion.105
  28.1 0.8 slice_bitcast_fusion.15
  29.0 1.4 fusion.65
  30.4 1.3 and_reduce_fusion
  32.8 1.3 select_reduce_fusion.1
  34.2 6.8 %all-to-all-start.1 = ((bf16[16,16,1152]{2,1,0:T(8,128)(2,1)}), bf16[16,16,1152]{2,1,0:T(8,128)(2,1)S(1)}, u32[]{:S(2)}, u32[]{:S(2)}) async-start(bf16[16,16,1152]{2,1,0:T(8,128)(2,1)} %select_reduce_fusion.1), calls=%async_computation.1 | async-start | bytes 1179648 | tf_op jit(solution)/shard_map/all_to_all | solution.py:30
  42.4 6.0 %fusion.101 = (bf16[64,1,128,256]{3,2,1,0:T(8,128)(2,1)}, bf16[64,1,128,256]{3,2,1,0:T(8,128)(2,1)}) fusion(bf16[64,2,128,256]{3,2,1,0:T(8,128)(2,1)} %param.32), kind=kLoop, calls=%fused_computation.192 | loop fusion | bytes 16777216 | tf_op jit(solution)/shard_map/slice | solution.py:140
  48.4 3.5 %all-to-all-done.1 = bf16[16,16,1152]{2,1,0:T(8,128)(2,1)S(1)} async-done(((bf16[16,16,1152]{2,1,0:T(8,128)(2,1)}), bf16[16,16,1152]{2,1,0:T(8,128)(2,1)S(1)}, u32[]{:S(2)}, u32[]{:S(2)}) %all-to-all-start.1) | async-done | bytes 589856 | tf_op jit(solution)/shard_map/all_to_all | solution.py:30
  53.9 6.8 %fusion.106 = (f32[256]{0:T(256)S(1)}, f32[256,8192]{1,0:T(8,128)}) fusion(bf16[256,256]{1,0:T(8,128)(2,1)S(1)} %reshape.592, bf16[8192,256]{1,0:T(8,128)(2,1)} %bitcast.173, pred[8192]{0:T(1024)(128)(4,1)S(1)} %bitcast.192), kind=kOutput, calls=%fused_computation.197 | convolution fusion | flops 1080033024 | bytes 12723200 | tf_op jit(solution)/shard_map/dot_general | solution.py:145
  60.8 6.3 %fusion.8 = f32[256,256]{1,0:T(8,128)S(1)} fusion(bf16[8192,256]{1,0:T(8,128)(2,1)} %bitcast.169, f32[256,8192]{1,0:T(8,128)} %get-tuple-element.121, f32[256]{0:T(256)S(1)} %broadcast_maximum_fusion), kind=kOutput, calls=%fused_computation.13 | convolution fusion | flops 1077936128 | bytes 12846080 | tf_op jit(solution)/shard_map/dot_general | solution.py:158
  67.1 1.1 copy-done
  68.2 1.3 copy-done.1
  69.5 1.4 fusion.24
  71.2 4.8 %fusion.2 = f32[256]{0:T(256)S(1)} fusion(f32[256,8192]{1,0:T(8,128)} %get-tuple-element.121, f32[256]{0:T(256)S(1)} %broadcast_maximum_fusion), kind=kLoop, calls=%fused_computation.8 | loop fusion | flops 4194048 | bytes 8390656 | tf_op jit(solution)/shard_map/reduce_sum | solution.py:155
  78.1 0.7 broadcast.393
  79.4 3.5 %all-to-all-start.2 = ((bf16[4,16,1152]{2,1,0:T(8,128)(2,1)}), bf16[4,16,1152]{2,1,0:T(8,128)(2,1)S(1)}, u32[]{:S(2)}, u32[]{:S(2)}) async-start(bf16[4,16,1152]{2,1,0:T(8,128)(2,1)} %bitcast_dynamic-update-slice_fusion), calls=%async_computation.2 | async-start | bytes 294912 | tf_op jit(solution)/shard_map/all_to_all | solution.py:23
  82.9 4.0 %fusion.107 = (f32[256]{0:T(256)S(1)}, f32[256,8192]{1,0:T(8,128)S(1)}) fusion(bf16[256,256]{1,0:T(8,128)(2,1)S(1)} %reshape.599, bf16[8192,256]{1,0:T(8,128)(2,1)} %bitcast.174, pred[8192]{0:T(1024)(128)(4,1)S(1)} %bitcast.191), kind=kOutput, calls=%fused_computation.198 | convolution fusion | flops 1080033024 | bytes 12723200 | tf_op jit(solution)/shard_map/dot_general | solution.py:145
  87.0 1.4 fusion.6
  88.4 1.6 fusion.23
  90.1 1.3 fusion.5
  92.1 1.3 select_reduce_fusion
  93.4 4.1 %all-to-all-start.3 = ((bf16[16,16,1152]{2,1,0:T(8,128)(2,1)}), bf16[16,16,1152]{2,1,0:T(8,128)(2,1)S(1)}, u32[]{:S(2)}, u32[]{:S(2)}) async-start(bf16[16,16,1152]{2,1,0:T(8,128)(2,1)} %select_reduce_fusion), calls=%async_computation.3 | async-start | bytes 1179648 | tf_op jit(solution)/shard_map/all_to_all | solution.py:30
  98.0 12.2 %all-to-all-done.3 = bf16[16,16,1152]{2,1,0:T(8,128)(2,1)S(1)} async-done(((bf16[16,16,1152]{2,1,0:T(8,128)(2,1)}), bf16[16,16,1152]{2,1,0:T(8,128)(2,1)S(1)}, u32[]{:S(2)}, u32[]{:S(2)}) %all-to-all-start.3) | async-done | bytes 589856 | tf_op jit(solution)/shard_map/all_to_all | solution.py:30
  111.5 3.0 %fusion.109 = f32[32,2048]{1,0:T(8,128)S(1)} fusion(bf16[32,1024]{1,0:T(8,128)(2,1)S(1)} %convert_element_type.260, bf16[1024,2048]{1,0:T(8,128)(2,1)} %param.36), kind=kOutput, calls=%fused_computation.200 | convolution fusion | flops 134217728 | bytes 4521984 | tf_op jit(solution)/shard_map/dot_general | solution.py:245
  114.6 2.3 %collective-permute-start = (f32[32,2048]{1,0:T(8,128)S(1)}, f32[32,2048]{1,0:T(8,128)S(1)}, u32[]{:S(2)}, u32[]{:S(2)}) collective-permute-start(f32[32,2048]{1,0:T(8,128)S(1)} %fusion.109), channel_id=1, source_target_pairs={{0,1},{1,0},{2,3},{3,2},{4,5},{5,4},{6,7},{7,6},{8,9},{9,8},{10,11... | collective-permute-start | bytes 786440 | tf_op jit(solution)/shard_map/ppermute | solution.py:246
  116.9 1.2 collective-permute-done
  118.7 1.1 collective-permute-start.2
  119.8 1.4 collective-permute-start.3
  121.3 5.8 %collective-permute-done.1 = bf16[32,2048]{1,0:T(8,128)(2,1)S(1)} collective-permute-done((bf16[32,2048]{1,0:T(8,128)(2,1)S(1)}, bf16[32,2048]{1,0:T(8,128)(2,1)S(1)}, u32[]{:S(2)}, u32[]{:S(2)}) %collective-permute-start.1) | collective-permute-done | bytes 131104 | tf_op jit(solution)/shard_map/ppermute | solution.py:255
  127.5 3.4 %fusion.12 = f32[128,16,64]{0,2,1:T(8,128)S(1)} fusion(bf16[32,2048]{1,0:T(8,128)(2,1)S(1)} %collective-permute-done.3, bf16[32,2048]{1,0:T(8,128)(2,1)S(1)} %collective-permute-done.2, bf16[32,2048]{1,0:T(8,128)(2,1)S(1)} %collective-permute-done.1, bf16[32,2048]{1,0:T(8,128)(2,1)S(1)} %fusion.34, bf16[16,3,64,2048]{3,2,1,0:T(8,128)(2,1)} %bitcast.208), kind=kOutput, calls=%fused_computation.19 | convolution fusion | flops 538968064 | bytes 5242880 | tf_op jit(solution)/shard_map/dot_general | solution.py:258
  130.9 3.4 %multiply_convert_fusion = bf16[128,16,64]{0,2,1:T(8,128)(2,1)S(1)} fusion(f32[128,16,64]{0,2,1:T(8,128)S(1)} %fusion.12, bf16[32,2048]{1,0:T(8,128)(2,1)S(1)} %collective-permute-done.3, bf16[32,2048]{1,0:T(8,128)(2,1)S(1)} %collective-permute-done.2, bf16[32,2048]{1,0:T(8,128)(2,1)S(1)} %collective-permute-done.1, bf16[32,2048]{1,0:T(8,128)(2,1)S(1)} %fusion.34, ...), kind=kOutput, calls=%fused_computation.56 | convolution fusion | flops 539754496 | bytes 5505024 | tf_op jit(solution)/shard_map/dot_general | solution.py:259
  134.8 3.0 %fusion.17 = f32[4,2,16,2048]{3,2,1,0:T(8,128)S(1)} fusion(bf16[4,2,16,16,64]{4,3,2,1,0:T(8,128)(2,1)S(1)} %bitcast.175, bf16[16,3,64,2048]{3,2,1,0:T(8,128)(2,1)} %bitcast.210), kind=kOutput, calls=%fused_computation.24 | convolution fusion | flops 536870912 | bytes 5505024 | tf_op jit(solution)/shard_map/dot_general | solution.py:262
  137.9 1.6 collective-permute-start.4
  139.9 1.1 collective-permute-done.4
  141.1 2.3 %collective-permute-start.5 = (f32[16,2048]{1,0:T(8,128)S(1)}, f32[16,2048]{1,0:T(8,128)S(1)}, u32[]{:S(2)}, u32[]{:S(2)}) collective-permute-start(f32[16,2048]{1,0:T(8,128)S(1)} %get-tuple-element.95), channel_id=1, source_target_pairs={{0,6},{2,0},{4,2},{6,4},{1,7},{3,1},{5,3},{7,5},{8,14},{10,8},{12,... | collective-permute-start | bytes 393224 | tf_op jit(solution)/shard_map/ppermute | solution.py:272
  144.9 1.6 collective-permute-done.5
  146.5 2.9 %collective-permute-done.6 = f32[16,2048]{1,0:T(8,128)S(1)} collective-permute-done((f32[16,2048]{1,0:T(8,128)S(1)}, f32[16,2048]{1,0:T(8,128)S(1)}, u32[]{:S(2)}, u32[]{:S(2)}) %collective-permute-start.6) | collective-permute-done | bytes 131104 | tf_op jit(solution)/shard_map/ppermute | solution.py:272
  149.4 3.2 %collective-permute-done.7 = f32[16,2048]{1,0:T(8,128)S(1)} collective-permute-done((f32[16,2048]{1,0:T(8,128)S(1)}, f32[16,2048]{1,0:T(8,128)S(1)}, u32[]{:S(2)}, u32[]{:S(2)}) %collective-permute-start.7) | collective-permute-done | bytes 131104 | tf_op jit(solution)/shard_map/ppermute | solution.py:272
  152.6 2.3 %all_gather.11 = bf16[32,2048]{1,0:T(8,128)(2,1)S(1)} all-gather(bf16[16,2048]{1,0:T(8,128)(2,1)S(1)} %fusion.47), channel_id=1, replica_groups=mesh['z'=4,'x'=4,'y'=4,'mlp'=2] {'mlp'}, dimensions={0}, use_global_device_ids=true | all-gather | bytes 196608 | tf_op jit(solution)/shard_map/all_gather | solution.py:275
  155.1 4.7 %convolution_convert_fusion = bf16[32,1536]{1,0:T(8,128)(2,1)} fusion(bf16[2048,1536]{1,0:T(8,128)(2,1)} %param.41, bf16[32,2048]{1,0:T(8,128)(2,1)S(1)} %all_gather.11, f32[2048]{0:T(1024)S(1)} %convert_element_type.269, f32[32]{0:T(128)S(1)} %add_rsqrt_fusion), kind=kOutput, calls=%fused_computation.27 | convolution fusion | flops 201637888 | bytes 6529152 | tf_op jit(solution)/shard_map/dot_general | solution.py:277
  (132 shorter events, 16.7 us)
Async XLA Ops:
  7.2 103.7 %all-gather.3.cloned.1.call-start = ((), (), s32[]{:S(2)}) async-start(), calls=%async_computation.4 | async-start | bytes 13369344 | tf_op jit(solution)/shard_map/all_gather | solution.py:121
  16.3 16.1 %all-to-all-start = ((bf16[4,16,1152]{2,1,0:T(8,128)(2,1)}), bf16[4,16,1152]{2,1,0:T(8,128)(2,1)S(1)}, u32[]{:S(2)}, u32[]{:S(2)}) async-start(bf16[4,16,1152]{2,1,0:T(8,128)(2,1)} %fusion.60), calls=%async_computation | async-start | bytes 294912 | tf_op jit(solution)/shard_map/all_to_all | solution.py:23
  34.2 17.7 %all-to-all-start.1 = ((bf16[16,16,1152]{2,1,0:T(8,128)(2,1)}), bf16[16,16,1152]{2,1,0:T(8,128)(2,1)S(1)}, u32[]{:S(2)}, u32[]{:S(2)}) async-start(bf16[16,16,1152]{2,1,0:T(8,128)(2,1)} %select_reduce_fusion.1), calls=%async_computation.1 | async-start | bytes 1179648 | tf_op jit(solution)/shard_map/all_to_all | solution.py:30
  60.8 7.4 %copy-start = (f32[256,8192]{1,0:T(8,128)S(1)}, f32[256,8192]{1,0:T(8,128)}, u32[]{:S(2)}) copy-start(f32[256,8192]{1,0:T(8,128)} %get-tuple-element.121) | copy-start | bytes 25165828
  60.8 8.7 %copy-start.1 = (bf16[64,1,128,256]{3,2,1,0:T(8,128)(2,1)S(1)}, bf16[64,1,128,256]{3,2,1,0:T(8,128)(2,1)}, u32[]{:S(2)}) copy-start(bf16[64,1,128,256]{3,2,1,0:T(8,128)(2,1)} %get-tuple-element.93) | copy-start | bytes 12582916
  79.4 12.2 %all-to-all-start.2 = ((bf16[4,16,1152]{2,1,0:T(8,128)(2,1)}), bf16[4,16,1152]{2,1,0:T(8,128)(2,1)S(1)}, u32[]{:S(2)}, u32[]{:S(2)}) async-start(bf16[4,16,1152]{2,1,0:T(8,128)(2,1)} %bitcast_dynamic-update-slice_fusion), calls=%async_computation.2 | async-start | bytes 294912 | tf_op jit(solution)/shard_map/all_to_all | solution.py:23
  82.9 4.0 %copy-start.2 = (bf16[64,1,128,256]{3,2,1,0:T(8,128)(2,1)S(1)}, bf16[64,1,128,256]{3,2,1,0:T(8,128)(2,1)}, u32[]{:S(2)}) copy-start(bf16[64,1,128,256]{3,2,1,0:T(8,128)(2,1)} %get-tuple-element.93) | copy-start | bytes 12582916
  90.0 26.9 %copy-start.5 = (bf16[2048]{0:T(1024)(128)(2,1)S(1)}, bf16[2048]{0:T(1024)(128)(2,1)}, u32[]{:S(2)}) copy-start(bf16[2048]{0:T(1024)(128)(2,1)} %param.37) | copy-start | bytes 12292
  90.0 28.0 %copy-start.4 = (bf16[32,2048]{1,0:T(8,128)(2,1)S(1)}, bf16[32,2048]{1,0:T(8,128)(2,1)}, u32[]{:S(2)}) copy-start(bf16[32,2048]{1,0:T(8,128)(2,1)} %param.26) | copy-start | bytes 393220
  91.4 29.9 %copy-start.3 = (bf16[32,2,256]{2,1,0:T(2,128)(2,1)S(1)}, bf16[32,2,256]{2,1,0:T(2,128)(2,1)}, u32[]{:S(2)}) copy-start(bf16[32,2,256]{2,1,0:T(2,128)(2,1)} %param.28) | copy-start | bytes 98308
  91.4 29.9 %copy-start.6 = (bf16[2048]{0:T(1024)(128)(2,1)S(1)}, bf16[2048]{0:T(1024)(128)(2,1)}, u32[]{:S(2)}) copy-start(bf16[2048]{0:T(1024)(128)(2,1)} %param.40) | copy-start | bytes 12292
  93.4 16.9 %all-to-all-start.3 = ((bf16[16,16,1152]{2,1,0:T(8,128)(2,1)}), bf16[16,16,1152]{2,1,0:T(8,128)(2,1)S(1)}, u32[]{:S(2)}, u32[]{:S(2)}) async-start(bf16[16,16,1152]{2,1,0:T(8,128)(2,1)} %select_reduce_fusion), calls=%async_computation.3 | async-start | bytes 1179648 | tf_op jit(solution)/shard_map/all_to_all | solution.py:30
  114.6 3.5 %collective-permute-start = (f32[32,2048]{1,0:T(8,128)S(1)}, f32[32,2048]{1,0:T(8,128)S(1)}, u32[]{:S(2)}, u32[]{:S(2)}) collective-permute-start(f32[32,2048]{1,0:T(8,128)S(1)} %fusion.109), channel_id=1, source_target_pairs={{0,1},{1,0},{2,3},{3,2},{4,5},{5,4},{6,7},{7,6},{8,9},{9,8},{10,11... | collective-permute-start | bytes 786440 | tf_op jit(solution)/shard_map/ppermute | solution.py:246
  118.3 8.8 %collective-permute-start.1 = (bf16[32,2048]{1,0:T(8,128)(2,1)S(1)}, bf16[32,2048]{1,0:T(8,128)(2,1)S(1)}, u32[]{:S(2)}, u32[]{:S(2)}) collective-permute-start(bf16[32,2048]{1,0:T(8,128)(2,1)S(1)} %fusion.34), channel_id=1, source_target_pairs={{0,2},{2,4},{4,6},{6,0},{1,3},{3,5},{5,7},{7,1},{8,10},{10,12},{12... | collective-permute-start | bytes 393224 | tf_op jit(solution)/shard_map/ppermute | solution.py:255
  118.7 8.5 %collective-permute-start.2 = (bf16[32,2048]{1,0:T(8,128)(2,1)S(1)}, bf16[32,2048]{1,0:T(8,128)(2,1)S(1)}, u32[]{:S(2)}, u32[]{:S(2)}) collective-permute-start(bf16[32,2048]{1,0:T(8,128)(2,1)S(1)} %fusion.34), channel_id=1, source_target_pairs={{0,4},{2,6},{4,0},{6,2},{1,5},{3,7},{5,1},{7,3},{8,12},{10,14},{12... | collective-permute-start | bytes 393224 | tf_op jit(solution)/shard_map/ppermute | solution.py:255
  119.8 7.6 %collective-permute-start.3 = (bf16[32,2048]{1,0:T(8,128)(2,1)S(1)}, bf16[32,2048]{1,0:T(8,128)(2,1)S(1)}, u32[]{:S(2)}, u32[]{:S(2)}) collective-permute-start(bf16[32,2048]{1,0:T(8,128)(2,1)S(1)} %fusion.34), channel_id=1, source_target_pairs={{0,6},{2,0},{4,2},{6,4},{1,7},{3,1},{5,3},{7,5},{8,14},{10,8},{12,... | collective-permute-start | bytes 393224 | tf_op jit(solution)/shard_map/ppermute | solution.py:255
  134.8 4.6 %copy-start.7 = (s32[2]{0:T(128)S(1)}, s32[2]{0:T(128)}, u32[]{:S(2)}) copy-start(s32[2]{0:T(128)} %param.31) | copy-start | bytes 28
  137.9 3.1 %collective-permute-start.4 = (f32[4,16,2048]{2,1,0:T(8,128)S(1)}, f32[4,16,2048]{2,1,0:T(8,128)S(1)}, u32[]{:S(2)}, u32[]{:S(2)}) collective-permute-start(f32[4,16,2048]{2,1,0:T(8,128)S(1)} %dynamic-slice_bitcast_fusion), channel_id=1, source_target_pairs={{0,1},{1,0},{2,3},{3,2},{4,5},{5,4},{6,7},{7,6},{8,9},{9,8},{10,11... | collective-permute-start | bytes 1572872 | tf_op jit(solution)/shard_map/ppermute | solution.py:268
  141.1 5.4 %collective-permute-start.5 = (f32[16,2048]{1,0:T(8,128)S(1)}, f32[16,2048]{1,0:T(8,128)S(1)}, u32[]{:S(2)}, u32[]{:S(2)}) collective-permute-start(f32[16,2048]{1,0:T(8,128)S(1)} %get-tuple-element.95), channel_id=1, source_target_pairs={{0,6},{2,0},{4,2},{6,4},{1,7},{3,1},{5,3},{7,5},{8,14},{10,8},{12,... | collective-permute-start | bytes 393224 | tf_op jit(solution)/shard_map/ppermute | solution.py:272
  143.4 6.0 %collective-permute-start.6 = (f32[16,2048]{1,0:T(8,128)S(1)}, f32[16,2048]{1,0:T(8,128)S(1)}, u32[]{:S(2)}, u32[]{:S(2)}) collective-permute-start(f32[16,2048]{1,0:T(8,128)S(1)} %get-tuple-element.97), channel_id=1, source_target_pairs={{0,4},{2,6},{4,0},{6,2},{1,5},{3,7},{5,1},{7,3},{8,12},{10,14},{12... | collective-permute-start | bytes 393224 | tf_op jit(solution)/shard_map/ppermute | solution.py:272
  143.4 9.1 %collective-permute-start.7 = (f32[16,2048]{1,0:T(8,128)S(1)}, f32[16,2048]{1,0:T(8,128)S(1)}, u32[]{:S(2)}, u32[]{:S(2)}) collective-permute-start(f32[16,2048]{1,0:T(8,128)S(1)} %get-tuple-element.96), channel_id=1, source_target_pairs={{0,2},{2,4},{4,6},{6,0},{1,3},{3,5},{5,7},{7,1},{8,10},{10,12},{12... | collective-permute-start | bytes 393224 | tf_op jit(solution)/shard_map/ppermute | solution.py:272
Sparse Core Ops, SparseCore 0:
  10.1 95.3 all-gather.2

commit v15 on v14

--- a/solution.py
+++ b/solution.py
@@ -272,7 +272,15 @@
         mlp_half = mlp_half + lax.ppermute(mine[shift], "y", perm)
     base_half = lax.dynamic_slice_in_dim(mixed, column * half_count, half_count, 0)
     out_half = (base_half.astype(jnp.float32) + mlp_half).astype(jnp.bfloat16)
-    hidden_out = lax.all_gather(out_half, "mlp", axis=0, tiled=True)
+    other_half = lax.ppermute(out_half, "mlp", [(0, 1), (1, 0)])
+    pair = jnp.stack([out_half, other_half])
+    hidden_out = jnp.concatenate(
+        [
+            lax.dynamic_index_in_dim(pair, column, 0, keepdims=False),
+            lax.dynamic_index_in_dim(pair, 1 - column, 0, keepdims=False),
+        ],
+        axis=0,
+    )
     next_normed = rms_scale(hidden_out, gain_next)
     next_qkv = jnp.dot(next_normed, w_next, preferred_element_type=jnp.float32).astype(jnp.bfloat16)
     accepted = compact_path(reach, accept_leaf, kv_in.reshape(2, tree_len, 2 * kv_width))

time: 168 us -> 167 us (level)
  blocking collectives: 2.34 us -> 0 us
    all_gather x1 -> x0, blocking collectives: 2.34 us -> none  [per_device(): hidden_out = lax.all_gather(out_half, 'mlp', axis=0, tiled=True)]
  transfers between devices with their start and end apart: 13 -> 14, of which waited for: 9 -> 10; matrix products, arithmetic and copies ran while one was open for 36% -> 36% of each run, Pallas kernels for 0% -> 0%
where the time goes in v15:
time: 167 us; the launch traced here: 166 us
  matrix products  42.1 us (25%)
  waiting for transfers between devices  32.8 us (20%)
  starting transfers between devices  30.9 us (19%)
  other arithmetic  21.1 us (13%)
  local copies, waits for them, and re-layouts  20.6 us (12%)
  between operations  18.6 us (11%)
    all_to_all x2, waiting for transfers between devices, route(): arrived = lax.all_to_all(second, ('x', 'y'), 0, 0, tiled=True)  15.8 us
    all_to_all x2, starting transfers between devices, route(): arrived = lax.all_to_all(second, ('x', 'y'), 0, 0, tiled=True)  10.8 us
    dot_general x2, matrix products, attend(): lax.dot_general(spread, key_rows, (((1,), (1,)), ((), ())), preferred_ele...  10.8 us
    all_to_all x2, starting transfers between devices, route(): middle = lax.all_to_all(first, 'z', 0, 0, tiled=True)  9.37 us
    ppermute x3, waiting for transfers between devices, per_device(): mlp_half = mlp_half + lax.ppermute(mine[shift], 'y', perm)  8.12 us
    dot_general x2, matrix products, attend(): jnp.dot(high, value_rows, preferred_element_type=jnp.float32)  7.72 us
    ppermute x3, waiting for transfers between devices, per_device(): shifted.append(lax.ppermute(normed, 'y', perm))  6.2 us
    reduce_sum x2, other arithmetic, attend(): total = total.reshape(rows) * factor + jnp.sum(weights, axis=-1)  6.12 us
  transfers between devices with their start and end apart: 14, of which 10 were waited for; matrix products, arithmetic and copies ran while one was open for 36% of the time, Pallas kernels for 0%

profile of v15, /device:TPU:1, one launch (start us, length us, event | category | flops | bytes accessed | tf_op | source)
XLA Modules:
  0.0 166.2 jit_solution(9510735675721650838)
XLA Ops:
  7.2 2.1 %pad_maximum_fusion = bf16[3,64,2048]{2,1,0:T(8,128)(2,1)} fusion(bf16[1,64,2048]{2,1,0:T(8,128)(2,1)} %bitcast.185, bf16[2,64,2048]{2,1,0:T(8,128)(2,1)} %param.38), kind=kLoop, calls=%fused_computation.51 | loop fusion | flops 393216 | bytes 1572864 | tf_op jit(solution)/shard_map/stack | solution.py:120
  13.4 0.7 slice_select_fusion
  14.3 0.8 fusion.108
  16.3 5.9 %all-to-all-start = ((bf16[4,16,1152]{2,1,0:T(8,128)(2,1)}), bf16[4,16,1152]{2,1,0:T(8,128)(2,1)S(1)}, u32[]{:S(2)}, u32[]{:S(2)}) async-start(bf16[4,16,1152]{2,1,0:T(8,128)(2,1)} %fusion.64), calls=%async_computation | async-start | bytes 294912 | tf_op jit(solution)/shard_map/all_to_all | solution.py:23
  22.2 1.0 reshape.605
  23.2 0.7 iota_compare_fusion.7
  24.0 1.1 fusion.28
  25.6 1.0 slice_reduce_fusion
  26.7 1.3 fusion.109
  28.1 0.8 slice_bitcast_fusion.15
  29.0 1.4 fusion.69
  30.4 1.3 and_reduce_fusion
  32.8 1.3 select_reduce_fusion.1
  34.2 6.8 %all-to-all-start.1 = ((bf16[16,16,1152]{2,1,0:T(8,128)(2,1)}), bf16[16,16,1152]{2,1,0:T(8,128)(2,1)S(1)}, u32[]{:S(2)}, u32[]{:S(2)}) async-start(bf16[16,16,1152]{2,1,0:T(8,128)(2,1)} %select_reduce_fusion.1), calls=%async_computation.1 | async-start | bytes 1179648 | tf_op jit(solution)/shard_map/all_to_all | solution.py:30
  42.4 6.0 %fusion.105 = (bf16[64,1,128,256]{3,2,1,0:T(8,128)(2,1)}, bf16[64,1,128,256]{3,2,1,0:T(8,128)(2,1)}) fusion(bf16[64,2,128,256]{3,2,1,0:T(8,128)(2,1)} %param.32), kind=kLoop, calls=%fused_computation.201 | loop fusion | bytes 16777216 | tf_op jit(solution)/shard_map/slice | solution.py:140
  48.4 3.5 %all-to-all-done.1 = bf16[16,16,1152]{2,1,0:T(8,128)(2,1)S(1)} async-done(((bf16[16,16,1152]{2,1,0:T(8,128)(2,1)}), bf16[16,16,1152]{2,1,0:T(8,128)(2,1)S(1)}, u32[]{:S(2)}, u32[]{:S(2)}) %all-to-all-start.1) | async-done | bytes 589856 | tf_op jit(solution)/shard_map/all_to_all | solution.py:30
  53.9 6.8 %fusion.110 = (f32[256]{0:T(256)S(1)}, f32[256,8192]{1,0:T(8,128)}) fusion(bf16[256,256]{1,0:T(8,128)(2,1)S(1)} %reshape.592, bf16[8192,256]{1,0:T(8,128)(2,1)} %bitcast.179, pred[8192]{0:T(1024)(128)(4,1)S(1)} %bitcast.199), kind=kOutput, calls=%fused_computation.206 | convolution fusion | flops 1080033024 | bytes 12723200 | tf_op jit(solution)/shard_map/dot_general | solution.py:145
  60.8 6.3 %fusion.8 = f32[256,256]{1,0:T(8,128)S(1)} fusion(bf16[8192,256]{1,0:T(8,128)(2,1)} %bitcast.175, f32[256,8192]{1,0:T(8,128)} %get-tuple-element.125, f32[256]{0:T(256)S(1)} %broadcast_maximum_fusion), kind=kOutput, calls=%fused_computation.13 | convolution fusion | flops 1077936128 | bytes 12846080 | tf_op jit(solution)/shard_map/dot_general | solution.py:158
  67.1 1.1 copy-done
  68.2 1.3 copy-done.1
  69.5 1.4 fusion.24
  71.2 4.8 %fusion.2 = f32[256]{0:T(256)S(1)} fusion(f32[256,8192]{1,0:T(8,128)} %get-tuple-element.125, f32[256]{0:T(256)S(1)} %broadcast_maximum_fusion), kind=kLoop, calls=%fused_computation.8 | loop fusion | flops 4194048 | bytes 8390656 | tf_op jit(solution)/shard_map/reduce_sum | solution.py:155
  78.1 0.7 broadcast.393
  79.4 3.5 %all-to-all-start.2 = ((bf16[4,16,1152]{2,1,0:T(8,128)(2,1)}), bf16[4,16,1152]{2,1,0:T(8,128)(2,1)S(1)}, u32[]{:S(2)}, u32[]{:S(2)}) async-start(bf16[4,16,1152]{2,1,0:T(8,128)(2,1)} %bitcast_dynamic-update-slice_fusion), calls=%async_computation.2 | async-start | bytes 294912 | tf_op jit(solution)/shard_map/all_to_all | solution.py:23
  82.9 4.0 %fusion.111 = (f32[256]{0:T(256)S(1)}, f32[256,8192]{1,0:T(8,128)S(1)}) fusion(bf16[256,256]{1,0:T(8,128)(2,1)S(1)} %reshape.599, bf16[8192,256]{1,0:T(8,128)(2,1)} %bitcast.180, pred[8192]{0:T(1024)(128)(4,1)S(1)} %bitcast.198), kind=kOutput, calls=%fused_computation.207 | convolution fusion | flops 1080033024 | bytes 12723200 | tf_op jit(solution)/shard_map/dot_general | solution.py:145
  87.0 1.4 fusion.6
  88.4 1.6 fusion.23
  90.1 1.3 fusion.5
  92.1 1.3 select_reduce_fusion
  93.4 4.1 %all-to-all-start.3 = ((bf16[16,16,1152]{2,1,0:T(8,128)(2,1)}), bf16[16,16,1152]{2,1,0:T(8,128)(2,1)S(1)}, u32[]{:S(2)}, u32[]{:S(2)}) async-start(bf16[16,16,1152]{2,1,0:T(8,128)(2,1)} %select_reduce_fusion), calls=%async_computation.3 | async-start | bytes 1179648 | tf_op jit(solution)/shard_map/all_to_all | solution.py:30
  98.0 12.3 %all-to-all-done.3 = bf16[16,16,1152]{2,1,0:T(8,128)(2,1)S(1)} async-done(((bf16[16,16,1152]{2,1,0:T(8,128)(2,1)}), bf16[16,16,1152]{2,1,0:T(8,128)(2,1)S(1)}, u32[]{:S(2)}, u32[]{:S(2)}) %all-to-all-start.3) | async-done | bytes 589856 | tf_op jit(solution)/shard_map/all_to_all | solution.py:30
  111.5 3.0 %fusion.113 = f32[32,2048]{1,0:T(8,128)S(1)} fusion(bf16[32,1024]{1,0:T(8,128)(2,1)S(1)} %convert_element_type.260, bf16[1024,2048]{1,0:T(8,128)(2,1)} %param.36), kind=kOutput, calls=%fused_computation.209 | convolution fusion | flops 134217728 | bytes 4521984 | tf_op jit(solution)/shard_map/dot_general | solution.py:245
  114.6 2.3 %collective-permute-start = (f32[32,2048]{1,0:T(8,128)S(1)}, f32[32,2048]{1,0:T(8,128)S(1)}, u32[]{:S(2)}, u32[]{:S(2)}) collective-permute-start(f32[32,2048]{1,0:T(8,128)S(1)} %fusion.113), channel_id=1, source_target_pairs={{0,1},{1,0},{2,3},{3,2},{4,5},{5,4},{6,7},{7,6},{8,9},{9,8},{10,11... | collective-permute-start | bytes 786440 | tf_op jit(solution)/shard_map/ppermute | solution.py:246
  116.9 1.2 collective-permute-done
  118.7 1.1 collective-permute-start.2
  119.8 1.4 collective-permute-start.3
  121.3 5.9 %collective-permute-done.1 = bf16[32,2048]{1,0:T(8,128)(2,1)S(1)} collective-permute-done((bf16[32,2048]{1,0:T(8,128)(2,1)S(1)}, bf16[32,2048]{1,0:T(8,128)(2,1)S(1)}, u32[]{:S(2)}, u32[]{:S(2)}) %collective-permute-start.1) | collective-permute-done | bytes 131104 | tf_op jit(solution)/shard_map/ppermute | solution.py:255
  127.5 3.4 %fusion.12 = f32[128,16,64]{0,2,1:T(8,128)S(1)} fusion(bf16[32,2048]{1,0:T(8,128)(2,1)S(1)} %collective-permute-done.3, bf16[32,2048]{1,0:T(8,128)(2,1)S(1)} %collective-permute-done.2, bf16[32,2048]{1,0:T(8,128)(2,1)S(1)} %collective-permute-done.1, bf16[32,2048]{1,0:T(8,128)(2,1)S(1)} %fusion.34, bf16[16,3,64,2048]{3,2,1,0:T(8,128)(2,1)} %bitcast.216), kind=kOutput, calls=%fused_computation.19 | convolution fusion | flops 538968064 | bytes 5242880 | tf_op jit(solution)/shard_map/dot_general | solution.py:258
  130.9 3.5 %multiply_convert_fusion = bf16[128,16,64]{0,2,1:T(8,128)(2,1)S(1)} fusion(f32[128,16,64]{0,2,1:T(8,128)S(1)} %fusion.12, bf16[32,2048]{1,0:T(8,128)(2,1)S(1)} %collective-permute-done.3, bf16[32,2048]{1,0:T(8,128)(2,1)S(1)} %collective-permute-done.2, bf16[32,2048]{1,0:T(8,128)(2,1)S(1)} %collective-permute-done.1, bf16[32,2048]{1,0:T(8,128)(2,1)S(1)} %fusion.34, ...), kind=kOutput, calls=%fused_computation.56 | convolution fusion | flops 539754496 | bytes 5505024 | tf_op jit(solution)/shard_map/dot_general | solution.py:259
  134.9 3.0 %fusion.17 = f32[4,2,16,2048]{3,2,1,0:T(8,128)S(1)} fusion(bf16[4,2,16,16,64]{4,3,2,1,0:T(8,128)(2,1)S(1)} %bitcast.181, bf16[16,3,64,2048]{3,2,1,0:T(8,128)(2,1)} %bitcast.218), kind=kOutput, calls=%fused_computation.24 | convolution fusion | flops 536870912 | bytes 5505024 | tf_op jit(solution)/shard_map/dot_general | solution.py:262
  137.9 1.6 collective-permute-start.4
  139.6 1.5 collective-permute-done.4
  141.1 2.3 %collective-permute-start.5 = (f32[16,2048]{1,0:T(8,128)S(1)}, f32[16,2048]{1,0:T(8,128)S(1)}, u32[]{:S(2)}, u32[]{:S(2)}) collective-permute-start(f32[16,2048]{1,0:T(8,128)S(1)} %get-tuple-element.97), channel_id=1, source_target_pairs={{0,6},{2,0},{4,2},{6,4},{1,7},{3,1},{5,3},{7,5},{8,14},{10,8},{12,... | collective-permute-start | bytes 393224 | tf_op jit(solution)/shard_map/ppermute | solution.py:272
  144.5 2.1 %collective-permute-done.5 = f32[16,2048]{1,0:T(8,128)S(1)} collective-permute-done((f32[16,2048]{1,0:T(8,128)S(1)}, f32[16,2048]{1,0:T(8,128)S(1)}, u32[]{:S(2)}, u32[]{:S(2)}) %collective-permute-start.5) | collective-permute-done | bytes 131104 | tf_op jit(solution)/shard_map/ppermute | solution.py:272
  146.5 2.9 %collective-permute-done.6 = f32[16,2048]{1,0:T(8,128)S(1)} collective-permute-done((f32[16,2048]{1,0:T(8,128)S(1)}, f32[16,2048]{1,0:T(8,128)S(1)}, u32[]{:S(2)}, u32[]{:S(2)}) %collective-permute-start.6) | collective-permute-done | bytes 131104 | tf_op jit(solution)/shard_map/ppermute | solution.py:272
  149.4 3.2 %collective-permute-done.7 = f32[16,2048]{1,0:T(8,128)S(1)} collective-permute-done((f32[16,2048]{1,0:T(8,128)S(1)}, f32[16,2048]{1,0:T(8,128)S(1)}, u32[]{:S(2)}, u32[]{:S(2)}) %collective-permute-start.7) | collective-permute-done | bytes 131104 | tf_op jit(solution)/shard_map/ppermute | solution.py:272
  152.6 0.9 collective-permute-start.8
  154.6 4.7 %convolution_convert_fusion = bf16[32,1536]{1,0:T(8,128)(2,1)} fusion(bf16[2048,1536]{1,0:T(8,128)(2,1)} %param.41, bf16[32,2048]{1,0:T(8,128)(2,1)S(1)} %get-tuple-element.82, f32[2048]{0:T(1024)S(1)} %convert_element_type.269, f32[32]{0:T(128)S(1)} %add_rsqrt_fusion), kind=kOutput, calls=%fused_computation.27 | convolution fusion | flops 201637888 | bytes 6529152 | tf_op jit(solution)/shard_map/dot_general | solution.py:285
  (135 shorter events, 16.1 us)
Async XLA Ops:
  7.2 103.7 %all-gather.3.cloned.1.call-start = ((), (), s32[]{:S(2)}) async-start(), calls=%async_computation.4 | async-start | bytes 13369344 | tf_op jit(solution)/shard_map/all_gather | solution.py:121
  16.3 16.1 %all-to-all-start = ((bf16[4,16,1152]{2,1,0:T(8,128)(2,1)}), bf16[4,16,1152]{2,1,0:T(8,128)(2,1)S(1)}, u32[]{:S(2)}, u32[]{:S(2)}) async-start(bf16[4,16,1152]{2,1,0:T(8,128)(2,1)} %fusion.64), calls=%async_computation | async-start | bytes 294912 | tf_op jit(solution)/shard_map/all_to_all | solution.py:23
  34.2 17.7 %all-to-all-start.1 = ((bf16[16,16,1152]{2,1,0:T(8,128)(2,1)}), bf16[16,16,1152]{2,1,0:T(8,128)(2,1)S(1)}, u32[]{:S(2)}, u32[]{:S(2)}) async-start(bf16[16,16,1152]{2,1,0:T(8,128)(2,1)} %select_reduce_fusion.1), calls=%async_computation.1 | async-start | bytes 1179648 | tf_op jit(solution)/shard_map/all_to_all | solution.py:30
  60.8 7.4 %copy-start = (f32[256,8192]{1,0:T(8,128)S(1)}, f32[256,8192]{1,0:T(8,128)}, u32[]{:S(2)}) copy-start(f32[256,8192]{1,0:T(8,128)} %get-tuple-element.125) | copy-start | bytes 25165828
  60.8 8.7 %copy-start.1 = (bf16[64,1,128,256]{3,2,1,0:T(8,128)(2,1)S(1)}, bf16[64,1,128,256]{3,2,1,0:T(8,128)(2,1)}, u32[]{:S(2)}) copy-start(bf16[64,1,128,256]{3,2,1,0:T(8,128)(2,1)} %get-tuple-element.95) | copy-start | bytes 12582916
  79.4 12.2 %all-to-all-start.2 = ((bf16[4,16,1152]{2,1,0:T(8,128)(2,1)}), bf16[4,16,1152]{2,1,0:T(8,128)(2,1)S(1)}, u32[]{:S(2)}, u32[]{:S(2)}) async-start(bf16[4,16,1152]{2,1,0:T(8,128)(2,1)} %bitcast_dynamic-update-slice_fusion), calls=%async_computation.2 | async-start | bytes 294912 | tf_op jit(solution)/shard_map/all_to_all | solution.py:23
  82.9 4.0 %copy-start.2 = (bf16[64,1,128,256]{3,2,1,0:T(8,128)(2,1)S(1)}, bf16[64,1,128,256]{3,2,1,0:T(8,128)(2,1)}, u32[]{:S(2)}) copy-start(bf16[64,1,128,256]{3,2,1,0:T(8,128)(2,1)} %get-tuple-element.95) | copy-start | bytes 12582916
  90.0 26.9 %copy-start.6 = (bf16[2048]{0:T(1024)(128)(2,1)S(1)}, bf16[2048]{0:T(1024)(128)(2,1)}, u32[]{:S(2)}) copy-start(bf16[2048]{0:T(1024)(128)(2,1)} %param.37) | copy-start | bytes 12292
  90.0 28.0 %copy-start.5 = (bf16[32,2048]{1,0:T(8,128)(2,1)S(1)}, bf16[32,2048]{1,0:T(8,128)(2,1)}, u32[]{:S(2)}) copy-start(bf16[32,2048]{1,0:T(8,128)(2,1)} %param.26) | copy-start | bytes 393220
  93.4 16.9 %all-to-all-start.3 = ((bf16[16,16,1152]{2,1,0:T(8,128)(2,1)}), bf16[16,16,1152]{2,1,0:T(8,128)(2,1)S(1)}, u32[]{:S(2)}, u32[]{:S(2)}) async-start(bf16[16,16,1152]{2,1,0:T(8,128)(2,1)} %select_reduce_fusion), calls=%async_computation.3 | async-start | bytes 1179648 | tf_op jit(solution)/shard_map/all_to_all | solution.py:30
  114.6 3.5 %collective-permute-start = (f32[32,2048]{1,0:T(8,128)S(1)}, f32[32,2048]{1,0:T(8,128)S(1)}, u32[]{:S(2)}, u32[]{:S(2)}) collective-permute-start(f32[32,2048]{1,0:T(8,128)S(1)} %fusion.113), channel_id=1, source_target_pairs={{0,1},{1,0},{2,3},{3,2},{4,5},{5,4},{6,7},{7,6},{8,9},{9,8},{10,11... | collective-permute-start | bytes 786440 | tf_op jit(solution)/shard_map/ppermute | solution.py:246
  118.3 8.8 %collective-permute-start.1 = (bf16[32,2048]{1,0:T(8,128)(2,1)S(1)}, bf16[32,2048]{1,0:T(8,128)(2,1)S(1)}, u32[]{:S(2)}, u32[]{:S(2)}) collective-permute-start(bf16[32,2048]{1,0:T(8,128)(2,1)S(1)} %fusion.34), channel_id=1, source_target_pairs={{0,2},{2,4},{4,6},{6,0},{1,3},{3,5},{5,7},{7,1},{8,10},{10,12},{12... | collective-permute-start | bytes 393224 | tf_op jit(solution)/shard_map/ppermute | solution.py:255
  118.7 8.5 %collective-permute-start.2 = (bf16[32,2048]{1,0:T(8,128)(2,1)S(1)}, bf16[32,2048]{1,0:T(8,128)(2,1)S(1)}, u32[]{:S(2)}, u32[]{:S(2)}) collective-permute-start(bf16[32,2048]{1,0:T(8,128)(2,1)S(1)} %fusion.34), channel_id=1, source_target_pairs={{0,4},{2,6},{4,0},{6,2},{1,5},{3,7},{5,1},{7,3},{8,12},{10,14},{12... | collective-permute-start | bytes 393224 | tf_op jit(solution)/shard_map/ppermute | solution.py:255
  119.8 7.6 %collective-permute-start.3 = (bf16[32,2048]{1,0:T(8,128)(2,1)S(1)}, bf16[32,2048]{1,0:T(8,128)(2,1)S(1)}, u32[]{:S(2)}, u32[]{:S(2)}) collective-permute-start(bf16[32,2048]{1,0:T(8,128)(2,1)S(1)} %fusion.34), channel_id=1, source_target_pairs={{0,6},{2,0},{4,2},{6,4},{1,7},{3,1},{5,3},{7,5},{8,14},{10,8},{12,... | collective-permute-start | bytes 393224 | tf_op jit(solution)/shard_map/ppermute | solution.py:255
  134.8 4.7 %copy-start.8 = (s32[2]{0:T(128)S(1)}, s32[2]{0:T(128)}, u32[]{:S(2)}) copy-start(s32[2]{0:T(128)} %param.31) | copy-start | bytes 28
  134.8 9.4 %copy-start.4 = (bf16[32,2,256]{2,1,0:T(2,128)(2,1)S(1)}, bf16[32,2,256]{2,1,0:T(2,128)(2,1)}, u32[]{:S(2)}) copy-start(bf16[32,2,256]{2,1,0:T(2,128)(2,1)} %param.28) | copy-start | bytes 98308
  134.8 18.8 %copy-start.7 = (bf16[2048]{0:T(1024)(128)(2,1)S(1)}, bf16[2048]{0:T(1024)(128)(2,1)}, u32[]{:S(2)}) copy-start(bf16[2048]{0:T(1024)(128)(2,1)} %param.40) | copy-start | bytes 12292
  137.9 3.1 %collective-permute-start.4 = (f32[4,16,2048]{2,1,0:T(8,128)S(1)}, f32[4,16,2048]{2,1,0:T(8,128)S(1)}, u32[]{:S(2)}, u32[]{:S(2)}) collective-permute-start(f32[4,16,2048]{2,1,0:T(8,128)S(1)} %dynamic-slice_bitcast_fusion), channel_id=1, source_target_pairs={{0,1},{1,0},{2,3},{3,2},{4,5},{5,4},{6,7},{7,6},{8,9},{9,8},{10,11... | collective-permute-start | bytes 1572872 | tf_op jit(solution)/shard_map/ppermute | solution.py:268
  141.1 5.4 %collective-permute-start.5 = (f32[16,2048]{1,0:T(8,128)S(1)}, f32[16,2048]{1,0:T(8,128)S(1)}, u32[]{:S(2)}, u32[]{:S(2)}) collective-permute-start(f32[16,2048]{1,0:T(8,128)S(1)} %get-tuple-element.97), channel_id=1, source_target_pairs={{0,6},{2,0},{4,2},{6,4},{1,7},{3,1},{5,3},{7,5},{8,14},{10,8},{12,... | collective-permute-start | bytes 393224 | tf_op jit(solution)/shard_map/ppermute | solution.py:272
  143.5 6.0 %collective-permute-start.6 = (f32[16,2048]{1,0:T(8,128)S(1)}, f32[16,2048]{1,0:T(8,128)S(1)}, u32[]{:S(2)}, u32[]{:S(2)}) collective-permute-start(f32[16,2048]{1,0:T(8,128)S(1)} %get-tuple-element.99), channel_id=1, source_target_pairs={{0,4},{2,6},{4,0},{6,2},{1,5},{3,7},{5,1},{7,3},{8,12},{10,14},{12... | collective-permute-start | bytes 393224 | tf_op jit(solution)/shard_map/ppermute | solution.py:272
  143.5 9.1 %collective-permute-start.7 = (f32[16,2048]{1,0:T(8,128)S(1)}, f32[16,2048]{1,0:T(8,128)S(1)}, u32[]{:S(2)}, u32[]{:S(2)}) collective-permute-start(f32[16,2048]{1,0:T(8,128)S(1)} %get-tuple-element.98), channel_id=1, source_target_pairs={{0,2},{2,4},{4,6},{6,0},{1,3},{3,5},{5,7},{7,1},{8,10},{10,12},{12... | collective-permute-start | bytes 393224 | tf_op jit(solution)/shard_map/ppermute | solution.py:272
  152.6 1.8 %collective-permute-start.8 = (bf16[16,2048]{1,0:T(8,128)(2,1)S(1)}, bf16[16,2048]{1,0:T(8,128)(2,1)S(1)}, u32[]{:S(2)}, u32[]{:S(2)}) collective-permute-start(bf16[16,2048]{1,0:T(8,128)(2,1)S(1)} %fusion.47), channel_id=1, source_target_pairs={{0,1},{1,0},{2,3},{3,2},{4,5},{5,4},{6,7},{7,6},{8,9},{9,8},{10,11... | collective-permute-start | bytes 196616 | tf_op jit(solution)/shard_map/ppermute | solution.py:275
  154.6 4.7 %copy-start.3 = (bf16[32,2048]{1,0:T(8,128)(2,1)}, bf16[32,2048]{1,0:T(8,128)(2,1)S(1)}, u32[]{:S(2)}) copy-start(bf16[32,2048]{1,0:T(8,128)(2,1)S(1)} %get-tuple-element.82) | copy-start | bytes 393220
Sparse Core Ops, SparseCore 0:
  10.1 95.3 all-gather.2

commit v16 on v15

--- a/solution.py
+++ b/solution.py
@@ -222,7 +222,7 @@
     )
     tree_scores = jnp.where(allowed, tree_scores, masked_score)
     tree_max = jnp.max(tree_scores, axis=-1)
-    tree_weights = jnp.where(allowed, jnp.exp(tree_scores - tree_max[..., None]), 0.0)
+    tree_weights = jnp.exp(tree_scores - tree_max[..., None])
     tree_total = jnp.sum(tree_weights, axis=-1)
     tree_high = tree_weights.astype(jnp.bfloat16)
     tree_low = (tree_weights - tree_high.astype(jnp.float32)).astype(jnp.bfloat16)

time: 167 us -> 167 us (level)
  no operation moved by 1% of the time
where the time goes in v16:
time: 167 us; the launch traced here: 166 us
  matrix products  42.1 us (25%)
  waiting for transfers between devices  32.8 us (20%)
  starting transfers between devices  30.9 us (19%)
  other arithmetic  21.1 us (13%)
  local copies, waits for them, and re-layouts  20.6 us (12%)
  between operations  18.6 us (11%)
    all_to_all x2, waiting for transfers between devices, route(): arrived = lax.all_to_all(second, ('x', 'y'), 0, 0, tiled=True)  15.8 us
    all_to_all x2, starting transfers between devices, route(): arrived = lax.all_to_all(second, ('x', 'y'), 0, 0, tiled=True)  10.8 us
    dot_general x2, matrix products, attend(): lax.dot_general(spread, key_rows, (((1,), (1,)), ((), ())), preferred_ele...  10.8 us
    all_to_all x2, starting transfers between devices, route(): middle = lax.all_to_all(first, 'z', 0, 0, tiled=True)  9.37 us
    ppermute x3, waiting for transfers between devices, per_device(): mlp_half = mlp_half + lax.ppermute(mine[shift], 'y', perm)  8.12 us
    dot_general x2, matrix products, attend(): jnp.dot(high, value_rows, preferred_element_type=jnp.float32)  7.72 us
    ppermute x3, waiting for transfers between devices, per_device(): shifted.append(lax.ppermute(normed, 'y', perm))  6.2 us
    reduce_sum x2, other arithmetic, attend(): total = total.reshape(rows) * factor + jnp.sum(weights, axis=-1)  6.12 us
  transfers between devices with their start and end apart: 14, of which 10 were waited for; matrix products, arithmetic and copies ran while one was open for 36% of the time, Pallas kernels for 0%

profile of v16, /device:TPU:1, one launch (start us, length us, event | category | flops | bytes accessed | tf_op | source)
XLA Modules:
  0.0 166.2 jit_solution(638883205627964225)
XLA Ops:
  7.2 2.1 %pad_maximum_fusion = bf16[3,64,2048]{2,1,0:T(8,128)(2,1)} fusion(bf16[1,64,2048]{2,1,0:T(8,128)(2,1)} %bitcast.185, bf16[2,64,2048]{2,1,0:T(8,128)(2,1)} %param.38), kind=kLoop, calls=%fused_computation.51 | loop fusion | flops 393216 | bytes 1572864 | tf_op jit(solution)/shard_map/stack | solution.py:120
  13.4 0.7 slice_select_fusion
  14.3 0.8 fusion.102
  16.3 5.9 %all-to-all-start = ((bf16[4,16,1152]{2,1,0:T(8,128)(2,1)}), bf16[4,16,1152]{2,1,0:T(8,128)(2,1)S(1)}, u32[]{:S(2)}, u32[]{:S(2)}) async-start(bf16[4,16,1152]{2,1,0:T(8,128)(2,1)} %fusion.60), calls=%async_computation | async-start | bytes 294912 | tf_op jit(solution)/shard_map/all_to_all | solution.py:23
  22.2 1.0 reshape.605
  23.2 1.0 slice_reduce_fusion
  24.3 0.7 iota_compare_fusion.7
  25.0 1.1 fusion.28
  26.7 1.3 fusion.103
  28.1 0.8 slice_bitcast_fusion.15
  29.0 1.4 fusion.65
  30.3 1.3 and_reduce_fusion
  32.8 1.3 select_reduce_fusion.1
  34.1 6.8 %all-to-all-start.1 = ((bf16[16,16,1152]{2,1,0:T(8,128)(2,1)}), bf16[16,16,1152]{2,1,0:T(8,128)(2,1)S(1)}, u32[]{:S(2)}, u32[]{:S(2)}) async-start(bf16[16,16,1152]{2,1,0:T(8,128)(2,1)} %select_reduce_fusion.1), calls=%async_computation.1 | async-start | bytes 1179648 | tf_op jit(solution)/shard_map/all_to_all | solution.py:30
  42.3 6.0 %fusion.99 = (bf16[64,1,128,256]{3,2,1,0:T(8,128)(2,1)}, bf16[64,1,128,256]{3,2,1,0:T(8,128)(2,1)}) fusion(bf16[64,2,128,256]{3,2,1,0:T(8,128)(2,1)} %param.32), kind=kLoop, calls=%fused_computation.195 | loop fusion | bytes 16777216 | tf_op jit(solution)/shard_map/slice | solution.py:140
  48.4 3.5 %all-to-all-done.1 = bf16[16,16,1152]{2,1,0:T(8,128)(2,1)S(1)} async-done(((bf16[16,16,1152]{2,1,0:T(8,128)(2,1)}), bf16[16,16,1152]{2,1,0:T(8,128)(2,1)S(1)}, u32[]{:S(2)}, u32[]{:S(2)}) %all-to-all-start.1) | async-done | bytes 589856 | tf_op jit(solution)/shard_map/all_to_all | solution.py:30
  53.9 6.8 %fusion.104 = (f32[256]{0:T(256)S(1)}, f32[256,8192]{1,0:T(8,128)}) fusion(bf16[256,256]{1,0:T(8,128)(2,1)S(1)} %reshape.592, bf16[8192,256]{1,0:T(8,128)(2,1)} %bitcast.179, pred[8192]{0:T(1024)(128)(4,1)S(1)} %bitcast.199), kind=kOutput, calls=%fused_computation.200 | convolution fusion | flops 1080033024 | bytes 12723200 | tf_op jit(solution)/shard_map/dot_general | solution.py:145
  60.8 6.3 %fusion.8 = f32[256,256]{1,0:T(8,128)S(1)} fusion(bf16[8192,256]{1,0:T(8,128)(2,1)} %bitcast.175, f32[256,8192]{1,0:T(8,128)} %get-tuple-element.125, f32[256]{0:T(256)S(1)} %broadcast_maximum_fusion), kind=kOutput, calls=%fused_computation.13 | convolution fusion | flops 1077936128 | bytes 12846080 | tf_op jit(solution)/shard_map/dot_general | solution.py:158
  67.1 1.1 copy-done
  68.2 1.3 copy-done.1
  69.5 1.4 fusion.24
  71.2 4.8 %fusion.2 = f32[256]{0:T(256)S(1)} fusion(f32[256,8192]{1,0:T(8,128)} %get-tuple-element.125, f32[256]{0:T(256)S(1)} %broadcast_maximum_fusion), kind=kLoop, calls=%fused_computation.8 | loop fusion | flops 4194048 | bytes 8390656 | tf_op jit(solution)/shard_map/reduce_sum | solution.py:155
  78.1 0.7 broadcast.393
  79.4 3.5 %all-to-all-start.2 = ((bf16[4,16,1152]{2,1,0:T(8,128)(2,1)}), bf16[4,16,1152]{2,1,0:T(8,128)(2,1)S(1)}, u32[]{:S(2)}, u32[]{:S(2)}) async-start(bf16[4,16,1152]{2,1,0:T(8,128)(2,1)} %bitcast_dynamic-update-slice_fusion), calls=%async_computation.2 | async-start | bytes 294912 | tf_op jit(solution)/shard_map/all_to_all | solution.py:23
  82.9 4.0 %fusion.105 = (f32[256]{0:T(256)S(1)}, f32[256,8192]{1,0:T(8,128)S(1)}) fusion(bf16[256,256]{1,0:T(8,128)(2,1)S(1)} %reshape.599, bf16[8192,256]{1,0:T(8,128)(2,1)} %bitcast.180, pred[8192]{0:T(1024)(128)(4,1)S(1)} %bitcast.198), kind=kOutput, calls=%fused_computation.201 | convolution fusion | flops 1080033024 | bytes 12723200 | tf_op jit(solution)/shard_map/dot_general | solution.py:145
  86.9 1.4 fusion.6
  88.4 1.6 fusion.23
  90.0 1.3 fusion.5
  92.1 1.3 select_reduce_fusion
  93.4 4.1 %all-to-all-start.3 = ((bf16[16,16,1152]{2,1,0:T(8,128)(2,1)}), bf16[16,16,1152]{2,1,0:T(8,128)(2,1)S(1)}, u32[]{:S(2)}, u32[]{:S(2)}) async-start(bf16[16,16,1152]{2,1,0:T(8,128)(2,1)} %select_reduce_fusion), calls=%async_computation.3 | async-start | bytes 1179648 | tf_op jit(solution)/shard_map/all_to_all | solution.py:30
  98.0 12.3 %all-to-all-done.3 = bf16[16,16,1152]{2,1,0:T(8,128)(2,1)S(1)} async-done(((bf16[16,16,1152]{2,1,0:T(8,128)(2,1)}), bf16[16,16,1152]{2,1,0:T(8,128)(2,1)S(1)}, u32[]{:S(2)}, u32[]{:S(2)}) %all-to-all-start.3) | async-done | bytes 589856 | tf_op jit(solution)/shard_map/all_to_all | solution.py:30
  111.5 3.0 %fusion.107 = f32[32,2048]{1,0:T(8,128)S(1)} fusion(bf16[32,1024]{1,0:T(8,128)(2,1)S(1)} %convert_element_type.260, bf16[1024,2048]{1,0:T(8,128)(2,1)} %param.36), kind=kOutput, calls=%fused_computation.203 | convolution fusion | flops 134217728 | bytes 4521984 | tf_op jit(solution)/shard_map/dot_general | solution.py:245
  114.5 2.3 %collective-permute-start = (f32[32,2048]{1,0:T(8,128)S(1)}, f32[32,2048]{1,0:T(8,128)S(1)}, u32[]{:S(2)}, u32[]{:S(2)}) collective-permute-start(f32[32,2048]{1,0:T(8,128)S(1)} %fusion.107), channel_id=1, source_target_pairs={{0,1},{1,0},{2,3},{3,2},{4,5},{5,4},{6,7},{7,6},{8,9},{9,8},{10,11... | collective-permute-start | bytes 786440 | tf_op jit(solution)/shard_map/ppermute | solution.py:246
  116.9 1.2 collective-permute-done
  118.7 1.1 collective-permute-start.2
  119.8 1.4 collective-permute-start.3
  121.3 5.9 %collective-permute-done.1 = bf16[32,2048]{1,0:T(8,128)(2,1)S(1)} collective-permute-done((bf16[32,2048]{1,0:T(8,128)(2,1)S(1)}, bf16[32,2048]{1,0:T(8,128)(2,1)S(1)}, u32[]{:S(2)}, u32[]{:S(2)}) %collective-permute-start.1) | collective-permute-done | bytes 131104 | tf_op jit(solution)/shard_map/ppermute | solution.py:255
  127.5 3.4 %fusion.12 = f32[128,16,64]{0,2,1:T(8,128)S(1)} fusion(bf16[32,2048]{1,0:T(8,128)(2,1)S(1)} %collective-permute-done.3, bf16[32,2048]{1,0:T(8,128)(2,1)S(1)} %collective-permute-done.2, bf16[32,2048]{1,0:T(8,128)(2,1)S(1)} %collective-permute-done.1, bf16[32,2048]{1,0:T(8,128)(2,1)S(1)} %fusion.34, bf16[16,3,64,2048]{3,2,1,0:T(8,128)(2,1)} %bitcast.216), kind=kOutput, calls=%fused_computation.19 | convolution fusion | flops 538968064 | bytes 5242880 | tf_op jit(solution)/shard_map/dot_general | solution.py:258
  130.9 3.5 %multiply_convert_fusion = bf16[128,16,64]{0,2,1:T(8,128)(2,1)S(1)} fusion(f32[128,16,64]{0,2,1:T(8,128)S(1)} %fusion.12, bf16[32,2048]{1,0:T(8,128)(2,1)S(1)} %collective-permute-done.3, bf16[32,2048]{1,0:T(8,128)(2,1)S(1)} %collective-permute-done.2, bf16[32,2048]{1,0:T(8,128)(2,1)S(1)} %collective-permute-done.1, bf16[32,2048]{1,0:T(8,128)(2,1)S(1)} %fusion.34, ...), kind=kOutput, calls=%fused_computation.56 | convolution fusion | flops 539754496 | bytes 5505024 | tf_op jit(solution)/shard_map/dot_general | solution.py:259
  134.8 3.0 %fusion.17 = f32[4,2,16,2048]{3,2,1,0:T(8,128)S(1)} fusion(bf16[4,2,16,16,64]{4,3,2,1,0:T(8,128)(2,1)S(1)} %bitcast.181, bf16[16,3,64,2048]{3,2,1,0:T(8,128)(2,1)} %bitcast.218), kind=kOutput, calls=%fused_computation.24 | convolution fusion | flops 536870912 | bytes 5505024 | tf_op jit(solution)/shard_map/dot_general | solution.py:262
  137.9 1.6 collective-permute-start.4
  139.5 1.5 collective-permute-done.4
  141.1 2.3 %collective-permute-start.5 = (f32[16,2048]{1,0:T(8,128)S(1)}, f32[16,2048]{1,0:T(8,128)S(1)}, u32[]{:S(2)}, u32[]{:S(2)}) collective-permute-start(f32[16,2048]{1,0:T(8,128)S(1)} %get-tuple-element.97), channel_id=1, source_target_pairs={{0,6},{2,0},{4,2},{6,4},{1,7},{3,1},{5,3},{7,5},{8,14},{10,8},{12,... | collective-permute-start | bytes 393224 | tf_op jit(solution)/shard_map/ppermute | solution.py:272
  144.4 2.1 %collective-permute-done.5 = f32[16,2048]{1,0:T(8,128)S(1)} collective-permute-done((f32[16,2048]{1,0:T(8,128)S(1)}, f32[16,2048]{1,0:T(8,128)S(1)}, u32[]{:S(2)}, u32[]{:S(2)}) %collective-permute-start.5) | collective-permute-done | bytes 131104 | tf_op jit(solution)/shard_map/ppermute | solution.py:272
  146.5 2.9 %collective-permute-done.6 = f32[16,2048]{1,0:T(8,128)S(1)} collective-permute-done((f32[16,2048]{1,0:T(8,128)S(1)}, f32[16,2048]{1,0:T(8,128)S(1)}, u32[]{:S(2)}, u32[]{:S(2)}) %collective-permute-start.6) | collective-permute-done | bytes 131104 | tf_op jit(solution)/shard_map/ppermute | solution.py:272
  149.4 3.2 %collective-permute-done.7 = f32[16,2048]{1,0:T(8,128)S(1)} collective-permute-done((f32[16,2048]{1,0:T(8,128)S(1)}, f32[16,2048]{1,0:T(8,128)S(1)}, u32[]{:S(2)}, u32[]{:S(2)}) %collective-permute-start.7) | collective-permute-done | bytes 131104 | tf_op jit(solution)/shard_map/ppermute | solution.py:272
  152.6 0.9 collective-permute-start.8
  154.6 4.7 %convolution_convert_fusion = bf16[32,1536]{1,0:T(8,128)(2,1)} fusion(bf16[2048,1536]{1,0:T(8,128)(2,1)} %param.41, bf16[32,2048]{1,0:T(8,128)(2,1)S(1)} %get-tuple-element.82, f32[2048]{0:T(1024)S(1)} %convert_element_type.269, f32[32]{0:T(128)S(1)} %add_rsqrt_fusion), kind=kOutput, calls=%fused_computation.27 | convolution fusion | flops 201637888 | bytes 6529152 | tf_op jit(solution)/shard_map/dot_general | solution.py:285
  (135 shorter events, 16.1 us)
Async XLA Ops:
  7.2 103.6 %all-gather.3.cloned.1.call-start = ((), (), s32[]{:S(2)}) async-start(), calls=%async_computation.4 | async-start | bytes 13369344 | tf_op jit(solution)/shard_map/all_gather | solution.py:121
  16.3 16.1 %all-to-all-start = ((bf16[4,16,1152]{2,1,0:T(8,128)(2,1)}), bf16[4,16,1152]{2,1,0:T(8,128)(2,1)S(1)}, u32[]{:S(2)}, u32[]{:S(2)}) async-start(bf16[4,16,1152]{2,1,0:T(8,128)(2,1)} %fusion.60), calls=%async_computation | async-start | bytes 294912 | tf_op jit(solution)/shard_map/all_to_all | solution.py:23
  34.1 17.7 %all-to-all-start.1 = ((bf16[16,16,1152]{2,1,0:T(8,128)(2,1)}), bf16[16,16,1152]{2,1,0:T(8,128)(2,1)S(1)}, u32[]{:S(2)}, u32[]{:S(2)}) async-start(bf16[16,16,1152]{2,1,0:T(8,128)(2,1)} %select_reduce_fusion.1), calls=%async_computation.1 | async-start | bytes 1179648 | tf_op jit(solution)/shard_map/all_to_all | solution.py:30
  60.8 7.4 %copy-start = (f32[256,8192]{1,0:T(8,128)S(1)}, f32[256,8192]{1,0:T(8,128)}, u32[]{:S(2)}) copy-start(f32[256,8192]{1,0:T(8,128)} %get-tuple-element.125) | copy-start | bytes 25165828
  60.8 8.7 %copy-start.1 = (bf16[64,1,128,256]{3,2,1,0:T(8,128)(2,1)S(1)}, bf16[64,1,128,256]{3,2,1,0:T(8,128)(2,1)}, u32[]{:S(2)}) copy-start(bf16[64,1,128,256]{3,2,1,0:T(8,128)(2,1)} %get-tuple-element.95) | copy-start | bytes 12582916
  79.4 12.2 %all-to-all-start.2 = ((bf16[4,16,1152]{2,1,0:T(8,128)(2,1)}), bf16[4,16,1152]{2,1,0:T(8,128)(2,1)S(1)}, u32[]{:S(2)}, u32[]{:S(2)}) async-start(bf16[4,16,1152]{2,1,0:T(8,128)(2,1)} %bitcast_dynamic-update-slice_fusion), calls=%async_computation.2 | async-start | bytes 294912 | tf_op jit(solution)/shard_map/all_to_all | solution.py:23
  82.9 4.0 %copy-start.2 = (bf16[64,1,128,256]{3,2,1,0:T(8,128)(2,1)S(1)}, bf16[64,1,128,256]{3,2,1,0:T(8,128)(2,1)}, u32[]{:S(2)}) copy-start(bf16[64,1,128,256]{3,2,1,0:T(8,128)(2,1)} %get-tuple-element.95) | copy-start | bytes 12582916
  90.0 26.8 %copy-start.6 = (bf16[2048]{0:T(1024)(128)(2,1)S(1)}, bf16[2048]{0:T(1024)(128)(2,1)}, u32[]{:S(2)}) copy-start(bf16[2048]{0:T(1024)(128)(2,1)} %param.37) | copy-start | bytes 12292
  90.0 28.0 %copy-start.5 = (bf16[32,2048]{1,0:T(8,128)(2,1)S(1)}, bf16[32,2048]{1,0:T(8,128)(2,1)}, u32[]{:S(2)}) copy-start(bf16[32,2048]{1,0:T(8,128)(2,1)} %param.26) | copy-start | bytes 393220
  93.4 16.9 %all-to-all-start.3 = ((bf16[16,16,1152]{2,1,0:T(8,128)(2,1)}), bf16[16,16,1152]{2,1,0:T(8,128)(2,1)S(1)}, u32[]{:S(2)}, u32[]{:S(2)}) async-start(bf16[16,16,1152]{2,1,0:T(8,128)(2,1)} %select_reduce_fusion), calls=%async_computation.3 | async-start | bytes 1179648 | tf_op jit(solution)/shard_map/all_to_all | solution.py:30
  114.5 3.5 %collective-permute-start = (f32[32,2048]{1,0:T(8,128)S(1)}, f32[32,2048]{1,0:T(8,128)S(1)}, u32[]{:S(2)}, u32[]{:S(2)}) collective-permute-start(f32[32,2048]{1,0:T(8,128)S(1)} %fusion.107), channel_id=1, source_target_pairs={{0,1},{1,0},{2,3},{3,2},{4,5},{5,4},{6,7},{7,6},{8,9},{9,8},{10,11... | collective-permute-start | bytes 786440 | tf_op jit(solution)/shard_map/ppermute | solution.py:246
  118.3 8.8 %collective-permute-start.1 = (bf16[32,2048]{1,0:T(8,128)(2,1)S(1)}, bf16[32,2048]{1,0:T(8,128)(2,1)S(1)}, u32[]{:S(2)}, u32[]{:S(2)}) collective-permute-start(bf16[32,2048]{1,0:T(8,128)(2,1)S(1)} %fusion.34), channel_id=1, source_target_pairs={{0,2},{2,4},{4,6},{6,0},{1,3},{3,5},{5,7},{7,1},{8,10},{10,12},{12... | collective-permute-start | bytes 393224 | tf_op jit(solution)/shard_map/ppermute | solution.py:255
  118.7 8.5 %collective-permute-start.2 = (bf16[32,2048]{1,0:T(8,128)(2,1)S(1)}, bf16[32,2048]{1,0:T(8,128)(2,1)S(1)}, u32[]{:S(2)}, u32[]{:S(2)}) collective-permute-start(bf16[32,2048]{1,0:T(8,128)(2,1)S(1)} %fusion.34), channel_id=1, source_target_pairs={{0,4},{2,6},{4,0},{6,2},{1,5},{3,7},{5,1},{7,3},{8,12},{10,14},{12... | collective-permute-start | bytes 393224 | tf_op jit(solution)/shard_map/ppermute | solution.py:255
  119.8 7.6 %collective-permute-start.3 = (bf16[32,2048]{1,0:T(8,128)(2,1)S(1)}, bf16[32,2048]{1,0:T(8,128)(2,1)S(1)}, u32[]{:S(2)}, u32[]{:S(2)}) collective-permute-start(bf16[32,2048]{1,0:T(8,128)(2,1)S(1)} %fusion.34), channel_id=1, source_target_pairs={{0,6},{2,0},{4,2},{6,4},{1,7},{3,1},{5,3},{7,5},{8,14},{10,8},{12,... | collective-permute-start | bytes 393224 | tf_op jit(solution)/shard_map/ppermute | solution.py:255
  134.8 4.7 %copy-start.8 = (s32[2]{0:T(128)S(1)}, s32[2]{0:T(128)}, u32[]{:S(2)}) copy-start(s32[2]{0:T(128)} %param.31) | copy-start | bytes 28
  134.8 9.4 %copy-start.4 = (bf16[32,2,256]{2,1,0:T(2,128)(2,1)S(1)}, bf16[32,2,256]{2,1,0:T(2,128)(2,1)}, u32[]{:S(2)}) copy-start(bf16[32,2,256]{2,1,0:T(2,128)(2,1)} %param.28) | copy-start | bytes 98308
  134.8 18.8 %copy-start.7 = (bf16[2048]{0:T(1024)(128)(2,1)S(1)}, bf16[2048]{0:T(1024)(128)(2,1)}, u32[]{:S(2)}) copy-start(bf16[2048]{0:T(1024)(128)(2,1)} %param.40) | copy-start | bytes 12292
  137.9 3.1 %collective-permute-start.4 = (f32[4,16,2048]{2,1,0:T(8,128)S(1)}, f32[4,16,2048]{2,1,0:T(8,128)S(1)}, u32[]{:S(2)}, u32[]{:S(2)}) collective-permute-start(f32[4,16,2048]{2,1,0:T(8,128)S(1)} %dynamic-slice_bitcast_fusion), channel_id=1, source_target_pairs={{0,1},{1,0},{2,3},{3,2},{4,5},{5,4},{6,7},{7,6},{8,9},{9,8},{10,11... | collective-permute-start | bytes 1572872 | tf_op jit(solution)/shard_map/ppermute | solution.py:268
  141.1 5.4 %collective-permute-start.5 = (f32[16,2048]{1,0:T(8,128)S(1)}, f32[16,2048]{1,0:T(8,128)S(1)}, u32[]{:S(2)}, u32[]{:S(2)}) collective-permute-start(f32[16,2048]{1,0:T(8,128)S(1)} %get-tuple-element.97), channel_id=1, source_target_pairs={{0,6},{2,0},{4,2},{6,4},{1,7},{3,1},{5,3},{7,5},{8,14},{10,8},{12,... | collective-permute-start | bytes 393224 | tf_op jit(solution)/shard_map/ppermute | solution.py:272
  143.4 6.0 %collective-permute-start.6 = (f32[16,2048]{1,0:T(8,128)S(1)}, f32[16,2048]{1,0:T(8,128)S(1)}, u32[]{:S(2)}, u32[]{:S(2)}) collective-permute-start(f32[16,2048]{1,0:T(8,128)S(1)} %get-tuple-element.99), channel_id=1, source_target_pairs={{0,4},{2,6},{4,0},{6,2},{1,5},{3,7},{5,1},{7,3},{8,12},{10,14},{12... | collective-permute-start | bytes 393224 | tf_op jit(solution)/shard_map/ppermute | solution.py:272
  143.4 9.1 %collective-permute-start.7 = (f32[16,2048]{1,0:T(8,128)S(1)}, f32[16,2048]{1,0:T(8,128)S(1)}, u32[]{:S(2)}, u32[]{:S(2)}) collective-permute-start(f32[16,2048]{1,0:T(8,128)S(1)} %get-tuple-element.98), channel_id=1, source_target_pairs={{0,2},{2,4},{4,6},{6,0},{1,3},{3,5},{5,7},{7,1},{8,10},{10,12},{12... | collective-permute-start | bytes 393224 | tf_op jit(solution)/shard_map/ppermute | solution.py:272
  152.6 1.8 %collective-permute-start.8 = (bf16[16,2048]{1,0:T(8,128)(2,1)S(1)}, bf16[16,2048]{1,0:T(8,128)(2,1)S(1)}, u32[]{:S(2)}, u32[]{:S(2)}) collective-permute-start(bf16[16,2048]{1,0:T(8,128)(2,1)S(1)} %fusion.47), channel_id=1, source_target_pairs={{0,1},{1,0},{2,3},{3,2},{4,5},{5,4},{6,7},{7,6},{8,9},{9,8},{10,11... | collective-permute-start | bytes 196616 | tf_op jit(solution)/shard_map/ppermute | solution.py:275
  154.6 4.7 %copy-start.3 = (bf16[32,2048]{1,0:T(8,128)(2,1)}, bf16[32,2048]{1,0:T(8,128)(2,1)S(1)}, u32[]{:S(2)}) copy-start(bf16[32,2048]{1,0:T(8,128)(2,1)S(1)} %get-tuple-element.82) | copy-start | bytes 393220
Sparse Core Ops, SparseCore 0:
  10.1 95.2 all-gather.2
